TPU v7x, 256 devices: a whole 4x4x8 slice. The times are simulated.
256 devices in a mesh: lon: 32 (over z, x_hi, core), lat: 8 (over y, x_lo).
Axes of the slice: x: 4 (x_hi: 2, x_lo: 2; x = x_hi * 2 + x_lo), y: 4, z: 8, core: 2. Of those that a mesh axis runs over, the one named last changes fastest.
Arguments:
- inputs: bfloat16 [384, 1536, 128], P('lat', 'lon'), may hold values from -6 to 6
- weight: bfloat16 [3, 3, 128, 128], replicated, may hold values from -0.1875 to 0.1875
- bias: float32 [128], replicated, may hold values from -3 to 3
- cotangent: bfloat16 [384, 1536, 128], P('lat', 'lon'), may hold values from -6 to 6
Outputs:
- outputs: bfloat16 [384, 1536, 128], P('lat', 'lon')
- input_grad: bfloat16 [384, 1536, 128], P('lat', 'lon')
- weight_grad: float32 [3, 3, 128, 128], replicated
- bias_grad: float32 [128], replicated
All inputs are finite; a program needn't handle non-finite values.
Results may differ from a plain program's by a relative error of at most 0.006.
Values may be sent and summed in bfloat16 or wider, within the bound.
No kernel may reach another device: no remote copies, remote signals or barrier semaphores. Data moves between devices by JAX's collectives and lax.ppermute only.
A program may use at most 64 MiB of HBM per device.

v0:
```python
import jax
import jax.numpy as jnp
from jax import lax
from jax.sharding import PartitionSpec as P


def extended(cells, sides, width, closed):
    for axis, dim in sides:
        count = lax.axis_size(axis)
        ends = count if closed else count - 1
        head = lax.slice_in_dim(cells, 0, width, axis=dim)
        tail = lax.slice_in_dim(cells, cells.shape[dim] - width, cells.shape[dim], axis=dim)
        cells = jnp.concatenate(
            [
                lax.ppermute(tail, axis, [(i, (i + 1) % count) for i in range(ends)]),
                cells,
                lax.ppermute(head, axis, [((i + 1) % count, i) for i in range(ends)]),
            ],
            axis=dim,
        )
    return cells


def from_behind(value, axis, steps):
    count = lax.axis_size(axis)
    pairs = [(source, (source + steps) % count) for source in range(count)]
    return lax.ppermute(value, axis, pairs)


def shards(inputs, weight, bias, cotangent):
    rows, cols, chans = inputs.shape
    band = lax.axis_index("lat")
    bands = lax.axis_size("lat")
    half = lax.axis_size("lon") // 2
    wide = extended(inputs, (("lon", 1),), 1, True)
    tall = extended(wide, (("lat", 0),), 1, False)
    far_top, far_bottom = from_behind((wide[0], wide[-1]), "lon", half)
    top = jnp.where(band == 0, far_top, tall[0])
    bottom = jnp.where(band == bands - 1, far_bottom, tall[-1])
    padded = jnp.concatenate([top[None], tall[1:-1], bottom[None]], axis=0)
    pre = jnp.zeros((rows * cols, chans), jnp.float32) + bias[None, :]
    for tap_a in range(3):
        for tap_b in range(3):
            window = padded[tap_a : tap_a + rows, tap_b : tap_b + cols].reshape(rows * cols, chans)
            pre = pre + jnp.dot(window, weight[tap_a, tap_b], preferred_element_type=jnp.float32)
    sig = jax.nn.sigmoid(pre)
    outputs = (pre * sig).astype(jnp.bfloat16).reshape(rows, cols, chans)
    flat_cot = cotangent.reshape(rows * cols, chans).astype(jnp.float32)
    pre_grad = (flat_cot * sig * (1.0 + pre * (1.0 - sig))).astype(jnp.bfloat16)
    padded_grad = jnp.zeros((rows + 2, cols + 2, chans), jnp.float32)
    taps = []
    for tap_a in range(3):
        for tap_b in range(3):
            back = jnp.dot(pre_grad, weight[tap_a, tap_b].T, preferred_element_type=jnp.float32)
            padded_grad = padded_grad.at[tap_a : tap_a + rows, tap_b : tap_b + cols].add(
                back.reshape(rows, cols, chans)
            )
            window = padded[tap_a : tap_a + rows, tap_b : tap_b + cols].reshape(rows * cols, chans)
            taps.append(
                lax.dot_general(
                    window, pre_grad, (((0,), (0,)), ((), ())), preferred_element_type=jnp.float32
                )
            )
    kernel_terms = jnp.concatenate(taps, axis=0)
    bias_terms = jnp.sum(pre_grad.astype(jnp.float32), axis=0)[None, :]
    edges = jnp.stack([padded_grad[0], padded_grad[-1]], axis=0)
    beside_all = extended(edges.astype(jnp.bfloat16), (("lat", 0),), 1, False).astype(edges.dtype)
    polar_top, polar_bottom = (
        from_behind(padded_grad[0].astype(jnp.bfloat16), "lon", half).astype(jnp.float32),
        from_behind(padded_grad[-1].astype(jnp.bfloat16), "lon", half).astype(jnp.float32),
    )
    inner = padded_grad[1:-1]
    inner = inner.at[0].add(beside_all[0] + jnp.where(band == 0, polar_top, 0.0))
    inner = inner.at[-1].add(beside_all[3] + jnp.where(band == bands - 1, polar_bottom, 0.0))
    sides = jnp.stack([inner[:, 0], inner[:, -1]], axis=1)
    beside = extended(sides.astype(jnp.bfloat16), (("lon", 1),), 1, True).astype(sides.dtype)
    core = inner[:, 1:-1]
    core = core.at[:, 0].add(beside[:, 0])
    core = core.at[:, -1].add(beside[:, 3])
    input_grad = core.astype(jnp.bfloat16)
    kernel_sum, bias_sum = lax.psum((kernel_terms, bias_terms), ("lon", "lat"))
    total_cells = rows * cols * lax.axis_size("lon") * lax.axis_size("lat")
    scale = 1.0 / jnp.sqrt(jnp.float32(total_cells))
    weight_grad = kernel_sum.reshape(3, 3, chans, chans) * scale
    bias_grad = bias_sum[0] * scale
    return (outputs, input_grad, weight_grad, bias_grad)


def solution(mesh):
    in_specs = (P("lat", "lon", None), P(), P(), P("lat", "lon", None))
    out_specs = (P("lat", "lon", None), P("lat", "lon", None), P(), P())
    return jax.shard_map(shards, mesh=mesh, in_specs=in_specs, out_specs=out_specs, check_vma=False)
```

profile of v0, /device:TPU:1, one launch (start us, length us, event | category | flops | bytes accessed | tf_op | source)
XLA Modules:
  0.0 389.1 jit_solution(4786037038212972449)
XLA Ops:
  7.2 1.0 fusion.60
  8.3 4.2 %collective-permute-start = (bf16[48,1,128]{2,1,0:T(2,128)(2,1)S(1)}, bf16[48,1,128]{2,1,0:T(2,128)(2,1)S(1)}, u32[]{:S(2)}, u32[]{:S(2)}) collective-permute-start(bf16[48,1,128]{2,1,0:T(2,128)(2,1)S(1)} %get-tuple-element.179), channel_id=1, source_target_pairs={{0,8},{8,16},{16,24},{24,32},{32,40},{40,48},{48,56},{56,64},{64,7... | collective-permute-start | bytes 36872 | tf_op jit(solution)/shard_map/ppermute | solution.py:15
  12.5 0.7 fusion.61
  13.1 1.4 fusion.22
  14.5 0.7 and_reduce_fusion
  15.2 0.6 fusion.62
  15.8 1.4 collective-permute-done.1
  17.3 2.2 collective-permute-start.3
  19.5 7.0 %collective-permute-start.4 = (bf16[50,128]{1,0:T(8,128)(2,1)S(1)}, bf16[50,128]{1,0:T(8,128)(2,1)S(1)}, u32[]{:S(2)}, u32[]{:S(2)}) collective-permute-start(bf16[50,128]{1,0:T(8,128)(2,1)S(1)} %bitcast.196), channel_id=1, source_target_pairs={{0,128},{8,136},{16,144},{24,152},{32,160},{40,168},{48,176},{56,1... | collective-permute-start | bytes 38408 | tf_op jit(solution)/shard_map/ppermute | solution.py:27
  26.5 1.3 collective-permute-start.5
  28.1 0.5 pad_maximum_fusion.1
  28.6 3.0 collective-permute-done.5
  31.7 2.9 collective-permute-done.2
  34.5 0.5 maximum_maximum_fusion
  35.0 0.7 fusion.57
  38.3 0.7 copy-done.5
  39.0 1.6 convert_reduce_fusion
  40.6 1.0 convolution_dynamic-update-slice_fusion.7
  41.6 1.0 convolution_dynamic-update-slice_fusion.6
  42.6 1.0 convolution_dynamic-update-slice_fusion.5
  43.6 1.0 convolution_dynamic-update-slice_fusion.4
  44.6 1.0 fusion.6
  45.6 1.0 convolution_dynamic-update-slice_fusion.3
  46.6 1.0 convolution_dynamic-update-slice_fusion.2
  47.6 1.0 convolution_dynamic-update-slice_fusion.1
  49.0 1.6 convolution_add_fusion.13
  50.6 10.7 %scatter-add.45 = f32[50,50,128]{2,1,0:T(8,128)S(1)} dynamic-update-slice(f32[50,50,128]{2,1,0:T(8,128)S(1)} %scatter-add.44, f32[48,48,128]{2,1,0:T(8,128)S(1)} %convolution_add_fusion.13, s32[]{:T(128)} %bitcast.28, s32[]{:T(128)} %bitcast.29, s32[]{:T(128)} %constant.375.clone.1) | dynamic-update-slice | bytes 2359300 | tf_op jit(solution)/shard_map/scatter-add | solution.py:55
  61.3 2.2 add_select_fusion
  63.5 10.7 %scatter-add.46 = f32[50,50,128]{2,1,0:T(8,128)S(1)} dynamic-update-slice(f32[50,50,128]{2,1,0:T(8,128)S(1)} %scatter-add.45, f32[48,48,128]{2,1,0:T(8,128)S(1)} %add_select_fusion, s32[]{:T(128)} %bitcast.31, s32[]{:T(128)} %bitcast.32, s32[]{:T(128)} %constant.375.clone.1) | dynamic-update-slice | bytes 2359300 | tf_op jit(solution)/shard_map/scatter-add | solution.py:55
  74.2 0.3 fusion.3
  74.9 9.3 %scatter-add.50 = f32[50,50,128]{2,1,0:T(8,128)S(1)} dynamic-update-slice(f32[50,50,128]{2,1,0:T(8,128)S(1)} %fusion.3, f32[48,48,128]{2,1,0:T(8,128)S(1)} %convolution_add_fusion.11, s32[]{:T(128)} %constant.383.clone.1, s32[]{:T(128)} %constant.383.clone.1, s32[]{:T(128)} %constant.375.clone.1) | dynamic-update-slice | bytes 2359300 | tf_op jit(solution)/shard_map/scatter-add | solution.py:55
  84.5 9.3 %scatter-add.51 = f32[50,50,128]{2,1,0:T(8,128)S(1)} dynamic-update-slice(f32[50,50,128]{2,1,0:T(8,128)S(1)} %scatter-add.50, f32[48,48,128]{2,1,0:T(8,128)S(1)} %convolution_add_fusion.10, s32[]{:T(128)} %constant.383.clone.1, s32[]{:T(128)} %constant.379.clone.1, s32[]{:T(128)} %constant.375.clone.1) | dynamic-update-slice | bytes 2359300 | tf_op jit(solution)/shard_map/scatter-add | solution.py:55
  93.8 0.3 fusion.2
  94.1 0.3 convolution_add_fusion.8
  94.4 9.2 %scatter-add.55 = f32[50,50,128]{2,1,0:T(8,128)S(1)} dynamic-update-slice(f32[50,50,128]{2,1,0:T(8,128)S(1)} %fusion.2, f32[48,48,128]{2,1,0:T(8,128)S(1)} %convolution_add_fusion.8, s32[]{:T(128)} %constant.379.clone.1, s32[]{:T(128)} %constant.383.clone.1, s32[]{:T(128)} %constant.375.clone.1) | dynamic-update-slice | bytes 2359300 | tf_op jit(solution)/shard_map/scatter-add | solution.py:55
  103.9 9.2 %scatter-add.56 = f32[50,50,128]{2,1,0:T(8,128)S(1)} dynamic-update-slice(f32[50,50,128]{2,1,0:T(8,128)S(1)} %scatter-add.55, f32[48,48,128]{2,1,0:T(8,128)S(1)} %convolution_add_fusion.7, s32[]{:T(128)} %constant.379.clone.1, s32[]{:T(128)} %constant.379.clone.1, s32[]{:T(128)} %constant.375.clone.1) | dynamic-update-slice | bytes 2359300 | tf_op jit(solution)/shard_map/scatter-add | solution.py:55
  113.1 4.7 %collective-permute-start.6 = (bf16[1,50,128]{2,1,0:T(8,128)(2,1)S(1)}, bf16[1,50,128]{2,1,0:T(8,128)(2,1)S(1)}, u32[]{:S(2)}, u32[]{:S(2)}) collective-permute-start(bf16[1,50,128]{2,1,0:T(8,128)(2,1)S(1)} %get-tuple-element.162), channel_id=1, source_target_pairs={{0,1},{1,2},{2,3},{3,4},{4,5},{5,6},{6,7},{8,9},{9,10},{10,11},{11... | collective-permute-start | bytes 38408 | tf_op jit(solution)/shard_map/ppermute | solution.py:15
  117.8 1.3 collective-permute-start.7
  119.4 2.1 convolution_dynamic-update-slice_fusion
  121.5 5.3 %collective-permute-start.9 = (bf16[50,128]{1,0:T(8,128)(2,1)S(1)}, bf16[50,128]{1,0:T(8,128)(2,1)S(1)}, u32[]{:S(2)}, u32[]{:S(2)}) collective-permute-start(bf16[50,128]{1,0:T(8,128)(2,1)S(1)} %bitcast.194), channel_id=1, source_target_pairs={{0,128},{8,136},{16,144},{24,152},{32,160},{40,168},{48,176},{56,1... | collective-permute-start | bytes 38408 | tf_op jit(solution)/shard_map/ppermute | solution.py:27
  126.8 81.0 %psum.15 = f32[1,128]{1,0:T(1,128)S(1)} all-reduce(f32[1,128]{1,0:T(1,128)S(1)} %bitcast.199), channel_id=1, replica_groups=mesh['lon'=32,'lat'=8] {'lon','lat'}, use_global_device_ids=true, to_apply=%region_3.4 | all-reduce | flops 128 | bytes 1024 | tf_op jit(solution)/shard_map/psum | solution.py:81
  208.0 1.8 collective-permute-start.10
  209.8 0.5 multiply_bitcast_fusion
  210.4 0.3 collective-permute-done.10
  210.8 4.1 %collective-permute-done.11 = bf16[48,1,128]{2,1,0:T(2,128)(2,1)S(1)} collective-permute-done((bf16[48,1,128]{2,1,0:T(2,128)(2,1)S(1)}, bf16[48,1,128]{2,1,0:T(2,128)(2,1)S(1)}, u32[]{:S(2)}, u32[]{:S(2)}) %collective-permute-start.11) | collective-permute-done | bytes 12320 | tf_op jit(solution)/shard_map/ppermute | solution.py:17
  215.4 0.9 convert_element_type.50
  216.3 164.0 %all-reduce.3.cloned.1.call-done = f32[1152,128]{1,0:T(8,128)} async-done(((f32[1152,128]{1,0:T(8,128)}), f32[1152,128]{1,0:T(8,128)}) %all-reduce.3.cloned.1.call-update) | async-done | bytes 589840 | tf_op jit(solution)/shard_map/psum | solution.py:81
  380.3 1.9 broadcast_multiply_fusion
  (52 shorter events, 5.4 us)
Async XLA Ops:
  7.2 7.3 %copy-start.3 = (s32[3]{0:T(128)S(1)}, s32[3]{0:T(128)}, u32[]{:S(2)}) copy-start(s32[3]{0:T(128)} %constant.381.clone.1) | copy-start | bytes 40
  7.2 10.1 %copy-start = (bf16[48,48,128]{2,1,0:T(8,128)(2,1)S(1)}, bf16[48,48,128]{2,1,0:T(8,128)(2,1)}, u32[]{:S(2)}) copy-start(bf16[48,48,128]{2,1,0:T(8,128)(2,1)} %param.30) | copy-start | bytes 1769476
  7.2 373.1 %all-reduce.3.cloned.1.call-start = ((), (), s32[]{:S(2)}) async-start(), calls=%async_computation | async-start | bytes 1179648 | tf_op jit(solution)/shard_map/psum | solution.py:81
  8.3 7.6 %collective-permute-start = (bf16[48,1,128]{2,1,0:T(2,128)(2,1)S(1)}, bf16[48,1,128]{2,1,0:T(2,128)(2,1)S(1)}, u32[]{:S(2)}, u32[]{:S(2)}) collective-permute-start(bf16[48,1,128]{2,1,0:T(2,128)(2,1)S(1)} %get-tuple-element.179), channel_id=1, source_target_pairs={{0,8},{8,16},{16,24},{24,32},{32,40},{40,48},{48,56},{56,64},{64,7... | collective-permute-start | bytes 36872 | tf_op jit(solution)/shard_map/ppermute | solution.py:15
  12.5 4.8 %collective-permute-start.1 = (bf16[48,1,128]{2,1,0:T(2,128)(2,1)S(1)}, bf16[48,1,128]{2,1,0:T(2,128)(2,1)S(1)}, u32[]{:S(2)}, u32[]{:S(2)}) collective-permute-start(bf16[48,1,128]{2,1,0:T(2,128)(2,1)S(1)} %get-tuple-element.180), channel_id=1, source_target_pairs={{8,0},{16,8},{24,16},{32,24},{40,32},{48,40},{56,48},{64,56},{72,6... | collective-permute-start | bytes 36872 | tf_op jit(solution)/shard_map/ppermute | solution.py:17
  17.3 17.3 %collective-permute-start.3 = (bf16[1,50,128]{2,1,0:T(8,128)(2,1)S(1)}, bf16[1,50,128]{2,1,0:T(8,128)(2,1)S(1)}, u32[]{:S(2)}, u32[]{:S(2)}) collective-permute-start(bf16[1,50,128]{2,1,0:T(8,128)(2,1)S(1)} %get-tuple-element.176), channel_id=1, source_target_pairs={{0,1},{1,2},{2,3},{3,4},{4,5},{5,6},{6,7},{8,9},{9,10},{10,11},{11... | collective-permute-start | bytes 38408 | tf_op jit(solution)/shard_map/ppermute | solution.py:15
  19.5 9.1 %collective-permute-start.4 = (bf16[50,128]{1,0:T(8,128)(2,1)S(1)}, bf16[50,128]{1,0:T(8,128)(2,1)S(1)}, u32[]{:S(2)}, u32[]{:S(2)}) collective-permute-start(bf16[50,128]{1,0:T(8,128)(2,1)S(1)} %bitcast.196), channel_id=1, source_target_pairs={{0,128},{8,136},{16,144},{24,152},{32,160},{40,168},{48,176},{56,1... | collective-permute-start | bytes 38408 | tf_op jit(solution)/shard_map/ppermute | solution.py:27
  26.5 5.2 %collective-permute-start.5 = (bf16[1,50,128]{2,1,0:T(8,128)(2,1)S(1)}, bf16[1,50,128]{2,1,0:T(8,128)(2,1)S(1)}, u32[]{:S(2)}, u32[]{:S(2)}) collective-permute-start(bf16[1,50,128]{2,1,0:T(8,128)(2,1)S(1)} %get-tuple-element.175), channel_id=1, source_target_pairs={{1,0},{2,1},{3,2},{4,3},{5,4},{6,5},{7,6},{9,8},{10,9},{11,10},{12... | collective-permute-start | bytes 38408 | tf_op jit(solution)/shard_map/ppermute | solution.py:17
  27.8 6.7 %collective-permute-start.2 = (bf16[50,128]{1,0:T(8,128)(2,1)S(1)}, bf16[50,128]{1,0:T(8,128)(2,1)S(1)}, u32[]{:S(2)}, u32[]{:S(2)}) collective-permute-start(bf16[50,128]{1,0:T(8,128)(2,1)S(1)} %bitcast.197), channel_id=1, source_target_pairs={{0,128},{8,136},{16,144},{24,152},{32,160},{40,168},{48,176},{56,1... | collective-permute-start | bytes 38408 | tf_op jit(solution)/shard_map/ppermute | solution.py:27
  35.0 1.0 copy-start.2
  35.7 2.6 copy-start.1
  35.7 0.7 copy-start.4
  37.9 1.1 copy-start.5
  113.1 94.8 %collective-permute-start.6 = (bf16[1,50,128]{2,1,0:T(8,128)(2,1)S(1)}, bf16[1,50,128]{2,1,0:T(8,128)(2,1)S(1)}, u32[]{:S(2)}, u32[]{:S(2)}) collective-permute-start(bf16[1,50,128]{2,1,0:T(8,128)(2,1)S(1)} %get-tuple-element.162), channel_id=1, source_target_pairs={{0,1},{1,2},{2,3},{3,4},{4,5},{5,6},{6,7},{8,9},{9,10},{10,11},{11... | collective-permute-start | bytes 38408 | tf_op jit(solution)/shard_map/ppermute | solution.py:15
  117.8 90.0 %collective-permute-start.7 = (bf16[1,50,128]{2,1,0:T(8,128)(2,1)S(1)}, bf16[1,50,128]{2,1,0:T(8,128)(2,1)S(1)}, u32[]{:S(2)}, u32[]{:S(2)}) collective-permute-start(bf16[1,50,128]{2,1,0:T(8,128)(2,1)S(1)} %get-tuple-element.163), channel_id=1, source_target_pairs={{1,0},{2,1},{3,2},{4,3},{5,4},{6,5},{7,6},{9,8},{10,9},{11,10},{12... | collective-permute-start | bytes 38408 | tf_op jit(solution)/shard_map/ppermute | solution.py:17
  119.1 88.8 %collective-permute-start.8 = (bf16[50,128]{1,0:T(8,128)(2,1)S(1)}, bf16[50,128]{1,0:T(8,128)(2,1)S(1)}, u32[]{:S(2)}, u32[]{:S(2)}) collective-permute-start(bf16[50,128]{1,0:T(8,128)(2,1)S(1)} %bitcast.195), channel_id=1, source_target_pairs={{0,128},{8,136},{16,144},{24,152},{32,160},{40,168},{48,176},{56,1... | collective-permute-start | bytes 38408 | tf_op jit(solution)/shard_map/ppermute | solution.py:27
  121.5 86.3 %collective-permute-start.9 = (bf16[50,128]{1,0:T(8,128)(2,1)S(1)}, bf16[50,128]{1,0:T(8,128)(2,1)S(1)}, u32[]{:S(2)}, u32[]{:S(2)}) collective-permute-start(bf16[50,128]{1,0:T(8,128)(2,1)S(1)} %bitcast.194), channel_id=1, source_target_pairs={{0,128},{8,136},{16,144},{24,152},{32,160},{40,168},{48,176},{56,1... | collective-permute-start | bytes 38408 | tf_op jit(solution)/shard_map/ppermute | solution.py:27
  208.0 2.7 collective-permute-start.10
  209.8 5.1 %collective-permute-start.11 = (bf16[48,1,128]{2,1,0:T(2,128)(2,1)S(1)}, bf16[48,1,128]{2,1,0:T(2,128)(2,1)S(1)}, u32[]{:S(2)}, u32[]{:S(2)}) collective-permute-start(bf16[48,1,128]{2,1,0:T(2,128)(2,1)S(1)} %get-tuple-element.172), channel_id=1, source_target_pairs={{8,0},{16,8},{24,16},{32,24},{40,32},{48,40},{56,48},{64,56},{72,6... | collective-permute-start | bytes 36872 | tf_op jit(solution)/shard_map/ppermute | solution.py:17
Sparse Core Ops, SparseCore 0:
  121.7 258.5 all-reduce.2
where the time goes:
time: 390 us; the launch traced here: 389 us
  waiting for transfers between devices  176 us (45%)
  blocking collectives  81 us (21%)
  local copies, waits for them, and re-layouts  62.9 us (16%)
  starting transfers between devices  28.4 us (7%)
  matrix products  21.1 us (5%)
  between operations  14.4 us (4%)
  other arithmetic  5.48 us (1%)
    psum x1, waiting for transfers between devices, shards(): kernel_sum, bias_sum = lax.psum((kernel_terms, bias_terms), ('lon', 'lat'))  164 us
    psum x1, blocking collectives, shards(): kernel_sum, bias_sum = lax.psum((kernel_terms, bias_terms), ('lon', 'lat'))  81 us
    scatter-add x7, local copies, waits for them, and re-layouts, shards(): padded_grad.at[tap_a:tap_a + rows, tap_b:tap_b + cols]  58.3 us
    ppermute x4, starting transfers between devices, extended(): lax.ppermute(tail, axis, [(i, (i + 1) % count) for i in range(ends)])  12.9 us
    ppermute x4, starting transfers between devices, from_behind(): return lax.ppermute(value, axis, pairs)  12.8 us
    dot_general x9, matrix products, shards(): lax.dot_general(window, pre_grad, (((0,), (0,)), ((), ())), preferred_ele...  10.1 us
    ppermute x4, waiting for transfers between devices, extended(): lax.ppermute(head, axis, [((i + 1) % count, i) for i in range(ends)])  8.55 us
  transfers between devices with their start and end apart: 13, of which 6 were waited for; matrix products, arithmetic and copies ran while one was open for 2% of the time, Pallas kernels for 0%

commit v1 on v0

--- a/solution.py
+++ b/solution.py
@@ -27,6 +27,43 @@
     return lax.ppermute(value, axis, pairs)
 
 
+def butterfly_sum(value, order):
+    shape = value.shape
+    data = value.reshape(-1)
+    parts = 1
+    for axis, _ in order:
+        parts *= 2
+    pad = (-data.shape[0]) % parts
+    data = jnp.pad(data, (0, pad))
+    history = []
+    for axis, step in order:
+        count = lax.axis_size(axis)
+        bit = (lax.axis_index(axis) // step) % 2
+        half = data.shape[0] // 2
+        pairs = [(i, i ^ step) for i in range(count)]
+        send = lax.dynamic_slice_in_dim(data, (1 - bit) * half, half)
+        keep = lax.dynamic_slice_in_dim(data, bit * half, half)
+        data = keep + lax.ppermute(send, axis, pairs)
+        history.append((axis, step, bit))
+    for axis, step, bit in reversed(history):
+        count = lax.axis_size(axis)
+        pairs = [(i, i ^ step) for i in range(count)]
+        other = lax.ppermute(data, axis, pairs)
+        data = jnp.where(bit == 0, jnp.concatenate([data, other]), jnp.concatenate([other, data]))
+    return data[: data.shape[0] - pad].reshape(shape)
+
+
+def halving_order(mesh_axes):
+    order = []
+    steps = {axis: 1 for axis in mesh_axes}
+    while any(steps[axis] < lax.axis_size(axis) for axis in mesh_axes):
+        for axis in mesh_axes:
+            if steps[axis] < lax.axis_size(axis):
+                order.append((axis, steps[axis]))
+                steps[axis] *= 2
+    return order
+
+
 def shards(inputs, weight, bias, cotangent):
     rows, cols, chans = inputs.shape
     band = lax.axis_index("lat")
@@ -47,14 +84,19 @@
     outputs = (pre * sig).astype(jnp.bfloat16).reshape(rows, cols, chans)
     flat_cot = cotangent.reshape(rows * cols, chans).astype(jnp.float32)
     pre_grad = (flat_cot * sig * (1.0 + pre * (1.0 - sig))).astype(jnp.bfloat16)
-    padded_grad = jnp.zeros((rows + 2, cols + 2, chans), jnp.float32)
+    grad_cells = pre_grad.reshape(rows, cols, chans)
+    flipped = jnp.transpose(weight[::-1, ::-1], (0, 1, 3, 2))
+    padded_grad = lax.conv_general_dilated(
+        jnp.pad(grad_cells, ((2, 2), (2, 2), (0, 0)))[None],
+        flipped,
+        (1, 1),
+        "VALID",
+        dimension_numbers=("NHWC", "HWIO", "NHWC"),
+        preferred_element_type=jnp.float32,
+    )[0]
     taps = []
     for tap_a in range(3):
         for tap_b in range(3):
-            back = jnp.dot(pre_grad, weight[tap_a, tap_b].T, preferred_element_type=jnp.float32)
-            padded_grad = padded_grad.at[tap_a : tap_a + rows, tap_b : tap_b + cols].add(
-                back.reshape(rows, cols, chans)
-            )
             window = padded[tap_a : tap_a + rows, tap_b : tap_b + cols].reshape(rows * cols, chans)
             taps.append(
                 lax.dot_general(
@@ -78,7 +120,8 @@
     core = core.at[:, 0].add(beside[:, 0])
     core = core.at[:, -1].add(beside[:, 3])
     input_grad = core.astype(jnp.bfloat16)
-    kernel_sum, bias_sum = lax.psum((kernel_terms, bias_terms), ("lon", "lat"))
+    sums = butterfly_sum(jnp.concatenate([kernel_terms, bias_terms], axis=0), halving_order(("lon", "lat")))
+    kernel_sum, bias_sum = sums[:-1], sums[-1:]
     total_cells = rows * cols * lax.axis_size("lon") * lax.axis_size("lat")
     scale = 1.0 / jnp.sqrt(jnp.float32(total_cells))
     weight_grad = kernel_sum.reshape(3, 3, chans, chans) * scale

time: 390 us -> 131 us (0.34)
  waiting for transfers between devices: 176 us -> 42.5 us
  blocking collectives: 81 us -> 0 us
  local copies, waits for them, and re-layouts: 62.9 us -> 6.13 us
  starting transfers between devices: 28.4 us -> 66.3 us
  between operations: 14.4 us -> 1.18 us
  matrix products: 21.1 us -> 10.1 us
    psum x1 -> x0, waiting for transfers between devices: 164 us -> none  [shards(): kernel_sum, bias_sum = lax.psum((kernel_terms, bias_terms), ('lon', 'lat'))]
    psum x1 -> x0, blocking collectives: 81 us -> none  [shards(): kernel_sum, bias_sum = lax.psum((kernel_terms, bias_terms), ('lon', 'lat'))]
    scatter-add x9 -> x2, local copies, waits for them, and re-layouts: 58.6 us -> 0.25 us  [the longest x1 0.13 us: shards(): inner.at[-1]]
    ppermute x0 -> x16, waiting for transfers between devices: none -> 33.2 us  [the longest x8 19.8 us: butterfly_sum(): data = keep + lax.ppermute(send, axis, pairs)]
    ppermute x0 -> x16, starting transfers between devices: none -> 27.6 us  [the longest x8 14.5 us: butterfly_sum(): other = lax.ppermute(data, axis, pairs)]
    ppermute x4, starting transfers between devices: 12.9 us -> 23.6 us  [extended(): lax.ppermute(tail, axis, [(i, (i + 1) % count) for i in range(ends)])]
    dot_general x9, matrix products: 10.1 us -> 3.22 us  [shards(): lax.dot_general(window, pre_grad, (((0,), (0,)), ((), ())), preferred_ele...]
    dot_general x9 -> x0, matrix products: 6.01 us -> none  [shards(): jnp.dot(pre_grad, weight[tap_a, tap_b].T, preferred_element_type=jnp.floa...]
  transfers between devices with their start and end apart: 13 -> 28, of which waited for: 6 -> 17; matrix products, arithmetic and copies ran while one was open for 2% -> 5% of each run, Pallas kernels for 0% -> 0%
where the time goes in v1:
time: 131 us; the launch traced here: 130 us
  starting transfers between devices  66.3 us (51%)
  waiting for transfers between devices  42.5 us (32%)
  matrix products  10.1 us (8%)
  local copies, waits for them, and re-layouts  6.13 us (5%)
  other arithmetic  4.14 us (3%)
    ppermute x4, starting transfers between devices, extended(): lax.ppermute(tail, axis, [(i, (i + 1) % count) for i in range(ends)])  23.6 us
    ppermute x8, waiting for transfers between devices, butterfly_sum(): data = keep + lax.ppermute(send, axis, pairs)  19.8 us
    ppermute x8, starting transfers between devices, butterfly_sum(): other = lax.ppermute(data, axis, pairs)  14.5 us
    ppermute x8, waiting for transfers between devices, butterfly_sum(): other = lax.ppermute(data, axis, pairs)  13.4 us
    ppermute x8, starting transfers between devices, butterfly_sum(): data = keep + lax.ppermute(send, axis, pairs)  13.1 us
    ppermute x4, starting transfers between devices, from_behind(): return lax.ppermute(value, axis, pairs)  12.6 us
    ppermute x4, waiting for transfers between devices, extended(): lax.ppermute(head, axis, [((i + 1) % count, i) for i in range(ends)])  6.58 us
    dot_general x9, matrix products, shards(): jnp.dot(window, weight[tap_a, tap_b], preferred_element_type=jnp.float32)  4.99 us
  transfers between devices with their start and end apart: 28, of which 17 were waited for; matrix products, arithmetic and copies ran while one was open for 5% of the time, Pallas kernels for 0%

profile of v1, /device:TPU:1, one launch (start us, length us, event | category | flops | bytes accessed | tf_op | source)
XLA Modules:
  0.0 130.3 jit_solution(14101553380811197756)
XLA Ops:
  0.6 1.0 fusion.49
  1.7 4.2 %collective-permute-start = (bf16[48,1,128]{2,1,0:T(2,128)(2,1)S(1)}, bf16[48,1,128]{2,1,0:T(2,128)(2,1)S(1)}, u32[]{:S(2)}, u32[]{:S(2)}) collective-permute-start(bf16[48,1,128]{2,1,0:T(2,128)(2,1)S(1)} %get-tuple-element.75), channel_id=1, source_target_pairs={{0,8},{8,16},{16,24},{24,32},{32,40},{40,48},{48,56},{56,64},{64,7... | collective-permute-start | bytes 36872 | tf_op jit(solution)/shard_map/ppermute | solution.py:15
  5.9 1.4 %fusion.19 = f32[2304,128]{1,0:T(8,128)S(1)} fusion(bf16[2304,128]{1,0:T(8,128)(2,1)} %bitcast.130, bf16[3,3,128,128]{3,2,1,0:T(8,128)(2,1)} %param.13), kind=kOutput, calls=%fused_computation.57 | convolution fusion | flops 75497472 | bytes 1802240 | tf_op jit(solution)/shard_map/dot_general | solution.py:82
  7.3 3.4 %collective-permute-done.1 = bf16[48,1,128]{2,1,0:T(2,128)(2,1)S(1)} collective-permute-done((bf16[48,1,128]{2,1,0:T(2,128)(2,1)S(1)}, bf16[48,1,128]{2,1,0:T(2,128)(2,1)S(1)}, u32[]{:S(2)}, u32[]{:S(2)}) %collective-permute-start.1) | collective-permute-done | bytes 12320 | tf_op jit(solution)/shard_map/ppermute | solution.py:17
  10.7 2.2 %collective-permute-start.3 = (bf16[1,50,128]{2,1,0:T(8,128)(2,1)S(1)}, bf16[1,50,128]{2,1,0:T(8,128)(2,1)S(1)}, u32[]{:S(2)}, u32[]{:S(2)}) collective-permute-start(bf16[1,50,128]{2,1,0:T(8,128)(2,1)S(1)} %get-tuple-element.70), channel_id=1, source_target_pairs={{0,1},{1,2},{2,3},{3,4},{4,5},{5,6},{6,7},{8,9},{9,10},{10,11},{11... | collective-permute-start | bytes 38408 | tf_op jit(solution)/shard_map/ppermute | solution.py:15
  12.9 7.0 %collective-permute-start.4 = (bf16[50,128]{1,0:T(8,128)(2,1)S(1)}, bf16[50,128]{1,0:T(8,128)(2,1)S(1)}, u32[]{:S(2)}, u32[]{:S(2)}) collective-permute-start(bf16[50,128]{1,0:T(8,128)(2,1)S(1)} %bitcast.154), channel_id=1, source_target_pairs={{0,128},{8,136},{16,144},{24,152},{32,160},{40,168},{48,176},{56,1... | collective-permute-start | bytes 38408 | tf_op jit(solution)/shard_map/ppermute | solution.py:27
  19.9 1.3 collective-permute-start.5
  21.3 0.5 pad_maximum_fusion.1
  21.8 3.2 %collective-permute-done.5 = bf16[1,50,128]{2,1,0:T(8,128)(2,1)S(1)} collective-permute-done((bf16[1,50,128]{2,1,0:T(8,128)(2,1)S(1)}, bf16[1,50,128]{2,1,0:T(8,128)(2,1)S(1)}, u32[]{:S(2)}, u32[]{:S(2)}) %collective-permute-start.5) | collective-permute-done | bytes 12832 | tf_op jit(solution)/shard_map/ppermute | solution.py:17
  25.1 2.7 %collective-permute-done.2 = bf16[50,128]{1,0:T(8,128)(2,1)S(1)} collective-permute-done((bf16[50,128]{1,0:T(8,128)(2,1)S(1)}, bf16[50,128]{1,0:T(8,128)(2,1)S(1)}, u32[]{:S(2)}, u32[]{:S(2)}) %collective-permute-start.2) | collective-permute-done | bytes 12832 | tf_op jit(solution)/shard_map/ppermute | solution.py:27
  27.8 0.5 maximum_maximum_fusion
  28.2 0.7 fusion.46
  31.5 0.8 copy-done.3
  32.2 1.6 %convert_reduce_fusion = (f32[128]{0:T(128)S(1)}, bf16[2304,128]{1,0:T(8,128)(2,1)S(1)}, bf16[2304,128]{1,0:T(8,128)(2,1)}) fusion(bf16[48,48,128]{2,1,0:T(8,128)(2,1)S(1)} %copy-done.3, f32[2304,128]{1,0:T(8,128)S(1)} %convolution_add_fusion.1, bf16[2304,128]{1,0:T(8,128)(2,1)S(1)} %bitcast.150, bf16[3,3,128,128]{3,2,1,0:T(8,128)(2,1)S(1)} %copy-done.1), kind=kOutput, calls=%fused_computation.16 | convolution fusion | flops 79921024 | bytes 3572224 | tf_op jit(solution)/shard_map/dot_general | solution.py:82
  37.2 2.2 %collective-permute-start.12 = (f32[73856]{0:T(1024)S(1)}, f32[73856]{0:T(1024)S(1)}, u32[]{:S(2)}, u32[]{:S(2)}) collective-permute-start(f32[73856]{0:T(1024)S(1)} %pad_dynamic-slice_fusion), channel_id=1, source_target_pairs={{0,8},{8,0},{16,24},{24,16},{32,40},{40,32},{48,56},{56,48},{64,72... | collective-permute-start | bytes 886280 | tf_op jit(solution)/shard_map/ppermute | solution.py:46
  39.4 1.2 collective-permute-done.12
  40.9 2.4 %collective-permute-start.13 = (f32[36928]{0:T(1024)S(1)}, f32[36928]{0:T(1024)S(1)}, u32[]{:S(2)}, u32[]{:S(2)}) collective-permute-start(f32[36928]{0:T(1024)S(1)} %dynamic_slice.51), channel_id=1, source_target_pairs={{0,1},{1,0},{2,3},{3,2},{4,5},{5,4},{6,7},{7,6},{8,9},{9,8},{10,11... | collective-permute-start | bytes 443144 | tf_op jit(solution)/shard_map/ppermute | solution.py:46
  43.4 3.9 %collective-permute-done.13 = f32[36928]{0:T(1024)S(1)} collective-permute-done((f32[36928]{0:T(1024)S(1)}, f32[36928]{0:T(1024)S(1)}, u32[]{:S(2)}, u32[]{:S(2)}) %collective-permute-start.13) | collective-permute-done | bytes 147744 | tf_op jit(solution)/shard_map/ppermute | solution.py:46
  47.5 1.7 %collective-permute-start.14 = (f32[18464]{0:T(1024)S(1)}, f32[18464]{0:T(1024)S(1)}, u32[]{:S(2)}, u32[]{:S(2)}) collective-permute-start(f32[18464]{0:T(1024)S(1)} %dynamic_slice.53), channel_id=1, source_target_pairs={{0,16},{8,24},{16,0},{24,8},{32,48},{40,56},{48,32},{56,40},{64,80... | collective-permute-start | bytes 221576 | tf_op jit(solution)/shard_map/ppermute | solution.py:46
  49.2 3.3 %collective-permute-done.14 = f32[18464]{0:T(1024)S(1)} collective-permute-done((f32[18464]{0:T(1024)S(1)}, f32[18464]{0:T(1024)S(1)}, u32[]{:S(2)}, u32[]{:S(2)}) %collective-permute-start.14) | collective-permute-done | bytes 73888 | tf_op jit(solution)/shard_map/ppermute | solution.py:46
  52.7 2.2 %collective-permute-start.15 = (f32[9232]{0:T(1024)S(1)}, f32[9232]{0:T(1024)S(1)}, u32[]{:S(2)}, u32[]{:S(2)}) collective-permute-start(f32[9232]{0:T(1024)S(1)} %dynamic_slice.55), channel_id=1, source_target_pairs={{0,2},{1,3},{2,0},{3,1},{4,6},{5,7},{6,4},{7,5},{8,10},{9,11},{10,... | collective-permute-start | bytes 110792 | tf_op jit(solution)/shard_map/ppermute | solution.py:46
  54.9 1.4 %collective-permute-done.15 = f32[9232]{0:T(1024)S(1)} collective-permute-done((f32[9232]{0:T(1024)S(1)}, f32[9232]{0:T(1024)S(1)}, u32[]{:S(2)}, u32[]{:S(2)}) %collective-permute-start.15) | collective-permute-done | bytes 36960 | tf_op jit(solution)/shard_map/ppermute | solution.py:46
  56.6 2.6 %collective-permute-done.16 = f32[4616]{0:T(1024)S(1)} collective-permute-done((f32[4616]{0:T(1024)S(1)}, f32[4616]{0:T(1024)S(1)}, u32[]{:S(2)}, u32[]{:S(2)}) %collective-permute-start.16) | collective-permute-done | bytes 18496 | tf_op jit(solution)/shard_map/ppermute | solution.py:46
  59.3 3.4 %collective-permute-start.17 = (f32[2308]{0:T(1024)S(1)}, f32[2308]{0:T(1024)S(1)}, u32[]{:S(2)}, u32[]{:S(2)}) collective-permute-start(f32[2308]{0:T(1024)S(1)} %dynamic_slice.59), channel_id=1, source_target_pairs={{0,4},{1,5},{2,6},{3,7},{4,0},{5,1},{6,2},{7,3},{8,12},{9,13},{10,... | collective-permute-start | bytes 27704 | tf_op jit(solution)/shard_map/ppermute | solution.py:46
  62.9 0.9 collective-permute-done.17
  64.5 2.9 %collective-permute-done.18 = f32[1154]{0:T(1024)S(1)} collective-permute-done((f32[1154]{0:T(1024)S(1)}, f32[1154]{0:T(1024)S(1)}, u32[]{:S(2)}, u32[]{:S(2)}) %collective-permute-start.18) | collective-permute-done | bytes 4648 | tf_op jit(solution)/shard_map/ppermute | solution.py:46
  67.6 1.0 collective-permute-start.19
  68.5 1.8 %convolution_select_fusion = f32[50,8,7,128]{3,1,2,0:T(8,128)S(1)} fusion(bf16[3,3,128,128]{3,2,1,0:T(8,128)(2,1)S(1)} %copy-done.1, bf16[52,1,7,2,128]{4,2,3,0,1:T(8,128)(2,1)S(1)} %slice.284, bf16[52,1,8,7,128]{4,2,3,0,1:T(8,128)(2,1)S(1)} %copy.10, pred[8,7]{0,1:T(8,128)(4,1)S(1)} %copy-done.4), kind=kOutput, calls=%fused_computation.11 | convolution fusion | flops 828987392 | bytes 2660408 | tf_op jit(solution)/shard_map/conv_general_dilated | solution.py:89
  70.4 3.6 %collective-permute-done.19 = f32[577]{0:T(1024)S(1)} collective-permute-done((f32[577]{0:T(1024)S(1)}, f32[577]{0:T(1024)S(1)}, u32[]{:S(2)}, u32[]{:S(2)}) %collective-permute-start.19) | collective-permute-done | bytes 2340 | tf_op jit(solution)/shard_map/ppermute | solution.py:46
  74.0 1.0 collective-permute-start.20
  75.0 5.4 %collective-permute-done.20 = f32[577]{0:T(1024)S(1)} collective-permute-done((f32[577]{0:T(1024)S(1)}, f32[577]{0:T(1024)S(1)}, u32[]{:S(2)}, u32[]{:S(2)}) %collective-permute-start.20) | collective-permute-done | bytes 2340 | tf_op jit(solution)/shard_map/ppermute | solution.py:51
  80.7 2.2 %collective-permute-start.6 = (bf16[1,50,128]{2,1,0:T(8,128)(2,1)S(1)}, bf16[1,50,128]{2,1,0:T(8,128)(2,1)S(1)}, u32[]{:S(2)}, u32[]{:S(2)}) collective-permute-start(bf16[1,50,128]{2,1,0:T(8,128)(2,1)S(1)} %get-tuple-element.80), channel_id=1, source_target_pairs={{0,1},{1,2},{2,3},{3,4},{4,5},{5,6},{6,7},{8,9},{9,10},{10,11},{11... | collective-permute-start | bytes 38408 | tf_op jit(solution)/shard_map/ppermute | solution.py:15
  83.0 0.9 collective-permute-done.21
  84.0 3.0 %collective-permute-start.22 = (f32[2308]{0:T(1024)S(1)}, f32[2308]{0:T(1024)S(1)}, u32[]{:S(2)}, u32[]{:S(2)}) collective-permute-start(f32[2308]{0:T(1024)S(1)} %maximum_select_fusion.6), channel_id=1, source_target_pairs={{0,4},{1,5},{2,6},{3,7},{4,0},{5,1},{6,2},{7,3},{8,12},{9,13},{10,... | collective-permute-start | bytes 27704 | tf_op jit(solution)/shard_map/ppermute | solution.py:51
  87.0 1.3 collective-permute-start.7
  88.3 1.5 %collective-permute-start.8 = (bf16[50,128]{1,0:T(8,128)(2,1)S(1)}, bf16[50,128]{1,0:T(8,128)(2,1)S(1)}, u32[]{:S(2)}, u32[]{:S(2)}) collective-permute-start(bf16[50,128]{1,0:T(8,128)(2,1)S(1)} %get-tuple-element.82), channel_id=1, source_target_pairs={{0,128},{8,136},{16,144},{24,152},{32,160},{40,168},{48,176},{56,1... | collective-permute-start | bytes 38408 | tf_op jit(solution)/shard_map/ppermute | solution.py:27
  89.8 4.0 %collective-permute-start.9 = (bf16[50,128]{1,0:T(8,128)(2,1)S(1)}, bf16[50,128]{1,0:T(8,128)(2,1)S(1)}, u32[]{:S(2)}, u32[]{:S(2)}) collective-permute-start(bf16[50,128]{1,0:T(8,128)(2,1)S(1)} %get-tuple-element.79), channel_id=1, source_target_pairs={{0,128},{8,136},{16,144},{24,152},{32,160},{40,168},{48,176},{56,1... | collective-permute-start | bytes 38408 | tf_op jit(solution)/shard_map/ppermute | solution.py:27
  94.3 2.5 %collective-permute-done.23 = f32[4616]{0:T(1024)S(1)} collective-permute-done((f32[4616]{0:T(1024)S(1)}, f32[4616]{0:T(1024)S(1)}, u32[]{:S(2)}, u32[]{:S(2)}) %collective-permute-start.23) | collective-permute-done | bytes 18496 | tf_op jit(solution)/shard_map/ppermute | solution.py:51
  96.9 3.2 %collective-permute-start.24 = (f32[9232]{0:T(1024)S(1)}, f32[9232]{0:T(1024)S(1)}, u32[]{:S(2)}, u32[]{:S(2)}) collective-permute-start(f32[9232]{0:T(1024)S(1)} %maximum_select_fusion.4), channel_id=1, source_target_pairs={{0,2},{1,3},{2,0},{3,1},{4,6},{5,7},{6,4},{7,5},{8,10},{9,11},{10,... | collective-permute-start | bytes 110792 | tf_op jit(solution)/shard_map/ppermute | solution.py:51
  100.2 1.2 collective-permute-done.24
  101.5 1.5 %collective-permute-start.25 = (f32[18464]{0:T(1024)S(1)}, f32[18464]{0:T(1024)S(1)}, u32[]{:S(2)}, u32[]{:S(2)}) collective-permute-start(f32[18464]{0:T(1024)S(1)} %maximum_select_fusion.3), channel_id=1, source_target_pairs={{0,16},{8,24},{16,0},{24,8},{32,48},{40,56},{48,32},{56,40},{64,80... | collective-permute-start | bytes 221576 | tf_op jit(solution)/shard_map/ppermute | solution.py:51
  103.3 3.3 %collective-permute-done.25 = f32[18464]{0:T(1024)S(1)} collective-permute-done((f32[18464]{0:T(1024)S(1)}, f32[18464]{0:T(1024)S(1)}, u32[]{:S(2)}, u32[]{:S(2)}) %collective-permute-start.25) | collective-permute-done | bytes 73888 | tf_op jit(solution)/shard_map/ppermute | solution.py:51
  106.8 0.8 collective-permute-start.26
  107.6 14.9 %collective-permute-start.10 = (bf16[48,1,128]{2,0,1:T(8,128)(2,1)S(1)}, bf16[48,1,128]{2,0,1:T(8,128)(2,1)S(1)}, u32[]{:S(2)}, u32[]{:S(2)}) collective-permute-start(bf16[48,1,128]{2,0,1:T(8,128)(2,1)S(1)} %get-tuple-element.71), channel_id=1, source_target_pairs={{0,8},{8,16},{16,24},{24,32},{32,40},{40,48},{48,56},{56,64},{64,7... | collective-permute-start | bytes 36872 | tf_op jit(solution)/shard_map/ppermute | solution.py:15
  122.7 4.9 %collective-permute-start.27 = (f32[73856]{0:T(1024)S(1)}, f32[73856]{0:T(1024)S(1)}, u32[]{:S(2)}, u32[]{:S(2)}) collective-permute-start(f32[73856]{0:T(1024)S(1)} %maximum_select_fusion.1), channel_id=1, source_target_pairs={{0,8},{8,0},{16,24},{24,16},{32,40},{40,32},{48,56},{56,48},{64,72... | collective-permute-start | bytes 886280 | tf_op jit(solution)/shard_map/ppermute | solution.py:51
  127.7 1.0 copy.17
  128.9 0.9 slice_multiply_fusion
  129.8 0.5 slice_multiply_fusion.1
  (100 shorter events, 10.3 us)
Async XLA Ops:
  0.6 10.0 %copy-start = (bf16[48,48,128]{2,1,0:T(8,128)(2,1)S(1)}, bf16[48,48,128]{2,1,0:T(8,128)(2,1)}, u32[]{:S(2)}) copy-start(bf16[48,48,128]{2,1,0:T(8,128)(2,1)} %param.12) | copy-start | bytes 1769476
  1.7 5.6 %collective-permute-start = (bf16[48,1,128]{2,1,0:T(2,128)(2,1)S(1)}, bf16[48,1,128]{2,1,0:T(2,128)(2,1)S(1)}, u32[]{:S(2)}, u32[]{:S(2)}) collective-permute-start(bf16[48,1,128]{2,1,0:T(2,128)(2,1)S(1)} %get-tuple-element.75), channel_id=1, source_target_pairs={{0,8},{8,16},{16,24},{24,32},{32,40},{40,48},{48,56},{56,64},{64,7... | collective-permute-start | bytes 36872 | tf_op jit(solution)/shard_map/ppermute | solution.py:15
  5.9 4.8 %collective-permute-start.1 = (bf16[48,1,128]{2,1,0:T(2,128)(2,1)S(1)}, bf16[48,1,128]{2,1,0:T(2,128)(2,1)S(1)}, u32[]{:S(2)}, u32[]{:S(2)}) collective-permute-start(bf16[48,1,128]{2,1,0:T(2,128)(2,1)S(1)} %get-tuple-element.76), channel_id=1, source_target_pairs={{8,0},{16,8},{24,16},{32,24},{40,32},{48,40},{56,48},{64,56},{72,6... | collective-permute-start | bytes 36872 | tf_op jit(solution)/shard_map/ppermute | solution.py:17
  10.7 17.1 %collective-permute-start.3 = (bf16[1,50,128]{2,1,0:T(8,128)(2,1)S(1)}, bf16[1,50,128]{2,1,0:T(8,128)(2,1)S(1)}, u32[]{:S(2)}, u32[]{:S(2)}) collective-permute-start(bf16[1,50,128]{2,1,0:T(8,128)(2,1)S(1)} %get-tuple-element.70), channel_id=1, source_target_pairs={{0,1},{1,2},{2,3},{3,4},{4,5},{5,6},{6,7},{8,9},{9,10},{10,11},{11... | collective-permute-start | bytes 38408 | tf_op jit(solution)/shard_map/ppermute | solution.py:15
  12.9 8.9 %collective-permute-start.4 = (bf16[50,128]{1,0:T(8,128)(2,1)S(1)}, bf16[50,128]{1,0:T(8,128)(2,1)S(1)}, u32[]{:S(2)}, u32[]{:S(2)}) collective-permute-start(bf16[50,128]{1,0:T(8,128)(2,1)S(1)} %bitcast.154), channel_id=1, source_target_pairs={{0,128},{8,136},{16,144},{24,152},{32,160},{40,168},{48,176},{56,1... | collective-permute-start | bytes 38408 | tf_op jit(solution)/shard_map/ppermute | solution.py:27
  19.9 5.2 %collective-permute-start.5 = (bf16[1,50,128]{2,1,0:T(8,128)(2,1)S(1)}, bf16[1,50,128]{2,1,0:T(8,128)(2,1)S(1)}, u32[]{:S(2)}, u32[]{:S(2)}) collective-permute-start(bf16[1,50,128]{2,1,0:T(8,128)(2,1)S(1)} %get-tuple-element.69), channel_id=1, source_target_pairs={{1,0},{2,1},{3,2},{4,3},{5,4},{6,5},{7,6},{9,8},{10,9},{11,10},{12... | collective-permute-start | bytes 38408 | tf_op jit(solution)/shard_map/ppermute | solution.py:17
  21.2 6.6 %collective-permute-start.2 = (bf16[50,128]{1,0:T(8,128)(2,1)S(1)}, bf16[50,128]{1,0:T(8,128)(2,1)S(1)}, u32[]{:S(2)}, u32[]{:S(2)}) collective-permute-start(bf16[50,128]{1,0:T(8,128)(2,1)S(1)} %bitcast.155), channel_id=1, source_target_pairs={{0,128},{8,136},{16,144},{24,152},{32,160},{40,168},{48,176},{56,1... | collective-permute-start | bytes 38408 | tf_op jit(solution)/shard_map/ppermute | solution.py:27
  28.2 1.0 copy-start.1
  28.9 0.7 copy-start.2
  31.1 1.1 copy-start.3
  37.2 3.4 %collective-permute-start.12 = (f32[73856]{0:T(1024)S(1)}, f32[73856]{0:T(1024)S(1)}, u32[]{:S(2)}, u32[]{:S(2)}) collective-permute-start(f32[73856]{0:T(1024)S(1)} %pad_dynamic-slice_fusion), channel_id=1, source_target_pairs={{0,8},{8,0},{16,24},{24,16},{32,40},{40,32},{48,56},{56,48},{64,72... | collective-permute-start | bytes 886280 | tf_op jit(solution)/shard_map/ppermute | solution.py:46
  40.9 6.4 %collective-permute-start.13 = (f32[36928]{0:T(1024)S(1)}, f32[36928]{0:T(1024)S(1)}, u32[]{:S(2)}, u32[]{:S(2)}) collective-permute-start(f32[36928]{0:T(1024)S(1)} %dynamic_slice.51), channel_id=1, source_target_pairs={{0,1},{1,0},{2,3},{3,2},{4,5},{5,4},{6,7},{7,6},{8,9},{9,8},{10,11... | collective-permute-start | bytes 443144 | tf_op jit(solution)/shard_map/ppermute | solution.py:46
  47.5 5.0 %collective-permute-start.14 = (f32[18464]{0:T(1024)S(1)}, f32[18464]{0:T(1024)S(1)}, u32[]{:S(2)}, u32[]{:S(2)}) collective-permute-start(f32[18464]{0:T(1024)S(1)} %dynamic_slice.53), channel_id=1, source_target_pairs={{0,16},{8,24},{16,0},{24,8},{32,48},{40,56},{48,32},{56,40},{64,80... | collective-permute-start | bytes 221576 | tf_op jit(solution)/shard_map/ppermute | solution.py:46
  52.7 3.6 %collective-permute-start.15 = (f32[9232]{0:T(1024)S(1)}, f32[9232]{0:T(1024)S(1)}, u32[]{:S(2)}, u32[]{:S(2)}) collective-permute-start(f32[9232]{0:T(1024)S(1)} %dynamic_slice.55), channel_id=1, source_target_pairs={{0,2},{1,3},{2,0},{3,1},{4,6},{5,7},{6,4},{7,5},{8,10},{9,11},{10,... | collective-permute-start | bytes 110792 | tf_op jit(solution)/shard_map/ppermute | solution.py:46
  56.5 2.7 %collective-permute-start.16 = (f32[4616]{0:T(1024)S(1)}, f32[4616]{0:T(1024)S(1)}, u32[]{:S(2)}, u32[]{:S(2)}) collective-permute-start(f32[4616]{0:T(1024)S(1)} %dynamic_slice.57), channel_id=1, source_target_pairs={{0,32},{8,40},{16,48},{24,56},{32,0},{40,8},{48,16},{56,24},{64,96... | collective-permute-start | bytes 55400 | tf_op jit(solution)/shard_map/ppermute | solution.py:46
  59.3 4.5 %collective-permute-start.17 = (f32[2308]{0:T(1024)S(1)}, f32[2308]{0:T(1024)S(1)}, u32[]{:S(2)}, u32[]{:S(2)}) collective-permute-start(f32[2308]{0:T(1024)S(1)} %dynamic_slice.59), channel_id=1, source_target_pairs={{0,4},{1,5},{2,6},{3,7},{4,0},{5,1},{6,2},{7,3},{8,12},{9,13},{10,... | collective-permute-start | bytes 27704 | tf_op jit(solution)/shard_map/ppermute | solution.py:46
  64.0 3.4 %collective-permute-start.18 = (f32[1154]{0:T(1024)S(1)}, f32[1154]{0:T(1024)S(1)}, u32[]{:S(2)}, u32[]{:S(2)}) collective-permute-start(f32[1154]{0:T(1024)S(1)} %dynamic_slice.61), channel_id=1, source_target_pairs={{0,64},{8,72},{16,80},{24,88},{32,96},{40,104},{48,112},{56,120},{... | collective-permute-start | bytes 13856 | tf_op jit(solution)/shard_map/ppermute | solution.py:46
  64.4 4.2 %copy-start.4 = (pred[8,7]{0,1:T(8,128)(4,1)S(1)}, pred[8,7]{0,1:T(8,128)(4,1)}, u32[]{:S(2)}) copy-start(pred[8,7]{0,1:T(8,128)(4,1)} %constant.268) | copy-start | bytes 172
  67.6 6.4 %collective-permute-start.19 = (f32[577]{0:T(1024)S(1)}, f32[577]{0:T(1024)S(1)}, u32[]{:S(2)}, u32[]{:S(2)}) collective-permute-start(f32[577]{0:T(1024)S(1)} %dynamic_slice.63), channel_id=1, source_target_pairs={{0,128},{8,136},{16,144},{24,152},{32,160},{40,168},{48,176},{56,1... | collective-permute-start | bytes 6932 | tf_op jit(solution)/shard_map/ppermute | solution.py:46
  74.0 6.4 %collective-permute-start.20 = (f32[577]{0:T(1024)S(1)}, f32[577]{0:T(1024)S(1)}, u32[]{:S(2)}, u32[]{:S(2)}) collective-permute-start(f32[577]{0:T(1024)S(1)} %dynamic-slice_add_fusion.6), channel_id=1, source_target_pairs={{0,128},{8,136},{16,144},{24,152},{32,160},{40,168},{48,176},{56,1... | collective-permute-start | bytes 6932 | tf_op jit(solution)/shard_map/ppermute | solution.py:51
  80.5 3.4 %collective-permute-start.21 = (f32[1154]{0:T(1024)S(1)}, f32[1154]{0:T(1024)S(1)}, u32[]{:S(2)}, u32[]{:S(2)}) collective-permute-start(f32[1154]{0:T(1024)S(1)} %maximum_select_fusion.7), channel_id=1, source_target_pairs={{0,64},{8,72},{16,80},{24,88},{32,96},{40,104},{48,112},{56,120},{... | collective-permute-start | bytes 13856 | tf_op jit(solution)/shard_map/ppermute | solution.py:51
  80.7 19.3 %collective-permute-start.6 = (bf16[1,50,128]{2,1,0:T(8,128)(2,1)S(1)}, bf16[1,50,128]{2,1,0:T(8,128)(2,1)S(1)}, u32[]{:S(2)}, u32[]{:S(2)}) collective-permute-start(bf16[1,50,128]{2,1,0:T(8,128)(2,1)S(1)} %get-tuple-element.80), channel_id=1, source_target_pairs={{0,1},{1,2},{2,3},{3,4},{4,5},{5,6},{6,7},{8,9},{9,10},{10,11},{11... | collective-permute-start | bytes 38408 | tf_op jit(solution)/shard_map/ppermute | solution.py:15
  84.0 10.0 %collective-permute-start.22 = (f32[2308]{0:T(1024)S(1)}, f32[2308]{0:T(1024)S(1)}, u32[]{:S(2)}, u32[]{:S(2)}) collective-permute-start(f32[2308]{0:T(1024)S(1)} %maximum_select_fusion.6), channel_id=1, source_target_pairs={{0,4},{1,5},{2,6},{3,7},{4,0},{5,1},{6,2},{7,3},{8,12},{9,13},{10,... | collective-permute-start | bytes 27704 | tf_op jit(solution)/shard_map/ppermute | solution.py:51
  87.0 13.0 %collective-permute-start.7 = (bf16[1,50,128]{2,1,0:T(8,128)(2,1)S(1)}, bf16[1,50,128]{2,1,0:T(8,128)(2,1)S(1)}, u32[]{:S(2)}, u32[]{:S(2)}) collective-permute-start(bf16[1,50,128]{2,1,0:T(8,128)(2,1)S(1)} %get-tuple-element.81), channel_id=1, source_target_pairs={{1,0},{2,1},{3,2},{4,3},{5,4},{6,5},{7,6},{9,8},{10,9},{11,10},{12... | collective-permute-start | bytes 38408 | tf_op jit(solution)/shard_map/ppermute | solution.py:17
  88.3 11.7 %collective-permute-start.8 = (bf16[50,128]{1,0:T(8,128)(2,1)S(1)}, bf16[50,128]{1,0:T(8,128)(2,1)S(1)}, u32[]{:S(2)}, u32[]{:S(2)}) collective-permute-start(bf16[50,128]{1,0:T(8,128)(2,1)S(1)} %get-tuple-element.82), channel_id=1, source_target_pairs={{0,128},{8,136},{16,144},{24,152},{32,160},{40,168},{48,176},{56,1... | collective-permute-start | bytes 38408 | tf_op jit(solution)/shard_map/ppermute | solution.py:27
  89.8 10.3 %collective-permute-start.9 = (bf16[50,128]{1,0:T(8,128)(2,1)S(1)}, bf16[50,128]{1,0:T(8,128)(2,1)S(1)}, u32[]{:S(2)}, u32[]{:S(2)}) collective-permute-start(bf16[50,128]{1,0:T(8,128)(2,1)S(1)} %get-tuple-element.79), channel_id=1, source_target_pairs={{0,128},{8,136},{16,144},{24,152},{32,160},{40,168},{48,176},{56,1... | collective-permute-start | bytes 38408 | tf_op jit(solution)/shard_map/ppermute | solution.py:27
  94.1 2.7 %collective-permute-start.23 = (f32[4616]{0:T(1024)S(1)}, f32[4616]{0:T(1024)S(1)}, u32[]{:S(2)}, u32[]{:S(2)}) collective-permute-start(f32[4616]{0:T(1024)S(1)} %maximum_select_fusion.5), channel_id=1, source_target_pairs={{0,32},{8,40},{16,48},{24,56},{32,0},{40,8},{48,16},{56,24},{64,96... | collective-permute-start | bytes 55400 | tf_op jit(solution)/shard_map/ppermute | solution.py:51
  96.9 4.6 %collective-permute-start.24 = (f32[9232]{0:T(1024)S(1)}, f32[9232]{0:T(1024)S(1)}, u32[]{:S(2)}, u32[]{:S(2)}) collective-permute-start(f32[9232]{0:T(1024)S(1)} %maximum_select_fusion.4), channel_id=1, source_target_pairs={{0,2},{1,3},{2,0},{3,1},{4,6},{5,7},{6,4},{7,5},{8,10},{9,11},{10,... | collective-permute-start | bytes 110792 | tf_op jit(solution)/shard_map/ppermute | solution.py:51
  101.5 5.1 %collective-permute-start.25 = (f32[18464]{0:T(1024)S(1)}, f32[18464]{0:T(1024)S(1)}, u32[]{:S(2)}, u32[]{:S(2)}) collective-permute-start(f32[18464]{0:T(1024)S(1)} %maximum_select_fusion.3), channel_id=1, source_target_pairs={{0,16},{8,24},{16,0},{24,8},{32,48},{40,56},{48,32},{56,40},{64,80... | collective-permute-start | bytes 221576 | tf_op jit(solution)/shard_map/ppermute | solution.py:51
  106.8 15.8 %collective-permute-start.26 = (f32[36928]{0:T(1024)S(1)}, f32[36928]{0:T(1024)S(1)}, u32[]{:S(2)}, u32[]{:S(2)}) collective-permute-start(f32[36928]{0:T(1024)S(1)} %maximum_select_fusion.2), channel_id=1, source_target_pairs={{0,1},{1,0},{2,3},{3,2},{4,5},{5,4},{6,7},{7,6},{8,9},{9,8},{10,11... | collective-permute-start | bytes 443144 | tf_op jit(solution)/shard_map/ppermute | solution.py:51
  107.6 20.0 %collective-permute-start.10 = (bf16[48,1,128]{2,0,1:T(8,128)(2,1)S(1)}, bf16[48,1,128]{2,0,1:T(8,128)(2,1)S(1)}, u32[]{:S(2)}, u32[]{:S(2)}) collective-permute-start(bf16[48,1,128]{2,0,1:T(8,128)(2,1)S(1)} %get-tuple-element.71), channel_id=1, source_target_pairs={{0,8},{8,16},{16,24},{24,32},{32,40},{40,48},{48,56},{56,64},{64,7... | collective-permute-start | bytes 36872 | tf_op jit(solution)/shard_map/ppermute | solution.py:15
  122.5 5.1 %collective-permute-start.11 = (bf16[48,1,128]{2,0,1:T(8,128)(2,1)S(1)}, bf16[48,1,128]{2,0,1:T(8,128)(2,1)S(1)}, u32[]{:S(2)}, u32[]{:S(2)}) collective-permute-start(bf16[48,1,128]{2,0,1:T(8,128)(2,1)S(1)} %get-tuple-element.72), channel_id=1, source_target_pairs={{8,0},{16,8},{24,16},{32,24},{40,32},{48,40},{56,48},{64,56},{72,6... | collective-permute-start | bytes 36872 | tf_op jit(solution)/shard_map/ppermute | solution.py:17
  122.7 6.1 %collective-permute-start.27 = (f32[73856]{0:T(1024)S(1)}, f32[73856]{0:T(1024)S(1)}, u32[]{:S(2)}, u32[]{:S(2)}) collective-permute-start(f32[73856]{0:T(1024)S(1)} %maximum_select_fusion.1), channel_id=1, source_target_pairs={{0,8},{8,0},{16,24},{24,16},{32,40},{40,32},{48,56},{56,48},{64,72... | collective-permute-start | bytes 886280 | tf_op jit(solution)/shard_map/ppermute | solution.py:51

commit v2 on v1

--- a/solution.py
+++ b/solution.py
@@ -27,16 +27,14 @@
     return lax.ppermute(value, axis, pairs)
 
 
-def butterfly_sum(value, order):
+def butterfly_sum(value, scatter, double):
     shape = value.shape
     data = value.reshape(-1)
-    parts = 1
-    for axis, _ in order:
-        parts *= 2
+    parts = 2 ** len(scatter)
     pad = (-data.shape[0]) % parts
     data = jnp.pad(data, (0, pad))
     history = []
-    for axis, step in order:
+    for axis, step in scatter:
         count = lax.axis_size(axis)
         bit = (lax.axis_index(axis) // step) % 2
         half = data.shape[0] // 2
@@ -45,6 +43,10 @@
         keep = lax.dynamic_slice_in_dim(data, bit * half, half)
         data = keep + lax.ppermute(send, axis, pairs)
         history.append((axis, step, bit))
+    for axis, step in double:
+        count = lax.axis_size(axis)
+        pairs = [(i, i ^ step) for i in range(count)]
+        data = data + lax.ppermute(data, axis, pairs)
     for axis, step, bit in reversed(history):
         count = lax.axis_size(axis)
         pairs = [(i, i ^ step) for i in range(count)]
@@ -53,15 +55,17 @@
     return data[: data.shape[0] - pad].reshape(shape)
 
 
-def halving_order(mesh_axes):
-    order = []
-    steps = {axis: 1 for axis in mesh_axes}
-    while any(steps[axis] < lax.axis_size(axis) for axis in mesh_axes):
-        for axis in mesh_axes:
-            if steps[axis] < lax.axis_size(axis):
-                order.append((axis, steps[axis]))
-                steps[axis] *= 2
-    return order
+def pairing_order(mesh_axes):
+    near = []
+    for axis in mesh_axes:
+        step = 1
+        while step < lax.axis_size(axis):
+            near.append((axis, step))
+            step *= 2
+    ranked = [("lon", 1), ("lat", 1), ("lon", 4), ("lat", 2)]
+    first = [pair for pair in ranked if pair in near]
+    rest = [pair for pair in near if pair not in first]
+    return first + rest
 
 
 def shards(inputs, weight, bias, cotangent):
@@ -120,7 +124,8 @@
     core = core.at[:, 0].add(beside[:, 0])
     core = core.at[:, -1].add(beside[:, 3])
     input_grad = core.astype(jnp.bfloat16)
-    sums = butterfly_sum(jnp.concatenate([kernel_terms, bias_terms], axis=0), halving_order(("lon", "lat")))
+    order = pairing_order(("lon", "lat"))
+    sums = butterfly_sum(jnp.concatenate([kernel_terms, bias_terms], axis=0), order[:3], order[3:])
     kernel_sum, bias_sum = sums[:-1], sums[-1:]
     total_cells = rows * cols * lax.axis_size("lon") * lax.axis_size("lat")
     scale = 1.0 / jnp.sqrt(jnp.float32(total_cells))

time: 131 us -> 104 us (0.79)
  waiting for transfers between devices: 42.5 us -> 26.6 us
  starting transfers between devices: 66.3 us -> 57.1 us
    ppermute x8 -> x3, waiting for transfers between devices: 19.8 us -> 5.9 us  [butterfly_sum(): data = keep + lax.ppermute(send, axis, pairs)]
    ppermute x8 -> x3, waiting for transfers between devices: 13.4 us -> 1.45 us  [butterfly_sum(): other = lax.ppermute(data, axis, pairs)]
    ppermute x0 -> x5, starting transfers between devices: none -> 11.9 us  [butterfly_sum(): data = data + lax.ppermute(data, axis, pairs)]
    ppermute x8 -> x3, starting transfers between devices: 14.5 us -> 5.15 us  [butterfly_sum(): other = lax.ppermute(data, axis, pairs)]
    ppermute x0 -> x5, waiting for transfers between devices: none -> 8.53 us  [butterfly_sum(): data = data + lax.ppermute(data, axis, pairs)]
    ppermute x8 -> x3, starting transfers between devices: 13.1 us -> 4.9 us  [butterfly_sum(): data = keep + lax.ppermute(send, axis, pairs)]
    ppermute x4, starting transfers between devices: 23.6 us -> 20 us  [extended(): lax.ppermute(tail, axis, [(i, (i + 1) % count) for i in range(ends)])]
    ppermute x4, waiting for transfers between devices: 6.58 us -> 8.01 us  [extended(): lax.ppermute(head, axis, [((i + 1) % count, i) for i in range(ends)])]
  transfers between devices with their start and end apart: 28 -> 23, of which waited for: 17 -> 12; matrix products, arithmetic and copies ran while one was open for 5% -> 6% of each run, Pallas kernels for 0% -> 0%
where the time goes in v2:
time: 104 us
  starting transfers between devices  57.1 us (55%)
  waiting for transfers between devices  26.6 us (26%)
  matrix products  10.1 us (10%)
  local copies, waits for them, and re-layouts  5.72 us (6%)
  other arithmetic  3.53 us (3%)
  between operations  1.13 us (1%)
    ppermute x4, starting transfers between devices, extended(): lax.ppermute(tail, axis, [(i, (i + 1) % count) for i in range(ends)])  20 us
    ppermute x4, starting transfers between devices, from_behind(): return lax.ppermute(value, axis, pairs)  12.6 us
    ppermute x5, starting transfers between devices, butterfly_sum(): data = data + lax.ppermute(data, axis, pairs)  11.9 us
    ppermute x5, waiting for transfers between devices, butterfly_sum(): data = data + lax.ppermute(data, axis, pairs)  8.53 us
    ppermute x4, waiting for transfers between devices, extended(): lax.ppermute(head, axis, [((i + 1) % count, i) for i in range(ends)])  8.01 us
    ppermute x3, waiting for transfers between devices, butterfly_sum(): data = keep + lax.ppermute(send, axis, pairs)  5.9 us
    ppermute x3, starting transfers between devices, butterfly_sum(): other = lax.ppermute(data, axis, pairs)  5.15 us
    dot_general x9, matrix products, shards(): jnp.dot(window, weight[tap_a, tap_b], preferred_element_type=jnp.float32)  4.99 us
  transfers between devices with their start and end apart: 23, of which 12 were waited for; matrix products, arithmetic and copies ran while one was open for 6% of the time, Pallas kernels for 0%

profile of v2, /device:TPU:1, one launch (start us, length us, event | category | flops | bytes accessed | tf_op | source)
XLA Modules:
  0.0 104.1 jit_solution(9665936549987386893)
XLA Ops:
  0.6 1.0 %fusion.48 = (bf16[48,1,128]{2,1,0:T(2,128)(2,1)S(1)}, bf16[48,1,128]{2,1,0:T(2,128)(2,1)S(1)}) fusion(bf16[48,48,128]{2,1,0:T(8,128)(2,1)} %param.12), kind=kLoop, calls=%fused_computation.105 | loop fusion | bytes 49152 | tf_op jit(solution)/shard_map/slice | solution.py:12
  1.7 4.2 %collective-permute-start = (bf16[48,1,128]{2,1,0:T(2,128)(2,1)S(1)}, bf16[48,1,128]{2,1,0:T(2,128)(2,1)S(1)}, u32[]{:S(2)}, u32[]{:S(2)}) collective-permute-start(bf16[48,1,128]{2,1,0:T(2,128)(2,1)S(1)} %get-tuple-element.75), channel_id=1, source_target_pairs={{0,8},{8,16},{16,24},{24,32},{32,40},{40,48},{48,56},{56,64},{64,7... | collective-permute-start | bytes 36872 | tf_op jit(solution)/shard_map/ppermute | solution.py:15
  5.9 1.4 %fusion.18 = f32[2304,128]{1,0:T(8,128)S(1)} fusion(bf16[2304,128]{1,0:T(8,128)(2,1)} %bitcast.130, bf16[3,3,128,128]{3,2,1,0:T(8,128)(2,1)} %param.13), kind=kOutput, calls=%fused_computation.52 | convolution fusion | flops 75497472 | bytes 1802240 | tf_op jit(solution)/shard_map/dot_general | solution.py:86
  7.3 3.4 %collective-permute-done.1 = bf16[48,1,128]{2,1,0:T(2,128)(2,1)S(1)} collective-permute-done((bf16[48,1,128]{2,1,0:T(2,128)(2,1)S(1)}, bf16[48,1,128]{2,1,0:T(2,128)(2,1)S(1)}, u32[]{:S(2)}, u32[]{:S(2)}) %collective-permute-start.1) | collective-permute-done | bytes 12320 | tf_op jit(solution)/shard_map/ppermute | solution.py:17
  10.7 2.2 %collective-permute-start.3 = (bf16[1,50,128]{2,1,0:T(8,128)(2,1)S(1)}, bf16[1,50,128]{2,1,0:T(8,128)(2,1)S(1)}, u32[]{:S(2)}, u32[]{:S(2)}) collective-permute-start(bf16[1,50,128]{2,1,0:T(8,128)(2,1)S(1)} %get-tuple-element.70), channel_id=1, source_target_pairs={{0,1},{1,2},{2,3},{3,4},{4,5},{5,6},{6,7},{8,9},{9,10},{10,11},{11... | collective-permute-start | bytes 38408 | tf_op jit(solution)/shard_map/ppermute | solution.py:15
  12.9 7.0 %collective-permute-start.4 = (bf16[50,128]{1,0:T(8,128)(2,1)S(1)}, bf16[50,128]{1,0:T(8,128)(2,1)S(1)}, u32[]{:S(2)}, u32[]{:S(2)}) collective-permute-start(bf16[50,128]{1,0:T(8,128)(2,1)S(1)} %bitcast.154), channel_id=1, source_target_pairs={{0,128},{8,136},{16,144},{24,152},{32,160},{40,168},{48,176},{56,1... | collective-permute-start | bytes 38408 | tf_op jit(solution)/shard_map/ppermute | solution.py:27
  19.9 1.3 %collective-permute-start.5 = (bf16[1,50,128]{2,1,0:T(8,128)(2,1)S(1)}, bf16[1,50,128]{2,1,0:T(8,128)(2,1)S(1)}, u32[]{:S(2)}, u32[]{:S(2)}) collective-permute-start(bf16[1,50,128]{2,1,0:T(8,128)(2,1)S(1)} %get-tuple-element.69), channel_id=1, source_target_pairs={{1,0},{2,1},{3,2},{4,3},{5,4},{6,5},{7,6},{9,8},{10,9},{11,10},{12... | collective-permute-start | bytes 38408 | tf_op jit(solution)/shard_map/ppermute | solution.py:17
  21.3 0.5 pad_maximum_fusion.1
  21.8 3.2 %collective-permute-done.5 = bf16[1,50,128]{2,1,0:T(8,128)(2,1)S(1)} collective-permute-done((bf16[1,50,128]{2,1,0:T(8,128)(2,1)S(1)}, bf16[1,50,128]{2,1,0:T(8,128)(2,1)S(1)}, u32[]{:S(2)}, u32[]{:S(2)}) %collective-permute-start.5) | collective-permute-done | bytes 12832 | tf_op jit(solution)/shard_map/ppermute | solution.py:17
  25.1 2.7 %collective-permute-done.2 = bf16[50,128]{1,0:T(8,128)(2,1)S(1)} collective-permute-done((bf16[50,128]{1,0:T(8,128)(2,1)S(1)}, bf16[50,128]{1,0:T(8,128)(2,1)S(1)}, u32[]{:S(2)}, u32[]{:S(2)}) %collective-permute-start.2) | collective-permute-done | bytes 12832 | tf_op jit(solution)/shard_map/ppermute | solution.py:27
  27.8 0.5 maximum_maximum_fusion
  28.2 0.7 fusion.45
  31.5 0.8 copy-done.3
  32.2 1.6 %convert_reduce_fusion = (f32[128]{0:T(128)S(1)}, bf16[2304,128]{1,0:T(8,128)(2,1)S(1)}, bf16[2304,128]{1,0:T(8,128)(2,1)}) fusion(bf16[48,48,128]{2,1,0:T(8,128)(2,1)S(1)} %copy-done.3, f32[2304,128]{1,0:T(8,128)S(1)} %convolution_add_fusion.1, bf16[2304,128]{1,0:T(8,128)(2,1)S(1)} %bitcast.148, bf16[3,3,128,128]{3,2,1,0:T(8,128)(2,1)S(1)} %copy-done.1), kind=kOutput, calls=%fused_computation.16 | convolution fusion | flops 79921024 | bytes 3572224 | tf_op jit(solution)/shard_map/dot_general | solution.py:86
  34.1 0.4 convolution_dynamic-update-slice_fusion.6
  34.5 0.4 convolution_dynamic-update-slice_fusion.5
  35.2 0.4 fusion.5
  35.6 0.4 convolution_dynamic-update-slice_fusion.3
  35.9 0.4 convolution_dynamic-update-slice_fusion.2
  36.3 0.4 convolution_dynamic-update-slice_fusion.1
  36.7 0.4 convolution_dynamic-update-slice_fusion
  37.2 2.2 %collective-permute-start.12 = (f32[73792]{0:T(1024)S(1)}, f32[73792]{0:T(1024)S(1)}, u32[]{:S(2)}, u32[]{:S(2)}) collective-permute-start(f32[73792]{0:T(1024)S(1)} %dynamic_slice.19), channel_id=1, source_target_pairs={{0,8},{8,0},{16,24},{24,16},{32,40},{40,32},{48,56},{56,48},{64,72... | collective-permute-start | bytes 885512 | tf_op jit(solution)/shard_map/ppermute | solution.py:44
  39.4 1.2 %collective-permute-done.12 = f32[73792]{0:T(1024)S(1)} collective-permute-done((f32[73792]{0:T(1024)S(1)}, f32[73792]{0:T(1024)S(1)}, u32[]{:S(2)}, u32[]{:S(2)}) %collective-permute-start.12) | collective-permute-done | bytes 295200 | tf_op jit(solution)/shard_map/ppermute | solution.py:44
  40.9 2.6 %collective-permute-start.13 = (f32[36896]{0:T(1024)S(1)}, f32[36896]{0:T(1024)S(1)}, u32[]{:S(2)}, u32[]{:S(2)}) collective-permute-start(f32[36896]{0:T(1024)S(1)} %dynamic_slice.21), channel_id=1, source_target_pairs={{0,1},{1,0},{2,3},{3,2},{4,5},{5,4},{6,7},{7,6},{8,9},{9,8},{10,11... | collective-permute-start | bytes 442760 | tf_op jit(solution)/shard_map/ppermute | solution.py:44
  44.1 3.3 %collective-permute-done.13 = f32[36896]{0:T(1024)S(1)} collective-permute-done((f32[36896]{0:T(1024)S(1)}, f32[36896]{0:T(1024)S(1)}, u32[]{:S(2)}, u32[]{:S(2)}) %collective-permute-start.13) | collective-permute-done | bytes 147616 | tf_op jit(solution)/shard_map/ppermute | solution.py:44
  47.8 1.8 %convolution_select_fusion = f32[50,8,7,128]{3,1,2,0:T(8,128)S(1)} fusion(bf16[3,3,128,128]{3,2,1,0:T(8,128)(2,1)S(1)} %copy-done.1, bf16[52,1,7,2,128]{4,2,3,0,1:T(8,128)(2,1)S(1)} %slice.281, bf16[52,1,8,7,128]{4,2,3,0,1:T(8,128)(2,1)S(1)} %copy.10, pred[8,7]{0,1:T(8,128)(4,1)S(1)} %copy-done.4), kind=kOutput, calls=%fused_computation.11 | convolution fusion | flops 828987392 | bytes 2660408 | tf_op jit(solution)/shard_map/conv_general_dilated | solution.py:93
  49.6 1.4 %collective-permute-done.14 = f32[18448]{0:T(1024)S(1)} collective-permute-done((f32[18448]{0:T(1024)S(1)}, f32[18448]{0:T(1024)S(1)}, u32[]{:S(2)}, u32[]{:S(2)}) %collective-permute-start.14) | collective-permute-done | bytes 73824 | tf_op jit(solution)/shard_map/ppermute | solution.py:44
  51.1 2.2 %collective-permute-start.15 = (f32[18448]{0:T(1024)S(1)}, f32[18448]{0:T(1024)S(1)}, u32[]{:S(2)}, u32[]{:S(2)}) collective-permute-start(f32[18448]{0:T(1024)S(1)} %dynamic-slice_add_fusion.2), channel_id=1, source_target_pairs={{0,2},{1,3},{2,0},{3,1},{4,6},{5,7},{6,4},{7,5},{8,10},{9,11},{10,... | collective-permute-start | bytes 221384 | tf_op jit(solution)/shard_map/ppermute | solution.py:49
  53.4 1.7 %collective-permute-done.15 = f32[18448]{0:T(1024)S(1)} collective-permute-done((f32[18448]{0:T(1024)S(1)}, f32[18448]{0:T(1024)S(1)}, u32[]{:S(2)}, u32[]{:S(2)}) %collective-permute-start.15) | collective-permute-done | bytes 73824 | tf_op jit(solution)/shard_map/ppermute | solution.py:49
  55.2 0.8 collective-permute-start.16
  56.1 2.5 %collective-permute-start.6 = (bf16[1,50,128]{2,1,0:T(8,128)(2,1)S(1)}, bf16[1,50,128]{2,1,0:T(8,128)(2,1)S(1)}, u32[]{:S(2)}, u32[]{:S(2)}) collective-permute-start(bf16[1,50,128]{2,1,0:T(8,128)(2,1)S(1)} %get-tuple-element.80), channel_id=1, source_target_pairs={{0,1},{1,2},{2,3},{3,4},{4,5},{5,6},{6,7},{8,9},{9,10},{10,11},{11... | collective-permute-start | bytes 38408 | tf_op jit(solution)/shard_map/ppermute | solution.py:15
  58.6 1.4 %collective-permute-done.16 = f32[18448]{0:T(1024)S(1)} collective-permute-done((f32[18448]{0:T(1024)S(1)}, f32[18448]{0:T(1024)S(1)}, u32[]{:S(2)}, u32[]{:S(2)}) %collective-permute-start.16) | collective-permute-done | bytes 73824 | tf_op jit(solution)/shard_map/ppermute | solution.py:49
  60.3 1.3 %collective-permute-start.7 = (bf16[1,50,128]{2,1,0:T(8,128)(2,1)S(1)}, bf16[1,50,128]{2,1,0:T(8,128)(2,1)S(1)}, u32[]{:S(2)}, u32[]{:S(2)}) collective-permute-start(bf16[1,50,128]{2,1,0:T(8,128)(2,1)S(1)} %get-tuple-element.81), channel_id=1, source_target_pairs={{1,0},{2,1},{3,2},{4,3},{5,4},{6,5},{7,6},{9,8},{10,9},{11,10},{12... | collective-permute-start | bytes 38408 | tf_op jit(solution)/shard_map/ppermute | solution.py:17
  61.6 3.4 %collective-permute-start.8 = (bf16[50,128]{1,0:T(8,128)(2,1)S(1)}, bf16[50,128]{1,0:T(8,128)(2,1)S(1)}, u32[]{:S(2)}, u32[]{:S(2)}) collective-permute-start(bf16[50,128]{1,0:T(8,128)(2,1)S(1)} %get-tuple-element.82), channel_id=1, source_target_pairs={{0,128},{8,136},{16,144},{24,152},{32,160},{40,168},{48,176},{56,1... | collective-permute-start | bytes 38408 | tf_op jit(solution)/shard_map/ppermute | solution.py:27
  65.0 2.0 %collective-permute-start.9 = (bf16[50,128]{1,0:T(8,128)(2,1)S(1)}, bf16[50,128]{1,0:T(8,128)(2,1)S(1)}, u32[]{:S(2)}, u32[]{:S(2)}) collective-permute-start(bf16[50,128]{1,0:T(8,128)(2,1)S(1)} %get-tuple-element.79), channel_id=1, source_target_pairs={{0,128},{8,136},{16,144},{24,152},{32,160},{40,168},{48,176},{56,1... | collective-permute-start | bytes 38408 | tf_op jit(solution)/shard_map/ppermute | solution.py:27
  67.3 3.4 %collective-permute-start.18 = (f32[18448]{0:T(1024)S(1)}, f32[18448]{0:T(1024)S(1)}, u32[]{:S(2)}, u32[]{:S(2)}) collective-permute-start(f32[18448]{0:T(1024)S(1)} %add.165), channel_id=1, source_target_pairs={{0,128},{8,136},{16,144},{24,152},{32,160},{40,168},{48,176},{56,1... | collective-permute-start | bytes 221384 | tf_op jit(solution)/shard_map/ppermute | solution.py:49
  70.9 3.8 %collective-permute-done.18 = f32[18448]{0:T(1024)S(1)} collective-permute-done((f32[18448]{0:T(1024)S(1)}, f32[18448]{0:T(1024)S(1)}, u32[]{:S(2)}, u32[]{:S(2)}) %collective-permute-start.18) | collective-permute-done | bytes 73824 | tf_op jit(solution)/shard_map/ppermute | solution.py:49
  74.8 5.1 %collective-permute-start.19 = (f32[18448]{0:T(1024)S(1)}, f32[18448]{0:T(1024)S(1)}, u32[]{:S(2)}, u32[]{:S(2)}) collective-permute-start(f32[18448]{0:T(1024)S(1)} %add.166), channel_id=1, source_target_pairs={{0,4},{1,5},{2,6},{3,7},{4,0},{5,1},{6,2},{7,3},{8,12},{9,13},{10,... | collective-permute-start | bytes 221384 | tf_op jit(solution)/shard_map/ppermute | solution.py:49
  80.1 1.6 %collective-permute-done.19 = f32[18448]{0:T(1024)S(1)} collective-permute-done((f32[18448]{0:T(1024)S(1)}, f32[18448]{0:T(1024)S(1)}, u32[]{:S(2)}, u32[]{:S(2)}) %collective-permute-start.19) | collective-permute-done | bytes 73824 | tf_op jit(solution)/shard_map/ppermute | solution.py:49
  81.7 1.7 %collective-permute-start.20 = (f32[18448]{0:T(1024)S(1)}, f32[18448]{0:T(1024)S(1)}, u32[]{:S(2)}, u32[]{:S(2)}) collective-permute-start(f32[18448]{0:T(1024)S(1)} %add.167), channel_id=1, source_target_pairs={{0,32},{8,40},{16,48},{24,56},{32,0},{40,8},{48,16},{56,24},{64,96... | collective-permute-start | bytes 221384 | tf_op jit(solution)/shard_map/ppermute | solution.py:53
  83.7 1.4 %collective-permute-done.20 = f32[18448]{0:T(1024)S(1)} collective-permute-done((f32[18448]{0:T(1024)S(1)}, f32[18448]{0:T(1024)S(1)}, u32[]{:S(2)}, u32[]{:S(2)}) %collective-permute-start.20) | collective-permute-done | bytes 73824 | tf_op jit(solution)/shard_map/ppermute | solution.py:53
  85.2 0.5 collective-permute-start.21
  85.7 11.1 %collective-permute-start.10 = (bf16[48,1,128]{2,0,1:T(8,128)(2,1)S(1)}, bf16[48,1,128]{2,0,1:T(8,128)(2,1)S(1)}, u32[]{:S(2)}, u32[]{:S(2)}) collective-permute-start(bf16[48,1,128]{2,0,1:T(8,128)(2,1)S(1)} %get-tuple-element.71), channel_id=1, source_target_pairs={{0,8},{8,16},{16,24},{24,32},{32,40},{40,48},{48,56},{56,64},{64,7... | collective-permute-start | bytes 36872 | tf_op jit(solution)/shard_map/ppermute | solution.py:15
  97.0 3.0 %collective-permute-start.22 = (f32[73792]{0:T(1024)S(1)}, f32[73792]{0:T(1024)S(1)}, u32[]{:S(2)}, u32[]{:S(2)}) collective-permute-start(f32[73792]{0:T(1024)S(1)} %maximum_select_fusion.1), channel_id=1, source_target_pairs={{0,8},{8,0},{16,24},{24,16},{32,40},{40,32},{48,56},{56,48},{64,72... | collective-permute-start | bytes 885512 | tf_op jit(solution)/shard_map/ppermute | solution.py:53
  100.0 1.4 %collective-permute-done.11 = bf16[48,1,128]{2,0,1:T(8,128)(2,1)S(1)} collective-permute-done((bf16[48,1,128]{2,0,1:T(8,128)(2,1)S(1)}, bf16[48,1,128]{2,0,1:T(8,128)(2,1)S(1)}, u32[]{:S(2)}, u32[]{:S(2)}) %collective-permute-start.11) | collective-permute-done | bytes 12320 | tf_op jit(solution)/shard_map/ppermute | solution.py:17
  101.5 1.0 copy.17
  102.7 0.9 slice_multiply_fusion
  103.6 0.5 slice_multiply_fusion.1
  (80 shorter events, 6.7 us)
Async XLA Ops:
  0.6 10.0 %copy-start = (bf16[48,48,128]{2,1,0:T(8,128)(2,1)S(1)}, bf16[48,48,128]{2,1,0:T(8,128)(2,1)}, u32[]{:S(2)}) copy-start(bf16[48,48,128]{2,1,0:T(8,128)(2,1)} %param.12) | copy-start | bytes 1769476
  1.7 5.6 %collective-permute-start = (bf16[48,1,128]{2,1,0:T(2,128)(2,1)S(1)}, bf16[48,1,128]{2,1,0:T(2,128)(2,1)S(1)}, u32[]{:S(2)}, u32[]{:S(2)}) collective-permute-start(bf16[48,1,128]{2,1,0:T(2,128)(2,1)S(1)} %get-tuple-element.75), channel_id=1, source_target_pairs={{0,8},{8,16},{16,24},{24,32},{32,40},{40,48},{48,56},{56,64},{64,7... | collective-permute-start | bytes 36872 | tf_op jit(solution)/shard_map/ppermute | solution.py:15
  5.9 4.8 %collective-permute-start.1 = (bf16[48,1,128]{2,1,0:T(2,128)(2,1)S(1)}, bf16[48,1,128]{2,1,0:T(2,128)(2,1)S(1)}, u32[]{:S(2)}, u32[]{:S(2)}) collective-permute-start(bf16[48,1,128]{2,1,0:T(2,128)(2,1)S(1)} %get-tuple-element.76), channel_id=1, source_target_pairs={{8,0},{16,8},{24,16},{32,24},{40,32},{48,40},{56,48},{64,56},{72,6... | collective-permute-start | bytes 36872 | tf_op jit(solution)/shard_map/ppermute | solution.py:17
  10.7 17.1 %collective-permute-start.3 = (bf16[1,50,128]{2,1,0:T(8,128)(2,1)S(1)}, bf16[1,50,128]{2,1,0:T(8,128)(2,1)S(1)}, u32[]{:S(2)}, u32[]{:S(2)}) collective-permute-start(bf16[1,50,128]{2,1,0:T(8,128)(2,1)S(1)} %get-tuple-element.70), channel_id=1, source_target_pairs={{0,1},{1,2},{2,3},{3,4},{4,5},{5,6},{6,7},{8,9},{9,10},{10,11},{11... | collective-permute-start | bytes 38408 | tf_op jit(solution)/shard_map/ppermute | solution.py:15
  12.9 8.9 %collective-permute-start.4 = (bf16[50,128]{1,0:T(8,128)(2,1)S(1)}, bf16[50,128]{1,0:T(8,128)(2,1)S(1)}, u32[]{:S(2)}, u32[]{:S(2)}) collective-permute-start(bf16[50,128]{1,0:T(8,128)(2,1)S(1)} %bitcast.154), channel_id=1, source_target_pairs={{0,128},{8,136},{16,144},{24,152},{32,160},{40,168},{48,176},{56,1... | collective-permute-start | bytes 38408 | tf_op jit(solution)/shard_map/ppermute | solution.py:27
  19.9 5.2 %collective-permute-start.5 = (bf16[1,50,128]{2,1,0:T(8,128)(2,1)S(1)}, bf16[1,50,128]{2,1,0:T(8,128)(2,1)S(1)}, u32[]{:S(2)}, u32[]{:S(2)}) collective-permute-start(bf16[1,50,128]{2,1,0:T(8,128)(2,1)S(1)} %get-tuple-element.69), channel_id=1, source_target_pairs={{1,0},{2,1},{3,2},{4,3},{5,4},{6,5},{7,6},{9,8},{10,9},{11,10},{12... | collective-permute-start | bytes 38408 | tf_op jit(solution)/shard_map/ppermute | solution.py:17
  21.2 6.6 %collective-permute-start.2 = (bf16[50,128]{1,0:T(8,128)(2,1)S(1)}, bf16[50,128]{1,0:T(8,128)(2,1)S(1)}, u32[]{:S(2)}, u32[]{:S(2)}) collective-permute-start(bf16[50,128]{1,0:T(8,128)(2,1)S(1)} %bitcast.155), channel_id=1, source_target_pairs={{0,128},{8,136},{16,144},{24,152},{32,160},{40,168},{48,176},{56,1... | collective-permute-start | bytes 38408 | tf_op jit(solution)/shard_map/ppermute | solution.py:27
  28.2 1.0 copy-start.1
  28.9 0.7 copy-start.2
  31.1 1.1 %copy-start.3 = (bf16[48,48,128]{2,1,0:T(8,128)(2,1)S(1)}, bf16[48,48,128]{2,1,0:T(8,128)(2,1)}, u32[]{:S(2)}) copy-start(bf16[48,48,128]{2,1,0:T(8,128)(2,1)} %param.15) | copy-start | bytes 1769476
  37.2 3.4 %collective-permute-start.12 = (f32[73792]{0:T(1024)S(1)}, f32[73792]{0:T(1024)S(1)}, u32[]{:S(2)}, u32[]{:S(2)}) collective-permute-start(f32[73792]{0:T(1024)S(1)} %dynamic_slice.19), channel_id=1, source_target_pairs={{0,8},{8,0},{16,24},{24,16},{32,40},{40,32},{48,56},{56,48},{64,72... | collective-permute-start | bytes 885512 | tf_op jit(solution)/shard_map/ppermute | solution.py:44
  40.9 6.6 %collective-permute-start.13 = (f32[36896]{0:T(1024)S(1)}, f32[36896]{0:T(1024)S(1)}, u32[]{:S(2)}, u32[]{:S(2)}) collective-permute-start(f32[36896]{0:T(1024)S(1)} %dynamic_slice.21), channel_id=1, source_target_pairs={{0,1},{1,0},{2,3},{3,2},{4,5},{5,4},{6,7},{7,6},{8,9},{9,8},{10,11... | collective-permute-start | bytes 442760 | tf_op jit(solution)/shard_map/ppermute | solution.py:44
  44.0 3.8 %copy-start.4 = (pred[8,7]{0,1:T(8,128)(4,1)S(1)}, pred[8,7]{0,1:T(8,128)(4,1)}, u32[]{:S(2)}) copy-start(pred[8,7]{0,1:T(8,128)(4,1)} %constant.193) | copy-start | bytes 172
  47.7 3.3 %collective-permute-start.14 = (f32[18448]{0:T(1024)S(1)}, f32[18448]{0:T(1024)S(1)}, u32[]{:S(2)}, u32[]{:S(2)}) collective-permute-start(f32[18448]{0:T(1024)S(1)} %dynamic_slice.23), channel_id=1, source_target_pairs={{0,32},{8,40},{16,48},{24,56},{32,0},{40,8},{48,16},{56,24},{64,96... | collective-permute-start | bytes 221384 | tf_op jit(solution)/shard_map/ppermute | solution.py:44
  51.1 4.0 %collective-permute-start.15 = (f32[18448]{0:T(1024)S(1)}, f32[18448]{0:T(1024)S(1)}, u32[]{:S(2)}, u32[]{:S(2)}) collective-permute-start(f32[18448]{0:T(1024)S(1)} %dynamic-slice_add_fusion.2), channel_id=1, source_target_pairs={{0,2},{1,3},{2,0},{3,1},{4,6},{5,7},{6,4},{7,5},{8,10},{9,11},{10,... | collective-permute-start | bytes 221384 | tf_op jit(solution)/shard_map/ppermute | solution.py:49
  55.2 4.8 %collective-permute-start.16 = (f32[18448]{0:T(1024)S(1)}, f32[18448]{0:T(1024)S(1)}, u32[]{:S(2)}, u32[]{:S(2)}) collective-permute-start(f32[18448]{0:T(1024)S(1)} %add.163), channel_id=1, source_target_pairs={{0,16},{8,24},{16,0},{24,8},{32,48},{40,56},{48,32},{56,40},{64,80... | collective-permute-start | bytes 221384 | tf_op jit(solution)/shard_map/ppermute | solution.py:49
  56.1 23.8 %collective-permute-start.6 = (bf16[1,50,128]{2,1,0:T(8,128)(2,1)S(1)}, bf16[1,50,128]{2,1,0:T(8,128)(2,1)S(1)}, u32[]{:S(2)}, u32[]{:S(2)}) collective-permute-start(bf16[1,50,128]{2,1,0:T(8,128)(2,1)S(1)} %get-tuple-element.80), channel_id=1, source_target_pairs={{0,1},{1,2},{2,3},{3,4},{4,5},{5,6},{6,7},{8,9},{9,10},{10,11},{11... | collective-permute-start | bytes 38408 | tf_op jit(solution)/shard_map/ppermute | solution.py:15
  60.0 7.3 %collective-permute-start.17 = (f32[18448]{0:T(1024)S(1)}, f32[18448]{0:T(1024)S(1)}, u32[]{:S(2)}, u32[]{:S(2)}) collective-permute-start(f32[18448]{0:T(1024)S(1)} %add.164), channel_id=1, source_target_pairs={{0,64},{8,72},{16,80},{24,88},{32,96},{40,104},{48,112},{56,120},{... | collective-permute-start | bytes 221384 | tf_op jit(solution)/shard_map/ppermute | solution.py:49
  60.3 19.6 %collective-permute-start.7 = (bf16[1,50,128]{2,1,0:T(8,128)(2,1)S(1)}, bf16[1,50,128]{2,1,0:T(8,128)(2,1)S(1)}, u32[]{:S(2)}, u32[]{:S(2)}) collective-permute-start(bf16[1,50,128]{2,1,0:T(8,128)(2,1)S(1)} %get-tuple-element.81), channel_id=1, source_target_pairs={{1,0},{2,1},{3,2},{4,3},{5,4},{6,5},{7,6},{9,8},{10,9},{11,10},{12... | collective-permute-start | bytes 38408 | tf_op jit(solution)/shard_map/ppermute | solution.py:17
  61.6 18.3 %collective-permute-start.8 = (bf16[50,128]{1,0:T(8,128)(2,1)S(1)}, bf16[50,128]{1,0:T(8,128)(2,1)S(1)}, u32[]{:S(2)}, u32[]{:S(2)}) collective-permute-start(bf16[50,128]{1,0:T(8,128)(2,1)S(1)} %get-tuple-element.82), channel_id=1, source_target_pairs={{0,128},{8,136},{16,144},{24,152},{32,160},{40,168},{48,176},{56,1... | collective-permute-start | bytes 38408 | tf_op jit(solution)/shard_map/ppermute | solution.py:27
  65.0 14.9 %collective-permute-start.9 = (bf16[50,128]{1,0:T(8,128)(2,1)S(1)}, bf16[50,128]{1,0:T(8,128)(2,1)S(1)}, u32[]{:S(2)}, u32[]{:S(2)}) collective-permute-start(bf16[50,128]{1,0:T(8,128)(2,1)S(1)} %get-tuple-element.79), channel_id=1, source_target_pairs={{0,128},{8,136},{16,144},{24,152},{32,160},{40,168},{48,176},{56,1... | collective-permute-start | bytes 38408 | tf_op jit(solution)/shard_map/ppermute | solution.py:27
  67.3 7.4 %collective-permute-start.18 = (f32[18448]{0:T(1024)S(1)}, f32[18448]{0:T(1024)S(1)}, u32[]{:S(2)}, u32[]{:S(2)}) collective-permute-start(f32[18448]{0:T(1024)S(1)} %add.165), channel_id=1, source_target_pairs={{0,128},{8,136},{16,144},{24,152},{32,160},{40,168},{48,176},{56,1... | collective-permute-start | bytes 221384 | tf_op jit(solution)/shard_map/ppermute | solution.py:49
  74.8 6.9 %collective-permute-start.19 = (f32[18448]{0:T(1024)S(1)}, f32[18448]{0:T(1024)S(1)}, u32[]{:S(2)}, u32[]{:S(2)}) collective-permute-start(f32[18448]{0:T(1024)S(1)} %add.166), channel_id=1, source_target_pairs={{0,4},{1,5},{2,6},{3,7},{4,0},{5,1},{6,2},{7,3},{8,12},{9,13},{10,... | collective-permute-start | bytes 221384 | tf_op jit(solution)/shard_map/ppermute | solution.py:49
  81.7 3.4 %collective-permute-start.20 = (f32[18448]{0:T(1024)S(1)}, f32[18448]{0:T(1024)S(1)}, u32[]{:S(2)}, u32[]{:S(2)}) collective-permute-start(f32[18448]{0:T(1024)S(1)} %add.167), channel_id=1, source_target_pairs={{0,32},{8,40},{16,48},{24,56},{32,0},{40,8},{48,16},{56,24},{64,96... | collective-permute-start | bytes 221384 | tf_op jit(solution)/shard_map/ppermute | solution.py:53
  85.2 11.6 %collective-permute-start.21 = (f32[36896]{0:T(1024)S(1)}, f32[36896]{0:T(1024)S(1)}, u32[]{:S(2)}, u32[]{:S(2)}) collective-permute-start(f32[36896]{0:T(1024)S(1)} %maximum_select_fusion.2), channel_id=1, source_target_pairs={{0,1},{1,0},{2,3},{3,2},{4,5},{5,4},{6,7},{7,6},{8,9},{9,8},{10,11... | collective-permute-start | bytes 442760 | tf_op jit(solution)/shard_map/ppermute | solution.py:53
  85.7 14.3 %collective-permute-start.10 = (bf16[48,1,128]{2,0,1:T(8,128)(2,1)S(1)}, bf16[48,1,128]{2,0,1:T(8,128)(2,1)S(1)}, u32[]{:S(2)}, u32[]{:S(2)}) collective-permute-start(bf16[48,1,128]{2,0,1:T(8,128)(2,1)S(1)} %get-tuple-element.71), channel_id=1, source_target_pairs={{0,8},{8,16},{16,24},{24,32},{32,40},{40,48},{48,56},{56,64},{64,7... | collective-permute-start | bytes 36872 | tf_op jit(solution)/shard_map/ppermute | solution.py:15
  96.8 4.6 %collective-permute-start.11 = (bf16[48,1,128]{2,0,1:T(8,128)(2,1)S(1)}, bf16[48,1,128]{2,0,1:T(8,128)(2,1)S(1)}, u32[]{:S(2)}, u32[]{:S(2)}) collective-permute-start(bf16[48,1,128]{2,0,1:T(8,128)(2,1)S(1)} %get-tuple-element.72), channel_id=1, source_target_pairs={{8,0},{16,8},{24,16},{32,24},{40,32},{48,40},{56,48},{64,56},{72,6... | collective-permute-start | bytes 36872 | tf_op jit(solution)/shard_map/ppermute | solution.py:17
  97.0 5.5 %collective-permute-start.22 = (f32[73792]{0:T(1024)S(1)}, f32[73792]{0:T(1024)S(1)}, u32[]{:S(2)}, u32[]{:S(2)}) collective-permute-start(f32[73792]{0:T(1024)S(1)} %maximum_select_fusion.1), channel_id=1, source_target_pairs={{0,8},{8,0},{16,24},{24,16},{32,40},{40,32},{48,56},{56,48},{64,72... | collective-permute-start | bytes 885512 | tf_op jit(solution)/shard_map/ppermute | solution.py:53

commit v3 on v2

--- a/solution.py
+++ b/solution.py
@@ -73,35 +73,57 @@
     band = lax.axis_index("lat")
     bands = lax.axis_size("lat")
     half = lax.axis_size("lon") // 2
-    wide = extended(inputs, (("lon", 1),), 1, True)
-    tall = extended(wide, (("lat", 0),), 1, False)
-    far_top, far_bottom = from_behind((wide[0], wide[-1]), "lon", half)
-    top = jnp.where(band == 0, far_top, tall[0])
-    bottom = jnp.where(band == bands - 1, far_bottom, tall[-1])
-    padded = jnp.concatenate([top[None], tall[1:-1], bottom[None]], axis=0)
-    pre = jnp.zeros((rows * cols, chans), jnp.float32) + bias[None, :]
-    for tap_a in range(3):
-        for tap_b in range(3):
-            window = padded[tap_a : tap_a + rows, tap_b : tap_b + cols].reshape(rows * cols, chans)
-            pre = pre + jnp.dot(window, weight[tap_a, tap_b], preferred_element_type=jnp.float32)
+    both = jnp.concatenate([inputs, cotangent], axis=2)
+    wide = extended(both, (("lon", 1),), 2, True)
+    tall = extended(wide, (("lat", 0),), 2, False)
+    far = from_behind(jnp.stack([wide[0], wide[-1]]), "lon", half)
+    tall = tall.at[1].set(jnp.where(band == 0, far[0], tall[1]))
+    tall = tall.at[rows + 2].set(jnp.where(band == bands - 1, far[1], tall[rows + 2]))
+    padded = tall[:, :, :chans]
+    flat_cot = tall[1:-1, 1:-1, chans:].reshape((rows + 2) * (cols + 2), chans).astype(jnp.float32)
+    pre = lax.conv_general_dilated(
+        padded[None],
+        weight,
+        (1, 1),
+        "VALID",
+        dimension_numbers=("NHWC", "HWIO", "NHWC"),
+        preferred_element_type=jnp.float32,
+    )[0].reshape((rows + 2) * (cols + 2), chans) + bias[None, :]
     sig = jax.nn.sigmoid(pre)
-    outputs = (pre * sig).astype(jnp.bfloat16).reshape(rows, cols, chans)
-    flat_cot = cotangent.reshape(rows * cols, chans).astype(jnp.float32)
-    pre_grad = (flat_cot * sig * (1.0 + pre * (1.0 - sig))).astype(jnp.bfloat16)
-    grad_cells = pre_grad.reshape(rows, cols, chans)
+    silu = (pre * sig).reshape(rows + 2, cols + 2, chans)
+    outputs = silu[1:-1, 1:-1].astype(jnp.bfloat16)
+    grad_ext = (flat_cot * sig * (1.0 + pre * (1.0 - sig))).astype(jnp.bfloat16).reshape(rows + 2, cols + 2, chans)
+    line = lax.broadcasted_iota(jnp.int32, (rows + 2, 1, 1), 0)
+    outside = ((line == 0) & (band == 0)) | ((line == rows + 1) & (band == bands - 1))
+    grad_ext = jnp.where(outside, jnp.zeros_like(grad_ext), grad_ext)
+    pre_grad = grad_ext[1:-1, 1:-1].reshape(rows * cols, chans)
     flipped = jnp.transpose(weight[::-1, ::-1], (0, 1, 3, 2))
-    padded_grad = lax.conv_general_dilated(
-        jnp.pad(grad_cells, ((2, 2), (2, 2), (0, 0)))[None],
+    cell_grad = lax.conv_general_dilated(
+        grad_ext[None],
         flipped,
         (1, 1),
         "VALID",
         dimension_numbers=("NHWC", "HWIO", "NHWC"),
         preferred_element_type=jnp.float32,
     )[0]
+    polar = []
+    for line_at, tap_a in ((1, 0), (rows, 2)):
+        ring = jnp.zeros((cols, chans), jnp.float32)
+        for tap_b in range(3):
+            ring = ring + jnp.dot(
+                grad_ext[line_at, tap_b : tap_b + cols],
+                weight[tap_a, 2 - tap_b].T,
+                preferred_element_type=jnp.float32,
+            )
+        polar.append(ring)
+    polar_in = from_behind(jnp.stack(polar).astype(jnp.bfloat16), "lon", half).astype(jnp.float32)
+    cell_grad = cell_grad.at[0].add(jnp.where(band == 0, polar_in[0], 0.0))
+    cell_grad = cell_grad.at[-1].add(jnp.where(band == bands - 1, polar_in[1], 0.0))
+    input_grad = cell_grad.astype(jnp.bfloat16)
     taps = []
     for tap_a in range(3):
         for tap_b in range(3):
-            window = padded[tap_a : tap_a + rows, tap_b : tap_b + cols].reshape(rows * cols, chans)
+            window = padded[tap_a + 1 : tap_a + 1 + rows, tap_b + 1 : tap_b + 1 + cols].reshape(rows * cols, chans)
             taps.append(
                 lax.dot_general(
                     window, pre_grad, (((0,), (0,)), ((), ())), preferred_element_type=jnp.float32
@@ -109,21 +131,6 @@
             )
     kernel_terms = jnp.concatenate(taps, axis=0)
     bias_terms = jnp.sum(pre_grad.astype(jnp.float32), axis=0)[None, :]
-    edges = jnp.stack([padded_grad[0], padded_grad[-1]], axis=0)
-    beside_all = extended(edges.astype(jnp.bfloat16), (("lat", 0),), 1, False).astype(edges.dtype)
-    polar_top, polar_bottom = (
-        from_behind(padded_grad[0].astype(jnp.bfloat16), "lon", half).astype(jnp.float32),
-        from_behind(padded_grad[-1].astype(jnp.bfloat16), "lon", half).astype(jnp.float32),
-    )
-    inner = padded_grad[1:-1]
-    inner = inner.at[0].add(beside_all[0] + jnp.where(band == 0, polar_top, 0.0))
-    inner = inner.at[-1].add(beside_all[3] + jnp.where(band == bands - 1, polar_bottom, 0.0))
-    sides = jnp.stack([inner[:, 0], inner[:, -1]], axis=1)
-    beside = extended(sides.astype(jnp.bfloat16), (("lon", 1),), 1, True).astype(sides.dtype)
-    core = inner[:, 1:-1]
-    core = core.at[:, 0].add(beside[:, 0])
-    core = core.at[:, -1].add(beside[:, 3])
-    input_grad = core.astype(jnp.bfloat16)
     order = pairing_order(("lon", "lat"))
     sums = butterfly_sum(jnp.concatenate([kernel_terms, bias_terms], axis=0), order[:3], order[3:])
     kernel_sum, bias_sum = sums[:-1], sums[-1:]

time: 104 us -> 98.8 us (0.950)
  starting transfers between devices: 57.1 us -> 46 us
  other arithmetic: 3.53 us -> 8.35 us
  waiting for transfers between devices: 26.6 us -> 22.6 us
  matrix products: 10.1 us -> 13.5 us
    ppermute x4 -> x2, starting transfers between devices: 20 us -> 6.42 us  [extended(): lax.ppermute(tail, axis, [(i, (i + 1) % count) for i in range(ends)])]
    ppermute x3, starting transfers between devices: 5.15 us -> 11.7 us  [butterfly_sum(): other = lax.ppermute(data, axis, pairs)]
    ppermute x4 -> x2, starting transfers between devices: 12.6 us -> 8.12 us  [from_behind(): return lax.ppermute(value, axis, pairs)]
    ppermute x4 -> x2, waiting for transfers between devices: 8.01 us -> 3.84 us  [extended(): lax.ppermute(head, axis, [((i + 1) % count, i) for i in range(ends)])]
    select_n x0 -> x1, other arithmetic: none -> 2.49 us  [shards(): grad_ext = jnp.where(outside, jnp.zeros_like(grad_ext), grad_ext)]
    conv_general_dilated x7 -> x11, local copies, waits for them, and re-layouts: 0.56 us -> 2.53 us  [the longest x4 1.76 us: shards(): lax.conv_general_dilated(padded[None], weight, (1, 1), 'VALID', dimension...]
    conv_general_dilated x1 -> x2, matrix products: 1.84 us -> 3.72 us  [the longest x1 1.9 us: shards(): lax.conv_general_dilated(padded[None], weight, (1, 1), 'VALID', dimension...]
    ppermute x4 -> x2, waiting for transfers between devices: 2.68 us -> 0.87 us  [from_behind(): return lax.ppermute(value, axis, pairs)]
  transfers between devices with their start and end apart: 23 -> 17, of which waited for: 12 -> 14; matrix products, arithmetic and copies ran while one was open for 6% -> 12% of each run, Pallas kernels for 0% -> 0%
where the time goes in v3:
time: 98.8 us; the launch traced here: 98.2 us
  starting transfers between devices  46 us (47%)
  waiting for transfers between devices  22.6 us (23%)
  matrix products  13.5 us (14%)
  other arithmetic  8.35 us (8%)
  local copies, waits for them, and re-layouts  6.75 us (7%)
  between operations  1.07 us (1%)
    ppermute x5, starting transfers between devices, butterfly_sum(): data = data + lax.ppermute(data, axis, pairs)  13.3 us
    ppermute x3, starting transfers between devices, butterfly_sum(): other = lax.ppermute(data, axis, pairs)  11.7 us
    ppermute x5, waiting for transfers between devices, butterfly_sum(): data = data + lax.ppermute(data, axis, pairs)  9.48 us
    ppermute x2, starting transfers between devices, from_behind(): return lax.ppermute(value, axis, pairs)  8.12 us
    ppermute x2, starting transfers between devices, extended(): lax.ppermute(tail, axis, [(i, (i + 1) % count) for i in range(ends)])  6.42 us
    ppermute x3, waiting for transfers between devices, butterfly_sum(): data = keep + lax.ppermute(send, axis, pairs)  5.36 us
    dot_general x6, matrix products, shards(): jnp.dot(grad_ext[line_at, tap_b:tap_b + cols], weight[tap_a, 2 - tap_b].T...  5.31 us
    ppermute x3, starting transfers between devices, butterfly_sum(): data = keep + lax.ppermute(send, axis, pairs)  5.15 us
  transfers between devices with their start and end apart: 17, of which 14 were waited for; matrix products, arithmetic and copies ran while one was open for 12% of the time, Pallas kernels for 0%

profile of v3, /device:TPU:1, one launch (start us, length us, event | category | flops | bytes accessed | tf_op | source)
XLA Modules:
  0.0 98.2 jit_solution(2576384811719228763)
XLA Ops:
  0.6 1.2 %constant_dynamic-update-slice_fusion.1 = bf16[48,48,256]{2,1,0:T(8,128)(2,1)S(1)} fusion(bf16[48,48,128]{2,1,0:T(8,128)(2,1)} %param.12), kind=kLoop, calls=%fused_computation.113 | loop fusion | bytes 1179648
  2.1 4.2 %collective-permute-start = (bf16[48,2,256]{2,1,0:T(2,128)(2,1)S(1)}, bf16[48,2,256]{2,1,0:T(2,128)(2,1)S(1)}, u32[]{:S(2)}, u32[]{:S(2)}) collective-permute-start(bf16[48,2,256]{2,1,0:T(2,128)(2,1)S(1)} %get-tuple-element.57), channel_id=1, source_target_pairs={{0,8},{8,16},{16,24},{24,32},{32,40},{40,48},{48,56},{56,64},{64,7... | collective-permute-start | bytes 147464 | tf_op jit(solution)/shard_map/ppermute | solution.py:15
  6.3 1.2 %collective-permute-done = bf16[48,2,256]{2,1,0:T(2,128)(2,1)S(1)} collective-permute-done((bf16[48,2,256]{2,1,0:T(2,128)(2,1)S(1)}, bf16[48,2,256]{2,1,0:T(2,128)(2,1)S(1)}, u32[]{:S(2)}, u32[]{:S(2)}) %collective-permute-start) | collective-permute-done | bytes 49184 | tf_op jit(solution)/shard_map/ppermute | solution.py:15
  7.5 3.8 %collective-permute-done.1 = bf16[48,2,256]{2,1,0:T(2,128)(2,1)S(1)} collective-permute-done((bf16[48,2,256]{2,1,0:T(2,128)(2,1)S(1)}, bf16[48,2,256]{2,1,0:T(2,128)(2,1)S(1)}, u32[]{:S(2)}, u32[]{:S(2)}) %collective-permute-start.1) | collective-permute-done | bytes 49184 | tf_op jit(solution)/shard_map/ppermute | solution.py:17
  11.4 2.2 %collective-permute-start.2 = (bf16[2,52,256]{2,1,0:T(8,128)(2,1)S(1)}, bf16[2,52,256]{2,1,0:T(8,128)(2,1)S(1)}, u32[]{:S(2)}, u32[]{:S(2)}) collective-permute-start(bf16[2,52,256]{2,1,0:T(8,128)(2,1)S(1)} %get-tuple-element.59), channel_id=1, source_target_pairs={{0,1},{1,2},{2,3},{3,4},{4,5},{5,6},{6,7},{8,9},{9,10},{10,11},{11... | collective-permute-start | bytes 159752 | tf_op jit(solution)/shard_map/ppermute | solution.py:15
  13.6 1.3 %collective-permute-start.3 = (bf16[2,52,256]{2,1,0:T(8,128)(2,1)S(1)}, bf16[2,52,256]{2,1,0:T(8,128)(2,1)S(1)}, u32[]{:S(2)}, u32[]{:S(2)}) collective-permute-start(bf16[2,52,256]{2,1,0:T(8,128)(2,1)S(1)} %get-tuple-element.60), channel_id=1, source_target_pairs={{1,0},{2,1},{3,2},{4,3},{5,4},{6,5},{7,6},{9,8},{10,9},{11,10},{12... | collective-permute-start | bytes 159752 | tf_op jit(solution)/shard_map/ppermute | solution.py:17
  15.0 7.2 %collective-permute-start.4 = (bf16[2,52,256]{2,1,0:T(8,128)(2,1)S(1)}, bf16[2,52,256]{2,1,0:T(8,128)(2,1)S(1)}, u32[]{:S(2)}, u32[]{:S(2)}) collective-permute-start(bf16[2,52,256]{2,1,0:T(8,128)(2,1)S(1)} %get-tuple-element.54), channel_id=1, source_target_pairs={{0,128},{8,136},{16,144},{24,152},{32,160},{40,168},{48,176},{56,1... | collective-permute-start | bytes 159752 | tf_op jit(solution)/shard_map/ppermute | solution.py:27
  22.2 0.8 pad_maximum_fusion
  23.0 0.9 collective-permute-done.4
  24.1 0.9 copy-done
  25.3 0.7 copy-done.3
  26.0 1.9 %convolution_select_fusion.1 = f32[50,8,7,128]{3,1,2,0:T(8,128)S(1)} fusion(bf16[3,3,128,128]{3,2,1,0:T(8,128)(2,1)S(1)} %copy-done.3, bf16[52,1,7,2,128]{4,2,3,0,1:T(8,128)(2,1)S(1)} %slice.267, bf16[52,1,8,7,128]{4,2,3,0,1:T(8,128)(2,1)S(1)} %copy.10, pred[8,7]{0,1:T(8,128)(4,1)S(1)} %copy-done.7), kind=kOutput, calls=%fused_computation.10 | convolution fusion | flops 828987392 | bytes 2660408 | tf_op jit(solution)/shard_map/conv_general_dilated | solution.py:84
  28.3 1.2 %reshape.185 = f32[50,1,56,128]{3,2,0,1:T(8,128)} reshape(f32[50,8,7,128]{3,2,1,0:T(8,128)S(1)} %copy.11) | data formatting | bytes 2867200 | tf_op jit(solution)/shard_map/conv_general_dilated | solution.py:84
  29.5 2.5 %fusion.29 = (bf16[50,50,128]{2,1,0:T(8,128)(2,1)S(1)}, f32[50,50,128]{2,1,0:T(8,128)S(1)}) fusion(bf16[52,52,256]{2,1,0:T(8,128)(2,1)} %copy-done, pred[50]{0:T(512)(128)(4,1)S(1)} %and_or_fusion, f32[128]{0:T(128)S(1)} %copy-done.5, f32[50,1,56,128]{3,2,0,1:T(8,128)} %reshape.185), kind=kLoop, calls=%fused_computation.52 | loop fusion | flops 3840000 | bytes 3840562 | tf_op jit(solution)/shard_map/jit(_where)/select_n | solution.py:98
  33.8 0.5 fusion.9
  34.8 0.5 fusion.7
  35.8 0.5 fusion.5
  37.0 1.8 %collective-permute-start.6 = (f32[73792]{0:T(1024)S(1)}, f32[73792]{0:T(1024)S(1)}, u32[]{:S(2)}, u32[]{:S(2)}) collective-permute-start(f32[73792]{0:T(1024)S(1)} %dynamic_slice.19), channel_id=1, source_target_pairs={{0,8},{8,0},{16,24},{24,16},{32,40},{40,32},{48,56},{56,48},{64,72... | collective-permute-start | bytes 885512 | tf_op jit(solution)/shard_map/ppermute | solution.py:44
  38.8 0.9 fusion.54
  40.3 2.9 %collective-permute-start.7 = (f32[36896]{0:T(1024)S(1)}, f32[36896]{0:T(1024)S(1)}, u32[]{:S(2)}, u32[]{:S(2)}) collective-permute-start(f32[36896]{0:T(1024)S(1)} %dynamic_slice.21), channel_id=1, source_target_pairs={{0,1},{1,0},{2,3},{3,2},{4,5},{5,4},{6,7},{7,6},{8,9},{9,8},{10,11... | collective-permute-start | bytes 442760 | tf_op jit(solution)/shard_map/ppermute | solution.py:44
  43.2 0.9 convolution_add_fusion.1
  44.1 3.1 %collective-permute-done.7 = f32[36896]{0:T(1024)S(1)} collective-permute-done((f32[36896]{0:T(1024)S(1)}, f32[36896]{0:T(1024)S(1)}, u32[]{:S(2)}, u32[]{:S(2)}) %collective-permute-start.7) | collective-permute-done | bytes 147616 | tf_op jit(solution)/shard_map/ppermute | solution.py:44
  47.8 0.9 fusion.58
  48.7 2.0 %collective-permute-done.8 = f32[18448]{0:T(1024)S(1)} collective-permute-done((f32[18448]{0:T(1024)S(1)}, f32[18448]{0:T(1024)S(1)}, u32[]{:S(2)}, u32[]{:S(2)}) %collective-permute-start.8) | collective-permute-done | bytes 73824 | tf_op jit(solution)/shard_map/ppermute | solution.py:44
  50.8 2.7 %collective-permute-start.9 = (f32[18448]{0:T(1024)S(1)}, f32[18448]{0:T(1024)S(1)}, u32[]{:S(2)}, u32[]{:S(2)}) collective-permute-start(f32[18448]{0:T(1024)S(1)} %dynamic-slice_add_fusion.2), channel_id=1, source_target_pairs={{0,2},{1,3},{2,0},{3,1},{4,6},{5,7},{6,4},{7,5},{8,10},{9,11},{10,... | collective-permute-start | bytes 221384 | tf_op jit(solution)/shard_map/ppermute | solution.py:49
  53.5 0.9 convolution_add_fusion.3
  54.4 0.9 collective-permute-done.9
  55.3 0.6 collective-permute-start.10
  55.9 0.9 fusion.15
  56.8 3.3 %collective-permute-done.10 = f32[18448]{0:T(1024)S(1)} collective-permute-done((f32[18448]{0:T(1024)S(1)}, f32[18448]{0:T(1024)S(1)}, u32[]{:S(2)}, u32[]{:S(2)}) %collective-permute-start.10) | collective-permute-done | bytes 73824 | tf_op jit(solution)/shard_map/ppermute | solution.py:49
  60.1 2.5 %collective-permute-start.11 = (f32[18448]{0:T(1024)S(1)}, f32[18448]{0:T(1024)S(1)}, u32[]{:S(2)}, u32[]{:S(2)}) collective-permute-start(f32[18448]{0:T(1024)S(1)} %add.129), channel_id=1, source_target_pairs={{0,64},{8,72},{16,80},{24,88},{32,96},{40,104},{48,112},{56,120},{... | collective-permute-start | bytes 221384 | tf_op jit(solution)/shard_map/ppermute | solution.py:49
  62.7 0.9 fusion.16
  63.6 0.9 collective-permute-done.11
  64.5 4.6 %collective-permute-start.12 = (f32[18448]{0:T(1024)S(1)}, f32[18448]{0:T(1024)S(1)}, u32[]{:S(2)}, u32[]{:S(2)}) collective-permute-start(f32[18448]{0:T(1024)S(1)} %add.130), channel_id=1, source_target_pairs={{0,128},{8,136},{16,144},{24,152},{32,160},{40,168},{48,176},{56,1... | collective-permute-start | bytes 221384 | tf_op jit(solution)/shard_map/ppermute | solution.py:49
  69.0 0.9 collective-permute-start.5
  69.9 2.8 %collective-permute-done.12 = f32[18448]{0:T(1024)S(1)} collective-permute-done((f32[18448]{0:T(1024)S(1)}, f32[18448]{0:T(1024)S(1)}, u32[]{:S(2)}, u32[]{:S(2)}) %collective-permute-start.12) | collective-permute-done | bytes 73824 | tf_op jit(solution)/shard_map/ppermute | solution.py:49
  72.7 2.8 %collective-permute-start.13 = (f32[18448]{0:T(1024)S(1)}, f32[18448]{0:T(1024)S(1)}, u32[]{:S(2)}, u32[]{:S(2)}) collective-permute-start(f32[18448]{0:T(1024)S(1)} %add.131), channel_id=1, source_target_pairs={{0,4},{1,5},{2,6},{3,7},{4,0},{5,1},{6,2},{7,3},{8,12},{9,13},{10,... | collective-permute-start | bytes 221384 | tf_op jit(solution)/shard_map/ppermute | solution.py:49
  76.0 1.6 %collective-permute-done.13 = f32[18448]{0:T(1024)S(1)} collective-permute-done((f32[18448]{0:T(1024)S(1)}, f32[18448]{0:T(1024)S(1)}, u32[]{:S(2)}, u32[]{:S(2)}) %collective-permute-start.13) | collective-permute-done | bytes 73824 | tf_op jit(solution)/shard_map/ppermute | solution.py:49
  77.6 1.5 %collective-permute-start.14 = (f32[18448]{0:T(1024)S(1)}, f32[18448]{0:T(1024)S(1)}, u32[]{:S(2)}, u32[]{:S(2)}) collective-permute-start(f32[18448]{0:T(1024)S(1)} %add.132), channel_id=1, source_target_pairs={{0,32},{8,40},{16,48},{24,56},{32,0},{40,8},{48,16},{56,24},{64,96... | collective-permute-start | bytes 221384 | tf_op jit(solution)/shard_map/ppermute | solution.py:53
  79.1 1.1 %fusion.3 = bf16[48,48,128]{2,1,0:T(8,128)(2,1)} fusion(f32[50,50,128]{2,1,0:T(8,128)S(1)} %add_divide_fusion, f32[50,50,128]{2,1,0:T(8,128)S(1)} %get-tuple-element.53), kind=kLoop, calls=%fused_computation.12 | loop fusion | flops 589824 | bytes 2949120 | tf_op jit(solution)/shard_map/convert.4
  80.7 0.8 collective-permute-done.14
  81.6 0.6 collective-permute-start.15
  82.2 1.8 %convolution_select_fusion = f32[48,8,7,128]{3,1,2,0:T(8,128)S(1)} fusion(bf16[3,3,128,128]{3,2,1,0:T(8,128)(2,1)S(1)} %copy-done.4, bf16[50,1,7,2,128]{4,2,3,0,1:T(8,128)(2,1)S(1)} %slice.272, bf16[50,1,8,7,128]{4,2,3,0,1:T(8,128)(2,1)S(1)} %copy.13, pred[8,7]{0,1:T(8,128)(4,1)S(1)} %copy-done.6), kind=kOutput, calls=%fused_computation.5 | convolution fusion | flops 795832320 | bytes 2567224 | tf_op jit(solution)/shard_map/conv_general_dilated | solution.py:101
  84.9 0.8 collective-permute-done.15
  85.9 9.5 %collective-permute-start.16 = (f32[73792]{0:T(1024)S(1)}, f32[73792]{0:T(1024)S(1)}, u32[]{:S(2)}, u32[]{:S(2)}) collective-permute-start(f32[73792]{0:T(1024)S(1)} %maximum_select_fusion.1), channel_id=1, source_target_pairs={{0,8},{8,0},{16,24},{24,16},{32,40},{40,32},{48,56},{56,48},{64,72... | collective-permute-start | bytes 885512 | tf_op jit(solution)/shard_map/ppermute | solution.py:53
  95.4 0.9 convert_element_type.23
  96.9 0.5 slice_multiply_fusion.2
  97.4 0.9 slice_multiply_fusion.1
  (70 shorter events, 8.4 us)
Async XLA Ops:
  0.6 1.2 %copy-start.2 = (bf16[48,48,128]{2,1,0:T(8,128)(2,1)S(1)}, bf16[48,48,128]{2,1,0:T(8,128)(2,1)}, u32[]{:S(2)}) copy-start(bf16[48,48,128]{2,1,0:T(8,128)(2,1)} %param.15) | copy-start | bytes 1769476
  2.1 5.4 %collective-permute-start = (bf16[48,2,256]{2,1,0:T(2,128)(2,1)S(1)}, bf16[48,2,256]{2,1,0:T(2,128)(2,1)S(1)}, u32[]{:S(2)}, u32[]{:S(2)}) collective-permute-start(bf16[48,2,256]{2,1,0:T(2,128)(2,1)S(1)} %get-tuple-element.57), channel_id=1, source_target_pairs={{0,8},{8,16},{16,24},{24,32},{32,40},{40,48},{48,56},{56,64},{64,7... | collective-permute-start | bytes 147464 | tf_op jit(solution)/shard_map/ppermute | solution.py:15
  6.3 5.0 %collective-permute-start.1 = (bf16[48,2,256]{2,1,0:T(2,128)(2,1)S(1)}, bf16[48,2,256]{2,1,0:T(2,128)(2,1)S(1)}, u32[]{:S(2)}, u32[]{:S(2)}) collective-permute-start(bf16[48,2,256]{2,1,0:T(2,128)(2,1)S(1)} %get-tuple-element.58), channel_id=1, source_target_pairs={{8,0},{16,8},{24,16},{32,24},{40,32},{48,40},{56,48},{64,56},{72,6... | collective-permute-start | bytes 147464 | tf_op jit(solution)/shard_map/ppermute | solution.py:17
  11.4 10.8 %collective-permute-start.2 = (bf16[2,52,256]{2,1,0:T(8,128)(2,1)S(1)}, bf16[2,52,256]{2,1,0:T(8,128)(2,1)S(1)}, u32[]{:S(2)}, u32[]{:S(2)}) collective-permute-start(bf16[2,52,256]{2,1,0:T(8,128)(2,1)S(1)} %get-tuple-element.59), channel_id=1, source_target_pairs={{0,1},{1,2},{2,3},{3,4},{4,5},{5,6},{6,7},{8,9},{9,10},{10,11},{11... | collective-permute-start | bytes 159752 | tf_op jit(solution)/shard_map/ppermute | solution.py:15
  13.6 8.6 %collective-permute-start.3 = (bf16[2,52,256]{2,1,0:T(8,128)(2,1)S(1)}, bf16[2,52,256]{2,1,0:T(8,128)(2,1)S(1)}, u32[]{:S(2)}, u32[]{:S(2)}) collective-permute-start(bf16[2,52,256]{2,1,0:T(8,128)(2,1)S(1)} %get-tuple-element.60), channel_id=1, source_target_pairs={{1,0},{2,1},{3,2},{4,3},{5,4},{6,5},{7,6},{9,8},{10,9},{11,10},{12... | collective-permute-start | bytes 159752 | tf_op jit(solution)/shard_map/ppermute | solution.py:17
  15.0 8.9 %collective-permute-start.4 = (bf16[2,52,256]{2,1,0:T(8,128)(2,1)S(1)}, bf16[2,52,256]{2,1,0:T(8,128)(2,1)S(1)}, u32[]{:S(2)}, u32[]{:S(2)}) collective-permute-start(bf16[2,52,256]{2,1,0:T(8,128)(2,1)S(1)} %get-tuple-element.54), channel_id=1, source_target_pairs={{0,128},{8,136},{16,144},{24,152},{32,160},{40,168},{48,176},{56,1... | collective-permute-start | bytes 159752 | tf_op jit(solution)/shard_map/ppermute | solution.py:27
  23.9 1.1 %copy-start = (bf16[52,52,256]{2,1,0:T(8,128)(2,1)}, bf16[52,52,256]{2,1,0:T(8,128)(2,1)S(1)}, u32[]{:S(2)}) copy-start(bf16[52,52,256]{2,1,0:T(8,128)(2,1)S(1)} %fusion.66) | copy-start | bytes 4153348
  25.0 1.0 copy-start.3
  25.0 1.0 copy-start.7
  28.3 1.3 %copy-start.5 = (f32[128]{0:T(128)S(1)}, f32[128]{0:T(128)}, u32[]{:S(2)}) copy-start(f32[128]{0:T(128)} %param.14) | copy-start | bytes 1540
  29.5 2.8 %copy-start.1 = (bf16[52,52,256]{2,1,0:T(8,128)(2,1)S(1)}, bf16[52,52,256]{2,1,0:T(8,128)(2,1)}, u32[]{:S(2)}) copy-start(bf16[52,52,256]{2,1,0:T(8,128)(2,1)} %copy-done) | copy-start | bytes 4153348
  37.0 3.0 %collective-permute-start.6 = (f32[73792]{0:T(1024)S(1)}, f32[73792]{0:T(1024)S(1)}, u32[]{:S(2)}, u32[]{:S(2)}) collective-permute-start(f32[73792]{0:T(1024)S(1)} %dynamic_slice.19), channel_id=1, source_target_pairs={{0,8},{8,0},{16,24},{24,16},{32,40},{40,32},{48,56},{56,48},{64,72... | collective-permute-start | bytes 885512 | tf_op jit(solution)/shard_map/ppermute | solution.py:44
  40.3 6.8 %collective-permute-start.7 = (f32[36896]{0:T(1024)S(1)}, f32[36896]{0:T(1024)S(1)}, u32[]{:S(2)}, u32[]{:S(2)}) collective-permute-start(f32[36896]{0:T(1024)S(1)} %dynamic_slice.21), channel_id=1, source_target_pairs={{0,1},{1,0},{2,3},{3,2},{4,5},{5,4},{6,7},{7,6},{8,9},{9,8},{10,11... | collective-permute-start | bytes 442760 | tf_op jit(solution)/shard_map/ppermute | solution.py:44
  47.3 3.3 %collective-permute-start.8 = (f32[18448]{0:T(1024)S(1)}, f32[18448]{0:T(1024)S(1)}, u32[]{:S(2)}, u32[]{:S(2)}) collective-permute-start(f32[18448]{0:T(1024)S(1)} %dynamic_slice.23), channel_id=1, source_target_pairs={{0,32},{8,40},{16,48},{24,56},{32,0},{40,8},{48,16},{56,24},{64,96... | collective-permute-start | bytes 221384 | tf_op jit(solution)/shard_map/ppermute | solution.py:44
  50.8 4.5 %collective-permute-start.9 = (f32[18448]{0:T(1024)S(1)}, f32[18448]{0:T(1024)S(1)}, u32[]{:S(2)}, u32[]{:S(2)}) collective-permute-start(f32[18448]{0:T(1024)S(1)} %dynamic-slice_add_fusion.2), channel_id=1, source_target_pairs={{0,2},{1,3},{2,0},{3,1},{4,6},{5,7},{6,4},{7,5},{8,10},{9,11},{10,... | collective-permute-start | bytes 221384 | tf_op jit(solution)/shard_map/ppermute | solution.py:49
  55.3 4.8 %collective-permute-start.10 = (f32[18448]{0:T(1024)S(1)}, f32[18448]{0:T(1024)S(1)}, u32[]{:S(2)}, u32[]{:S(2)}) collective-permute-start(f32[18448]{0:T(1024)S(1)} %add.128), channel_id=1, source_target_pairs={{0,16},{8,24},{16,0},{24,8},{32,48},{40,56},{48,32},{56,40},{64,80... | collective-permute-start | bytes 221384 | tf_op jit(solution)/shard_map/ppermute | solution.py:49
  60.1 4.3 %collective-permute-start.11 = (f32[18448]{0:T(1024)S(1)}, f32[18448]{0:T(1024)S(1)}, u32[]{:S(2)}, u32[]{:S(2)}) collective-permute-start(f32[18448]{0:T(1024)S(1)} %add.129), channel_id=1, source_target_pairs={{0,64},{8,72},{16,80},{24,88},{32,96},{40,104},{48,112},{56,120},{... | collective-permute-start | bytes 221384 | tf_op jit(solution)/shard_map/ppermute | solution.py:49
  64.5 8.2 %collective-permute-start.12 = (f32[18448]{0:T(1024)S(1)}, f32[18448]{0:T(1024)S(1)}, u32[]{:S(2)}, u32[]{:S(2)}) collective-permute-start(f32[18448]{0:T(1024)S(1)} %add.130), channel_id=1, source_target_pairs={{0,128},{8,136},{16,144},{24,152},{32,160},{40,168},{48,176},{56,1... | collective-permute-start | bytes 221384 | tf_op jit(solution)/shard_map/ppermute | solution.py:49
  69.0 15.8 %collective-permute-start.5 = (bf16[2,48,128]{2,1,0:T(8,128)(2,1)S(1)}, bf16[2,48,128]{2,1,0:T(8,128)(2,1)S(1)}, u32[]{:S(2)}, u32[]{:S(2)}) collective-permute-start(bf16[2,48,128]{2,1,0:T(8,128)(2,1)S(1)} %pad_maximum_fusion.1), channel_id=1, source_target_pairs={{0,128},{8,136},{16,144},{24,152},{32,160},{40,168},{48,176},{56,1... | collective-permute-start | bytes 73736 | tf_op jit(solution)/shard_map/ppermute | solution.py:27
  72.7 4.8 %collective-permute-start.13 = (f32[18448]{0:T(1024)S(1)}, f32[18448]{0:T(1024)S(1)}, u32[]{:S(2)}, u32[]{:S(2)}) collective-permute-start(f32[18448]{0:T(1024)S(1)} %add.131), channel_id=1, source_target_pairs={{0,4},{1,5},{2,6},{3,7},{4,0},{5,1},{6,2},{7,3},{8,12},{9,13},{10,... | collective-permute-start | bytes 221384 | tf_op jit(solution)/shard_map/ppermute | solution.py:49
  77.6 3.9 %collective-permute-start.14 = (f32[18448]{0:T(1024)S(1)}, f32[18448]{0:T(1024)S(1)}, u32[]{:S(2)}, u32[]{:S(2)}) collective-permute-start(f32[18448]{0:T(1024)S(1)} %add.132), channel_id=1, source_target_pairs={{0,32},{8,40},{16,48},{24,56},{32,0},{40,8},{48,16},{56,24},{64,96... | collective-permute-start | bytes 221384 | tf_op jit(solution)/shard_map/ppermute | solution.py:53
  80.5 1.7 %copy-start.4 = (bf16[3,3,128,128]{3,2,1,0:T(8,128)(2,1)S(1)}, bf16[3,3,128,128]{3,2,1,0:T(8,128)(2,1)}, u32[]{:S(2)}) copy-start(bf16[3,3,128,128]{3,2,1,0:T(8,128)(2,1)} %param.13) | copy-start | bytes 884740
  80.5 1.7 %copy-start.6 = (pred[8,7]{0,1:T(8,128)(4,1)S(1)}, pred[8,7]{0,1:T(8,128)(4,1)}, u32[]{:S(2)}) copy-start(pred[8,7]{0,1:T(8,128)(4,1)} %constant.203) | copy-start | bytes 172
  81.6 4.1 %collective-permute-start.15 = (f32[36896]{0:T(1024)S(1)}, f32[36896]{0:T(1024)S(1)}, u32[]{:S(2)}, u32[]{:S(2)}) collective-permute-start(f32[36896]{0:T(1024)S(1)} %maximum_select_fusion.2), channel_id=1, source_target_pairs={{0,1},{1,0},{2,3},{3,2},{4,5},{5,4},{6,7},{7,6},{8,9},{9,8},{10,11... | collective-permute-start | bytes 442760 | tf_op jit(solution)/shard_map/ppermute | solution.py:53
  85.9 10.7 %collective-permute-start.16 = (f32[73792]{0:T(1024)S(1)}, f32[73792]{0:T(1024)S(1)}, u32[]{:S(2)}, u32[]{:S(2)}) collective-permute-start(f32[73792]{0:T(1024)S(1)} %maximum_select_fusion.1), channel_id=1, source_target_pairs={{0,8},{8,0},{16,24},{24,16},{32,40},{40,32},{48,56},{56,48},{64,72... | collective-permute-start | bytes 885512 | tf_op jit(solution)/shard_map/ppermute | solution.py:53

commit v4 on v3

--- a/solution.py
+++ b/solution.py
@@ -43,9 +43,7 @@
         keep = lax.dynamic_slice_in_dim(data, bit * half, half)
         data = keep + lax.ppermute(send, axis, pairs)
         history.append((axis, step, bit))
-    for axis, step in double:
-        count = lax.axis_size(axis)
-        pairs = [(i, i ^ step) for i in range(count)]
+    for axis, pairs in double:
         data = data + lax.ppermute(data, axis, pairs)
     for axis, step, bit in reversed(history):
         count = lax.axis_size(axis)
@@ -68,6 +66,32 @@
     return first + rest
 
 
+def reflected_ring_pairs(count, stride, size):
+    pairs = []
+    for i in range(count):
+        z = (i // stride) % size
+        if z % 2 == 0:
+            w = (size - 2 - z) % size
+        else:
+            w = (size - z) % size
+        pairs.append((i, i + (w - z) * stride))
+    return pairs
+
+
+def doubling_plan(rest):
+    plan = []
+    lon = lax.axis_size("lon")
+    for axis, step in rest:
+        count = lax.axis_size(axis)
+        pairs = [(i, i ^ step) for i in range(count)]
+        if axis == "lat" and step == 4 and count == 8:
+            pairs = [(i, (3 - i // 2) * 2 + i % 2) for i in range(count)]
+        if axis == "lon" and step == 16 and count == 32:
+            pairs = reflected_ring_pairs(lon, 4, 8)
+        plan.append((axis, pairs))
+    return plan
+
+
 def shards(inputs, weight, bias, cotangent):
     rows, cols, chans = inputs.shape
     band = lax.axis_index("lat")
@@ -80,7 +104,7 @@
     tall = tall.at[1].set(jnp.where(band == 0, far[0], tall[1]))
     tall = tall.at[rows + 2].set(jnp.where(band == bands - 1, far[1], tall[rows + 2]))
     padded = tall[:, :, :chans]
-    flat_cot = tall[1:-1, 1:-1, chans:].reshape((rows + 2) * (cols + 2), chans).astype(jnp.float32)
+    ring_cot = tall[1:-1, 1:-1, chans:].astype(jnp.float32)
     pre = lax.conv_general_dilated(
         padded[None],
         weight,
@@ -88,11 +112,10 @@
         "VALID",
         dimension_numbers=("NHWC", "HWIO", "NHWC"),
         preferred_element_type=jnp.float32,
-    )[0].reshape((rows + 2) * (cols + 2), chans) + bias[None, :]
+    )[0] + bias
     sig = jax.nn.sigmoid(pre)
-    silu = (pre * sig).reshape(rows + 2, cols + 2, chans)
-    outputs = silu[1:-1, 1:-1].astype(jnp.bfloat16)
-    grad_ext = (flat_cot * sig * (1.0 + pre * (1.0 - sig))).astype(jnp.bfloat16).reshape(rows + 2, cols + 2, chans)
+    outputs = (pre * sig)[1:-1, 1:-1].astype(jnp.bfloat16)
+    grad_ext = (ring_cot * sig * (1.0 + pre * (1.0 - sig))).astype(jnp.bfloat16)
     line = lax.broadcasted_iota(jnp.int32, (rows + 2, 1, 1), 0)
     outside = ((line == 0) & (band == 0)) | ((line == rows + 1) & (band == bands - 1))
     grad_ext = jnp.where(outside, jnp.zeros_like(grad_ext), grad_ext)
@@ -132,7 +155,7 @@
     kernel_terms = jnp.concatenate(taps, axis=0)
     bias_terms = jnp.sum(pre_grad.astype(jnp.float32), axis=0)[None, :]
     order = pairing_order(("lon", "lat"))
-    sums = butterfly_sum(jnp.concatenate([kernel_terms, bias_terms], axis=0), order[:3], order[3:])
+    sums = butterfly_sum(jnp.concatenate([kernel_terms, bias_terms], axis=0), order[:3], doubling_plan(order[3:]))
     kernel_sum, bias_sum = sums[:-1], sums[-1:]
     total_cells = rows * cols * lax.axis_size("lon") * lax.axis_size("lat")
     scale = 1.0 / jnp.sqrt(jnp.float32(total_cells))

time: 98.8 us -> 96.9 us (0.981)
  waiting for transfers between devices: 22.6 us -> 19.7 us
  starting transfers between devices: 46 us -> 47 us
    ppermute x5, waiting for transfers between devices: 9.48 us -> 6.51 us  [butterfly_sum(): data = data + lax.ppermute(data, axis, pairs)]
    ppermute x2, starting transfers between devices: 8.12 us -> 9.94 us  [from_behind(): return lax.ppermute(value, axis, pairs)]
    ppermute x5, starting transfers between devices: 13.3 us -> 12 us  [butterfly_sum(): data = data + lax.ppermute(data, axis, pairs)]
  transfers between devices with their start and end apart: 17 -> 17, of which waited for: 14 -> 13; matrix products, arithmetic and copies ran while one was open for 12% -> 12% of each run, Pallas kernels for 0% -> 0%
where the time goes in v4:
time: 96.9 us; the launch traced here: 96.3 us
  starting transfers between devices  47 us (49%)
  waiting for transfers between devices  19.7 us (20%)
  matrix products  13.5 us (14%)
  other arithmetic  8.35 us (9%)
  local copies, waits for them, and re-layouts  6.75 us (7%)
  between operations  1.07 us (1%)
    ppermute x3, starting transfers between devices, butterfly_sum(): other = lax.ppermute(data, axis, pairs)  12.2 us
    ppermute x5, starting transfers between devices, butterfly_sum(): data = data + lax.ppermute(data, axis, pairs)  12 us
    ppermute x2, starting transfers between devices, from_behind(): return lax.ppermute(value, axis, pairs)  9.94 us
    ppermute x5, waiting for transfers between devices, butterfly_sum(): data = data + lax.ppermute(data, axis, pairs)  6.51 us
    ppermute x2, starting transfers between devices, extended(): lax.ppermute(tail, axis, [(i, (i + 1) % count) for i in range(ends)])  6.42 us
    ppermute x3, waiting for transfers between devices, butterfly_sum(): data = keep + lax.ppermute(send, axis, pairs)  5.36 us
    dot_general x6, matrix products, shards(): jnp.dot(grad_ext[line_at, tap_b:tap_b + cols], weight[tap_a, 2 - tap_b].T...  5.31 us
    ppermute x3, starting transfers between devices, butterfly_sum(): data = keep + lax.ppermute(send, axis, pairs)  5.15 us
  transfers between devices with their start and end apart: 17, of which 13 were waited for; matrix products, arithmetic and copies ran while one was open for 12% of the time, Pallas kernels for 0%

profile of v4, /device:TPU:1, one launch (start us, length us, event | category | flops | bytes accessed | tf_op | source)
XLA Modules:
  0.0 96.3 jit_solution(2203658046330040270)
XLA Ops:
  0.6 1.2 %constant_dynamic-update-slice_fusion.1 = bf16[48,48,256]{2,1,0:T(8,128)(2,1)S(1)} fusion(bf16[48,48,128]{2,1,0:T(8,128)(2,1)} %param.12), kind=kLoop, calls=%fused_computation.113 | loop fusion | bytes 1179648
  2.1 4.2 %collective-permute-start = (bf16[48,2,256]{2,1,0:T(2,128)(2,1)S(1)}, bf16[48,2,256]{2,1,0:T(2,128)(2,1)S(1)}, u32[]{:S(2)}, u32[]{:S(2)}) collective-permute-start(bf16[48,2,256]{2,1,0:T(2,128)(2,1)S(1)} %get-tuple-element.57), channel_id=1, source_target_pairs={{0,8},{8,16},{16,24},{24,32},{32,40},{40,48},{48,56},{56,64},{64,7... | collective-permute-start | bytes 147464 | tf_op jit(solution)/shard_map/ppermute | solution.py:15
  6.3 1.2 %collective-permute-done = bf16[48,2,256]{2,1,0:T(2,128)(2,1)S(1)} collective-permute-done((bf16[48,2,256]{2,1,0:T(2,128)(2,1)S(1)}, bf16[48,2,256]{2,1,0:T(2,128)(2,1)S(1)}, u32[]{:S(2)}, u32[]{:S(2)}) %collective-permute-start) | collective-permute-done | bytes 49184 | tf_op jit(solution)/shard_map/ppermute | solution.py:15
  7.5 3.8 %collective-permute-done.1 = bf16[48,2,256]{2,1,0:T(2,128)(2,1)S(1)} collective-permute-done((bf16[48,2,256]{2,1,0:T(2,128)(2,1)S(1)}, bf16[48,2,256]{2,1,0:T(2,128)(2,1)S(1)}, u32[]{:S(2)}, u32[]{:S(2)}) %collective-permute-start.1) | collective-permute-done | bytes 49184 | tf_op jit(solution)/shard_map/ppermute | solution.py:17
  11.4 2.2 %collective-permute-start.2 = (bf16[2,52,256]{2,1,0:T(8,128)(2,1)S(1)}, bf16[2,52,256]{2,1,0:T(8,128)(2,1)S(1)}, u32[]{:S(2)}, u32[]{:S(2)}) collective-permute-start(bf16[2,52,256]{2,1,0:T(8,128)(2,1)S(1)} %get-tuple-element.59), channel_id=1, source_target_pairs={{0,1},{1,2},{2,3},{3,4},{4,5},{5,6},{6,7},{8,9},{9,10},{10,11},{11... | collective-permute-start | bytes 159752 | tf_op jit(solution)/shard_map/ppermute | solution.py:15
  13.6 1.3 %collective-permute-start.3 = (bf16[2,52,256]{2,1,0:T(8,128)(2,1)S(1)}, bf16[2,52,256]{2,1,0:T(8,128)(2,1)S(1)}, u32[]{:S(2)}, u32[]{:S(2)}) collective-permute-start(bf16[2,52,256]{2,1,0:T(8,128)(2,1)S(1)} %get-tuple-element.60), channel_id=1, source_target_pairs={{1,0},{2,1},{3,2},{4,3},{5,4},{6,5},{7,6},{9,8},{10,9},{11,10},{12... | collective-permute-start | bytes 159752 | tf_op jit(solution)/shard_map/ppermute | solution.py:17
  15.0 7.2 %collective-permute-start.4 = (bf16[2,52,256]{2,1,0:T(8,128)(2,1)S(1)}, bf16[2,52,256]{2,1,0:T(8,128)(2,1)S(1)}, u32[]{:S(2)}, u32[]{:S(2)}) collective-permute-start(bf16[2,52,256]{2,1,0:T(8,128)(2,1)S(1)} %get-tuple-element.54), channel_id=1, source_target_pairs={{0,128},{8,136},{16,144},{24,152},{32,160},{40,168},{48,176},{56,1... | collective-permute-start | bytes 159752 | tf_op jit(solution)/shard_map/ppermute | solution.py:27
  22.2 0.8 pad_maximum_fusion
  23.0 0.9 collective-permute-done.4
  24.1 0.9 copy-done
  25.3 0.7 copy-done.3
  26.0 1.9 %convolution_select_fusion.1 = f32[50,8,7,128]{3,1,2,0:T(8,128)S(1)} fusion(bf16[3,3,128,128]{3,2,1,0:T(8,128)(2,1)S(1)} %copy-done.3, bf16[52,1,7,2,128]{4,2,3,0,1:T(8,128)(2,1)S(1)} %slice.267, bf16[52,1,8,7,128]{4,2,3,0,1:T(8,128)(2,1)S(1)} %copy.10, pred[8,7]{0,1:T(8,128)(4,1)S(1)} %copy-done.7), kind=kOutput, calls=%fused_computation.10 | convolution fusion | flops 828987392 | bytes 2660408 | tf_op jit(solution)/shard_map/conv_general_dilated | solution.py:108
  28.3 1.2 %reshape.171 = f32[50,1,56,128]{3,2,0,1:T(8,128)} reshape(f32[50,8,7,128]{3,2,1,0:T(8,128)S(1)} %copy.11) | data formatting | bytes 2867200 | tf_op jit(solution)/shard_map/conv_general_dilated | solution.py:108
  29.5 2.5 %fusion.29 = (bf16[50,50,128]{2,1,0:T(8,128)(2,1)S(1)}, f32[50,50,128]{2,1,0:T(8,128)S(1)}) fusion(bf16[52,52,256]{2,1,0:T(8,128)(2,1)} %copy-done, pred[50]{0:T(512)(128)(4,1)S(1)} %and_or_fusion, f32[128]{0:T(128)S(1)} %copy-done.5, f32[50,1,56,128]{3,2,0,1:T(8,128)} %reshape.171), kind=kLoop, calls=%fused_computation.52 | loop fusion | flops 3840000 | bytes 3840562 | tf_op jit(solution)/shard_map/jit(_where)/select_n | solution.py:121
  32.8 0.5 fusion.11
  33.8 0.5 fusion.9
  34.8 0.5 fusion.7
  35.8 0.5 fusion.5
  37.0 1.8 %collective-permute-start.6 = (f32[73792]{0:T(1024)S(1)}, f32[73792]{0:T(1024)S(1)}, u32[]{:S(2)}, u32[]{:S(2)}) collective-permute-start(f32[73792]{0:T(1024)S(1)} %dynamic_slice.19), channel_id=1, source_target_pairs={{0,8},{8,0},{16,24},{24,16},{32,40},{40,32},{48,56},{56,48},{64,72... | collective-permute-start | bytes 885512 | tf_op jit(solution)/shard_map/ppermute | solution.py:44
  38.8 0.9 fusion.54
  40.3 2.9 %collective-permute-start.7 = (f32[36896]{0:T(1024)S(1)}, f32[36896]{0:T(1024)S(1)}, u32[]{:S(2)}, u32[]{:S(2)}) collective-permute-start(f32[36896]{0:T(1024)S(1)} %dynamic_slice.21), channel_id=1, source_target_pairs={{0,1},{1,0},{2,3},{3,2},{4,5},{5,4},{6,7},{7,6},{8,9},{9,8},{10,11... | collective-permute-start | bytes 442760 | tf_op jit(solution)/shard_map/ppermute | solution.py:44
  43.2 0.9 convolution_add_fusion.1
  44.1 3.1 %collective-permute-done.7 = f32[36896]{0:T(1024)S(1)} collective-permute-done((f32[36896]{0:T(1024)S(1)}, f32[36896]{0:T(1024)S(1)}, u32[]{:S(2)}, u32[]{:S(2)}) %collective-permute-start.7) | collective-permute-done | bytes 147616 | tf_op jit(solution)/shard_map/ppermute | solution.py:44
  47.8 0.9 fusion.58
  48.7 2.0 %collective-permute-done.8 = f32[18448]{0:T(1024)S(1)} collective-permute-done((f32[18448]{0:T(1024)S(1)}, f32[18448]{0:T(1024)S(1)}, u32[]{:S(2)}, u32[]{:S(2)}) %collective-permute-start.8) | collective-permute-done | bytes 73824 | tf_op jit(solution)/shard_map/ppermute | solution.py:44
  50.8 2.7 %collective-permute-start.9 = (f32[18448]{0:T(1024)S(1)}, f32[18448]{0:T(1024)S(1)}, u32[]{:S(2)}, u32[]{:S(2)}) collective-permute-start(f32[18448]{0:T(1024)S(1)} %dynamic-slice_add_fusion.2), channel_id=1, source_target_pairs={{0,2},{1,3},{2,0},{3,1},{4,6},{5,7},{6,4},{7,5},{8,10},{9,11},{10,... | collective-permute-start | bytes 221384 | tf_op jit(solution)/shard_map/ppermute | solution.py:47
  53.5 0.9 convolution_add_fusion.3
  54.4 0.9 collective-permute-done.9
  55.3 0.6 collective-permute-start.10
  55.9 0.9 fusion.15
  56.8 3.3 %collective-permute-done.10 = f32[18448]{0:T(1024)S(1)} collective-permute-done((f32[18448]{0:T(1024)S(1)}, f32[18448]{0:T(1024)S(1)}, u32[]{:S(2)}, u32[]{:S(2)}) %collective-permute-start.10) | collective-permute-done | bytes 73824 | tf_op jit(solution)/shard_map/ppermute | solution.py:47
  60.1 2.5 %collective-permute-start.11 = (f32[18448]{0:T(1024)S(1)}, f32[18448]{0:T(1024)S(1)}, u32[]{:S(2)}, u32[]{:S(2)}) collective-permute-start(f32[18448]{0:T(1024)S(1)} %add.124), channel_id=1, source_target_pairs={{0,64},{8,72},{16,80},{24,88},{32,96},{40,104},{48,112},{56,120},{... | collective-permute-start | bytes 221384 | tf_op jit(solution)/shard_map/ppermute | solution.py:47
  62.7 0.9 fusion.16
  63.6 0.9 collective-permute-done.11
  64.5 3.1 %collective-permute-start.12 = (f32[18448]{0:T(1024)S(1)}, f32[18448]{0:T(1024)S(1)}, u32[]{:S(2)}, u32[]{:S(2)}) collective-permute-start(f32[18448]{0:T(1024)S(1)} %add.125), channel_id=1, source_target_pairs={{0,192},{8,200},{16,208},{24,216},{32,224},{40,232},{48,240},{56,2... | collective-permute-start | bytes 221384 | tf_op jit(solution)/shard_map/ppermute | solution.py:47
  67.6 2.7 %collective-permute-start.5 = (bf16[2,48,128]{2,1,0:T(8,128)(2,1)S(1)}, bf16[2,48,128]{2,1,0:T(8,128)(2,1)S(1)}, u32[]{:S(2)}, u32[]{:S(2)}) collective-permute-start(bf16[2,48,128]{2,1,0:T(8,128)(2,1)S(1)} %pad_maximum_fusion.1), channel_id=1, source_target_pairs={{0,128},{8,136},{16,144},{24,152},{32,160},{40,168},{48,176},{56,1... | collective-permute-start | bytes 73736 | tf_op jit(solution)/shard_map/ppermute | solution.py:27
  70.3 3.0 %collective-permute-start.13 = (f32[18448]{0:T(1024)S(1)}, f32[18448]{0:T(1024)S(1)}, u32[]{:S(2)}, u32[]{:S(2)}) collective-permute-start(f32[18448]{0:T(1024)S(1)} %add.126), channel_id=1, source_target_pairs={{0,6},{1,7},{2,4},{3,5},{4,2},{5,3},{6,0},{7,1},{8,14},{9,15},{10,... | collective-permute-start | bytes 221384 | tf_op jit(solution)/shard_map/ppermute | solution.py:47
  73.7 1.4 %collective-permute-done.13 = f32[18448]{0:T(1024)S(1)} collective-permute-done((f32[18448]{0:T(1024)S(1)}, f32[18448]{0:T(1024)S(1)}, u32[]{:S(2)}, u32[]{:S(2)}) %collective-permute-start.13) | collective-permute-done | bytes 73824 | tf_op jit(solution)/shard_map/ppermute | solution.py:47
  75.1 2.1 %collective-permute-start.14 = (f32[18448]{0:T(1024)S(1)}, f32[18448]{0:T(1024)S(1)}, u32[]{:S(2)}, u32[]{:S(2)}) collective-permute-start(f32[18448]{0:T(1024)S(1)} %add.127), channel_id=1, source_target_pairs={{0,32},{8,40},{16,48},{24,56},{32,0},{40,8},{48,16},{56,24},{64,96... | collective-permute-start | bytes 221384 | tf_op jit(solution)/shard_map/ppermute | solution.py:51
  77.2 1.1 %fusion.3 = bf16[48,48,128]{2,1,0:T(8,128)(2,1)} fusion(f32[50,50,128]{2,1,0:T(8,128)S(1)} %add_divide_fusion, f32[50,50,128]{2,1,0:T(8,128)S(1)} %get-tuple-element.53), kind=kLoop, calls=%fused_computation.12 | loop fusion | flops 589824 | bytes 2949120 | tf_op jit(solution)/shard_map/convert.4
  78.8 0.8 collective-permute-done.14
  79.7 0.6 collective-permute-start.15
  80.3 1.8 %convolution_select_fusion = f32[48,8,7,128]{3,1,2,0:T(8,128)S(1)} fusion(bf16[3,3,128,128]{3,2,1,0:T(8,128)(2,1)S(1)} %copy-done.4, bf16[50,1,7,2,128]{4,2,3,0,1:T(8,128)(2,1)S(1)} %slice.272, bf16[50,1,8,7,128]{4,2,3,0,1:T(8,128)(2,1)S(1)} %copy.13, pred[8,7]{0,1:T(8,128)(4,1)S(1)} %copy-done.6), kind=kOutput, calls=%fused_computation.5 | convolution fusion | flops 795832320 | bytes 2567224 | tf_op jit(solution)/shard_map/conv_general_dilated | solution.py:124
  83.0 0.8 collective-permute-done.15
  84.0 9.5 %collective-permute-start.16 = (f32[73792]{0:T(1024)S(1)}, f32[73792]{0:T(1024)S(1)}, u32[]{:S(2)}, u32[]{:S(2)}) collective-permute-start(f32[73792]{0:T(1024)S(1)} %maximum_select_fusion.1), channel_id=1, source_target_pairs={{0,8},{8,0},{16,24},{24,16},{32,40},{40,32},{48,56},{56,48},{64,72... | collective-permute-start | bytes 885512 | tf_op jit(solution)/shard_map/ppermute | solution.py:51
  93.5 0.9 convert_element_type.21
  94.9 0.5 slice_multiply_fusion.2
  95.4 0.9 slice_multiply_fusion.1
  (70 shorter events, 7.9 us)
Async XLA Ops:
  0.6 1.2 %copy-start.2 = (bf16[48,48,128]{2,1,0:T(8,128)(2,1)S(1)}, bf16[48,48,128]{2,1,0:T(8,128)(2,1)}, u32[]{:S(2)}) copy-start(bf16[48,48,128]{2,1,0:T(8,128)(2,1)} %param.15) | copy-start | bytes 1769476
  2.1 5.4 %collective-permute-start = (bf16[48,2,256]{2,1,0:T(2,128)(2,1)S(1)}, bf16[48,2,256]{2,1,0:T(2,128)(2,1)S(1)}, u32[]{:S(2)}, u32[]{:S(2)}) collective-permute-start(bf16[48,2,256]{2,1,0:T(2,128)(2,1)S(1)} %get-tuple-element.57), channel_id=1, source_target_pairs={{0,8},{8,16},{16,24},{24,32},{32,40},{40,48},{48,56},{56,64},{64,7... | collective-permute-start | bytes 147464 | tf_op jit(solution)/shard_map/ppermute | solution.py:15
  6.3 5.0 %collective-permute-start.1 = (bf16[48,2,256]{2,1,0:T(2,128)(2,1)S(1)}, bf16[48,2,256]{2,1,0:T(2,128)(2,1)S(1)}, u32[]{:S(2)}, u32[]{:S(2)}) collective-permute-start(bf16[48,2,256]{2,1,0:T(2,128)(2,1)S(1)} %get-tuple-element.58), channel_id=1, source_target_pairs={{8,0},{16,8},{24,16},{32,24},{40,32},{48,40},{56,48},{64,56},{72,6... | collective-permute-start | bytes 147464 | tf_op jit(solution)/shard_map/ppermute | solution.py:17
  11.4 10.8 %collective-permute-start.2 = (bf16[2,52,256]{2,1,0:T(8,128)(2,1)S(1)}, bf16[2,52,256]{2,1,0:T(8,128)(2,1)S(1)}, u32[]{:S(2)}, u32[]{:S(2)}) collective-permute-start(bf16[2,52,256]{2,1,0:T(8,128)(2,1)S(1)} %get-tuple-element.59), channel_id=1, source_target_pairs={{0,1},{1,2},{2,3},{3,4},{4,5},{5,6},{6,7},{8,9},{9,10},{10,11},{11... | collective-permute-start | bytes 159752 | tf_op jit(solution)/shard_map/ppermute | solution.py:15
  13.6 8.6 %collective-permute-start.3 = (bf16[2,52,256]{2,1,0:T(8,128)(2,1)S(1)}, bf16[2,52,256]{2,1,0:T(8,128)(2,1)S(1)}, u32[]{:S(2)}, u32[]{:S(2)}) collective-permute-start(bf16[2,52,256]{2,1,0:T(8,128)(2,1)S(1)} %get-tuple-element.60), channel_id=1, source_target_pairs={{1,0},{2,1},{3,2},{4,3},{5,4},{6,5},{7,6},{9,8},{10,9},{11,10},{12... | collective-permute-start | bytes 159752 | tf_op jit(solution)/shard_map/ppermute | solution.py:17
  15.0 8.9 %collective-permute-start.4 = (bf16[2,52,256]{2,1,0:T(8,128)(2,1)S(1)}, bf16[2,52,256]{2,1,0:T(8,128)(2,1)S(1)}, u32[]{:S(2)}, u32[]{:S(2)}) collective-permute-start(bf16[2,52,256]{2,1,0:T(8,128)(2,1)S(1)} %get-tuple-element.54), channel_id=1, source_target_pairs={{0,128},{8,136},{16,144},{24,152},{32,160},{40,168},{48,176},{56,1... | collective-permute-start | bytes 159752 | tf_op jit(solution)/shard_map/ppermute | solution.py:27
  23.9 1.1 %copy-start = (bf16[52,52,256]{2,1,0:T(8,128)(2,1)}, bf16[52,52,256]{2,1,0:T(8,128)(2,1)S(1)}, u32[]{:S(2)}) copy-start(bf16[52,52,256]{2,1,0:T(8,128)(2,1)S(1)} %fusion.66) | copy-start | bytes 4153348
  25.0 1.0 copy-start.3
  25.0 1.0 copy-start.7
  28.3 1.3 %copy-start.5 = (f32[128]{0:T(128)S(1)}, f32[128]{0:T(128)}, u32[]{:S(2)}) copy-start(f32[128]{0:T(128)} %param.14) | copy-start | bytes 1540
  29.5 2.8 %copy-start.1 = (bf16[52,52,256]{2,1,0:T(8,128)(2,1)S(1)}, bf16[52,52,256]{2,1,0:T(8,128)(2,1)}, u32[]{:S(2)}) copy-start(bf16[52,52,256]{2,1,0:T(8,128)(2,1)} %copy-done) | copy-start | bytes 4153348
  37.0 3.0 %collective-permute-start.6 = (f32[73792]{0:T(1024)S(1)}, f32[73792]{0:T(1024)S(1)}, u32[]{:S(2)}, u32[]{:S(2)}) collective-permute-start(f32[73792]{0:T(1024)S(1)} %dynamic_slice.19), channel_id=1, source_target_pairs={{0,8},{8,0},{16,24},{24,16},{32,40},{40,32},{48,56},{56,48},{64,72... | collective-permute-start | bytes 885512 | tf_op jit(solution)/shard_map/ppermute | solution.py:44
  40.3 6.8 %collective-permute-start.7 = (f32[36896]{0:T(1024)S(1)}, f32[36896]{0:T(1024)S(1)}, u32[]{:S(2)}, u32[]{:S(2)}) collective-permute-start(f32[36896]{0:T(1024)S(1)} %dynamic_slice.21), channel_id=1, source_target_pairs={{0,1},{1,0},{2,3},{3,2},{4,5},{5,4},{6,7},{7,6},{8,9},{9,8},{10,11... | collective-permute-start | bytes 442760 | tf_op jit(solution)/shard_map/ppermute | solution.py:44
  47.3 3.3 %collective-permute-start.8 = (f32[18448]{0:T(1024)S(1)}, f32[18448]{0:T(1024)S(1)}, u32[]{:S(2)}, u32[]{:S(2)}) collective-permute-start(f32[18448]{0:T(1024)S(1)} %dynamic_slice.23), channel_id=1, source_target_pairs={{0,32},{8,40},{16,48},{24,56},{32,0},{40,8},{48,16},{56,24},{64,96... | collective-permute-start | bytes 221384 | tf_op jit(solution)/shard_map/ppermute | solution.py:44
  50.8 4.5 %collective-permute-start.9 = (f32[18448]{0:T(1024)S(1)}, f32[18448]{0:T(1024)S(1)}, u32[]{:S(2)}, u32[]{:S(2)}) collective-permute-start(f32[18448]{0:T(1024)S(1)} %dynamic-slice_add_fusion.2), channel_id=1, source_target_pairs={{0,2},{1,3},{2,0},{3,1},{4,6},{5,7},{6,4},{7,5},{8,10},{9,11},{10,... | collective-permute-start | bytes 221384 | tf_op jit(solution)/shard_map/ppermute | solution.py:47
  55.3 4.8 %collective-permute-start.10 = (f32[18448]{0:T(1024)S(1)}, f32[18448]{0:T(1024)S(1)}, u32[]{:S(2)}, u32[]{:S(2)}) collective-permute-start(f32[18448]{0:T(1024)S(1)} %add.123), channel_id=1, source_target_pairs={{0,16},{8,24},{16,0},{24,8},{32,48},{40,56},{48,32},{56,40},{64,80... | collective-permute-start | bytes 221384 | tf_op jit(solution)/shard_map/ppermute | solution.py:47
  60.1 4.3 %collective-permute-start.11 = (f32[18448]{0:T(1024)S(1)}, f32[18448]{0:T(1024)S(1)}, u32[]{:S(2)}, u32[]{:S(2)}) collective-permute-start(f32[18448]{0:T(1024)S(1)} %add.124), channel_id=1, source_target_pairs={{0,64},{8,72},{16,80},{24,88},{32,96},{40,104},{48,112},{56,120},{... | collective-permute-start | bytes 221384 | tf_op jit(solution)/shard_map/ppermute | solution.py:47
  64.5 5.8 %collective-permute-start.12 = (f32[18448]{0:T(1024)S(1)}, f32[18448]{0:T(1024)S(1)}, u32[]{:S(2)}, u32[]{:S(2)}) collective-permute-start(f32[18448]{0:T(1024)S(1)} %add.125), channel_id=1, source_target_pairs={{0,192},{8,200},{16,208},{24,216},{32,224},{40,232},{48,240},{56,2... | collective-permute-start | bytes 221384 | tf_op jit(solution)/shard_map/ppermute | solution.py:47
  67.6 15.4 %collective-permute-start.5 = (bf16[2,48,128]{2,1,0:T(8,128)(2,1)S(1)}, bf16[2,48,128]{2,1,0:T(8,128)(2,1)S(1)}, u32[]{:S(2)}, u32[]{:S(2)}) collective-permute-start(bf16[2,48,128]{2,1,0:T(8,128)(2,1)S(1)} %pad_maximum_fusion.1), channel_id=1, source_target_pairs={{0,128},{8,136},{16,144},{24,152},{32,160},{40,168},{48,176},{56,1... | collective-permute-start | bytes 73736 | tf_op jit(solution)/shard_map/ppermute | solution.py:27
  70.3 4.8 %collective-permute-start.13 = (f32[18448]{0:T(1024)S(1)}, f32[18448]{0:T(1024)S(1)}, u32[]{:S(2)}, u32[]{:S(2)}) collective-permute-start(f32[18448]{0:T(1024)S(1)} %add.126), channel_id=1, source_target_pairs={{0,6},{1,7},{2,4},{3,5},{4,2},{5,3},{6,0},{7,1},{8,14},{9,15},{10,... | collective-permute-start | bytes 221384 | tf_op jit(solution)/shard_map/ppermute | solution.py:47
  75.1 4.5 %collective-permute-start.14 = (f32[18448]{0:T(1024)S(1)}, f32[18448]{0:T(1024)S(1)}, u32[]{:S(2)}, u32[]{:S(2)}) collective-permute-start(f32[18448]{0:T(1024)S(1)} %add.127), channel_id=1, source_target_pairs={{0,32},{8,40},{16,48},{24,56},{32,0},{40,8},{48,16},{56,24},{64,96... | collective-permute-start | bytes 221384 | tf_op jit(solution)/shard_map/ppermute | solution.py:51
  78.6 1.7 %copy-start.4 = (bf16[3,3,128,128]{3,2,1,0:T(8,128)(2,1)S(1)}, bf16[3,3,128,128]{3,2,1,0:T(8,128)(2,1)}, u32[]{:S(2)}) copy-start(bf16[3,3,128,128]{3,2,1,0:T(8,128)(2,1)} %param.13) | copy-start | bytes 884740
  78.7 1.7 %copy-start.6 = (pred[8,7]{0,1:T(8,128)(4,1)S(1)}, pred[8,7]{0,1:T(8,128)(4,1)}, u32[]{:S(2)}) copy-start(pred[8,7]{0,1:T(8,128)(4,1)} %constant.203) | copy-start | bytes 172
  79.7 4.1 %collective-permute-start.15 = (f32[36896]{0:T(1024)S(1)}, f32[36896]{0:T(1024)S(1)}, u32[]{:S(2)}, u32[]{:S(2)}) collective-permute-start(f32[36896]{0:T(1024)S(1)} %maximum_select_fusion.2), channel_id=1, source_target_pairs={{0,1},{1,0},{2,3},{3,2},{4,5},{5,4},{6,7},{7,6},{8,9},{9,8},{10,11... | collective-permute-start | bytes 442760 | tf_op jit(solution)/shard_map/ppermute | solution.py:51
  84.0 10.7 %collective-permute-start.16 = (f32[73792]{0:T(1024)S(1)}, f32[73792]{0:T(1024)S(1)}, u32[]{:S(2)}, u32[]{:S(2)}) collective-permute-start(f32[73792]{0:T(1024)S(1)} %maximum_select_fusion.1), channel_id=1, source_target_pairs={{0,8},{8,0},{16,24},{24,16},{32,40},{40,32},{48,56},{56,48},{64,72... | collective-permute-start | bytes 885512 | tf_op jit(solution)/shard_map/ppermute | solution.py:51

commit v5 on v4

--- a/solution.py
+++ b/solution.py
@@ -100,9 +100,9 @@
     both = jnp.concatenate([inputs, cotangent], axis=2)
     wide = extended(both, (("lon", 1),), 2, True)
     tall = extended(wide, (("lat", 0),), 2, False)
-    far = from_behind(jnp.stack([wide[0], wide[-1]]), "lon", half)
+    far = from_behind(jnp.stack([wide[0], wide[1], wide[-2], wide[-1]]), "lon", half)
     tall = tall.at[1].set(jnp.where(band == 0, far[0], tall[1]))
-    tall = tall.at[rows + 2].set(jnp.where(band == bands - 1, far[1], tall[rows + 2]))
+    tall = tall.at[rows + 2].set(jnp.where(band == bands - 1, far[3], tall[rows + 2]))
     padded = tall[:, :, :chans]
     ring_cot = tall[1:-1, 1:-1, chans:].astype(jnp.float32)
     pre = lax.conv_general_dilated(
@@ -130,18 +130,31 @@
         preferred_element_type=jnp.float32,
     )[0]
     polar = []
-    for line_at, tap_a in ((1, 0), (rows, 2)):
+    for window, cot_line, tap_a in (
+        (jnp.stack([wide[0], far[0], far[1]]), far[0], 0),
+        (jnp.stack([far[2], far[3], wide[-1]]), far[3], 2),
+    ):
+        pre_line = lax.conv_general_dilated(
+            window[None, :, :, :chans],
+            weight,
+            (1, 1),
+            "VALID",
+            dimension_numbers=("NHWC", "HWIO", "NHWC"),
+            preferred_element_type=jnp.float32,
+        )[0, 0] + bias
+        sig_line = jax.nn.sigmoid(pre_line)
+        cot_far = cot_line[1:-1, chans:].astype(jnp.float32)
+        grad_line = (cot_far * sig_line * (1.0 + pre_line * (1.0 - sig_line))).astype(jnp.bfloat16)
         ring = jnp.zeros((cols, chans), jnp.float32)
         for tap_b in range(3):
             ring = ring + jnp.dot(
-                grad_ext[line_at, tap_b : tap_b + cols],
+                grad_line[tap_b : tap_b + cols],
                 weight[tap_a, 2 - tap_b].T,
                 preferred_element_type=jnp.float32,
             )
         polar.append(ring)
-    polar_in = from_behind(jnp.stack(polar).astype(jnp.bfloat16), "lon", half).astype(jnp.float32)
-    cell_grad = cell_grad.at[0].add(jnp.where(band == 0, polar_in[0], 0.0))
-    cell_grad = cell_grad.at[-1].add(jnp.where(band == bands - 1, polar_in[1], 0.0))
+    cell_grad = cell_grad.at[0].add(jnp.where(band == 0, polar[0], 0.0))
+    cell_grad = cell_grad.at[-1].add(jnp.where(band == bands - 1, polar[1], 0.0))
     input_grad = cell_grad.astype(jnp.bfloat16)
     taps = []
     for tap_a in range(3):

time: 96.9 us -> 115 us (1.19)
  waiting for transfers between devices: 19.7 us -> 26.3 us
  local copies, waits for them, and re-layouts: 6.75 us -> 13.3 us
  matrix products: 13.5 us -> 17.1 us
  other arithmetic: 8.35 us -> 9.93 us
    dot_general x9, matrix products: 4.42 us -> 12.3 us  [shards(): lax.dot_general(window, pre_grad, (((0,), (0,)), ((), ())), preferred_ele...]
    dot_general x6, matrix products: 5.31 us -> 0.77 us  [shards(): jnp.dot(grad_line[tap_b:tap_b + cols], weight[tap_a, 2 - tap_b].T, prefer...]
    ppermute x5, waiting for transfers between devices: 6.51 us -> 9.43 us  [butterfly_sum(): data = data + lax.ppermute(data, axis, pairs)]
    ppermute x2 -> x1, starting transfers between devices: 9.94 us -> 7.21 us  [from_behind(): return lax.ppermute(value, axis, pairs)]
    ppermute x5, starting transfers between devices: 12 us -> 14.2 us  [butterfly_sum(): data = data + lax.ppermute(data, axis, pairs)]
    ppermute x3, waiting for transfers between devices: 1.9 us -> 4.01 us  [butterfly_sum(): other = lax.ppermute(data, axis, pairs)]
    dynamic_slice x3, local copies, waits for them, and re-layouts: 0.36 us -> 2.03 us  [butterfly_sum(): send = lax.dynamic_slice_in_dim(data, (1 - bit) * half, half)]
    conv_general_dilated x7 -> x8, local copies, waits for them, and re-layouts: 0.77 us -> 2.27 us  [shards(): lax.conv_general_dilated(grad_ext[None], flipped, (1, 1), 'VALID', dimens...]
  transfers between devices with their start and end apart: 17 -> 16, of which waited for: 13 -> 13; matrix products, arithmetic and copies ran while one was open for 12% -> 8% of each run, Pallas kernels for 0% -> 0%
where the time goes in v5:
time: 115 us; the launch traced here: 114 us
  starting transfers between devices  46.5 us (40%)
  waiting for transfers between devices  26.3 us (23%)
  matrix products  17.1 us (15%)
  local copies, waits for them, and re-layouts  13.3 us (12%)
  other arithmetic  9.93 us (9%)
  between operations  1.17 us (1%)
    ppermute x5, starting transfers between devices, butterfly_sum(): data = data + lax.ppermute(data, axis, pairs)  14.2 us
    dot_general x9, matrix products, shards(): lax.dot_general(window, pre_grad, (((0,), (0,)), ((), ())), preferred_ele...  12.3 us
    ppermute x3, starting transfers between devices, butterfly_sum(): other = lax.ppermute(data, axis, pairs)  12.1 us
    ppermute x5, waiting for transfers between devices, butterfly_sum(): data = data + lax.ppermute(data, axis, pairs)  9.43 us
    ppermute x1, starting transfers between devices, from_behind(): return lax.ppermute(value, axis, pairs)  7.21 us
    ppermute x2, starting transfers between devices, extended(): lax.ppermute(tail, axis, [(i, (i + 1) % count) for i in range(ends)])  6.42 us
    ppermute x3, waiting for transfers between devices, butterfly_sum(): data = keep + lax.ppermute(send, axis, pairs)  5.96 us
    ppermute x3, starting transfers between devices, butterfly_sum(): data = keep + lax.ppermute(send, axis, pairs)  5.33 us
  transfers between devices with their start and end apart: 16, of which 13 were waited for; matrix products, arithmetic and copies ran while one was open for 8% of the time, Pallas kernels for 0%

profile of v5, /device:TPU:1, one launch (start us, length us, event | category | flops | bytes accessed | tf_op | source)
XLA Modules:
  0.0 114.3 jit_solution(10262262978771773385)
XLA Ops:
  0.6 1.2 %constant_dynamic-update-slice_fusion.1 = bf16[48,48,256]{2,1,0:T(8,128)(2,1)S(1)} fusion(bf16[48,48,128]{2,1,0:T(8,128)(2,1)} %param.12), kind=kLoop, calls=%fused_computation.139 | loop fusion | bytes 1179648
  2.1 4.2 %collective-permute-start = (bf16[48,2,256]{2,1,0:T(2,128)(2,1)S(1)}, bf16[48,2,256]{2,1,0:T(2,128)(2,1)S(1)}, u32[]{:S(2)}, u32[]{:S(2)}) collective-permute-start(bf16[48,2,256]{2,1,0:T(2,128)(2,1)S(1)} %get-tuple-element.58), channel_id=1, source_target_pairs={{0,8},{8,16},{16,24},{24,32},{32,40},{40,48},{48,56},{56,64},{64,7... | collective-permute-start | bytes 147464 | tf_op jit(solution)/shard_map/ppermute | solution.py:15
  6.4 1.1 collective-permute-done
  7.5 3.8 %collective-permute-done.1 = bf16[48,2,256]{2,1,0:T(2,128)(2,1)S(1)} collective-permute-done((bf16[48,2,256]{2,1,0:T(2,128)(2,1)S(1)}, bf16[48,2,256]{2,1,0:T(2,128)(2,1)S(1)}, u32[]{:S(2)}, u32[]{:S(2)}) %collective-permute-start.1) | collective-permute-done | bytes 49184 | tf_op jit(solution)/shard_map/ppermute | solution.py:17
  11.4 2.2 %collective-permute-start.2 = (bf16[2,52,256]{2,1,0:T(8,128)(2,1)S(1)}, bf16[2,52,256]{2,1,0:T(8,128)(2,1)S(1)}, u32[]{:S(2)}, u32[]{:S(2)}) collective-permute-start(bf16[2,52,256]{2,1,0:T(8,128)(2,1)S(1)} %get-tuple-element.56), channel_id=1, source_target_pairs={{0,1},{1,2},{2,3},{3,4},{4,5},{5,6},{6,7},{8,9},{9,10},{10,11},{11... | collective-permute-start | bytes 159752 | tf_op jit(solution)/shard_map/ppermute | solution.py:15
  13.6 1.3 %collective-permute-start.3 = (bf16[2,52,256]{2,1,0:T(8,128)(2,1)S(1)}, bf16[2,52,256]{2,1,0:T(8,128)(2,1)S(1)}, u32[]{:S(2)}, u32[]{:S(2)}) collective-permute-start(bf16[2,52,256]{2,1,0:T(8,128)(2,1)S(1)} %get-tuple-element.57), channel_id=1, source_target_pairs={{1,0},{2,1},{3,2},{4,3},{5,4},{6,5},{7,6},{9,8},{10,9},{11,10},{12... | collective-permute-start | bytes 159752 | tf_op jit(solution)/shard_map/ppermute | solution.py:17
  14.9 7.2 %collective-permute-start.4 = (bf16[4,52,256]{2,1,0:T(8,128)(2,1)S(1)}, bf16[4,52,256]{2,1,0:T(8,128)(2,1)S(1)}, u32[]{:S(2)}, u32[]{:S(2)}) collective-permute-start(bf16[4,52,256]{2,1,0:T(8,128)(2,1)S(1)} %pad_maximum_fusion.1), channel_id=1, source_target_pairs={{0,128},{8,136},{16,144},{24,152},{32,160},{40,168},{48,176},{56,1... | collective-permute-start | bytes 319496 | tf_op jit(solution)/shard_map/ppermute | solution.py:27
  22.9 2.0 %collective-permute-done.4 = bf16[4,52,256]{2,1,0:T(8,128)(2,1)S(1)} collective-permute-done((bf16[4,52,256]{2,1,0:T(8,128)(2,1)S(1)}, bf16[4,52,256]{2,1,0:T(8,128)(2,1)S(1)}, u32[]{:S(2)}, u32[]{:S(2)}) %collective-permute-start.4) | collective-permute-done | bytes 106528 | tf_op jit(solution)/shard_map/ppermute | solution.py:27
  25.8 0.9 copy-done
  27.7 1.8 %convolution_select_fusion.1 = f32[50,8,7,128]{3,1,2,0:T(8,128)S(1)} fusion(bf16[3,3,128,128]{3,2,1,0:T(8,128)(2,1)S(1)} %copy-done.5, bf16[52,1,7,2,128]{4,2,3,0,1:T(8,128)(2,1)S(1)} %slice.299, bf16[52,1,8,7,128]{4,2,3,0,1:T(8,128)(2,1)S(1)} %copy.10, pred[8,7]{0,1:T(8,128)(4,1)S(1)} %copy-done.10), kind=kOutput, calls=%fused_computation.10 | convolution fusion | flops 828987392 | bytes 2660408 | tf_op jit(solution)/shard_map/conv_general_dilated | solution.py:108
  29.9 1.2 %reshape.174 = f32[50,1,56,128]{3,2,0,1:T(8,128)} reshape(f32[50,8,7,128]{3,2,1,0:T(8,128)S(1)} %copy.11) | data formatting | bytes 2867200 | tf_op jit(solution)/shard_map/conv_general_dilated | solution.py:108
  31.1 2.4 %fusion.33 = (bf16[50,50,128]{2,1,0:T(8,128)(2,1)S(1)}, f32[50,50,128]{2,1,0:T(8,128)S(1)}) fusion(bf16[52,52,256]{2,1,0:T(8,128)(2,1)} %copy-done, pred[50]{0:T(512)(128)(4,1)S(1)} %and_or_fusion, f32[128]{0:T(128)S(1)} %copy-done.9, f32[50,1,56,128]{3,2,0,1:T(8,128)} %reshape.174), kind=kLoop, calls=%fused_computation.58 | loop fusion | flops 3840000 | bytes 3840562 | tf_op jit(solution)/shard_map/jit(_where)/select_n | solution.py:121
  33.9 2.2 %fusion.12 = f32[1153,128]{1,0:T(8,128)} fusion(bf16[52,52,256]{2,1,0:T(8,128)(2,1)} %copy-done, bf16[50,50,128]{2,1,0:T(8,128)(2,1)S(1)} %get-tuple-element.52), kind=kOutput, calls=%fused_computation.32 | convolution fusion | flops 75497472 | bytes 1245184 | tf_op jit(solution)/shard_map/dot_general | solution.py:164
  36.3 2.3 %fusion.11 = f32[1153,128]{1,0:T(8,128)} fusion(f32[1153,128]{1,0:T(8,128)} %fusion.12, bf16[52,52,256]{2,1,0:T(8,128)(2,1)} %copy-done, bf16[50,50,128]{2,1,0:T(8,128)(2,1)S(1)} %get-tuple-element.52), kind=kOutput, calls=%fused_computation.30 | convolution fusion | flops 75497472 | bytes 1245184 | tf_op jit(solution)/shard_map/dot_general | solution.py:164
  38.6 1.1 fusion.10
  39.7 1.1 fusion.9
  40.8 1.1 fusion.8
  41.9 1.1 fusion.7
  43.0 1.1 fusion.6
  44.1 1.1 fusion.5
  45.2 1.1 fusion.4
  46.4 1.3 %dynamic-update-slice.21 = f32[1153,128]{1,0:T(8,128)} dynamic-update-slice(f32[1153,128]{1,0:T(8,128)} %fusion.4, f32[1,128]{1,0:T(1,128)S(1)} %bitcast.151, s32[]{} %constant.230, s32[]{} %constant.221) | dynamic-update-slice | bytes 1028 | tf_op jit(solution)/shard_map/concatenate | solution.py:171
  47.6 1.8 %dynamic_slice.19 = f32[73792]{0:T(1024)} dynamic-slice(f32[147584]{0:T(1024)} %bitcast.145, s32[]{:T(128)S(6)} %select_n.114), dynamic_slice_sizes={73792} | dynamic-slice | bytes 590340 | tf_op jit(solution)/shard_map/dynamic_slice | solution.py:42
  49.5 1.4 %collective-permute-start.5 = (f32[73792]{0:T(1024)}, f32[73792]{0:T(1024)}, u32[]{:S(2)}, u32[]{:S(2)}) collective-permute-start(f32[73792]{0:T(1024)} %dynamic_slice.19), channel_id=1, source_target_pairs={{0,8},{8,0},{16,24},{24,16},{32,40},{40,32},{48,56},{56,48},{64,72... | collective-permute-start | bytes 885512 | tf_op jit(solution)/shard_map/ppermute | solution.py:44
  50.9 0.9 pad.10
  51.8 1.4 %reshape.177 = bf16[50,1,8,7,128]{4,3,2,0,1:T(8,128)(2,1)S(1)} reshape(bf16[50,1,56,128]{3,2,0,1:T(8,128)(2,1)} %pad.10) | data formatting | bytes 1433600 | tf_op jit(solution)/shard_map/conv_general_dilated | solution.py:124
  53.4 1.8 %convolution_select_fusion = f32[48,8,7,128]{3,1,2,0:T(8,128)S(1)} fusion(bf16[3,3,128,128]{3,2,1,0:T(8,128)(2,1)S(1)} %copy-done.6, bf16[50,1,7,2,128]{4,2,3,0,1:T(8,128)(2,1)S(1)} %slice.304, bf16[50,1,8,7,128]{4,2,3,0,1:T(8,128)(2,1)S(1)} %copy.13, pred[8,7]{0,1:T(8,128)(4,1)S(1)} %copy-done.11), kind=kOutput, calls=%fused_computation.5 | convolution fusion | flops 795832320 | bytes 2567224 | tf_op jit(solution)/shard_map/conv_general_dilated | solution.py:124
  55.7 1.1 copy-done.3
  56.8 1.1 dynamic-slice_add_fusion
  58.0 2.7 %collective-permute-start.6 = (f32[36896]{0:T(1024)S(1)}, f32[36896]{0:T(1024)S(1)}, u32[]{:S(2)}, u32[]{:S(2)}) collective-permute-start(f32[36896]{0:T(1024)S(1)} %dynamic_slice.21), channel_id=1, source_target_pairs={{0,1},{1,0},{2,3},{3,2},{4,5},{5,4},{6,7},{7,6},{8,9},{9,8},{10,11... | collective-permute-start | bytes 442760 | tf_op jit(solution)/shard_map/ppermute | solution.py:44
  60.9 4.1 %collective-permute-done.6 = f32[36896]{0:T(1024)S(1)} collective-permute-done((f32[36896]{0:T(1024)S(1)}, f32[36896]{0:T(1024)S(1)}, u32[]{:S(2)}, u32[]{:S(2)}) %collective-permute-start.6) | collective-permute-done | bytes 147616 | tf_op jit(solution)/shard_map/ppermute | solution.py:44
  65.2 1.2 %collective-permute-start.7 = (f32[18448]{0:T(1024)S(1)}, f32[18448]{0:T(1024)S(1)}, u32[]{:S(2)}, u32[]{:S(2)}) collective-permute-start(f32[18448]{0:T(1024)S(1)} %dynamic_slice.23), channel_id=1, source_target_pairs={{0,32},{8,40},{16,48},{24,56},{32,0},{40,8},{48,16},{56,24},{64,96... | collective-permute-start | bytes 221384 | tf_op jit(solution)/shard_map/ppermute | solution.py:44
  66.7 1.8 %collective-permute-done.7 = f32[18448]{0:T(1024)S(1)} collective-permute-done((f32[18448]{0:T(1024)S(1)}, f32[18448]{0:T(1024)S(1)}, u32[]{:S(2)}, u32[]{:S(2)}) %collective-permute-start.7) | collective-permute-done | bytes 73824 | tf_op jit(solution)/shard_map/ppermute | solution.py:44
  68.6 2.5 %collective-permute-start.8 = (f32[18448]{0:T(1024)S(1)}, f32[18448]{0:T(1024)S(1)}, u32[]{:S(2)}, u32[]{:S(2)}) collective-permute-start(f32[18448]{0:T(1024)S(1)} %dynamic-slice_add_fusion.2), channel_id=1, source_target_pairs={{0,2},{1,3},{2,0},{3,1},{4,6},{5,7},{6,4},{7,5},{8,10},{9,11},{10,... | collective-permute-start | bytes 221384 | tf_op jit(solution)/shard_map/ppermute | solution.py:47
  71.2 1.7 %collective-permute-done.8 = f32[18448]{0:T(1024)S(1)} collective-permute-done((f32[18448]{0:T(1024)S(1)}, f32[18448]{0:T(1024)S(1)}, u32[]{:S(2)}, u32[]{:S(2)}) %collective-permute-start.8) | collective-permute-done | bytes 73824 | tf_op jit(solution)/shard_map/ppermute | solution.py:47
  73.0 1.4 %collective-permute-start.9 = (f32[18448]{0:T(1024)S(1)}, f32[18448]{0:T(1024)S(1)}, u32[]{:S(2)}, u32[]{:S(2)}) collective-permute-start(f32[18448]{0:T(1024)S(1)} %add.158), channel_id=1, source_target_pairs={{0,16},{8,24},{16,0},{24,8},{32,48},{40,56},{48,32},{56,40},{64,80... | collective-permute-start | bytes 221384 | tf_op jit(solution)/shard_map/ppermute | solution.py:47
  74.5 3.3 %collective-permute-done.9 = f32[18448]{0:T(1024)S(1)} collective-permute-done((f32[18448]{0:T(1024)S(1)}, f32[18448]{0:T(1024)S(1)}, u32[]{:S(2)}, u32[]{:S(2)}) %collective-permute-start.9) | collective-permute-done | bytes 73824 | tf_op jit(solution)/shard_map/ppermute | solution.py:47
  77.8 2.3 %collective-permute-start.10 = (f32[18448]{0:T(1024)S(1)}, f32[18448]{0:T(1024)S(1)}, u32[]{:S(2)}, u32[]{:S(2)}) collective-permute-start(f32[18448]{0:T(1024)S(1)} %add.159), channel_id=1, source_target_pairs={{0,64},{8,72},{16,80},{24,88},{32,96},{40,104},{48,112},{56,120},{... | collective-permute-start | bytes 221384 | tf_op jit(solution)/shard_map/ppermute | solution.py:47
  82.1 4.9 %collective-permute-start.11 = (f32[18448]{0:T(1024)S(1)}, f32[18448]{0:T(1024)S(1)}, u32[]{:S(2)}, u32[]{:S(2)}) collective-permute-start(f32[18448]{0:T(1024)S(1)} %add.160), channel_id=1, source_target_pairs={{0,192},{8,200},{16,208},{24,216},{32,224},{40,232},{48,240},{56,2... | collective-permute-start | bytes 221384 | tf_op jit(solution)/shard_map/ppermute | solution.py:47
  87.1 1.7 %collective-permute-done.11 = f32[18448]{0:T(1024)S(1)} collective-permute-done((f32[18448]{0:T(1024)S(1)}, f32[18448]{0:T(1024)S(1)}, u32[]{:S(2)}, u32[]{:S(2)}) %collective-permute-start.11) | collective-permute-done | bytes 73824 | tf_op jit(solution)/shard_map/ppermute | solution.py:47
  88.9 3.1 %collective-permute-start.12 = (f32[18448]{0:T(1024)S(1)}, f32[18448]{0:T(1024)S(1)}, u32[]{:S(2)}, u32[]{:S(2)}) collective-permute-start(f32[18448]{0:T(1024)S(1)} %add.161), channel_id=1, source_target_pairs={{0,6},{1,7},{2,4},{3,5},{4,2},{5,3},{6,0},{7,1},{8,14},{9,15},{10,... | collective-permute-start | bytes 221384 | tf_op jit(solution)/shard_map/ppermute | solution.py:47
  92.1 2.0 %collective-permute-done.12 = f32[18448]{0:T(1024)S(1)} collective-permute-done((f32[18448]{0:T(1024)S(1)}, f32[18448]{0:T(1024)S(1)}, u32[]{:S(2)}, u32[]{:S(2)}) %collective-permute-start.12) | collective-permute-done | bytes 73824 | tf_op jit(solution)/shard_map/ppermute | solution.py:47
  94.0 1.7 %collective-permute-start.13 = (f32[18448]{0:T(1024)S(1)}, f32[18448]{0:T(1024)S(1)}, u32[]{:S(2)}, u32[]{:S(2)}) collective-permute-start(f32[18448]{0:T(1024)S(1)} %add.162), channel_id=1, source_target_pairs={{0,32},{8,40},{16,48},{24,56},{32,0},{40,8},{48,16},{56,24},{64,96... | collective-permute-start | bytes 221384 | tf_op jit(solution)/shard_map/ppermute | solution.py:51
  95.9 1.7 %collective-permute-done.13 = f32[18448]{0:T(1024)S(1)} collective-permute-done((f32[18448]{0:T(1024)S(1)}, f32[18448]{0:T(1024)S(1)}, u32[]{:S(2)}, u32[]{:S(2)}) %collective-permute-start.13) | collective-permute-done | bytes 73824 | tf_op jit(solution)/shard_map/ppermute | solution.py:51
  98.6 0.9 convert_element_type.32
  99.5 2.3 %collective-permute-done.14 = f32[36896]{0:T(1024)S(1)} collective-permute-done((f32[36896]{0:T(1024)S(1)}, f32[36896]{0:T(1024)S(1)}, u32[]{:S(2)}, u32[]{:S(2)}) %collective-permute-start.14) | collective-permute-done | bytes 147616 | tf_op jit(solution)/shard_map/ppermute | solution.py:51
  102.0 9.5 %collective-permute-start.15 = (f32[73792]{0:T(1024)S(1)}, f32[73792]{0:T(1024)S(1)}, u32[]{:S(2)}, u32[]{:S(2)}) collective-permute-start(f32[73792]{0:T(1024)S(1)} %maximum_select_fusion.1), channel_id=1, source_target_pairs={{0,8},{8,0},{16,24},{24,16},{32,40},{40,32},{48,56},{56,48},{64,72... | collective-permute-start | bytes 885512 | tf_op jit(solution)/shard_map/ppermute | solution.py:51
  111.5 1.2 %fusion.3 = bf16[48,48,128]{2,1,0:T(8,128)(2,1)} fusion(f32[50,50,128]{2,1,0:T(8,128)S(1)} %add_divide_fusion, f32[50,50,128]{2,1,0:T(8,128)S(1)} %get-tuple-element.53), kind=kLoop, calls=%fused_computation.12 | loop fusion | flops 589824 | bytes 2949120 | tf_op jit(solution)/shard_map/convert
  (88 shorter events, 10.5 us)
Async XLA Ops:
  0.6 1.2 %copy-start.4 = (bf16[48,48,128]{2,1,0:T(8,128)(2,1)S(1)}, bf16[48,48,128]{2,1,0:T(8,128)(2,1)}, u32[]{:S(2)}) copy-start(bf16[48,48,128]{2,1,0:T(8,128)(2,1)} %param.15) | copy-start | bytes 1769476
  2.1 5.4 %collective-permute-start = (bf16[48,2,256]{2,1,0:T(2,128)(2,1)S(1)}, bf16[48,2,256]{2,1,0:T(2,128)(2,1)S(1)}, u32[]{:S(2)}, u32[]{:S(2)}) collective-permute-start(bf16[48,2,256]{2,1,0:T(2,128)(2,1)S(1)} %get-tuple-element.58), channel_id=1, source_target_pairs={{0,8},{8,16},{16,24},{24,32},{32,40},{40,48},{48,56},{56,64},{64,7... | collective-permute-start | bytes 147464 | tf_op jit(solution)/shard_map/ppermute | solution.py:15
  6.3 5.0 %collective-permute-start.1 = (bf16[48,2,256]{2,1,0:T(2,128)(2,1)S(1)}, bf16[48,2,256]{2,1,0:T(2,128)(2,1)S(1)}, u32[]{:S(2)}, u32[]{:S(2)}) collective-permute-start(bf16[48,2,256]{2,1,0:T(2,128)(2,1)S(1)} %get-tuple-element.59), channel_id=1, source_target_pairs={{8,0},{16,8},{24,16},{32,24},{40,32},{48,40},{56,48},{64,56},{72,6... | collective-permute-start | bytes 147464 | tf_op jit(solution)/shard_map/ppermute | solution.py:17
  11.4 10.8 %collective-permute-start.2 = (bf16[2,52,256]{2,1,0:T(8,128)(2,1)S(1)}, bf16[2,52,256]{2,1,0:T(8,128)(2,1)S(1)}, u32[]{:S(2)}, u32[]{:S(2)}) collective-permute-start(bf16[2,52,256]{2,1,0:T(8,128)(2,1)S(1)} %get-tuple-element.56), channel_id=1, source_target_pairs={{0,1},{1,2},{2,3},{3,4},{4,5},{5,6},{6,7},{8,9},{9,10},{10,11},{11... | collective-permute-start | bytes 159752 | tf_op jit(solution)/shard_map/ppermute | solution.py:15
  13.6 8.5 %collective-permute-start.3 = (bf16[2,52,256]{2,1,0:T(8,128)(2,1)S(1)}, bf16[2,52,256]{2,1,0:T(8,128)(2,1)S(1)}, u32[]{:S(2)}, u32[]{:S(2)}) collective-permute-start(bf16[2,52,256]{2,1,0:T(8,128)(2,1)S(1)} %get-tuple-element.57), channel_id=1, source_target_pairs={{1,0},{2,1},{3,2},{4,3},{5,4},{6,5},{7,6},{9,8},{10,9},{11,10},{12... | collective-permute-start | bytes 159752 | tf_op jit(solution)/shard_map/ppermute | solution.py:17
  14.9 10.0 %collective-permute-start.4 = (bf16[4,52,256]{2,1,0:T(8,128)(2,1)S(1)}, bf16[4,52,256]{2,1,0:T(8,128)(2,1)S(1)}, u32[]{:S(2)}, u32[]{:S(2)}) collective-permute-start(bf16[4,52,256]{2,1,0:T(8,128)(2,1)S(1)} %pad_maximum_fusion.1), channel_id=1, source_target_pairs={{0,128},{8,136},{16,144},{24,152},{32,160},{40,168},{48,176},{56,1... | collective-permute-start | bytes 319496 | tf_op jit(solution)/shard_map/ppermute | solution.py:27
  25.6 1.2 %copy-start = (bf16[52,52,256]{2,1,0:T(8,128)(2,1)}, bf16[52,52,256]{2,1,0:T(8,128)(2,1)S(1)}, u32[]{:S(2)}) copy-start(bf16[52,52,256]{2,1,0:T(8,128)(2,1)S(1)} %get-tuple-element.62) | copy-start | bytes 4153348
  26.7 1.0 copy-start.5
  26.7 1.0 copy-start.10
  29.9 1.2 %copy-start.9 = (f32[128]{0:T(128)S(1)}, f32[128]{0:T(128)}, u32[]{:S(2)}) copy-start(f32[128]{0:T(128)} %param.14) | copy-start | bytes 1540
  36.2 2.3 %copy-start.1 = (bf16[52,52,256]{2,1,0:T(8,128)(2,1)S(1)}, bf16[52,52,256]{2,1,0:T(8,128)(2,1)}, u32[]{:S(2)}) copy-start(bf16[52,52,256]{2,1,0:T(8,128)(2,1)} %copy-done) | copy-start | bytes 4153348
  49.5 6.2 %collective-permute-start.5 = (f32[73792]{0:T(1024)}, f32[73792]{0:T(1024)}, u32[]{:S(2)}, u32[]{:S(2)}) collective-permute-start(f32[73792]{0:T(1024)} %dynamic_slice.19), channel_id=1, source_target_pairs={{0,8},{8,0},{16,24},{24,16},{32,40},{40,32},{48,56},{56,48},{64,72... | collective-permute-start | bytes 885512 | tf_op jit(solution)/shard_map/ppermute | solution.py:44
  51.8 1.6 %copy-start.6 = (bf16[3,3,128,128]{3,2,1,0:T(8,128)(2,1)S(1)}, bf16[3,3,128,128]{3,2,1,0:T(8,128)(2,1)}, u32[]{:S(2)}) copy-start(bf16[3,3,128,128]{3,2,1,0:T(8,128)(2,1)} %param.13) | copy-start | bytes 884740
  51.8 1.6 %copy-start.11 = (pred[8,7]{0,1:T(8,128)(4,1)S(1)}, pred[8,7]{0,1:T(8,128)(4,1)}, u32[]{:S(2)}) copy-start(pred[8,7]{0,1:T(8,128)(4,1)} %constant.212) | copy-start | bytes 172
  55.3 25.0 %copy-start.2 = (f32[48,8,7,128]{3,1,2,0:T(8,128)}, f32[48,8,7,128]{3,1,2,0:T(8,128)S(1)}, u32[]{:S(2)}) copy-start(f32[48,8,7,128]{3,1,2,0:T(8,128)S(1)} %convolution_select_fusion) | copy-start | bytes 4128772
  55.3 1.5 %copy-start.3 = (f32[1153,128]{1,0:T(8,128)S(1)}, f32[1153,128]{1,0:T(8,128)}, u32[]{:S(2)}) copy-start(f32[1153,128]{1,0:T(8,128)} %dynamic-update-slice.21) | copy-start | bytes 1771012
  55.7 15.5 %copy-start.7 = (bf16[52,256]{1,0:T(8,128)(2,1)S(1)}, bf16[52,256]{1,0:T(8,128)(2,1)}, u32[]{:S(2)}) copy-start(bf16[52,256]{1,0:T(8,128)(2,1)} %get-tuple-element.60) | copy-start | bytes 79876
  55.7 15.5 %copy-start.8 = (bf16[52,256]{1,0:T(8,128)(2,1)S(1)}, bf16[52,256]{1,0:T(8,128)(2,1)}, u32[]{:S(2)}) copy-start(bf16[52,256]{1,0:T(8,128)(2,1)} %get-tuple-element.61) | copy-start | bytes 79876
  58.0 7.0 %collective-permute-start.6 = (f32[36896]{0:T(1024)S(1)}, f32[36896]{0:T(1024)S(1)}, u32[]{:S(2)}, u32[]{:S(2)}) collective-permute-start(f32[36896]{0:T(1024)S(1)} %dynamic_slice.21), channel_id=1, source_target_pairs={{0,1},{1,0},{2,3},{3,2},{4,5},{5,4},{6,7},{7,6},{8,9},{9,8},{10,11... | collective-permute-start | bytes 442760 | tf_op jit(solution)/shard_map/ppermute | solution.py:44
  65.2 3.3 %collective-permute-start.7 = (f32[18448]{0:T(1024)S(1)}, f32[18448]{0:T(1024)S(1)}, u32[]{:S(2)}, u32[]{:S(2)}) collective-permute-start(f32[18448]{0:T(1024)S(1)} %dynamic_slice.23), channel_id=1, source_target_pairs={{0,32},{8,40},{16,48},{24,56},{32,0},{40,8},{48,16},{56,24},{64,96... | collective-permute-start | bytes 221384 | tf_op jit(solution)/shard_map/ppermute | solution.py:44
  68.6 4.3 %collective-permute-start.8 = (f32[18448]{0:T(1024)S(1)}, f32[18448]{0:T(1024)S(1)}, u32[]{:S(2)}, u32[]{:S(2)}) collective-permute-start(f32[18448]{0:T(1024)S(1)} %dynamic-slice_add_fusion.2), channel_id=1, source_target_pairs={{0,2},{1,3},{2,0},{3,1},{4,6},{5,7},{6,4},{7,5},{8,10},{9,11},{10,... | collective-permute-start | bytes 221384 | tf_op jit(solution)/shard_map/ppermute | solution.py:47
  73.0 4.8 %collective-permute-start.9 = (f32[18448]{0:T(1024)S(1)}, f32[18448]{0:T(1024)S(1)}, u32[]{:S(2)}, u32[]{:S(2)}) collective-permute-start(f32[18448]{0:T(1024)S(1)} %add.158), channel_id=1, source_target_pairs={{0,16},{8,24},{16,0},{24,8},{32,48},{40,56},{48,32},{56,40},{64,80... | collective-permute-start | bytes 221384 | tf_op jit(solution)/shard_map/ppermute | solution.py:47
  77.8 4.2 %collective-permute-start.10 = (f32[18448]{0:T(1024)S(1)}, f32[18448]{0:T(1024)S(1)}, u32[]{:S(2)}, u32[]{:S(2)}) collective-permute-start(f32[18448]{0:T(1024)S(1)} %add.159), channel_id=1, source_target_pairs={{0,64},{8,72},{16,80},{24,88},{32,96},{40,104},{48,112},{56,120},{... | collective-permute-start | bytes 221384 | tf_op jit(solution)/shard_map/ppermute | solution.py:47
  80.6 0.7 slice-start
  82.1 6.8 %collective-permute-start.11 = (f32[18448]{0:T(1024)S(1)}, f32[18448]{0:T(1024)S(1)}, u32[]{:S(2)}, u32[]{:S(2)}) collective-permute-start(f32[18448]{0:T(1024)S(1)} %add.160), channel_id=1, source_target_pairs={{0,192},{8,200},{16,208},{24,216},{32,224},{40,232},{48,240},{56,2... | collective-permute-start | bytes 221384 | tf_op jit(solution)/shard_map/ppermute | solution.py:47
  88.9 5.1 %collective-permute-start.12 = (f32[18448]{0:T(1024)S(1)}, f32[18448]{0:T(1024)S(1)}, u32[]{:S(2)}, u32[]{:S(2)}) collective-permute-start(f32[18448]{0:T(1024)S(1)} %add.161), channel_id=1, source_target_pairs={{0,6},{1,7},{2,4},{3,5},{4,2},{5,3},{6,0},{7,1},{8,14},{9,15},{10,... | collective-permute-start | bytes 221384 | tf_op jit(solution)/shard_map/ppermute | solution.py:47
  94.0 3.5 %collective-permute-start.13 = (f32[18448]{0:T(1024)S(1)}, f32[18448]{0:T(1024)S(1)}, u32[]{:S(2)}, u32[]{:S(2)}) collective-permute-start(f32[18448]{0:T(1024)S(1)} %add.162), channel_id=1, source_target_pairs={{0,32},{8,40},{16,48},{24,56},{32,0},{40,8},{48,16},{56,24},{64,96... | collective-permute-start | bytes 221384 | tf_op jit(solution)/shard_map/ppermute | solution.py:51
  97.7 4.1 %collective-permute-start.14 = (f32[36896]{0:T(1024)S(1)}, f32[36896]{0:T(1024)S(1)}, u32[]{:S(2)}, u32[]{:S(2)}) collective-permute-start(f32[36896]{0:T(1024)S(1)} %maximum_select_fusion.2), channel_id=1, source_target_pairs={{0,1},{1,0},{2,3},{3,2},{4,5},{5,4},{6,7},{7,6},{8,9},{9,8},{10,11... | collective-permute-start | bytes 442760 | tf_op jit(solution)/shard_map/ppermute | solution.py:51
  102.0 10.8 %collective-permute-start.15 = (f32[73792]{0:T(1024)S(1)}, f32[73792]{0:T(1024)S(1)}, u32[]{:S(2)}, u32[]{:S(2)}) collective-permute-start(f32[73792]{0:T(1024)S(1)} %maximum_select_fusion.1), channel_id=1, source_target_pairs={{0,8},{8,0},{16,24},{24,16},{32,40},{40,32},{48,56},{56,48},{64,72... | collective-permute-start | bytes 885512 | tf_op jit(solution)/shard_map/ppermute | solution.py:51

commit v6 on v5

--- a/solution.py
+++ b/solution.py
@@ -134,14 +134,14 @@
         (jnp.stack([wide[0], far[0], far[1]]), far[0], 0),
         (jnp.stack([far[2], far[3], wide[-1]]), far[3], 2),
     ):
-        pre_line = lax.conv_general_dilated(
-            window[None, :, :, :chans],
-            weight,
-            (1, 1),
-            "VALID",
-            dimension_numbers=("NHWC", "HWIO", "NHWC"),
-            preferred_element_type=jnp.float32,
-        )[0, 0] + bias
+        pre_line = bias + jnp.zeros((cols + 2, chans), jnp.float32)
+        for tap_a_in in range(3):
+            for tap_b_in in range(3):
+                pre_line = pre_line + jnp.dot(
+                    window[tap_a_in, tap_b_in : tap_b_in + cols + 2, :chans],
+                    weight[tap_a_in, tap_b_in],
+                    preferred_element_type=jnp.float32,
+                )
         sig_line = jax.nn.sigmoid(pre_line)
         cot_far = cot_line[1:-1, chans:].astype(jnp.float32)
         grad_line = (cot_far * sig_line * (1.0 + pre_line * (1.0 - sig_line))).astype(jnp.bfloat16)

time: 115 us -> 109 us (0.948)
  matrix products: 17.1 us -> 13.3 us
  waiting for transfers between devices: 26.3 us -> 24.4 us
    dot_general x9, matrix products: 12.3 us -> 4.49 us  [shards(): lax.dot_general(window, pre_grad, (((0,), (0,)), ((), ())), preferred_ele...]
    dot_general x0 -> x18, matrix products: none -> 4.38 us  [shards(): jnp.dot(window[tap_a_in, tap_b_in:tap_b_in + cols + 2, :chans], weight[ta...]
    ppermute x1, waiting for transfers between devices: 1.97 us -> 0.01 us  [from_behind(): return lax.ppermute(value, axis, pairs)]
    unnamed x27 -> x39, local copies, waits for them, and re-layouts: 4.46 us -> 5.35 us
  transfers between devices with their start and end apart: 16 -> 16, of which waited for: 13 -> 12; matrix products, arithmetic and copies ran while one was open for 8% -> 12% of each run, Pallas kernels for 0% -> 0%
where the time goes in v6:
time: 109 us
  starting transfers between devices  46 us (42%)
  waiting for transfers between devices  24.4 us (22%)
  local copies, waits for them, and re-layouts  14 us (13%)
  matrix products  13.3 us (12%)
  other arithmetic  10 us (9%)
  between operations  1.22 us (1%)
    ppermute x5, starting transfers between devices, butterfly_sum(): data = data + lax.ppermute(data, axis, pairs)  14.2 us
    ppermute x3, starting transfers between devices, butterfly_sum(): other = lax.ppermute(data, axis, pairs)  12 us
    ppermute x5, waiting for transfers between devices, butterfly_sum(): data = data + lax.ppermute(data, axis, pairs)  9.27 us
    ppermute x1, starting transfers between devices, from_behind(): return lax.ppermute(value, axis, pairs)  7.21 us
    ppermute x2, starting transfers between devices, extended(): lax.ppermute(tail, axis, [(i, (i + 1) % count) for i in range(ends)])  6.42 us
    ppermute x3, waiting for transfers between devices, butterfly_sum(): data = keep + lax.ppermute(send, axis, pairs)  6.14 us
    unnamed x39, local copies, waits for them, and re-layouts  5.35 us
    ppermute x3, starting transfers between devices, butterfly_sum(): data = keep + lax.ppermute(send, axis, pairs)  4.76 us
  transfers between devices with their start and end apart: 16, of which 12 were waited for; matrix products, arithmetic and copies ran while one was open for 12% of the time, Pallas kernels for 0%

profile of v6, /device:TPU:1, one launch (start us, length us, event | category | flops | bytes accessed | tf_op | source)
XLA Modules:
  0.0 108.9 jit_solution(4056019360618286543)
XLA Ops:
  0.6 1.2 %constant_dynamic-update-slice_fusion.1 = bf16[48,48,256]{2,1,0:T(8,128)(2,1)S(1)} fusion(bf16[48,48,128]{2,1,0:T(8,128)(2,1)} %param.12), kind=kLoop, calls=%fused_computation.172 | loop fusion | bytes 1179648
  2.1 4.2 %collective-permute-start = (bf16[48,2,256]{2,1,0:T(2,128)(2,1)S(1)}, bf16[48,2,256]{2,1,0:T(2,128)(2,1)S(1)}, u32[]{:S(2)}, u32[]{:S(2)}) collective-permute-start(bf16[48,2,256]{2,1,0:T(2,128)(2,1)S(1)} %get-tuple-element.56), channel_id=1, source_target_pairs={{0,8},{8,16},{16,24},{24,32},{32,40},{40,48},{48,56},{56,64},{64,7... | collective-permute-start | bytes 147464 | tf_op jit(solution)/shard_map/ppermute | solution.py:15
  6.4 1.1 collective-permute-done
  7.5 3.8 %collective-permute-done.1 = bf16[48,2,256]{2,1,0:T(2,128)(2,1)S(1)} collective-permute-done((bf16[48,2,256]{2,1,0:T(2,128)(2,1)S(1)}, bf16[48,2,256]{2,1,0:T(2,128)(2,1)S(1)}, u32[]{:S(2)}, u32[]{:S(2)}) %collective-permute-start.1) | collective-permute-done | bytes 49184 | tf_op jit(solution)/shard_map/ppermute | solution.py:17
  11.4 2.2 %collective-permute-start.2 = (bf16[2,52,256]{2,1,0:T(8,128)(2,1)S(1)}, bf16[2,52,256]{2,1,0:T(8,128)(2,1)S(1)}, u32[]{:S(2)}, u32[]{:S(2)}) collective-permute-start(bf16[2,52,256]{2,1,0:T(8,128)(2,1)S(1)} %get-tuple-element.54), channel_id=1, source_target_pairs={{0,1},{1,2},{2,3},{3,4},{4,5},{5,6},{6,7},{8,9},{9,10},{10,11},{11... | collective-permute-start | bytes 159752 | tf_op jit(solution)/shard_map/ppermute | solution.py:15
  13.6 1.3 %collective-permute-start.3 = (bf16[2,52,256]{2,1,0:T(8,128)(2,1)S(1)}, bf16[2,52,256]{2,1,0:T(8,128)(2,1)S(1)}, u32[]{:S(2)}, u32[]{:S(2)}) collective-permute-start(bf16[2,52,256]{2,1,0:T(8,128)(2,1)S(1)} %get-tuple-element.55), channel_id=1, source_target_pairs={{1,0},{2,1},{3,2},{4,3},{5,4},{6,5},{7,6},{9,8},{10,9},{11,10},{12... | collective-permute-start | bytes 159752 | tf_op jit(solution)/shard_map/ppermute | solution.py:17
  14.9 7.2 %collective-permute-start.4 = (bf16[4,52,256]{2,1,0:T(8,128)(2,1)S(1)}, bf16[4,52,256]{2,1,0:T(8,128)(2,1)S(1)}, u32[]{:S(2)}, u32[]{:S(2)}) collective-permute-start(bf16[4,52,256]{2,1,0:T(8,128)(2,1)S(1)} %pad_maximum_fusion.1), channel_id=1, source_target_pairs={{0,128},{8,136},{16,144},{24,152},{32,160},{40,168},{48,176},{56,1... | collective-permute-start | bytes 319496 | tf_op jit(solution)/shard_map/ppermute | solution.py:27
  22.3 0.8 fusion.98
  23.1 0.7 fusion.93
  23.8 0.7 fusion.68
  24.7 0.8 pad_maximum_fusion
  25.5 0.6 slice_bitcast_fusion.2
  26.4 0.9 copy-done
  28.0 1.8 %convolution_select_fusion.1 = f32[50,8,7,128]{3,1,2,0:T(8,128)S(1)} fusion(bf16[3,3,128,128]{3,2,1,0:T(8,128)(2,1)S(1)} %copy-done.2, bf16[52,1,7,2,128]{4,2,3,0,1:T(8,128)(2,1)S(1)} %slice.394, bf16[52,1,8,7,128]{4,2,3,0,1:T(8,128)(2,1)S(1)} %copy.10, pred[8,7]{0,1:T(8,128)(4,1)S(1)} %copy-done.17), kind=kOutput, calls=%fused_computation.10 | convolution fusion | flops 828987392 | bytes 2660408 | tf_op jit(solution)/shard_map/conv_general_dilated | solution.py:108
  30.2 1.2 %reshape.174 = f32[50,1,56,128]{3,2,0,1:T(8,128)} reshape(f32[50,8,7,128]{3,2,1,0:T(8,128)S(1)} %copy.11) | data formatting | bytes 2867200 | tf_op jit(solution)/shard_map/conv_general_dilated | solution.py:108
  31.5 2.5 %fusion.49 = (bf16[50,50,128]{2,1,0:T(8,128)(2,1)S(1)}, f32[50,50,128]{2,1,0:T(8,128)S(1)}) fusion(bf16[52,52,256]{2,1,0:T(8,128)(2,1)} %copy-done, pred[50]{0:T(512)(128)(4,1)S(1)} %and_or_fusion, f32[128]{0:T(128)S(1)} %copy-done.15, f32[50,1,56,128]{3,2,0,1:T(8,128)} %reshape.174), kind=kLoop, calls=%fused_computation.74 | loop fusion | flops 3840000 | bytes 3840562 | tf_op jit(solution)/shard_map/jit(_where)/select_n | solution.py:121
  38.9 0.8 copy-done.5
  39.7 1.3 %dynamic-update-slice.21 = f32[1153,128]{1,0:T(8,128)} dynamic-update-slice(f32[1153,128]{1,0:T(8,128)} %copy-done.5, f32[1,128]{1,0:T(1,128)S(1)} %bitcast.208, s32[]{} %constant.220, s32[]{} %constant.211) | dynamic-update-slice | bytes 1028 | tf_op jit(solution)/shard_map/concatenate | solution.py:171
  40.9 1.8 %dynamic_slice.19 = f32[73792]{0:T(1024)} dynamic-slice(f32[147584]{0:T(1024)} %bitcast.204, s32[]{:T(128)S(6)} %select_n.114), dynamic_slice_sizes={73792} | dynamic-slice | bytes 590340 | tf_op jit(solution)/shard_map/dynamic_slice | solution.py:42
  42.8 0.8 collective-permute-start.5
  43.6 1.0 pad.10
  44.6 1.3 %reshape.177 = bf16[50,1,8,7,128]{4,3,2,0,1:T(8,128)(2,1)S(1)} reshape(bf16[50,1,56,128]{3,2,0,1:T(8,128)(2,1)} %pad.10) | data formatting | bytes 1433600 | tf_op jit(solution)/shard_map/conv_general_dilated | solution.py:124
  46.1 0.8 copy-done.3
  46.9 1.8 %convolution_select_fusion = f32[48,8,7,128]{3,1,2,0:T(8,128)S(1)} fusion(bf16[3,3,128,128]{3,2,1,0:T(8,128)(2,1)S(1)} %copy-done.3, bf16[50,1,7,2,128]{4,2,3,0,1:T(8,128)(2,1)S(1)} %slice.399, bf16[50,1,8,7,128]{4,2,3,0,1:T(8,128)(2,1)S(1)} %copy.13, pred[8,7]{0,1:T(8,128)(4,1)S(1)} %copy-done.16), kind=kOutput, calls=%fused_computation.5 | convolution fusion | flops 795832320 | bytes 2567224 | tf_op jit(solution)/shard_map/conv_general_dilated | solution.py:124
  50.7 0.6 copy-done.6
  51.3 1.1 %dynamic-slice_add_fusion = f32[73792]{0:T(1024)S(1)} fusion(f32[73792]{0:T(1024)} %collective-permute-done.5, f32[147584]{0:T(1024)S(1)} %bitcast.205, s32[]{:T(128)S(6)} %select_n.113), kind=kLoop, calls=%fused_computation.89 | loop fusion | flops 73792 | bytes 885508 | tf_op jit(solution)/shard_map/add | solution.py:44
  52.5 2.7 %collective-permute-start.6 = (f32[36896]{0:T(1024)S(1)}, f32[36896]{0:T(1024)S(1)}, u32[]{:S(2)}, u32[]{:S(2)}) collective-permute-start(f32[36896]{0:T(1024)S(1)} %dynamic_slice.21), channel_id=1, source_target_pairs={{0,1},{1,0},{2,3},{3,2},{4,5},{5,4},{6,7},{7,6},{8,9},{9,8},{10,11... | collective-permute-start | bytes 442760 | tf_op jit(solution)/shard_map/ppermute | solution.py:44
  55.3 4.2 %collective-permute-done.6 = f32[36896]{0:T(1024)S(1)} collective-permute-done((f32[36896]{0:T(1024)S(1)}, f32[36896]{0:T(1024)S(1)}, u32[]{:S(2)}, u32[]{:S(2)}) %collective-permute-start.6) | collective-permute-done | bytes 147616 | tf_op jit(solution)/shard_map/ppermute | solution.py:44
  59.7 1.3 %collective-permute-start.7 = (f32[18448]{0:T(1024)S(1)}, f32[18448]{0:T(1024)S(1)}, u32[]{:S(2)}, u32[]{:S(2)}) collective-permute-start(f32[18448]{0:T(1024)S(1)} %dynamic_slice.23), channel_id=1, source_target_pairs={{0,32},{8,40},{16,48},{24,56},{32,0},{40,8},{48,16},{56,24},{64,96... | collective-permute-start | bytes 221384 | tf_op jit(solution)/shard_map/ppermute | solution.py:44
  61.1 2.0 %collective-permute-done.7 = f32[18448]{0:T(1024)S(1)} collective-permute-done((f32[18448]{0:T(1024)S(1)}, f32[18448]{0:T(1024)S(1)}, u32[]{:S(2)}, u32[]{:S(2)}) %collective-permute-start.7) | collective-permute-done | bytes 73824 | tf_op jit(solution)/shard_map/ppermute | solution.py:44
  63.2 2.5 %collective-permute-start.8 = (f32[18448]{0:T(1024)S(1)}, f32[18448]{0:T(1024)S(1)}, u32[]{:S(2)}, u32[]{:S(2)}) collective-permute-start(f32[18448]{0:T(1024)S(1)} %dynamic-slice_add_fusion.2), channel_id=1, source_target_pairs={{0,2},{1,3},{2,0},{3,1},{4,6},{5,7},{6,4},{7,5},{8,10},{9,11},{10,... | collective-permute-start | bytes 221384 | tf_op jit(solution)/shard_map/ppermute | solution.py:47
  65.9 1.6 %collective-permute-done.8 = f32[18448]{0:T(1024)S(1)} collective-permute-done((f32[18448]{0:T(1024)S(1)}, f32[18448]{0:T(1024)S(1)}, u32[]{:S(2)}, u32[]{:S(2)}) %collective-permute-start.8) | collective-permute-done | bytes 73824 | tf_op jit(solution)/shard_map/ppermute | solution.py:47
  67.5 1.4 %collective-permute-start.9 = (f32[18448]{0:T(1024)S(1)}, f32[18448]{0:T(1024)S(1)}, u32[]{:S(2)}, u32[]{:S(2)}) collective-permute-start(f32[18448]{0:T(1024)S(1)} %add.222), channel_id=1, source_target_pairs={{0,16},{8,24},{16,0},{24,8},{32,48},{40,56},{48,32},{56,40},{64,80... | collective-permute-start | bytes 221384 | tf_op jit(solution)/shard_map/ppermute | solution.py:47
  69.0 3.3 %collective-permute-done.9 = f32[18448]{0:T(1024)S(1)} collective-permute-done((f32[18448]{0:T(1024)S(1)}, f32[18448]{0:T(1024)S(1)}, u32[]{:S(2)}, u32[]{:S(2)}) %collective-permute-start.9) | collective-permute-done | bytes 73824 | tf_op jit(solution)/shard_map/ppermute | solution.py:47
  72.4 2.3 %collective-permute-start.10 = (f32[18448]{0:T(1024)S(1)}, f32[18448]{0:T(1024)S(1)}, u32[]{:S(2)}, u32[]{:S(2)}) collective-permute-start(f32[18448]{0:T(1024)S(1)} %add.223), channel_id=1, source_target_pairs={{0,64},{8,72},{16,80},{24,88},{32,96},{40,104},{48,112},{56,120},{... | collective-permute-start | bytes 221384 | tf_op jit(solution)/shard_map/ppermute | solution.py:47
  75.9 0.7 collective-permute-done.10
  76.6 5.0 %collective-permute-start.11 = (f32[18448]{0:T(1024)S(1)}, f32[18448]{0:T(1024)S(1)}, u32[]{:S(2)}, u32[]{:S(2)}) collective-permute-start(f32[18448]{0:T(1024)S(1)} %add.224), channel_id=1, source_target_pairs={{0,192},{8,200},{16,208},{24,216},{32,224},{40,232},{48,240},{56,2... | collective-permute-start | bytes 221384 | tf_op jit(solution)/shard_map/ppermute | solution.py:47
  81.7 1.7 %collective-permute-done.11 = f32[18448]{0:T(1024)S(1)} collective-permute-done((f32[18448]{0:T(1024)S(1)}, f32[18448]{0:T(1024)S(1)}, u32[]{:S(2)}, u32[]{:S(2)}) %collective-permute-start.11) | collective-permute-done | bytes 73824 | tf_op jit(solution)/shard_map/ppermute | solution.py:47
  83.4 3.1 %collective-permute-start.12 = (f32[18448]{0:T(1024)S(1)}, f32[18448]{0:T(1024)S(1)}, u32[]{:S(2)}, u32[]{:S(2)}) collective-permute-start(f32[18448]{0:T(1024)S(1)} %add.225), channel_id=1, source_target_pairs={{0,6},{1,7},{2,4},{3,5},{4,2},{5,3},{6,0},{7,1},{8,14},{9,15},{10,... | collective-permute-start | bytes 221384 | tf_op jit(solution)/shard_map/ppermute | solution.py:47
  86.6 2.0 %collective-permute-done.12 = f32[18448]{0:T(1024)S(1)} collective-permute-done((f32[18448]{0:T(1024)S(1)}, f32[18448]{0:T(1024)S(1)}, u32[]{:S(2)}, u32[]{:S(2)}) %collective-permute-start.12) | collective-permute-done | bytes 73824 | tf_op jit(solution)/shard_map/ppermute | solution.py:47
  88.6 1.7 %collective-permute-start.13 = (f32[18448]{0:T(1024)S(1)}, f32[18448]{0:T(1024)S(1)}, u32[]{:S(2)}, u32[]{:S(2)}) collective-permute-start(f32[18448]{0:T(1024)S(1)} %add.226), channel_id=1, source_target_pairs={{0,32},{8,40},{16,48},{24,56},{32,0},{40,8},{48,16},{56,24},{64,96... | collective-permute-start | bytes 221384 | tf_op jit(solution)/shard_map/ppermute | solution.py:51
  90.4 1.7 %collective-permute-done.13 = f32[18448]{0:T(1024)S(1)} collective-permute-done((f32[18448]{0:T(1024)S(1)}, f32[18448]{0:T(1024)S(1)}, u32[]{:S(2)}, u32[]{:S(2)}) %collective-permute-start.13) | collective-permute-done | bytes 73824 | tf_op jit(solution)/shard_map/ppermute | solution.py:51
  92.2 0.8 collective-permute-start.14
  93.1 0.9 convert_element_type.32
  94.0 2.3 %collective-permute-done.14 = f32[36896]{0:T(1024)S(1)} collective-permute-done((f32[36896]{0:T(1024)S(1)}, f32[36896]{0:T(1024)S(1)}, u32[]{:S(2)}, u32[]{:S(2)}) %collective-permute-start.14) | collective-permute-done | bytes 147616 | tf_op jit(solution)/shard_map/ppermute | solution.py:51
  96.5 9.5 %collective-permute-start.15 = (f32[73792]{0:T(1024)S(1)}, f32[73792]{0:T(1024)S(1)}, u32[]{:S(2)}, u32[]{:S(2)}) collective-permute-start(f32[73792]{0:T(1024)S(1)} %maximum_select_fusion.1), channel_id=1, source_target_pairs={{0,8},{8,0},{16,24},{24,16},{32,40},{40,32},{48,56},{56,48},{64,72... | collective-permute-start | bytes 885512 | tf_op jit(solution)/shard_map/ppermute | solution.py:51
  106.0 1.2 %fusion.3 = bf16[48,48,128]{2,1,0:T(8,128)(2,1)} fusion(f32[50,50,128]{2,1,0:T(8,128)S(1)} %add_divide_fusion, f32[50,50,128]{2,1,0:T(8,128)S(1)} %get-tuple-element.53), kind=kLoop, calls=%fused_computation.12 | loop fusion | flops 589824 | bytes 2949120 | tf_op jit(solution)/shard_map/convert
  108.0 0.9 slice_multiply_fusion.1
  (103 shorter events, 12.5 us)
Async XLA Ops:
  0.6 1.2 %copy-start.7 = (bf16[48,48,128]{2,1,0:T(8,128)(2,1)S(1)}, bf16[48,48,128]{2,1,0:T(8,128)(2,1)}, u32[]{:S(2)}) copy-start(bf16[48,48,128]{2,1,0:T(8,128)(2,1)} %param.15) | copy-start | bytes 1769476
  1.9 20.3 %copy-start.2 = (bf16[3,3,128,128]{3,2,1,0:T(8,128)(2,1)S(1)}, bf16[3,3,128,128]{3,2,1,0:T(8,128)(2,1)}, u32[]{:S(2)}) copy-start(bf16[3,3,128,128]{3,2,1,0:T(8,128)(2,1)} %param.13) | copy-start | bytes 884740
  2.1 5.4 %collective-permute-start = (bf16[48,2,256]{2,1,0:T(2,128)(2,1)S(1)}, bf16[48,2,256]{2,1,0:T(2,128)(2,1)S(1)}, u32[]{:S(2)}, u32[]{:S(2)}) collective-permute-start(bf16[48,2,256]{2,1,0:T(2,128)(2,1)S(1)} %get-tuple-element.56), channel_id=1, source_target_pairs={{0,8},{8,16},{16,24},{24,32},{32,40},{40,48},{48,56},{56,64},{64,7... | collective-permute-start | bytes 147464 | tf_op jit(solution)/shard_map/ppermute | solution.py:15
  6.3 5.0 %collective-permute-start.1 = (bf16[48,2,256]{2,1,0:T(2,128)(2,1)S(1)}, bf16[48,2,256]{2,1,0:T(2,128)(2,1)S(1)}, u32[]{:S(2)}, u32[]{:S(2)}) collective-permute-start(bf16[48,2,256]{2,1,0:T(2,128)(2,1)S(1)} %get-tuple-element.57), channel_id=1, source_target_pairs={{8,0},{16,8},{24,16},{32,24},{40,32},{48,40},{56,48},{64,56},{72,6... | collective-permute-start | bytes 147464 | tf_op jit(solution)/shard_map/ppermute | solution.py:17
  11.4 13.3 %collective-permute-start.2 = (bf16[2,52,256]{2,1,0:T(8,128)(2,1)S(1)}, bf16[2,52,256]{2,1,0:T(8,128)(2,1)S(1)}, u32[]{:S(2)}, u32[]{:S(2)}) collective-permute-start(bf16[2,52,256]{2,1,0:T(8,128)(2,1)S(1)} %get-tuple-element.54), channel_id=1, source_target_pairs={{0,1},{1,2},{2,3},{3,4},{4,5},{5,6},{6,7},{8,9},{9,10},{10,11},{11... | collective-permute-start | bytes 159752 | tf_op jit(solution)/shard_map/ppermute | solution.py:15
  13.6 11.1 %collective-permute-start.3 = (bf16[2,52,256]{2,1,0:T(8,128)(2,1)S(1)}, bf16[2,52,256]{2,1,0:T(8,128)(2,1)S(1)}, u32[]{:S(2)}, u32[]{:S(2)}) collective-permute-start(bf16[2,52,256]{2,1,0:T(8,128)(2,1)S(1)} %get-tuple-element.55), channel_id=1, source_target_pairs={{1,0},{2,1},{3,2},{4,3},{5,4},{6,5},{7,6},{9,8},{10,9},{11,10},{12... | collective-permute-start | bytes 159752 | tf_op jit(solution)/shard_map/ppermute | solution.py:17
  14.9 10.5 %collective-permute-start.4 = (bf16[4,52,256]{2,1,0:T(8,128)(2,1)S(1)}, bf16[4,52,256]{2,1,0:T(8,128)(2,1)S(1)}, u32[]{:S(2)}, u32[]{:S(2)}) collective-permute-start(bf16[4,52,256]{2,1,0:T(8,128)(2,1)S(1)} %pad_maximum_fusion.1), channel_id=1, source_target_pairs={{0,128},{8,136},{16,144},{24,152},{32,160},{40,168},{48,176},{56,1... | collective-permute-start | bytes 319496 | tf_op jit(solution)/shard_map/ppermute | solution.py:27
  25.5 0.9 copy-start.8
  26.2 1.2 %copy-start = (bf16[52,52,256]{2,1,0:T(8,128)(2,1)}, bf16[52,52,256]{2,1,0:T(8,128)(2,1)S(1)}, u32[]{:S(2)}) copy-start(bf16[52,52,256]{2,1,0:T(8,128)(2,1)S(1)} %get-tuple-element.60) | copy-start | bytes 4153348
  27.3 0.7 copy-start.17
  30.2 1.3 %copy-start.15 = (f32[128]{0:T(128)S(1)}, f32[128]{0:T(128)}, u32[]{:S(2)}) copy-start(f32[128]{0:T(128)} %param.14) | copy-start | bytes 1540
  31.5 2.8 %copy-start.1 = (bf16[52,52,256]{2,1,0:T(8,128)(2,1)S(1)}, bf16[52,52,256]{2,1,0:T(8,128)(2,1)}, u32[]{:S(2)}) copy-start(bf16[52,52,256]{2,1,0:T(8,128)(2,1)} %copy-done) | copy-start | bytes 4153348
  38.8 0.8 copy-start.5
  42.8 7.9 %collective-permute-start.5 = (f32[73792]{0:T(1024)}, f32[73792]{0:T(1024)}, u32[]{:S(2)}, u32[]{:S(2)}) collective-permute-start(f32[73792]{0:T(1024)} %dynamic_slice.19), channel_id=1, source_target_pairs={{0,8},{8,0},{16,24},{24,16},{32,40},{40,32},{48,56},{56,48},{64,72... | collective-permute-start | bytes 885512 | tf_op jit(solution)/shard_map/ppermute | solution.py:44
  44.6 1.5 %copy-start.16 = (pred[8,7]{0,1:T(8,128)(4,1)S(1)}, pred[8,7]{0,1:T(8,128)(4,1)}, u32[]{:S(2)}) copy-start(pred[8,7]{0,1:T(8,128)(4,1)} %constant.204) | copy-start | bytes 172
  45.9 1.0 copy-start.3
  46.9 1.8 %copy-start.9 = (bf16[4,52,256]{2,1,0:T(8,128)(2,1)S(1)}, bf16[4,52,256]{2,1,0:T(8,128)(2,1)}, u32[]{:S(2)}) copy-start(bf16[4,52,256]{2,1,0:T(8,128)(2,1)} %copy-done.8) | copy-start | bytes 319492
  46.9 3.1 %copy-start.11 = (f32[50,128]{1,0:T(8,128)S(1)}, f32[50,128]{1,0:T(8,128)}, u32[]{:S(2)}) copy-start(f32[50,128]{1,0:T(8,128)} %fusion.68) | copy-start | bytes 76804
  46.9 3.1 %copy-start.14 = (bf16[52,256]{1,0:T(8,128)(2,1)S(1)}, bf16[52,256]{1,0:T(8,128)(2,1)}, u32[]{:S(2)}) copy-start(bf16[52,256]{1,0:T(8,128)(2,1)} %get-tuple-element.58) | copy-start | bytes 79876
  48.7 26.0 %copy-start.4 = (f32[48,8,7,128]{3,1,2,0:T(8,128)}, f32[48,8,7,128]{3,1,2,0:T(8,128)S(1)}, u32[]{:S(2)}) copy-start(f32[48,8,7,128]{3,1,2,0:T(8,128)S(1)} %convolution_select_fusion) | copy-start | bytes 4128772
  50.2 1.1 copy-start.6
  50.6 15.1 %copy-start.10 = (f32[50,128]{1,0:T(8,128)S(1)}, f32[50,128]{1,0:T(8,128)}, u32[]{:S(2)}) copy-start(f32[50,128]{1,0:T(8,128)} %fusion.93) | copy-start | bytes 76804
  50.6 15.1 %copy-start.12 = (f32[50,128]{1,0:T(8,128)S(1)}, f32[50,128]{1,0:T(8,128)}, u32[]{:S(2)}) copy-start(f32[50,128]{1,0:T(8,128)} %fusion.98) | copy-start | bytes 76804
  50.6 15.1 %copy-start.13 = (bf16[52,256]{1,0:T(8,128)(2,1)S(1)}, bf16[52,256]{1,0:T(8,128)(2,1)}, u32[]{:S(2)}) copy-start(bf16[52,256]{1,0:T(8,128)(2,1)} %get-tuple-element.59) | copy-start | bytes 79876
  52.5 7.0 %collective-permute-start.6 = (f32[36896]{0:T(1024)S(1)}, f32[36896]{0:T(1024)S(1)}, u32[]{:S(2)}, u32[]{:S(2)}) collective-permute-start(f32[36896]{0:T(1024)S(1)} %dynamic_slice.21), channel_id=1, source_target_pairs={{0,1},{1,0},{2,3},{3,2},{4,5},{5,4},{6,7},{7,6},{8,9},{9,8},{10,11... | collective-permute-start | bytes 442760 | tf_op jit(solution)/shard_map/ppermute | solution.py:44
  59.7 3.3 %collective-permute-start.7 = (f32[18448]{0:T(1024)S(1)}, f32[18448]{0:T(1024)S(1)}, u32[]{:S(2)}, u32[]{:S(2)}) collective-permute-start(f32[18448]{0:T(1024)S(1)} %dynamic_slice.23), channel_id=1, source_target_pairs={{0,32},{8,40},{16,48},{24,56},{32,0},{40,8},{48,16},{56,24},{64,96... | collective-permute-start | bytes 221384 | tf_op jit(solution)/shard_map/ppermute | solution.py:44
  63.2 4.3 %collective-permute-start.8 = (f32[18448]{0:T(1024)S(1)}, f32[18448]{0:T(1024)S(1)}, u32[]{:S(2)}, u32[]{:S(2)}) collective-permute-start(f32[18448]{0:T(1024)S(1)} %dynamic-slice_add_fusion.2), channel_id=1, source_target_pairs={{0,2},{1,3},{2,0},{3,1},{4,6},{5,7},{6,4},{7,5},{8,10},{9,11},{10,... | collective-permute-start | bytes 221384 | tf_op jit(solution)/shard_map/ppermute | solution.py:47
  67.5 4.8 %collective-permute-start.9 = (f32[18448]{0:T(1024)S(1)}, f32[18448]{0:T(1024)S(1)}, u32[]{:S(2)}, u32[]{:S(2)}) collective-permute-start(f32[18448]{0:T(1024)S(1)} %add.222), channel_id=1, source_target_pairs={{0,16},{8,24},{16,0},{24,8},{32,48},{40,56},{48,32},{56,40},{64,80... | collective-permute-start | bytes 221384 | tf_op jit(solution)/shard_map/ppermute | solution.py:47
  72.4 4.2 %collective-permute-start.10 = (f32[18448]{0:T(1024)S(1)}, f32[18448]{0:T(1024)S(1)}, u32[]{:S(2)}, u32[]{:S(2)}) collective-permute-start(f32[18448]{0:T(1024)S(1)} %add.223), channel_id=1, source_target_pairs={{0,64},{8,72},{16,80},{24,88},{32,96},{40,104},{48,112},{56,120},{... | collective-permute-start | bytes 221384 | tf_op jit(solution)/shard_map/ppermute | solution.py:47
  75.1 0.7 slice-start
  76.6 6.8 %collective-permute-start.11 = (f32[18448]{0:T(1024)S(1)}, f32[18448]{0:T(1024)S(1)}, u32[]{:S(2)}, u32[]{:S(2)}) collective-permute-start(f32[18448]{0:T(1024)S(1)} %add.224), channel_id=1, source_target_pairs={{0,192},{8,200},{16,208},{24,216},{32,224},{40,232},{48,240},{56,2... | collective-permute-start | bytes 221384 | tf_op jit(solution)/shard_map/ppermute | solution.py:47
  83.4 5.1 %collective-permute-start.12 = (f32[18448]{0:T(1024)S(1)}, f32[18448]{0:T(1024)S(1)}, u32[]{:S(2)}, u32[]{:S(2)}) collective-permute-start(f32[18448]{0:T(1024)S(1)} %add.225), channel_id=1, source_target_pairs={{0,6},{1,7},{2,4},{3,5},{4,2},{5,3},{6,0},{7,1},{8,14},{9,15},{10,... | collective-permute-start | bytes 221384 | tf_op jit(solution)/shard_map/ppermute | solution.py:47
  88.6 3.5 %collective-permute-start.13 = (f32[18448]{0:T(1024)S(1)}, f32[18448]{0:T(1024)S(1)}, u32[]{:S(2)}, u32[]{:S(2)}) collective-permute-start(f32[18448]{0:T(1024)S(1)} %add.226), channel_id=1, source_target_pairs={{0,32},{8,40},{16,48},{24,56},{32,0},{40,8},{48,16},{56,24},{64,96... | collective-permute-start | bytes 221384 | tf_op jit(solution)/shard_map/ppermute | solution.py:51
  92.2 4.1 %collective-permute-start.14 = (f32[36896]{0:T(1024)S(1)}, f32[36896]{0:T(1024)S(1)}, u32[]{:S(2)}, u32[]{:S(2)}) collective-permute-start(f32[36896]{0:T(1024)S(1)} %maximum_select_fusion.2), channel_id=1, source_target_pairs={{0,1},{1,0},{2,3},{3,2},{4,5},{5,4},{6,7},{7,6},{8,9},{9,8},{10,11... | collective-permute-start | bytes 442760 | tf_op jit(solution)/shard_map/ppermute | solution.py:51
  96.5 10.8 %collective-permute-start.15 = (f32[73792]{0:T(1024)S(1)}, f32[73792]{0:T(1024)S(1)}, u32[]{:S(2)}, u32[]{:S(2)}) collective-permute-start(f32[73792]{0:T(1024)S(1)} %maximum_select_fusion.1), channel_id=1, source_target_pairs={{0,8},{8,0},{16,24},{24,16},{32,40},{40,32},{48,56},{56,48},{64,72... | collective-permute-start | bytes 885512 | tf_op jit(solution)/shard_map/ppermute | solution.py:51

commit v7 on v6

--- a/solution.py
+++ b/solution.py
@@ -27,7 +27,7 @@
     return lax.ppermute(value, axis, pairs)
 
 
-def butterfly_sum(value, scatter, double):
+def butterfly_sum(value, scatter, double, rider):
     shape = value.shape
     data = value.reshape(-1)
     parts = 2 ** len(scatter)
@@ -43,6 +43,7 @@
         keep = lax.dynamic_slice_in_dim(data, bit * half, half)
         data = keep + lax.ppermute(send, axis, pairs)
         history.append((axis, step, bit))
+    data, rider = lax.optimization_barrier((data, rider))
     for axis, pairs in double:
         data = data + lax.ppermute(data, axis, pairs)
     for axis, step, bit in reversed(history):
@@ -50,7 +51,7 @@
         pairs = [(i, i ^ step) for i in range(count)]
         other = lax.ppermute(data, axis, pairs)
         data = jnp.where(bit == 0, jnp.concatenate([data, other]), jnp.concatenate([other, data]))
-    return data[: data.shape[0] - pad].reshape(shape)
+    return data[: data.shape[0] - pad].reshape(shape), rider
 
 
 def pairing_order(mesh_axes):
@@ -120,6 +121,24 @@
     outside = ((line == 0) & (band == 0)) | ((line == rows + 1) & (band == bands - 1))
     grad_ext = jnp.where(outside, jnp.zeros_like(grad_ext), grad_ext)
     pre_grad = grad_ext[1:-1, 1:-1].reshape(rows * cols, chans)
+    taps = []
+    for tap_a in range(3):
+        for tap_b in range(3):
+            window = padded[tap_a + 1 : tap_a + 1 + rows, tap_b + 1 : tap_b + 1 + cols].reshape(rows * cols, chans)
+            taps.append(
+                lax.dot_general(
+                    window, pre_grad, (((0,), (0,)), ((), ())), preferred_element_type=jnp.float32
+                )
+            )
+    kernel_terms = jnp.concatenate(taps, axis=0)
+    bias_terms = jnp.sum(pre_grad.astype(jnp.float32), axis=0)[None, :]
+    order = pairing_order(("lon", "lat"))
+    sums, (grad_ext, wide_ends, far) = butterfly_sum(
+        jnp.concatenate([kernel_terms, bias_terms], axis=0),
+        order[:3],
+        doubling_plan(order[3:]),
+        (grad_ext, jnp.stack([wide[0], wide[-1]]), far),
+    )
     flipped = jnp.transpose(weight[::-1, ::-1], (0, 1, 3, 2))
     cell_grad = lax.conv_general_dilated(
         grad_ext[None],
@@ -131,8 +150,8 @@
     )[0]
     polar = []
     for window, cot_line, tap_a in (
-        (jnp.stack([wide[0], far[0], far[1]]), far[0], 0),
-        (jnp.stack([far[2], far[3], wide[-1]]), far[3], 2),
+        (jnp.stack([wide_ends[0], far[0], far[1]]), far[0], 0),
+        (jnp.stack([far[2], far[3], wide_ends[1]]), far[3], 2),
     ):
         pre_line = bias + jnp.zeros((cols + 2, chans), jnp.float32)
         for tap_a_in in range(3):
@@ -156,19 +175,6 @@
     cell_grad = cell_grad.at[0].add(jnp.where(band == 0, polar[0], 0.0))
     cell_grad = cell_grad.at[-1].add(jnp.where(band == bands - 1, polar[1], 0.0))
     input_grad = cell_grad.astype(jnp.bfloat16)
-    taps = []
-    for tap_a in range(3):
-        for tap_b in range(3):
-            window = padded[tap_a + 1 : tap_a + 1 + rows, tap_b + 1 : tap_b + 1 + cols].reshape(rows * cols, chans)
-            taps.append(
-                lax.dot_general(
-                    window, pre_grad, (((0,), (0,)), ((), ())), preferred_element_type=jnp.float32
-                )
-            )
-    kernel_terms = jnp.concatenate(taps, axis=0)
-    bias_terms = jnp.sum(pre_grad.astype(jnp.float32), axis=0)[None, :]
-    order = pairing_order(("lon", "lat"))
-    sums = butterfly_sum(jnp.concatenate([kernel_terms, bias_terms], axis=0), order[:3], doubling_plan(order[3:]))
     kernel_sum, bias_sum = sums[:-1], sums[-1:]
     total_cells = rows * cols * lax.axis_size("lon") * lax.axis_size("lat")
     scale = 1.0 / jnp.sqrt(jnp.float32(total_cells))

time: 109 us -> 107 us (0.982)
  local copies, waits for them, and re-layouts: 14 us -> 10.2 us
  waiting for transfers between devices: 24.4 us -> 28 us
  matrix products: 13.3 us -> 11.5 us
    ppermute x3, waiting for transfers between devices: 4.02 us -> 6.9 us  [butterfly_sum(): other = lax.ppermute(data, axis, pairs)]
    ppermute x3, starting transfers between devices: 12 us -> 9.59 us  [butterfly_sum(): other = lax.ppermute(data, axis, pairs)]
    ppermute x1, waiting for transfers between devices: 0.01 us -> 1.98 us  [from_behind(): return lax.ppermute(value, axis, pairs)]
    ppermute x3, starting transfers between devices: 4.76 us -> 6.72 us  [butterfly_sum(): data = keep + lax.ppermute(send, axis, pairs)]
    dot_general x18, matrix products: 4.38 us -> 2.56 us  [shards(): jnp.dot(window[tap_a_in, tap_b_in:tap_b_in + cols + 2, :chans], weight[ta...]
    conv_general_dilated x8, local copies, waits for them, and re-layouts: 2.24 us -> 1.12 us  [shards(): lax.conv_general_dilated(grad_ext[None], flipped, (1, 1), 'VALID', dimens...]
    unnamed x39 -> x23, local copies, waits for them, and re-layouts: 5.35 us -> 4.24 us
  transfers between devices with their start and end apart: 16 -> 16, of which waited for: 12 -> 13; matrix products, arithmetic and copies ran while one was open for 12% -> 5% of each run, Pallas kernels for 0% -> 0%
where the time goes in v7:
time: 107 us
  starting transfers between devices  46.3 us (43%)
  waiting for transfers between devices  28 us (26%)
  matrix products  11.5 us (11%)
  local copies, waits for them, and re-layouts  10.2 us (10%)
  other arithmetic  9.62 us (9%)
  between operations  1.12 us (1%)
    ppermute x5, starting transfers between devices, butterfly_sum(): data = data + lax.ppermute(data, axis, pairs)  15.1 us
    ppermute x3, starting transfers between devices, butterfly_sum(): other = lax.ppermute(data, axis, pairs)  9.59 us
    ppermute x5, waiting for transfers between devices, butterfly_sum(): data = data + lax.ppermute(data, axis, pairs)  8.71 us
    ppermute x1, starting transfers between devices, from_behind(): return lax.ppermute(value, axis, pairs)  7.21 us
    ppermute x3, waiting for transfers between devices, butterfly_sum(): other = lax.ppermute(data, axis, pairs)  6.9 us
    ppermute x3, starting transfers between devices, butterfly_sum(): data = keep + lax.ppermute(send, axis, pairs)  6.72 us
    ppermute x2, starting transfers between devices, extended(): lax.ppermute(tail, axis, [(i, (i + 1) % count) for i in range(ends)])  6.42 us
    ppermute x3, waiting for transfers between devices, butterfly_sum(): data = keep + lax.ppermute(send, axis, pairs)  5.45 us
  transfers between devices with their start and end apart: 16, of which 13 were waited for; matrix products, arithmetic and copies ran while one was open for 5% of the time, Pallas kernels for 0%

profile of v7, /device:TPU:1, one launch (start us, length us, event | category | flops | bytes accessed | tf_op | source)
XLA Modules:
  0.0 106.8 jit_solution(1270949885058461455)
XLA Ops:
  0.6 1.2 %constant_dynamic-update-slice_fusion.1 = bf16[48,48,256]{2,1,0:T(8,128)(2,1)S(1)} fusion(bf16[48,48,128]{2,1,0:T(8,128)(2,1)} %param.12), kind=kLoop, calls=%fused_computation.169 | loop fusion | bytes 1179648
  2.1 4.2 %collective-permute-start = (bf16[48,2,256]{2,1,0:T(2,128)(2,1)S(1)}, bf16[48,2,256]{2,1,0:T(2,128)(2,1)S(1)}, u32[]{:S(2)}, u32[]{:S(2)}) collective-permute-start(bf16[48,2,256]{2,1,0:T(2,128)(2,1)S(1)} %get-tuple-element.65), channel_id=1, source_target_pairs={{0,8},{8,16},{16,24},{24,32},{32,40},{40,48},{48,56},{56,64},{64,7... | collective-permute-start | bytes 147464 | tf_op jit(solution)/shard_map/ppermute | solution.py:15
  6.3 1.1 %collective-permute-done = bf16[48,2,256]{2,1,0:T(2,128)(2,1)S(1)} collective-permute-done((bf16[48,2,256]{2,1,0:T(2,128)(2,1)S(1)}, bf16[48,2,256]{2,1,0:T(2,128)(2,1)S(1)}, u32[]{:S(2)}, u32[]{:S(2)}) %collective-permute-start) | collective-permute-done | bytes 49184 | tf_op jit(solution)/shard_map/ppermute | solution.py:15
  7.5 3.8 %collective-permute-done.1 = bf16[48,2,256]{2,1,0:T(2,128)(2,1)S(1)} collective-permute-done((bf16[48,2,256]{2,1,0:T(2,128)(2,1)S(1)}, bf16[48,2,256]{2,1,0:T(2,128)(2,1)S(1)}, u32[]{:S(2)}, u32[]{:S(2)}) %collective-permute-start.1) | collective-permute-done | bytes 49184 | tf_op jit(solution)/shard_map/ppermute | solution.py:17
  11.3 0.7 fusion.53
  12.0 2.2 %collective-permute-start.2 = (bf16[2,52,256]{2,1,0:T(8,128)(2,1)S(1)}, bf16[2,52,256]{2,1,0:T(8,128)(2,1)S(1)}, u32[]{:S(2)}, u32[]{:S(2)}) collective-permute-start(bf16[2,52,256]{2,1,0:T(8,128)(2,1)S(1)} %get-tuple-element.69), channel_id=1, source_target_pairs={{0,1},{1,2},{2,3},{3,4},{4,5},{5,6},{6,7},{8,9},{9,10},{10,11},{11... | collective-permute-start | bytes 159752 | tf_op jit(solution)/shard_map/ppermute | solution.py:15
  14.2 1.3 %collective-permute-start.3 = (bf16[2,52,256]{2,1,0:T(8,128)(2,1)S(1)}, bf16[2,52,256]{2,1,0:T(8,128)(2,1)S(1)}, u32[]{:S(2)}, u32[]{:S(2)}) collective-permute-start(bf16[2,52,256]{2,1,0:T(8,128)(2,1)S(1)} %get-tuple-element.70), channel_id=1, source_target_pairs={{1,0},{2,1},{3,2},{4,3},{5,4},{6,5},{7,6},{9,8},{10,9},{11,10},{12... | collective-permute-start | bytes 159752 | tf_op jit(solution)/shard_map/ppermute | solution.py:17
  15.6 7.2 %collective-permute-start.4 = (bf16[4,52,256]{2,1,0:T(8,128)(2,1)S(1)}, bf16[4,52,256]{2,1,0:T(8,128)(2,1)S(1)}, u32[]{:S(2)}, u32[]{:S(2)}) collective-permute-start(bf16[4,52,256]{2,1,0:T(8,128)(2,1)S(1)} %pad_maximum_fusion.1), channel_id=1, source_target_pairs={{0,128},{8,136},{16,144},{24,152},{32,160},{40,168},{48,176},{56,1... | collective-permute-start | bytes 319496 | tf_op jit(solution)/shard_map/ppermute | solution.py:27
  22.8 0.8 pad_maximum_fusion
  23.6 2.0 %collective-permute-done.4 = bf16[4,52,256]{2,1,0:T(8,128)(2,1)S(1)} collective-permute-done((bf16[4,52,256]{2,1,0:T(8,128)(2,1)S(1)}, bf16[4,52,256]{2,1,0:T(8,128)(2,1)S(1)}, u32[]{:S(2)}, u32[]{:S(2)}) %collective-permute-start.4) | collective-permute-done | bytes 106528 | tf_op jit(solution)/shard_map/ppermute | solution.py:27
  26.1 0.7 copy-done.2
  26.8 1.8 %convolution_select_fusion.1 = f32[50,8,7,128]{3,1,2,0:T(8,128)S(1)} fusion(bf16[3,3,128,128]{3,2,1,0:T(8,128)(2,1)S(1)} %copy-done.2, bf16[52,1,7,2,128]{4,2,3,0,1:T(8,128)(2,1)S(1)} %slice.404, bf16[52,1,8,7,128]{4,2,3,0,1:T(8,128)(2,1)S(1)} %copy.12, pred[8,7]{0,1:T(8,128)(4,1)S(1)} %copy-done.9), kind=kOutput, calls=%fused_computation.10 | convolution fusion | flops 828987392 | bytes 2660408 | tf_op jit(solution)/shard_map/conv_general_dilated | solution.py:109
  29.0 1.3 %reshape.174 = f32[50,1,56,128]{3,2,0,1:T(8,128)} reshape(f32[50,8,7,128]{3,2,1,0:T(8,128)S(1)} %copy.13) | data formatting | bytes 2867200 | tf_op jit(solution)/shard_map/conv_general_dilated | solution.py:109
  30.3 2.2 %fusion.33 = (bf16[50,50,128]{2,1,0:T(8,128)(2,1)S(1)}, f32[50,50,128]{2,1,0:T(8,128)S(1)}) fusion(bf16[52,52,256]{2,1,0:T(8,128)(2,1)S(1)} %fusion.88, pred[50]{0:T(512)(128)(4,1)S(1)} %and_or_fusion, f32[128]{0:T(128)S(1)} %copy-done.7, f32[50,1,56,128]{3,2,0,1:T(8,128)} %reshape.174), kind=kLoop, calls=%fused_computation.74 | loop fusion | flops 3840000 | bytes 3840562 | tf_op jit(solution)/shard_map/jit(_where)/select_n | solution.py:122
  33.8 0.5 fusion.10
  34.3 0.5 fusion.9
  34.8 0.5 fusion.8
  35.3 0.5 fusion.7
  36.9 0.5 fusion.4
  37.4 0.9 copy-done.4
  38.2 1.3 %dynamic-update-slice.21 = f32[1153,128]{1,0:T(8,128)} dynamic-update-slice(f32[1153,128]{1,0:T(8,128)} %copy-done.4, f32[1,128]{1,0:T(1,128)S(1)} %bitcast.208, s32[]{} %constant.222, s32[]{} %constant.213) | dynamic-update-slice | bytes 1028 | tf_op jit(solution)/shard_map/concatenate | solution.py:137
  39.5 1.1 %dynamic_slice.19 = f32[73792]{0:T(1024)S(1)} dynamic-slice(f32[147584]{0:T(1024)} %bitcast.204, s32[]{:T(128)S(6)} %select_n.104), dynamic_slice_sizes={73792} | dynamic-slice | bytes 590340 | tf_op jit(solution)/shard_map/dynamic_slice | solution.py:42
  40.6 1.7 %collective-permute-start.5 = (f32[73792]{0:T(1024)S(1)}, f32[73792]{0:T(1024)S(1)}, u32[]{:S(2)}, u32[]{:S(2)}) collective-permute-start(f32[73792]{0:T(1024)S(1)} %dynamic_slice.19), channel_id=1, source_target_pairs={{0,8},{8,0},{16,24},{24,16},{32,40},{40,32},{48,56},{56,48},{64,72... | collective-permute-start | bytes 885512 | tf_op jit(solution)/shard_map/ppermute | solution.py:44
  42.3 1.2 %collective-permute-done.5 = f32[73792]{0:T(1024)S(1)} collective-permute-done((f32[73792]{0:T(1024)S(1)}, f32[73792]{0:T(1024)S(1)}, u32[]{:S(2)}, u32[]{:S(2)}) %collective-permute-start.5) | collective-permute-done | bytes 295200 | tf_op jit(solution)/shard_map/ppermute | solution.py:44
  43.6 1.1 %dynamic-slice_add_fusion = f32[73792]{0:T(1024)S(1)} fusion(f32[73792]{0:T(1024)S(1)} %collective-permute-done.5, f32[147584]{0:T(1024)} %bitcast.205, s32[]{:T(128)S(6)} %select_n.103), kind=kLoop, calls=%fused_computation.89 | loop fusion | flops 73792 | bytes 885508 | tf_op jit(solution)/shard_map/add | solution.py:44
  44.8 2.7 %collective-permute-start.6 = (f32[36896]{0:T(1024)S(1)}, f32[36896]{0:T(1024)S(1)}, u32[]{:S(2)}, u32[]{:S(2)}) collective-permute-start(f32[36896]{0:T(1024)S(1)} %dynamic_slice.21), channel_id=1, source_target_pairs={{0,1},{1,0},{2,3},{3,2},{4,5},{5,4},{6,7},{7,6},{8,9},{9,8},{10,11... | collective-permute-start | bytes 442760 | tf_op jit(solution)/shard_map/ppermute | solution.py:44
  47.8 3.6 %collective-permute-done.6 = f32[36896]{0:T(1024)S(1)} collective-permute-done((f32[36896]{0:T(1024)S(1)}, f32[36896]{0:T(1024)S(1)}, u32[]{:S(2)}, u32[]{:S(2)}) %collective-permute-start.6) | collective-permute-done | bytes 147616 | tf_op jit(solution)/shard_map/ppermute | solution.py:44
  51.6 2.3 %collective-permute-start.7 = (f32[18448]{0:T(1024)S(1)}, f32[18448]{0:T(1024)S(1)}, u32[]{:S(2)}, u32[]{:S(2)}) collective-permute-start(f32[18448]{0:T(1024)S(1)} %dynamic_slice.23), channel_id=1, source_target_pairs={{0,32},{8,40},{16,48},{24,56},{32,0},{40,8},{48,16},{56,24},{64,96... | collective-permute-start | bytes 221384 | tf_op jit(solution)/shard_map/ppermute | solution.py:44
  54.0 1.1 %fusion.3 = bf16[48,48,128]{2,1,0:T(8,128)(2,1)} fusion(f32[50,50,128]{2,1,0:T(8,128)S(1)} %add_divide_fusion, f32[50,50,128]{2,1,0:T(8,128)S(1)} %get-tuple-element.64), kind=kLoop, calls=%fused_computation.12 | loop fusion | flops 589824 | bytes 2949120 | tf_op jit(solution)/shard_map/convert
  55.1 0.7 collective-permute-done.7
  56.8 1.8 %convolution_select_fusion = f32[48,8,7,128]{3,1,2,0:T(8,128)S(1)} fusion(bf16[3,3,128,128]{3,2,1,0:T(8,128)(2,1)S(1)} %copy-done.2, bf16[50,1,7,2,128]{4,2,3,0,1:T(8,128)(2,1)S(1)} %slice.419, bf16[50,1,8,7,128]{4,2,3,0,1:T(8,128)(2,1)S(1)} %copy.15, pred[8,7]{0,1:T(8,128)(4,1)S(1)} %copy-done.8), kind=kOutput, calls=%fused_computation.5 | convolution fusion | flops 795832320 | bytes 2567224 | tf_op jit(solution)/shard_map/conv_general_dilated | solution.py:143
  58.8 0.6 copy-done.6
  61.4 2.2 %collective-permute-start.8 = (f32[18448]{0:T(1024)S(1)}, f32[18448]{0:T(1024)S(1)}, u32[]{:S(2)}, u32[]{:S(2)}) collective-permute-start(f32[18448]{0:T(1024)S(1)} %dynamic-slice_add_fusion.2), channel_id=1, source_target_pairs={{0,2},{1,3},{2,0},{3,1},{4,6},{5,7},{6,4},{7,5},{8,10},{9,11},{10,... | collective-permute-start | bytes 221384 | tf_op jit(solution)/shard_map/ppermute | solution.py:48
  64.7 0.6 collective-permute-done.8
  65.4 2.0 %collective-permute-start.9 = (f32[18448]{0:T(1024)S(1)}, f32[18448]{0:T(1024)S(1)}, u32[]{:S(2)}, u32[]{:S(2)}) collective-permute-start(f32[18448]{0:T(1024)S(1)} %add.222), channel_id=1, source_target_pairs={{0,16},{8,24},{16,0},{24,8},{32,48},{40,56},{48,32},{56,40},{64,80... | collective-permute-start | bytes 221384 | tf_op jit(solution)/shard_map/ppermute | solution.py:48
  67.5 2.7 %collective-permute-done.9 = f32[18448]{0:T(1024)S(1)} collective-permute-done((f32[18448]{0:T(1024)S(1)}, f32[18448]{0:T(1024)S(1)}, u32[]{:S(2)}, u32[]{:S(2)}) %collective-permute-start.9) | collective-permute-done | bytes 73824 | tf_op jit(solution)/shard_map/ppermute | solution.py:48
  70.2 2.9 %collective-permute-start.10 = (f32[18448]{0:T(1024)S(1)}, f32[18448]{0:T(1024)S(1)}, u32[]{:S(2)}, u32[]{:S(2)}) collective-permute-start(f32[18448]{0:T(1024)S(1)} %add.223), channel_id=1, source_target_pairs={{0,64},{8,72},{16,80},{24,88},{32,96},{40,104},{48,112},{56,120},{... | collective-permute-start | bytes 221384 | tf_op jit(solution)/shard_map/ppermute | solution.py:48
  73.2 1.7 %collective-permute-done.10 = f32[18448]{0:T(1024)S(1)} collective-permute-done((f32[18448]{0:T(1024)S(1)}, f32[18448]{0:T(1024)S(1)}, u32[]{:S(2)}, u32[]{:S(2)}) %collective-permute-start.10) | collective-permute-done | bytes 73824 | tf_op jit(solution)/shard_map/ppermute | solution.py:48
  74.9 5.0 %collective-permute-start.11 = (f32[18448]{0:T(1024)S(1)}, f32[18448]{0:T(1024)S(1)}, u32[]{:S(2)}, u32[]{:S(2)}) collective-permute-start(f32[18448]{0:T(1024)S(1)} %add.224), channel_id=1, source_target_pairs={{0,192},{8,200},{16,208},{24,216},{32,224},{40,232},{48,240},{56,2... | collective-permute-start | bytes 221384 | tf_op jit(solution)/shard_map/ppermute | solution.py:48
  80.1 1.8 %collective-permute-done.11 = f32[18448]{0:T(1024)S(1)} collective-permute-done((f32[18448]{0:T(1024)S(1)}, f32[18448]{0:T(1024)S(1)}, u32[]{:S(2)}, u32[]{:S(2)}) %collective-permute-start.11) | collective-permute-done | bytes 73824 | tf_op jit(solution)/shard_map/ppermute | solution.py:48
  81.8 3.0 %collective-permute-start.12 = (f32[18448]{0:T(1024)S(1)}, f32[18448]{0:T(1024)S(1)}, u32[]{:S(2)}, u32[]{:S(2)}) collective-permute-start(f32[18448]{0:T(1024)S(1)} %add.225), channel_id=1, source_target_pairs={{0,6},{1,7},{2,4},{3,5},{4,2},{5,3},{6,0},{7,1},{8,14},{9,15},{10,... | collective-permute-start | bytes 221384 | tf_op jit(solution)/shard_map/ppermute | solution.py:48
  85.0 1.9 %collective-permute-done.12 = f32[18448]{0:T(1024)S(1)} collective-permute-done((f32[18448]{0:T(1024)S(1)}, f32[18448]{0:T(1024)S(1)}, u32[]{:S(2)}, u32[]{:S(2)}) %collective-permute-start.12) | collective-permute-done | bytes 73824 | tf_op jit(solution)/shard_map/ppermute | solution.py:48
  87.3 3.0 %collective-permute-done.13 = f32[18448]{0:T(1024)S(1)} collective-permute-done((f32[18448]{0:T(1024)S(1)}, f32[18448]{0:T(1024)S(1)}, u32[]{:S(2)}, u32[]{:S(2)}) %collective-permute-start.13) | collective-permute-done | bytes 73824 | tf_op jit(solution)/shard_map/ppermute | solution.py:52
  90.6 3.9 %collective-permute-done.14 = f32[36896]{0:T(1024)S(1)} collective-permute-done((f32[36896]{0:T(1024)S(1)}, f32[36896]{0:T(1024)S(1)}, u32[]{:S(2)}, u32[]{:S(2)}) %collective-permute-start.14) | collective-permute-done | bytes 147616 | tf_op jit(solution)/shard_map/ppermute | solution.py:52
  94.7 9.3 %collective-permute-start.15 = (f32[73792]{0:T(1024)S(1)}, f32[73792]{0:T(1024)S(1)}, u32[]{:S(2)}, u32[]{:S(2)}) collective-permute-start(f32[73792]{0:T(1024)S(1)} %maximum_select_fusion.1), channel_id=1, source_target_pairs={{0,8},{8,0},{16,24},{24,16},{32,40},{40,32},{48,56},{56,48},{64,72... | collective-permute-start | bytes 885512 | tf_op jit(solution)/shard_map/ppermute | solution.py:52
  104.3 0.9 convert_element_type.33
  105.4 0.5 slice_multiply_fusion.2
  105.9 0.9 slice_multiply_fusion.1
  (89 shorter events, 10.3 us)
Async XLA Ops:
  0.6 1.2 %copy-start.5 = (bf16[48,48,128]{2,1,0:T(8,128)(2,1)S(1)}, bf16[48,48,128]{2,1,0:T(8,128)(2,1)}, u32[]{:S(2)}) copy-start(bf16[48,48,128]{2,1,0:T(8,128)(2,1)} %param.15) | copy-start | bytes 1769476
  2.1 5.4 %collective-permute-start = (bf16[48,2,256]{2,1,0:T(2,128)(2,1)S(1)}, bf16[48,2,256]{2,1,0:T(2,128)(2,1)S(1)}, u32[]{:S(2)}, u32[]{:S(2)}) collective-permute-start(bf16[48,2,256]{2,1,0:T(2,128)(2,1)S(1)} %get-tuple-element.65), channel_id=1, source_target_pairs={{0,8},{8,16},{16,24},{24,32},{32,40},{40,48},{48,56},{56,64},{64,7... | collective-permute-start | bytes 147464 | tf_op jit(solution)/shard_map/ppermute | solution.py:15
  6.3 5.0 %collective-permute-start.1 = (bf16[48,2,256]{2,1,0:T(2,128)(2,1)S(1)}, bf16[48,2,256]{2,1,0:T(2,128)(2,1)S(1)}, u32[]{:S(2)}, u32[]{:S(2)}) collective-permute-start(bf16[48,2,256]{2,1,0:T(2,128)(2,1)S(1)} %get-tuple-element.66), channel_id=1, source_target_pairs={{8,0},{16,8},{24,16},{32,24},{40,32},{48,40},{56,48},{64,56},{72,6... | collective-permute-start | bytes 147464 | tf_op jit(solution)/shard_map/ppermute | solution.py:17
  12.0 10.8 %collective-permute-start.2 = (bf16[2,52,256]{2,1,0:T(8,128)(2,1)S(1)}, bf16[2,52,256]{2,1,0:T(8,128)(2,1)S(1)}, u32[]{:S(2)}, u32[]{:S(2)}) collective-permute-start(bf16[2,52,256]{2,1,0:T(8,128)(2,1)S(1)} %get-tuple-element.69), channel_id=1, source_target_pairs={{0,1},{1,2},{2,3},{3,4},{4,5},{5,6},{6,7},{8,9},{9,10},{10,11},{11... | collective-permute-start | bytes 159752 | tf_op jit(solution)/shard_map/ppermute | solution.py:15
  14.2 8.5 %collective-permute-start.3 = (bf16[2,52,256]{2,1,0:T(8,128)(2,1)S(1)}, bf16[2,52,256]{2,1,0:T(8,128)(2,1)S(1)}, u32[]{:S(2)}, u32[]{:S(2)}) collective-permute-start(bf16[2,52,256]{2,1,0:T(8,128)(2,1)S(1)} %get-tuple-element.70), channel_id=1, source_target_pairs={{1,0},{2,1},{3,2},{4,3},{5,4},{6,5},{7,6},{9,8},{10,9},{11,10},{12... | collective-permute-start | bytes 159752 | tf_op jit(solution)/shard_map/ppermute | solution.py:17
  15.6 10.0 %collective-permute-start.4 = (bf16[4,52,256]{2,1,0:T(8,128)(2,1)S(1)}, bf16[4,52,256]{2,1,0:T(8,128)(2,1)S(1)}, u32[]{:S(2)}, u32[]{:S(2)}) collective-permute-start(bf16[4,52,256]{2,1,0:T(8,128)(2,1)S(1)} %pad_maximum_fusion.1), channel_id=1, source_target_pairs={{0,128},{8,136},{16,144},{24,152},{32,160},{40,168},{48,176},{56,1... | collective-permute-start | bytes 319496 | tf_op jit(solution)/shard_map/ppermute | solution.py:27
  25.8 1.0 copy-start.2
  25.9 1.0 copy-start.9
  29.0 1.3 %copy-start.7 = (f32[128]{0:T(128)S(1)}, f32[128]{0:T(128)}, u32[]{:S(2)}) copy-start(f32[128]{0:T(128)} %param.14) | copy-start | bytes 1540
  32.4 4.4 %copy-start = (bf16[50,50,128]{2,1,0:T(8,128)(2,1)}, bf16[50,50,128]{2,1,0:T(8,128)(2,1)S(1)}, u32[]{:S(2)}) copy-start(bf16[50,50,128]{2,1,0:T(8,128)(2,1)S(1)} %get-tuple-element.56) | copy-start | bytes 1920004
  37.4 0.9 copy-start.4
  40.6 2.9 %collective-permute-start.5 = (f32[73792]{0:T(1024)S(1)}, f32[73792]{0:T(1024)S(1)}, u32[]{:S(2)}, u32[]{:S(2)}) collective-permute-start(f32[73792]{0:T(1024)S(1)} %dynamic_slice.19), channel_id=1, source_target_pairs={{0,8},{8,0},{16,24},{24,16},{32,40},{40,32},{48,56},{56,48},{64,72... | collective-permute-start | bytes 885512 | tf_op jit(solution)/shard_map/ppermute | solution.py:44
  44.8 6.6 %collective-permute-start.6 = (f32[36896]{0:T(1024)S(1)}, f32[36896]{0:T(1024)S(1)}, u32[]{:S(2)}, u32[]{:S(2)}) collective-permute-start(f32[36896]{0:T(1024)S(1)} %dynamic_slice.21), channel_id=1, source_target_pairs={{0,1},{1,0},{2,3},{3,2},{4,5},{5,4},{6,7},{7,6},{8,9},{9,8},{10,11... | collective-permute-start | bytes 442760 | tf_op jit(solution)/shard_map/ppermute | solution.py:44
  51.6 4.4 %copy-start.1 = (bf16[50,50,128]{2,1,0:T(8,128)(2,1)S(1)}, bf16[50,50,128]{2,1,0:T(8,128)(2,1)}, u32[]{:S(2)}) copy-start(bf16[50,50,128]{2,1,0:T(8,128)(2,1)} %copy-done) | copy-start | bytes 1920004
  51.6 4.1 %collective-permute-start.7 = (f32[18448]{0:T(1024)S(1)}, f32[18448]{0:T(1024)S(1)}, u32[]{:S(2)}, u32[]{:S(2)}) collective-permute-start(f32[18448]{0:T(1024)S(1)} %dynamic_slice.23), channel_id=1, source_target_pairs={{0,32},{8,40},{16,48},{24,56},{32,0},{40,8},{48,16},{56,24},{64,96... | collective-permute-start | bytes 221384 | tf_op jit(solution)/shard_map/ppermute | solution.py:44
  56.1 0.7 copy-start.8
  58.6 1.1 %copy-start.3 = (f32[48,8,7,128]{3,1,2,0:T(8,128)}, f32[48,8,7,128]{3,1,2,0:T(8,128)S(1)}, u32[]{:S(2)}) copy-start(f32[48,8,7,128]{3,1,2,0:T(8,128)S(1)} %convolution_select_fusion) | copy-start | bytes 4128772
  58.6 0.9 copy-start.6
  61.4 4.0 %collective-permute-start.8 = (f32[18448]{0:T(1024)S(1)}, f32[18448]{0:T(1024)S(1)}, u32[]{:S(2)}, u32[]{:S(2)}) collective-permute-start(f32[18448]{0:T(1024)S(1)} %dynamic-slice_add_fusion.2), channel_id=1, source_target_pairs={{0,2},{1,3},{2,0},{3,1},{4,6},{5,7},{6,4},{7,5},{8,10},{9,11},{10,... | collective-permute-start | bytes 221384 | tf_op jit(solution)/shard_map/ppermute | solution.py:48
  63.7 0.7 slice-start
  65.4 4.8 %collective-permute-start.9 = (f32[18448]{0:T(1024)S(1)}, f32[18448]{0:T(1024)S(1)}, u32[]{:S(2)}, u32[]{:S(2)}) collective-permute-start(f32[18448]{0:T(1024)S(1)} %add.222), channel_id=1, source_target_pairs={{0,16},{8,24},{16,0},{24,8},{32,48},{40,56},{48,32},{56,40},{64,80... | collective-permute-start | bytes 221384 | tf_op jit(solution)/shard_map/ppermute | solution.py:48
  70.2 4.7 %collective-permute-start.10 = (f32[18448]{0:T(1024)S(1)}, f32[18448]{0:T(1024)S(1)}, u32[]{:S(2)}, u32[]{:S(2)}) collective-permute-start(f32[18448]{0:T(1024)S(1)} %add.223), channel_id=1, source_target_pairs={{0,64},{8,72},{16,80},{24,88},{32,96},{40,104},{48,112},{56,120},{... | collective-permute-start | bytes 221384 | tf_op jit(solution)/shard_map/ppermute | solution.py:48
  74.9 6.9 %collective-permute-start.11 = (f32[18448]{0:T(1024)S(1)}, f32[18448]{0:T(1024)S(1)}, u32[]{:S(2)}, u32[]{:S(2)}) collective-permute-start(f32[18448]{0:T(1024)S(1)} %add.224), channel_id=1, source_target_pairs={{0,192},{8,200},{16,208},{24,216},{32,224},{40,232},{48,240},{56,2... | collective-permute-start | bytes 221384 | tf_op jit(solution)/shard_map/ppermute | solution.py:48
  81.8 5.1 %collective-permute-start.12 = (f32[18448]{0:T(1024)S(1)}, f32[18448]{0:T(1024)S(1)}, u32[]{:S(2)}, u32[]{:S(2)}) collective-permute-start(f32[18448]{0:T(1024)S(1)} %add.225), channel_id=1, source_target_pairs={{0,6},{1,7},{2,4},{3,5},{4,2},{5,3},{6,0},{7,1},{8,14},{9,15},{10,... | collective-permute-start | bytes 221384 | tf_op jit(solution)/shard_map/ppermute | solution.py:48
  86.9 3.3 %collective-permute-start.13 = (f32[18448]{0:T(1024)S(1)}, f32[18448]{0:T(1024)S(1)}, u32[]{:S(2)}, u32[]{:S(2)}) collective-permute-start(f32[18448]{0:T(1024)S(1)} %add.226), channel_id=1, source_target_pairs={{0,32},{8,40},{16,48},{24,56},{32,0},{40,8},{48,16},{56,24},{64,96... | collective-permute-start | bytes 221384 | tf_op jit(solution)/shard_map/ppermute | solution.py:52
  90.4 4.1 %collective-permute-start.14 = (f32[36896]{0:T(1024)S(1)}, f32[36896]{0:T(1024)S(1)}, u32[]{:S(2)}, u32[]{:S(2)}) collective-permute-start(f32[36896]{0:T(1024)S(1)} %maximum_select_fusion.2), channel_id=1, source_target_pairs={{0,1},{1,0},{2,3},{3,2},{4,5},{5,4},{6,7},{7,6},{8,9},{9,8},{10,11... | collective-permute-start | bytes 442760 | tf_op jit(solution)/shard_map/ppermute | solution.py:52
  94.7 10.5 %collective-permute-start.15 = (f32[73792]{0:T(1024)S(1)}, f32[73792]{0:T(1024)S(1)}, u32[]{:S(2)}, u32[]{:S(2)}) collective-permute-start(f32[73792]{0:T(1024)S(1)} %maximum_select_fusion.1), channel_id=1, source_target_pairs={{0,8},{8,0},{16,24},{24,16},{32,40},{40,32},{48,56},{56,48},{64,72... | collective-permute-start | bytes 885512 | tf_op jit(solution)/shard_map/ppermute | solution.py:52

commit v8 on v4

--- a/solution.py
+++ b/solution.py
@@ -98,11 +98,11 @@
     bands = lax.axis_size("lat")
     half = lax.axis_size("lon") // 2
     both = jnp.concatenate([inputs, cotangent], axis=2)
-    wide = extended(both, (("lon", 1),), 2, True)
-    tall = extended(wide, (("lat", 0),), 2, False)
-    far = from_behind(jnp.stack([wide[0], wide[-1]]), "lon", half)
+    tall = extended(both, (("lat", 0),), 2, False)
+    far = from_behind(jnp.stack([both[0], both[-1]]), "lon", half)
     tall = tall.at[1].set(jnp.where(band == 0, far[0], tall[1]))
     tall = tall.at[rows + 2].set(jnp.where(band == bands - 1, far[1], tall[rows + 2]))
+    tall = extended(tall, (("lon", 1),), 2, True)
     padded = tall[:, :, :chans]
     ring_cot = tall[1:-1, 1:-1, chans:].astype(jnp.float32)
     pre = lax.conv_general_dilated(

time: 96.9 us -> 101 us (1.042)
  matrix products: 13.5 us -> 9.46 us
  local copies, waits for them, and re-layouts: 6.75 us -> 10.2 us
  waiting for transfers between devices: 19.7 us -> 22.4 us
    dot_general x6, matrix products: 5.31 us -> 1.53 us  [shards(): jnp.dot(grad_ext[line_at, tap_b:tap_b + cols], weight[tap_a, 2 - tap_b].T...]
    ppermute x5, starting transfers between devices: 12 us -> 15.2 us  [butterfly_sum(): data = data + lax.ppermute(data, axis, pairs)]
    ppermute x3, starting transfers between devices: 5.15 us -> 2.96 us  [butterfly_sum(): data = keep + lax.ppermute(send, axis, pairs)]
    ppermute x3, waiting for transfers between devices: 5.36 us -> 7.27 us  [butterfly_sum(): data = keep + lax.ppermute(send, axis, pairs)]
    ppermute x2, starting transfers between devices: 6.42 us -> 8.28 us  [extended(): lax.ppermute(tail, axis, [(i, (i + 1) % count) for i in range(ends)])]
    ppermute x3, starting transfers between devices: 12.2 us -> 10.4 us  [butterfly_sum(): other = lax.ppermute(data, axis, pairs)]
    concatenate x1, local copies, waits for them, and re-layouts: 0.04 us -> 1.32 us  [shards(): jnp.concatenate([kernel_terms, bias_terms], axis=0)]
    ppermute x5, waiting for transfers between devices: 6.51 us -> 7.71 us  [butterfly_sum(): data = data + lax.ppermute(data, axis, pairs)]
  transfers between devices with their start and end apart: 17 -> 17, of which waited for: 13 -> 12; matrix products, arithmetic and copies ran while one was open for 12% -> 7% of each run, Pallas kernels for 0% -> 0%
where the time goes in v8:
time: 101 us; the launch traced here: 100 us
  starting transfers between devices  47.6 us (47%)
  waiting for transfers between devices  22.4 us (22%)
  local copies, waits for them, and re-layouts  10.2 us (10%)
  matrix products  9.46 us (9%)
  other arithmetic  9.29 us (9%)
  between operations  1.18 us (1%)
    ppermute x5, starting transfers between devices, butterfly_sum(): data = data + lax.ppermute(data, axis, pairs)  15.2 us
    ppermute x3, starting transfers between devices, butterfly_sum(): other = lax.ppermute(data, axis, pairs)  10.4 us
    ppermute x2, starting transfers between devices, from_behind(): return lax.ppermute(value, axis, pairs)  9.4 us
    ppermute x2, starting transfers between devices, extended(): lax.ppermute(tail, axis, [(i, (i + 1) % count) for i in range(ends)])  8.28 us
    ppermute x5, waiting for transfers between devices, butterfly_sum(): data = data + lax.ppermute(data, axis, pairs)  7.71 us
    ppermute x3, waiting for transfers between devices, butterfly_sum(): data = keep + lax.ppermute(send, axis, pairs)  7.27 us
    dot_general x9, matrix products, shards(): lax.dot_general(window, pre_grad, (((0,), (0,)), ((), ())), preferred_ele...  4.21 us
    unnamed x19, local copies, waits for them, and re-layouts  4.19 us
  transfers between devices with their start and end apart: 17, of which 12 were waited for; matrix products, arithmetic and copies ran while one was open for 7% of the time, Pallas kernels for 0%

profile of v8, /device:TPU:1, one launch (start us, length us, event | category | flops | bytes accessed | tf_op | source)
XLA Modules:
  0.0 100.1 jit_solution(17302575183412729575)
XLA Ops:
  0.6 1.2 %constant_dynamic-update-slice_fusion.1 = bf16[48,48,256]{2,1,0:T(8,128)(2,1)S(1)} fusion(bf16[48,48,128]{2,1,0:T(8,128)(2,1)} %param.12), kind=kLoop, calls=%fused_computation.110 | loop fusion | bytes 1179648
  2.0 3.9 %collective-permute-start = (bf16[2,48,256]{2,1,0:T(8,128)(2,1)S(1)}, bf16[2,48,256]{2,1,0:T(8,128)(2,1)S(1)}, u32[]{:S(2)}, u32[]{:S(2)}) collective-permute-start(bf16[2,48,256]{2,1,0:T(8,128)(2,1)S(1)} %get-tuple-element.58), channel_id=1, source_target_pairs={{0,1},{1,2},{2,3},{3,4},{4,5},{5,6},{6,7},{8,9},{9,10},{10,11},{11... | collective-permute-start | bytes 147464 | tf_op jit(solution)/shard_map/ppermute | solution.py:15
  6.0 1.3 %collective-permute-start.1 = (bf16[2,48,256]{2,1,0:T(8,128)(2,1)S(1)}, bf16[2,48,256]{2,1,0:T(8,128)(2,1)S(1)}, u32[]{:S(2)}, u32[]{:S(2)}) collective-permute-start(bf16[2,48,256]{2,1,0:T(8,128)(2,1)S(1)} %get-tuple-element.59), channel_id=1, source_target_pairs={{1,0},{2,1},{3,2},{4,3},{5,4},{6,5},{7,6},{9,8},{10,9},{11,10},{12... | collective-permute-start | bytes 147464 | tf_op jit(solution)/shard_map/ppermute | solution.py:17
  7.3 7.0 %collective-permute-start.2 = (bf16[2,48,256]{2,1,0:T(8,128)(2,1)S(1)}, bf16[2,48,256]{2,1,0:T(8,128)(2,1)S(1)}, u32[]{:S(2)}, u32[]{:S(2)}) collective-permute-start(bf16[2,48,256]{2,1,0:T(8,128)(2,1)S(1)} %pad_maximum_fusion.6), channel_id=1, source_target_pairs={{0,128},{8,136},{16,144},{24,152},{32,160},{40,168},{48,176},{56,1... | collective-permute-start | bytes 147464 | tf_op jit(solution)/shard_map/ppermute | solution.py:27
  14.5 1.3 %collective-permute-done.2 = bf16[2,48,256]{2,1,0:T(8,128)(2,1)S(1)} collective-permute-done((bf16[2,48,256]{2,1,0:T(8,128)(2,1)S(1)}, bf16[2,48,256]{2,1,0:T(8,128)(2,1)S(1)}, u32[]{:S(2)}, u32[]{:S(2)}) %collective-permute-start.2) | collective-permute-done | bytes 49184 | tf_op jit(solution)/shard_map/ppermute | solution.py:27
  15.9 4.3 %collective-permute-start.3 = (bf16[52,2,256]{2,1,0:T(2,128)(2,1)S(1)}, bf16[52,2,256]{2,1,0:T(2,128)(2,1)S(1)}, u32[]{:S(2)}, u32[]{:S(2)}) collective-permute-start(bf16[52,2,256]{2,1,0:T(2,128)(2,1)S(1)} %get-tuple-element.54), channel_id=1, source_target_pairs={{0,8},{8,16},{16,24},{24,32},{32,40},{40,48},{48,56},{56,64},{64,7... | collective-permute-start | bytes 159752 | tf_op jit(solution)/shard_map/ppermute | solution.py:15
  20.3 1.2 %collective-permute-done.3 = bf16[52,2,256]{2,1,0:T(2,128)(2,1)S(1)} collective-permute-done((bf16[52,2,256]{2,1,0:T(2,128)(2,1)S(1)}, bf16[52,2,256]{2,1,0:T(2,128)(2,1)S(1)}, u32[]{:S(2)}, u32[]{:S(2)}) %collective-permute-start.3) | collective-permute-done | bytes 53280 | tf_op jit(solution)/shard_map/ppermute | solution.py:15
  21.5 3.8 %collective-permute-done.4 = bf16[52,2,256]{2,1,0:T(2,128)(2,1)S(1)} collective-permute-done((bf16[52,2,256]{2,1,0:T(2,128)(2,1)S(1)}, bf16[52,2,256]{2,1,0:T(2,128)(2,1)S(1)}, u32[]{:S(2)}, u32[]{:S(2)}) %collective-permute-start.4) | collective-permute-done | bytes 53280 | tf_op jit(solution)/shard_map/ppermute | solution.py:17
  25.3 0.9 pad_maximum_fusion
  26.8 0.8 copy-done.3
  27.5 1.9 %convolution_select_fusion.1 = f32[50,8,7,128]{3,1,2,0:T(8,128)S(1)} fusion(bf16[3,3,128,128]{3,2,1,0:T(8,128)(2,1)S(1)} %copy-done.3, bf16[52,1,7,2,128]{4,2,3,0,1:T(8,128)(2,1)S(1)} %slice.280, bf16[52,1,8,7,128]{4,2,3,0,1:T(8,128)(2,1)S(1)} %copy.10, pred[8,7]{0,1:T(8,128)(4,1)S(1)} %copy-done.7), kind=kOutput, calls=%fused_computation.14 | convolution fusion | flops 828987392 | bytes 2660408 | tf_op jit(solution)/shard_map/conv_general_dilated | solution.py:108
  29.8 1.3 %reshape.171 = f32[50,1,56,128]{3,2,0,1:T(8,128)} reshape(f32[50,8,7,128]{3,2,1,0:T(8,128)S(1)} %copy.11) | data formatting | bytes 2867200 | tf_op jit(solution)/shard_map/conv_general_dilated | solution.py:108
  31.1 2.2 %fusion.29 = (bf16[50,50,128]{2,1,0:T(8,128)(2,1)S(1)}, f32[50,50,128]{2,1,0:T(8,128)S(1)}) fusion(bf16[52,2,256]{2,1,0:T(2,128)(2,1)S(1)} %collective-permute-done.4, bf16[52,48,256]{2,1,0:T(8,128)(2,1)S(1)} %fusion.63, bf16[52,2,256]{2,1,0:T(2,128)(2,1)S(1)} %collective-permute-done.3, pred[50]{0:T(512)(128)(4,1)S(1)} %and_or_fusion, f32[128]{0:T(128)S(1)} %copy-done.5, ...), kind=kLoop, calls=%fused_computation.61 | loop fusion | flops 5440000 | bytes 4585010 | tf_op jit(solution)/shard_map/jit(_where)/select_n | solution.py:121
  33.6 0.5 fusion.12
  34.5 0.5 fusion.10
  35.1 0.5 fusion.9
  36.0 0.5 fusion.7
  36.5 0.5 fusion.6
  37.4 0.5 fusion.4
  37.9 0.8 copy-done.1
  38.8 1.3 %dynamic-update-slice.21 = f32[1153,128]{1,0:T(8,128)} dynamic-update-slice(f32[1153,128]{1,0:T(8,128)} %copy-done.1, f32[1,128]{1,0:T(1,128)S(1)} %bitcast.119, s32[]{} %constant.219, s32[]{} %constant.210) | dynamic-update-slice | bytes 1028 | tf_op jit(solution)/shard_map/concatenate | solution.py:158
  40.1 1.1 %dynamic_slice.19 = f32[73792]{0:T(1024)S(1)} dynamic-slice(f32[147584]{0:T(1024)} %bitcast.115, s32[]{:T(128)S(6)} %select_n.116), dynamic_slice_sizes={73792} | dynamic-slice | bytes 590340 | tf_op jit(solution)/shard_map/dynamic_slice | solution.py:42
  41.6 0.9 fusion.47
  42.4 0.6 collective-permute-done.6
  43.1 1.1 %dynamic-slice_add_fusion = f32[73792]{0:T(1024)S(1)} fusion(f32[73792]{0:T(1024)S(1)} %collective-permute-done.6, f32[147584]{0:T(1024)} %bitcast.116, s32[]{:T(128)S(6)} %select_n.115), kind=kLoop, calls=%fused_computation.78 | loop fusion | flops 73792 | bytes 885508 | tf_op jit(solution)/shard_map/add | solution.py:44
  44.3 2.1 %collective-permute-start.7 = (f32[36896]{0:T(1024)S(1)}, f32[36896]{0:T(1024)S(1)}, u32[]{:S(2)}, u32[]{:S(2)}) collective-permute-start(f32[36896]{0:T(1024)S(1)} %dynamic_slice.21), channel_id=1, source_target_pairs={{0,1},{1,0},{2,3},{3,2},{4,5},{5,4},{6,7},{7,6},{8,9},{9,8},{10,11... | collective-permute-start | bytes 442760 | tf_op jit(solution)/shard_map/ppermute | solution.py:44
  46.5 4.0 %collective-permute-done.7 = f32[36896]{0:T(1024)S(1)} collective-permute-done((f32[36896]{0:T(1024)S(1)}, f32[36896]{0:T(1024)S(1)}, u32[]{:S(2)}, u32[]{:S(2)}) %collective-permute-start.7) | collective-permute-done | bytes 147616 | tf_op jit(solution)/shard_map/ppermute | solution.py:44
  50.8 0.6 collective-permute-start.8
  51.5 2.6 %collective-permute-done.8 = f32[18448]{0:T(1024)S(1)} collective-permute-done((f32[18448]{0:T(1024)S(1)}, f32[18448]{0:T(1024)S(1)}, u32[]{:S(2)}, u32[]{:S(2)}) %collective-permute-start.8) | collective-permute-done | bytes 73824 | tf_op jit(solution)/shard_map/ppermute | solution.py:44
  54.2 2.9 %collective-permute-start.9 = (f32[18448]{0:T(1024)S(1)}, f32[18448]{0:T(1024)S(1)}, u32[]{:S(2)}, u32[]{:S(2)}) collective-permute-start(f32[18448]{0:T(1024)S(1)} %dynamic-slice_add_fusion.2), channel_id=1, source_target_pairs={{0,2},{1,3},{2,0},{3,1},{4,6},{5,7},{6,4},{7,5},{8,10},{9,11},{10,... | collective-permute-start | bytes 221384 | tf_op jit(solution)/shard_map/ppermute | solution.py:47
  57.2 1.7 %collective-permute-done.9 = f32[18448]{0:T(1024)S(1)} collective-permute-done((f32[18448]{0:T(1024)S(1)}, f32[18448]{0:T(1024)S(1)}, u32[]{:S(2)}, u32[]{:S(2)}) %collective-permute-start.9) | collective-permute-done | bytes 73824 | tf_op jit(solution)/shard_map/ppermute | solution.py:47
  58.9 2.0 %collective-permute-start.10 = (f32[18448]{0:T(1024)S(1)}, f32[18448]{0:T(1024)S(1)}, u32[]{:S(2)}, u32[]{:S(2)}) collective-permute-start(f32[18448]{0:T(1024)S(1)} %add.123), channel_id=1, source_target_pairs={{0,16},{8,24},{16,0},{24,8},{32,48},{40,56},{48,32},{56,40},{64,80... | collective-permute-start | bytes 221384 | tf_op jit(solution)/shard_map/ppermute | solution.py:47
  61.1 2.7 %collective-permute-done.10 = f32[18448]{0:T(1024)S(1)} collective-permute-done((f32[18448]{0:T(1024)S(1)}, f32[18448]{0:T(1024)S(1)}, u32[]{:S(2)}, u32[]{:S(2)}) %collective-permute-start.10) | collective-permute-done | bytes 73824 | tf_op jit(solution)/shard_map/ppermute | solution.py:47
  63.8 3.9 %collective-permute-start.11 = (f32[18448]{0:T(1024)S(1)}, f32[18448]{0:T(1024)S(1)}, u32[]{:S(2)}, u32[]{:S(2)}) collective-permute-start(f32[18448]{0:T(1024)S(1)} %add.124), channel_id=1, source_target_pairs={{0,64},{8,72},{16,80},{24,88},{32,96},{40,104},{48,112},{56,120},{... | collective-permute-start | bytes 221384 | tf_op jit(solution)/shard_map/ppermute | solution.py:47
  67.8 1.7 %collective-permute-done.11 = f32[18448]{0:T(1024)S(1)} collective-permute-done((f32[18448]{0:T(1024)S(1)}, f32[18448]{0:T(1024)S(1)}, u32[]{:S(2)}, u32[]{:S(2)}) %collective-permute-start.11) | collective-permute-done | bytes 73824 | tf_op jit(solution)/shard_map/ppermute | solution.py:47
  69.5 3.4 %collective-permute-start.12 = (f32[18448]{0:T(1024)S(1)}, f32[18448]{0:T(1024)S(1)}, u32[]{:S(2)}, u32[]{:S(2)}) collective-permute-start(f32[18448]{0:T(1024)S(1)} %add.125), channel_id=1, source_target_pairs={{0,192},{8,200},{16,208},{24,216},{32,224},{40,232},{48,240},{56,2... | collective-permute-start | bytes 221384 | tf_op jit(solution)/shard_map/ppermute | solution.py:47
  72.9 2.4 %collective-permute-start.5 = (bf16[2,48,128]{2,1,0:T(8,128)(2,1)S(1)}, bf16[2,48,128]{2,1,0:T(8,128)(2,1)S(1)}, u32[]{:S(2)}, u32[]{:S(2)}) collective-permute-start(bf16[2,48,128]{2,1,0:T(8,128)(2,1)S(1)} %pad_maximum_fusion.7), channel_id=1, source_target_pairs={{0,128},{8,136},{16,144},{24,152},{32,160},{40,168},{48,176},{56,1... | collective-permute-start | bytes 73736 | tf_op jit(solution)/shard_map/ppermute | solution.py:27
  75.3 3.0 %collective-permute-start.13 = (f32[18448]{0:T(1024)S(1)}, f32[18448]{0:T(1024)S(1)}, u32[]{:S(2)}, u32[]{:S(2)}) collective-permute-start(f32[18448]{0:T(1024)S(1)} %add.126), channel_id=1, source_target_pairs={{0,6},{1,7},{2,4},{3,5},{4,2},{5,3},{6,0},{7,1},{8,14},{9,15},{10,... | collective-permute-start | bytes 221384 | tf_op jit(solution)/shard_map/ppermute | solution.py:47
  78.6 1.7 %collective-permute-done.13 = f32[18448]{0:T(1024)S(1)} collective-permute-done((f32[18448]{0:T(1024)S(1)}, f32[18448]{0:T(1024)S(1)}, u32[]{:S(2)}, u32[]{:S(2)}) %collective-permute-start.13) | collective-permute-done | bytes 73824 | tf_op jit(solution)/shard_map/ppermute | solution.py:47
  80.4 2.0 %collective-permute-start.14 = (f32[18448]{0:T(1024)S(1)}, f32[18448]{0:T(1024)S(1)}, u32[]{:S(2)}, u32[]{:S(2)}) collective-permute-start(f32[18448]{0:T(1024)S(1)} %add.127), channel_id=1, source_target_pairs={{0,32},{8,40},{16,48},{24,56},{32,0},{40,8},{48,16},{56,24},{64,96... | collective-permute-start | bytes 221384 | tf_op jit(solution)/shard_map/ppermute | solution.py:51
  82.4 1.1 %fusion.3 = bf16[48,48,128]{2,1,0:T(8,128)(2,1)} fusion(f32[50,50,128]{2,1,0:T(8,128)S(1)} %add_divide_fusion, f32[50,50,128]{2,1,0:T(8,128)S(1)} %get-tuple-element.53), kind=kLoop, calls=%fused_computation.21 | loop fusion | flops 589824 | bytes 2949120 | tf_op jit(solution)/shard_map/convert.4
  84.0 0.7 collective-permute-done.14
  85.3 1.8 %convolution_select_fusion = f32[48,8,7,128]{3,1,2,0:T(8,128)S(1)} fusion(bf16[3,3,128,128]{3,2,1,0:T(8,128)(2,1)S(1)} %copy-done.4, bf16[50,1,7,2,128]{4,2,3,0,1:T(8,128)(2,1)S(1)} %slice.284, bf16[50,1,8,7,128]{4,2,3,0,1:T(8,128)(2,1)S(1)} %copy.13, pred[8,7]{0,1:T(8,128)(4,1)S(1)} %copy-done.6), kind=kOutput, calls=%fused_computation.9 | convolution fusion | flops 795832320 | bytes 2567224 | tf_op jit(solution)/shard_map/conv_general_dilated | solution.py:124
  87.4 0.8 copy-done
  89.3 7.9 %collective-permute-start.16 = (f32[73792]{0:T(1024)S(1)}, f32[73792]{0:T(1024)S(1)}, u32[]{:S(2)}, u32[]{:S(2)}) collective-permute-start(f32[73792]{0:T(1024)S(1)} %maximum_select_fusion.1), channel_id=1, source_target_pairs={{0,8},{8,0},{16,24},{24,16},{32,40},{40,32},{48,56},{56,48},{64,72... | collective-permute-start | bytes 885512 | tf_op jit(solution)/shard_map/ppermute | solution.py:51
  97.3 0.9 convert_element_type.21
  98.7 0.5 slice_multiply_fusion.2
  99.2 0.9 slice_multiply_fusion.1
  (73 shorter events, 7.3 us)
Async XLA Ops:
  0.6 1.2 %copy-start.2 = (bf16[48,48,128]{2,1,0:T(8,128)(2,1)S(1)}, bf16[48,48,128]{2,1,0:T(8,128)(2,1)}, u32[]{:S(2)}) copy-start(bf16[48,48,128]{2,1,0:T(8,128)(2,1)} %param.15) | copy-start | bytes 1769476
  2.0 12.3 %collective-permute-start = (bf16[2,48,256]{2,1,0:T(8,128)(2,1)S(1)}, bf16[2,48,256]{2,1,0:T(8,128)(2,1)S(1)}, u32[]{:S(2)}, u32[]{:S(2)}) collective-permute-start(bf16[2,48,256]{2,1,0:T(8,128)(2,1)S(1)} %get-tuple-element.58), channel_id=1, source_target_pairs={{0,1},{1,2},{2,3},{3,4},{4,5},{5,6},{6,7},{8,9},{9,10},{10,11},{11... | collective-permute-start | bytes 147464 | tf_op jit(solution)/shard_map/ppermute | solution.py:15
  6.0 8.3 %collective-permute-start.1 = (bf16[2,48,256]{2,1,0:T(8,128)(2,1)S(1)}, bf16[2,48,256]{2,1,0:T(8,128)(2,1)S(1)}, u32[]{:S(2)}, u32[]{:S(2)}) collective-permute-start(bf16[2,48,256]{2,1,0:T(8,128)(2,1)S(1)} %get-tuple-element.59), channel_id=1, source_target_pairs={{1,0},{2,1},{3,2},{4,3},{5,4},{6,5},{7,6},{9,8},{10,9},{11,10},{12... | collective-permute-start | bytes 147464 | tf_op jit(solution)/shard_map/ppermute | solution.py:17
  7.3 8.5 %collective-permute-start.2 = (bf16[2,48,256]{2,1,0:T(8,128)(2,1)S(1)}, bf16[2,48,256]{2,1,0:T(8,128)(2,1)S(1)}, u32[]{:S(2)}, u32[]{:S(2)}) collective-permute-start(bf16[2,48,256]{2,1,0:T(8,128)(2,1)S(1)} %pad_maximum_fusion.6), channel_id=1, source_target_pairs={{0,128},{8,136},{16,144},{24,152},{32,160},{40,168},{48,176},{56,1... | collective-permute-start | bytes 147464 | tf_op jit(solution)/shard_map/ppermute | solution.py:27
  15.9 5.6 %collective-permute-start.3 = (bf16[52,2,256]{2,1,0:T(2,128)(2,1)S(1)}, bf16[52,2,256]{2,1,0:T(2,128)(2,1)S(1)}, u32[]{:S(2)}, u32[]{:S(2)}) collective-permute-start(bf16[52,2,256]{2,1,0:T(2,128)(2,1)S(1)} %get-tuple-element.54), channel_id=1, source_target_pairs={{0,8},{8,16},{16,24},{24,32},{32,40},{40,48},{48,56},{56,64},{64,7... | collective-permute-start | bytes 159752 | tf_op jit(solution)/shard_map/ppermute | solution.py:15
  20.3 5.1 %collective-permute-start.4 = (bf16[52,2,256]{2,1,0:T(2,128)(2,1)S(1)}, bf16[52,2,256]{2,1,0:T(2,128)(2,1)S(1)}, u32[]{:S(2)}, u32[]{:S(2)}) collective-permute-start(bf16[52,2,256]{2,1,0:T(2,128)(2,1)S(1)} %get-tuple-element.55), channel_id=1, source_target_pairs={{8,0},{16,8},{24,16},{32,24},{40,32},{48,40},{56,48},{64,56},{72,6... | collective-permute-start | bytes 159752 | tf_op jit(solution)/shard_map/ppermute | solution.py:17
  26.6 1.0 copy-start.3
  26.6 1.0 copy-start.7
  29.8 1.3 %copy-start.5 = (f32[128]{0:T(128)S(1)}, f32[128]{0:T(128)}, u32[]{:S(2)}) copy-start(f32[128]{0:T(128)} %param.14) | copy-start | bytes 1540
  37.9 0.8 copy-start.1
  38.8 7.6 %copy-start.4 = (bf16[3,3,128,128]{3,2,1,0:T(8,128)(2,1)S(1)}, bf16[3,3,128,128]{3,2,1,0:T(8,128)(2,1)}, u32[]{:S(2)}) copy-start(bf16[3,3,128,128]{3,2,1,0:T(8,128)(2,1)} %param.13) | copy-start | bytes 884740
  41.2 1.9 %collective-permute-start.6 = (f32[73792]{0:T(1024)S(1)}, f32[73792]{0:T(1024)S(1)}, u32[]{:S(2)}, u32[]{:S(2)}) collective-permute-start(f32[73792]{0:T(1024)S(1)} %dynamic_slice.19), channel_id=1, source_target_pairs={{0,8},{8,0},{16,24},{24,16},{32,40},{40,32},{48,56},{56,48},{64,72... | collective-permute-start | bytes 885512 | tf_op jit(solution)/shard_map/ppermute | solution.py:44
  44.3 6.3 %collective-permute-start.7 = (f32[36896]{0:T(1024)S(1)}, f32[36896]{0:T(1024)S(1)}, u32[]{:S(2)}, u32[]{:S(2)}) collective-permute-start(f32[36896]{0:T(1024)S(1)} %dynamic_slice.21), channel_id=1, source_target_pairs={{0,1},{1,0},{2,3},{3,2},{4,5},{5,4},{6,7},{7,6},{8,9},{9,8},{10,11... | collective-permute-start | bytes 442760 | tf_op jit(solution)/shard_map/ppermute | solution.py:44
  50.8 3.3 %collective-permute-start.8 = (f32[18448]{0:T(1024)S(1)}, f32[18448]{0:T(1024)S(1)}, u32[]{:S(2)}, u32[]{:S(2)}) collective-permute-start(f32[18448]{0:T(1024)S(1)} %dynamic_slice.23), channel_id=1, source_target_pairs={{0,32},{8,40},{16,48},{24,56},{32,0},{40,8},{48,16},{56,24},{64,96... | collective-permute-start | bytes 221384 | tf_op jit(solution)/shard_map/ppermute | solution.py:44
  54.2 4.7 %collective-permute-start.9 = (f32[18448]{0:T(1024)S(1)}, f32[18448]{0:T(1024)S(1)}, u32[]{:S(2)}, u32[]{:S(2)}) collective-permute-start(f32[18448]{0:T(1024)S(1)} %dynamic-slice_add_fusion.2), channel_id=1, source_target_pairs={{0,2},{1,3},{2,0},{3,1},{4,6},{5,7},{6,4},{7,5},{8,10},{9,11},{10,... | collective-permute-start | bytes 221384 | tf_op jit(solution)/shard_map/ppermute | solution.py:47
  58.9 4.8 %collective-permute-start.10 = (f32[18448]{0:T(1024)S(1)}, f32[18448]{0:T(1024)S(1)}, u32[]{:S(2)}, u32[]{:S(2)}) collective-permute-start(f32[18448]{0:T(1024)S(1)} %add.123), channel_id=1, source_target_pairs={{0,16},{8,24},{16,0},{24,8},{32,48},{40,56},{48,32},{56,40},{64,80... | collective-permute-start | bytes 221384 | tf_op jit(solution)/shard_map/ppermute | solution.py:47
  63.8 5.7 %collective-permute-start.11 = (f32[18448]{0:T(1024)S(1)}, f32[18448]{0:T(1024)S(1)}, u32[]{:S(2)}, u32[]{:S(2)}) collective-permute-start(f32[18448]{0:T(1024)S(1)} %add.124), channel_id=1, source_target_pairs={{0,64},{8,72},{16,80},{24,88},{32,96},{40,104},{48,112},{56,120},{... | collective-permute-start | bytes 221384 | tf_op jit(solution)/shard_map/ppermute | solution.py:47
  69.5 5.8 %collective-permute-start.12 = (f32[18448]{0:T(1024)S(1)}, f32[18448]{0:T(1024)S(1)}, u32[]{:S(2)}, u32[]{:S(2)}) collective-permute-start(f32[18448]{0:T(1024)S(1)} %add.125), channel_id=1, source_target_pairs={{0,192},{8,200},{16,208},{24,216},{32,224},{40,232},{48,240},{56,2... | collective-permute-start | bytes 221384 | tf_op jit(solution)/shard_map/ppermute | solution.py:47
  72.9 16.3 %collective-permute-start.5 = (bf16[2,48,128]{2,1,0:T(8,128)(2,1)S(1)}, bf16[2,48,128]{2,1,0:T(8,128)(2,1)S(1)}, u32[]{:S(2)}, u32[]{:S(2)}) collective-permute-start(bf16[2,48,128]{2,1,0:T(8,128)(2,1)S(1)} %pad_maximum_fusion.7), channel_id=1, source_target_pairs={{0,128},{8,136},{16,144},{24,152},{32,160},{40,168},{48,176},{56,1... | collective-permute-start | bytes 73736 | tf_op jit(solution)/shard_map/ppermute | solution.py:27
  75.3 5.1 %collective-permute-start.13 = (f32[18448]{0:T(1024)S(1)}, f32[18448]{0:T(1024)S(1)}, u32[]{:S(2)}, u32[]{:S(2)}) collective-permute-start(f32[18448]{0:T(1024)S(1)} %add.126), channel_id=1, source_target_pairs={{0,6},{1,7},{2,4},{3,5},{4,2},{5,3},{6,0},{7,1},{8,14},{9,15},{10,... | collective-permute-start | bytes 221384 | tf_op jit(solution)/shard_map/ppermute | solution.py:47
  80.4 4.4 %collective-permute-start.14 = (f32[18448]{0:T(1024)S(1)}, f32[18448]{0:T(1024)S(1)}, u32[]{:S(2)}, u32[]{:S(2)}) collective-permute-start(f32[18448]{0:T(1024)S(1)} %add.127), channel_id=1, source_target_pairs={{0,32},{8,40},{16,48},{24,56},{32,0},{40,8},{48,16},{56,24},{64,96... | collective-permute-start | bytes 221384 | tf_op jit(solution)/shard_map/ppermute | solution.py:51
  83.8 1.5 %copy-start.6 = (pred[8,7]{0,1:T(8,128)(4,1)S(1)}, pred[8,7]{0,1:T(8,128)(4,1)}, u32[]{:S(2)}) copy-start(pred[8,7]{0,1:T(8,128)(4,1)} %constant.203) | copy-start | bytes 172
  84.9 4.3 %collective-permute-start.15 = (f32[36896]{0:T(1024)S(1)}, f32[36896]{0:T(1024)S(1)}, u32[]{:S(2)}, u32[]{:S(2)}) collective-permute-start(f32[36896]{0:T(1024)S(1)} %maximum_select_fusion.2), channel_id=1, source_target_pairs={{0,1},{1,0},{2,3},{3,2},{4,5},{5,4},{6,7},{7,6},{8,9},{9,8},{10,11... | collective-permute-start | bytes 442760 | tf_op jit(solution)/shard_map/ppermute | solution.py:51
  87.2 1.1 %copy-start = (f32[48,8,7,128]{3,1,2,0:T(8,128)}, f32[48,8,7,128]{3,1,2,0:T(8,128)S(1)}, u32[]{:S(2)}) copy-start(f32[48,8,7,128]{3,1,2,0:T(8,128)S(1)} %convolution_select_fusion) | copy-start | bytes 4128772
  88.4 0.7 slice-start
  89.3 9.1 %collective-permute-start.16 = (f32[73792]{0:T(1024)S(1)}, f32[73792]{0:T(1024)S(1)}, u32[]{:S(2)}, u32[]{:S(2)}) collective-permute-start(f32[73792]{0:T(1024)S(1)} %maximum_select_fusion.1), channel_id=1, source_target_pairs={{0,8},{8,0},{16,24},{24,16},{32,40},{40,32},{48,56},{56,48},{64,72... | collective-permute-start | bytes 885512 | tf_op jit(solution)/shard_map/ppermute | solution.py:51

commit v9 on v4

--- a/solution.py
+++ b/solution.py
@@ -140,9 +140,6 @@
             )
         polar.append(ring)
     polar_in = from_behind(jnp.stack(polar).astype(jnp.bfloat16), "lon", half).astype(jnp.float32)
-    cell_grad = cell_grad.at[0].add(jnp.where(band == 0, polar_in[0], 0.0))
-    cell_grad = cell_grad.at[-1].add(jnp.where(band == bands - 1, polar_in[1], 0.0))
-    input_grad = cell_grad.astype(jnp.bfloat16)
     taps = []
     for tap_a in range(3):
         for tap_b in range(3):
@@ -155,8 +152,13 @@
     kernel_terms = jnp.concatenate(taps, axis=0)
     bias_terms = jnp.sum(pre_grad.astype(jnp.float32), axis=0)[None, :]
     order = pairing_order(("lon", "lat"))
-    sums = butterfly_sum(jnp.concatenate([kernel_terms, bias_terms], axis=0), order[:3], doubling_plan(order[3:]))
+    terms, polar_in = lax.optimization_barrier((jnp.concatenate([kernel_terms, bias_terms], axis=0), polar_in))
+    sums = butterfly_sum(terms, order[:3], doubling_plan(order[3:]))
     kernel_sum, bias_sum = sums[:-1], sums[-1:]
+    cell_grad = cell_grad.at[0].add(jnp.where(band == 0, polar_in[0], 0.0))
+    cell_grad = cell_grad.at[-1].add(jnp.where(band == bands - 1, polar_in[1], 0.0))
+    input_grad = cell_grad.astype(jnp.bfloat16)
+
     total_cells = rows * cols * lax.axis_size("lon") * lax.axis_size("lat")
     scale = 1.0 / jnp.sqrt(jnp.float32(total_cells))
     weight_grad = kernel_sum.reshape(3, 3, chans, chans) * scale

time: 96.9 us -> 102 us (1.053)
  waiting for transfers between devices: 19.7 us -> 33.6 us
  matrix products: 13.5 us -> 9.06 us
  starting transfers between devices: 47 us -> 43.2 us
    ppermute x5, waiting for transfers between devices: 6.51 us -> 16.9 us  [butterfly_sum(): data = data + lax.ppermute(data, axis, pairs)]
    dot_general x6, matrix products: 5.31 us -> 0.87 us  [shards(): jnp.dot(grad_ext[line_at, tap_b:tap_b + cols], weight[tap_a, 2 - tap_b].T...]
    ppermute x5, starting transfers between devices: 12 us -> 7.82 us  [butterfly_sum(): data = data + lax.ppermute(data, axis, pairs)]
    ppermute x2, starting transfers between devices: 9.94 us -> 12.9 us  [from_behind(): return lax.ppermute(value, axis, pairs)]
    ppermute x3, starting transfers between devices: 12.2 us -> 9.54 us  [butterfly_sum(): other = lax.ppermute(data, axis, pairs)]
    ppermute x3, waiting for transfers between devices: 5.36 us -> 7.55 us  [butterfly_sum(): data = keep + lax.ppermute(send, axis, pairs)]
    ppermute x3, waiting for transfers between devices: 1.9 us -> 3.29 us  [butterfly_sum(): other = lax.ppermute(data, axis, pairs)]
  transfers between devices with their start and end apart: 17 -> 17, of which waited for: 13 -> 14; matrix products, arithmetic and copies ran while one was open for 12% -> 10% of each run, Pallas kernels for 0% -> 0%
where the time goes in v9:
time: 102 us
  starting transfers between devices  43.2 us (42%)
  waiting for transfers between devices  33.6 us (33%)
  matrix products  9.06 us (9%)
  other arithmetic  8.38 us (8%)
  local copies, waits for them, and re-layouts  6.74 us (7%)
  between operations  1.07 us (1%)
    ppermute x5, waiting for transfers between devices, butterfly_sum(): data = data + lax.ppermute(data, axis, pairs)  16.9 us
    ppermute x2, starting transfers between devices, from_behind(): return lax.ppermute(value, axis, pairs)  12.9 us
    ppermute x3, starting transfers between devices, butterfly_sum(): other = lax.ppermute(data, axis, pairs)  9.54 us
    ppermute x5, starting transfers between devices, butterfly_sum(): data = data + lax.ppermute(data, axis, pairs)  7.82 us
    ppermute x3, waiting for transfers between devices, butterfly_sum(): data = keep + lax.ppermute(send, axis, pairs)  7.55 us
    ppermute x2, starting transfers between devices, extended(): lax.ppermute(tail, axis, [(i, (i + 1) % count) for i in range(ends)])  6.42 us
    ppermute x3, starting transfers between devices, butterfly_sum(): data = keep + lax.ppermute(send, axis, pairs)  5.18 us
    dot_general x9, matrix products, shards(): lax.dot_general(window, pre_grad, (((0,), (0,)), ((), ())), preferred_ele...  4.47 us
  transfers between devices with their start and end apart: 17, of which 14 were waited for; matrix products, arithmetic and copies ran while one was open for 10% of the time, Pallas kernels for 0%

profile of v9, /device:TPU:1, one launch (start us, length us, event | category | flops | bytes accessed | tf_op | source)
XLA Modules:
  0.0 102.1 jit_solution(2916002233926950846)
XLA Ops:
  0.6 1.2 %constant_dynamic-update-slice_fusion.1 = bf16[48,48,256]{2,1,0:T(8,128)(2,1)S(1)} fusion(bf16[48,48,128]{2,1,0:T(8,128)(2,1)} %param.12), kind=kLoop, calls=%fused_computation.111 | loop fusion | bytes 1179648
  2.1 4.2 %collective-permute-start = (bf16[48,2,256]{2,1,0:T(2,128)(2,1)S(1)}, bf16[48,2,256]{2,1,0:T(2,128)(2,1)S(1)}, u32[]{:S(2)}, u32[]{:S(2)}) collective-permute-start(bf16[48,2,256]{2,1,0:T(2,128)(2,1)S(1)} %get-tuple-element.61), channel_id=1, source_target_pairs={{0,8},{8,16},{16,24},{24,32},{32,40},{40,48},{48,56},{56,64},{64,7... | collective-permute-start | bytes 147464 | tf_op jit(solution)/shard_map/ppermute | solution.py:15
  6.3 1.2 %collective-permute-done = bf16[48,2,256]{2,1,0:T(2,128)(2,1)S(1)} collective-permute-done((bf16[48,2,256]{2,1,0:T(2,128)(2,1)S(1)}, bf16[48,2,256]{2,1,0:T(2,128)(2,1)S(1)}, u32[]{:S(2)}, u32[]{:S(2)}) %collective-permute-start) | collective-permute-done | bytes 49184 | tf_op jit(solution)/shard_map/ppermute | solution.py:15
  7.5 3.8 %collective-permute-done.1 = bf16[48,2,256]{2,1,0:T(2,128)(2,1)S(1)} collective-permute-done((bf16[48,2,256]{2,1,0:T(2,128)(2,1)S(1)}, bf16[48,2,256]{2,1,0:T(2,128)(2,1)S(1)}, u32[]{:S(2)}, u32[]{:S(2)}) %collective-permute-start.1) | collective-permute-done | bytes 49184 | tf_op jit(solution)/shard_map/ppermute | solution.py:17
  11.4 2.2 %collective-permute-start.2 = (bf16[2,52,256]{2,1,0:T(8,128)(2,1)S(1)}, bf16[2,52,256]{2,1,0:T(8,128)(2,1)S(1)}, u32[]{:S(2)}, u32[]{:S(2)}) collective-permute-start(bf16[2,52,256]{2,1,0:T(8,128)(2,1)S(1)} %get-tuple-element.63), channel_id=1, source_target_pairs={{0,1},{1,2},{2,3},{3,4},{4,5},{5,6},{6,7},{8,9},{9,10},{10,11},{11... | collective-permute-start | bytes 159752 | tf_op jit(solution)/shard_map/ppermute | solution.py:15
  13.6 1.3 %collective-permute-start.3 = (bf16[2,52,256]{2,1,0:T(8,128)(2,1)S(1)}, bf16[2,52,256]{2,1,0:T(8,128)(2,1)S(1)}, u32[]{:S(2)}, u32[]{:S(2)}) collective-permute-start(bf16[2,52,256]{2,1,0:T(8,128)(2,1)S(1)} %get-tuple-element.64), channel_id=1, source_target_pairs={{1,0},{2,1},{3,2},{4,3},{5,4},{6,5},{7,6},{9,8},{10,9},{11,10},{12... | collective-permute-start | bytes 159752 | tf_op jit(solution)/shard_map/ppermute | solution.py:17
  15.0 7.2 %collective-permute-start.4 = (bf16[2,52,256]{2,1,0:T(8,128)(2,1)S(1)}, bf16[2,52,256]{2,1,0:T(8,128)(2,1)S(1)}, u32[]{:S(2)}, u32[]{:S(2)}) collective-permute-start(bf16[2,52,256]{2,1,0:T(8,128)(2,1)S(1)} %get-tuple-element.58), channel_id=1, source_target_pairs={{0,128},{8,136},{16,144},{24,152},{32,160},{40,168},{48,176},{56,1... | collective-permute-start | bytes 159752 | tf_op jit(solution)/shard_map/ppermute | solution.py:27
  22.2 0.8 pad_maximum_fusion
  23.0 0.9 collective-permute-done.4
  24.1 0.9 copy-done
  25.3 0.7 copy-done.3
  26.0 1.9 %convolution_select_fusion.1 = f32[50,8,7,128]{3,1,2,0:T(8,128)S(1)} fusion(bf16[3,3,128,128]{3,2,1,0:T(8,128)(2,1)S(1)} %copy-done.3, bf16[52,1,7,2,128]{4,2,3,0,1:T(8,128)(2,1)S(1)} %slice.267, bf16[52,1,8,7,128]{4,2,3,0,1:T(8,128)(2,1)S(1)} %copy.10, pred[8,7]{0,1:T(8,128)(4,1)S(1)} %copy-done.7), kind=kOutput, calls=%fused_computation.10 | convolution fusion | flops 828987392 | bytes 2660408 | tf_op jit(solution)/shard_map/conv_general_dilated | solution.py:108
  28.3 1.2 %reshape.171 = f32[50,1,56,128]{3,2,0,1:T(8,128)} reshape(f32[50,8,7,128]{3,2,1,0:T(8,128)S(1)} %copy.11) | data formatting | bytes 2867200 | tf_op jit(solution)/shard_map/conv_general_dilated | solution.py:108
  29.5 2.5 %fusion.29 = (bf16[50,50,128]{2,1,0:T(8,128)(2,1)S(1)}, f32[50,50,128]{2,1,0:T(8,128)S(1)}) fusion(bf16[52,52,256]{2,1,0:T(8,128)(2,1)} %copy-done, pred[50]{0:T(512)(128)(4,1)S(1)} %and_or_fusion, f32[128]{0:T(128)S(1)} %copy-done.5, f32[50,1,56,128]{3,2,0,1:T(8,128)} %reshape.171), kind=kLoop, calls=%fused_computation.52 | loop fusion | flops 3840000 | bytes 3840562 | tf_op jit(solution)/shard_map/jit(_where)/select_n | solution.py:121
  32.3 0.5 fusion.12
  33.4 5.7 %collective-permute-start.5 = (bf16[2,48,128]{2,1,0:T(8,128)(2,1)S(1)}, bf16[2,48,128]{2,1,0:T(8,128)(2,1)S(1)}, u32[]{:S(2)}, u32[]{:S(2)}) collective-permute-start(bf16[2,48,128]{2,1,0:T(8,128)(2,1)S(1)} %pad_maximum_fusion.1), channel_id=1, source_target_pairs={{0,128},{8,136},{16,144},{24,152},{32,160},{40,168},{48,176},{56,1... | collective-permute-start | bytes 73736 | tf_op jit(solution)/shard_map/ppermute | solution.py:27
  39.2 0.5 fusion.11
  39.7 0.5 fusion.10
  40.2 0.5 fusion.9
  40.7 0.5 fusion.8
  41.2 0.5 fusion.7
  41.7 0.5 fusion.6
  42.2 0.5 fusion.5
  42.7 0.5 fusion.4
  43.7 1.8 %collective-permute-start.6 = (f32[73792]{0:T(1024)S(1)}, f32[73792]{0:T(1024)S(1)}, u32[]{:S(2)}, u32[]{:S(2)}) collective-permute-start(f32[73792]{0:T(1024)S(1)} %dynamic_slice.19), channel_id=1, source_target_pairs={{0,8},{8,0},{16,24},{24,16},{32,40},{40,32},{48,56},{56,48},{64,72... | collective-permute-start | bytes 885512 | tf_op jit(solution)/shard_map/ppermute | solution.py:44
  45.5 1.2 %collective-permute-done.6 = f32[73792]{0:T(1024)S(1)} collective-permute-done((f32[73792]{0:T(1024)S(1)}, f32[73792]{0:T(1024)S(1)}, u32[]{:S(2)}, u32[]{:S(2)}) %collective-permute-start.6) | collective-permute-done | bytes 295200 | tf_op jit(solution)/shard_map/ppermute | solution.py:44
  47.0 2.4 %collective-permute-start.7 = (f32[36896]{0:T(1024)S(1)}, f32[36896]{0:T(1024)S(1)}, u32[]{:S(2)}, u32[]{:S(2)}) collective-permute-start(f32[36896]{0:T(1024)S(1)} %dynamic_slice.21), channel_id=1, source_target_pairs={{0,1},{1,0},{2,3},{3,2},{4,5},{5,4},{6,7},{7,6},{8,9},{9,8},{10,11... | collective-permute-start | bytes 442760 | tf_op jit(solution)/shard_map/ppermute | solution.py:44
  49.4 3.9 %collective-permute-done.7 = f32[36896]{0:T(1024)S(1)} collective-permute-done((f32[36896]{0:T(1024)S(1)}, f32[36896]{0:T(1024)S(1)}, u32[]{:S(2)}, u32[]{:S(2)}) %collective-permute-start.7) | collective-permute-done | bytes 147616 | tf_op jit(solution)/shard_map/ppermute | solution.py:44
  53.6 0.9 collective-permute-start.8
  54.5 2.4 %collective-permute-done.8 = f32[18448]{0:T(1024)S(1)} collective-permute-done((f32[18448]{0:T(1024)S(1)}, f32[18448]{0:T(1024)S(1)}, u32[]{:S(2)}, u32[]{:S(2)}) %collective-permute-start.8) | collective-permute-done | bytes 73824 | tf_op jit(solution)/shard_map/ppermute | solution.py:44
  57.0 2.3 %collective-permute-start.9 = (f32[18448]{0:T(1024)S(1)}, f32[18448]{0:T(1024)S(1)}, u32[]{:S(2)}, u32[]{:S(2)}) collective-permute-start(f32[18448]{0:T(1024)S(1)} %dynamic-slice_add_fusion.2), channel_id=1, source_target_pairs={{0,2},{1,3},{2,0},{3,1},{4,6},{5,7},{6,4},{7,5},{8,10},{9,11},{10,... | collective-permute-start | bytes 221384 | tf_op jit(solution)/shard_map/ppermute | solution.py:47
  59.4 1.8 %collective-permute-done.9 = f32[18448]{0:T(1024)S(1)} collective-permute-done((f32[18448]{0:T(1024)S(1)}, f32[18448]{0:T(1024)S(1)}, u32[]{:S(2)}, u32[]{:S(2)}) %collective-permute-start.9) | collective-permute-done | bytes 73824 | tf_op jit(solution)/shard_map/ppermute | solution.py:47
  61.2 1.7 %collective-permute-start.10 = (f32[18448]{0:T(1024)S(1)}, f32[18448]{0:T(1024)S(1)}, u32[]{:S(2)}, u32[]{:S(2)}) collective-permute-start(f32[18448]{0:T(1024)S(1)} %add.123), channel_id=1, source_target_pairs={{0,16},{8,24},{16,0},{24,8},{32,48},{40,56},{48,32},{56,40},{64,80... | collective-permute-start | bytes 221384 | tf_op jit(solution)/shard_map/ppermute | solution.py:47
  62.8 3.2 %collective-permute-done.10 = f32[18448]{0:T(1024)S(1)} collective-permute-done((f32[18448]{0:T(1024)S(1)}, f32[18448]{0:T(1024)S(1)}, u32[]{:S(2)}, u32[]{:S(2)}) %collective-permute-start.10) | collective-permute-done | bytes 73824 | tf_op jit(solution)/shard_map/ppermute | solution.py:47
  66.2 4.9 %collective-permute-done.11 = f32[18448]{0:T(1024)S(1)} collective-permute-done((f32[18448]{0:T(1024)S(1)}, f32[18448]{0:T(1024)S(1)}, u32[]{:S(2)}, u32[]{:S(2)}) %collective-permute-start.11) | collective-permute-done | bytes 73824 | tf_op jit(solution)/shard_map/ppermute | solution.py:47
  71.1 0.6 collective-permute-start.12
  71.7 5.4 %collective-permute-done.12 = f32[18448]{0:T(1024)S(1)} collective-permute-done((f32[18448]{0:T(1024)S(1)}, f32[18448]{0:T(1024)S(1)}, u32[]{:S(2)}, u32[]{:S(2)}) %collective-permute-start.12) | collective-permute-done | bytes 73824 | tf_op jit(solution)/shard_map/ppermute | solution.py:47
  77.1 3.0 %collective-permute-start.13 = (f32[18448]{0:T(1024)S(1)}, f32[18448]{0:T(1024)S(1)}, u32[]{:S(2)}, u32[]{:S(2)}) collective-permute-start(f32[18448]{0:T(1024)S(1)} %add.126), channel_id=1, source_target_pairs={{0,6},{1,7},{2,4},{3,5},{4,2},{5,3},{6,0},{7,1},{8,14},{9,15},{10,... | collective-permute-start | bytes 221384 | tf_op jit(solution)/shard_map/ppermute | solution.py:47
  80.5 1.7 %collective-permute-done.13 = f32[18448]{0:T(1024)S(1)} collective-permute-done((f32[18448]{0:T(1024)S(1)}, f32[18448]{0:T(1024)S(1)}, u32[]{:S(2)}, u32[]{:S(2)}) %collective-permute-start.13) | collective-permute-done | bytes 73824 | tf_op jit(solution)/shard_map/ppermute | solution.py:47
  82.3 1.1 %fusion.3 = bf16[48,48,128]{2,1,0:T(8,128)(2,1)} fusion(f32[50,50,128]{2,1,0:T(8,128)S(1)} %add_divide_fusion, f32[50,50,128]{2,1,0:T(8,128)S(1)} %get-tuple-element.57), kind=kLoop, calls=%fused_computation.12 | loop fusion | flops 589824 | bytes 2949120 | tf_op jit(solution)/shard_map/convert.4
  83.9 1.6 %collective-permute-done.14 = f32[18448]{0:T(1024)S(1)} collective-permute-done((f32[18448]{0:T(1024)S(1)}, f32[18448]{0:T(1024)S(1)}, u32[]{:S(2)}, u32[]{:S(2)}) %collective-permute-start.14) | collective-permute-done | bytes 73824 | tf_op jit(solution)/shard_map/ppermute | solution.py:51
  86.0 1.8 %convolution_select_fusion = f32[48,8,7,128]{3,1,2,0:T(8,128)S(1)} fusion(bf16[3,3,128,128]{3,2,1,0:T(8,128)(2,1)S(1)} %copy-done.4, bf16[50,1,7,2,128]{4,2,3,0,1:T(8,128)(2,1)S(1)} %slice.272, bf16[50,1,8,7,128]{4,2,3,0,1:T(8,128)(2,1)S(1)} %copy.13, pred[8,7]{0,1:T(8,128)(4,1)S(1)} %copy-done.6), kind=kOutput, calls=%fused_computation.5 | convolution fusion | flops 795832320 | bytes 2567224 | tf_op jit(solution)/shard_map/conv_general_dilated | solution.py:124
  88.2 0.4 copy.21
  88.6 1.4 %collective-permute-done.15 = f32[36896]{0:T(1024)S(1)} collective-permute-done((f32[36896]{0:T(1024)S(1)}, f32[36896]{0:T(1024)S(1)}, u32[]{:S(2)}, u32[]{:S(2)}) %collective-permute-start.15) | collective-permute-done | bytes 147616 | tf_op jit(solution)/shard_map/ppermute | solution.py:51
  90.2 9.1 %collective-permute-start.16 = (f32[73792]{0:T(1024)S(1)}, f32[73792]{0:T(1024)S(1)}, u32[]{:S(2)}, u32[]{:S(2)}) collective-permute-start(f32[73792]{0:T(1024)S(1)} %maximum_select_fusion.1), channel_id=1, source_target_pairs={{0,8},{8,0},{16,24},{24,16},{32,40},{40,32},{48,56},{56,48},{64,72... | collective-permute-start | bytes 885512 | tf_op jit(solution)/shard_map/ppermute | solution.py:51
  99.3 0.9 convert_element_type.22
  100.7 0.5 slice_multiply_fusion.2
  101.2 0.9 slice_multiply_fusion.1
  (70 shorter events, 5.8 us)
Async XLA Ops:
  0.6 1.2 %copy-start.2 = (bf16[48,48,128]{2,1,0:T(8,128)(2,1)S(1)}, bf16[48,48,128]{2,1,0:T(8,128)(2,1)}, u32[]{:S(2)}) copy-start(bf16[48,48,128]{2,1,0:T(8,128)(2,1)} %param.15) | copy-start | bytes 1769476
  2.1 5.4 %collective-permute-start = (bf16[48,2,256]{2,1,0:T(2,128)(2,1)S(1)}, bf16[48,2,256]{2,1,0:T(2,128)(2,1)S(1)}, u32[]{:S(2)}, u32[]{:S(2)}) collective-permute-start(bf16[48,2,256]{2,1,0:T(2,128)(2,1)S(1)} %get-tuple-element.61), channel_id=1, source_target_pairs={{0,8},{8,16},{16,24},{24,32},{32,40},{40,48},{48,56},{56,64},{64,7... | collective-permute-start | bytes 147464 | tf_op jit(solution)/shard_map/ppermute | solution.py:15
  6.3 5.0 %collective-permute-start.1 = (bf16[48,2,256]{2,1,0:T(2,128)(2,1)S(1)}, bf16[48,2,256]{2,1,0:T(2,128)(2,1)S(1)}, u32[]{:S(2)}, u32[]{:S(2)}) collective-permute-start(bf16[48,2,256]{2,1,0:T(2,128)(2,1)S(1)} %get-tuple-element.62), channel_id=1, source_target_pairs={{8,0},{16,8},{24,16},{32,24},{40,32},{48,40},{56,48},{64,56},{72,6... | collective-permute-start | bytes 147464 | tf_op jit(solution)/shard_map/ppermute | solution.py:17
  11.4 10.8 %collective-permute-start.2 = (bf16[2,52,256]{2,1,0:T(8,128)(2,1)S(1)}, bf16[2,52,256]{2,1,0:T(8,128)(2,1)S(1)}, u32[]{:S(2)}, u32[]{:S(2)}) collective-permute-start(bf16[2,52,256]{2,1,0:T(8,128)(2,1)S(1)} %get-tuple-element.63), channel_id=1, source_target_pairs={{0,1},{1,2},{2,3},{3,4},{4,5},{5,6},{6,7},{8,9},{9,10},{10,11},{11... | collective-permute-start | bytes 159752 | tf_op jit(solution)/shard_map/ppermute | solution.py:15
  13.6 8.6 %collective-permute-start.3 = (bf16[2,52,256]{2,1,0:T(8,128)(2,1)S(1)}, bf16[2,52,256]{2,1,0:T(8,128)(2,1)S(1)}, u32[]{:S(2)}, u32[]{:S(2)}) collective-permute-start(bf16[2,52,256]{2,1,0:T(8,128)(2,1)S(1)} %get-tuple-element.64), channel_id=1, source_target_pairs={{1,0},{2,1},{3,2},{4,3},{5,4},{6,5},{7,6},{9,8},{10,9},{11,10},{12... | collective-permute-start | bytes 159752 | tf_op jit(solution)/shard_map/ppermute | solution.py:17
  15.0 8.9 %collective-permute-start.4 = (bf16[2,52,256]{2,1,0:T(8,128)(2,1)S(1)}, bf16[2,52,256]{2,1,0:T(8,128)(2,1)S(1)}, u32[]{:S(2)}, u32[]{:S(2)}) collective-permute-start(bf16[2,52,256]{2,1,0:T(8,128)(2,1)S(1)} %get-tuple-element.58), channel_id=1, source_target_pairs={{0,128},{8,136},{16,144},{24,152},{32,160},{40,168},{48,176},{56,1... | collective-permute-start | bytes 159752 | tf_op jit(solution)/shard_map/ppermute | solution.py:27
  23.9 1.1 %copy-start = (bf16[52,52,256]{2,1,0:T(8,128)(2,1)}, bf16[52,52,256]{2,1,0:T(8,128)(2,1)S(1)}, u32[]{:S(2)}) copy-start(bf16[52,52,256]{2,1,0:T(8,128)(2,1)S(1)} %fusion.66) | copy-start | bytes 4153348
  25.0 1.0 copy-start.3
  25.0 1.0 copy-start.7
  28.3 1.3 %copy-start.5 = (f32[128]{0:T(128)S(1)}, f32[128]{0:T(128)}, u32[]{:S(2)}) copy-start(f32[128]{0:T(128)} %param.14) | copy-start | bytes 1540
  29.5 2.8 %copy-start.1 = (bf16[52,52,256]{2,1,0:T(8,128)(2,1)S(1)}, bf16[52,52,256]{2,1,0:T(8,128)(2,1)}, u32[]{:S(2)}) copy-start(bf16[52,52,256]{2,1,0:T(8,128)(2,1)} %copy-done) | copy-start | bytes 4153348
  33.4 10.1 %collective-permute-start.5 = (bf16[2,48,128]{2,1,0:T(8,128)(2,1)S(1)}, bf16[2,48,128]{2,1,0:T(8,128)(2,1)S(1)}, u32[]{:S(2)}, u32[]{:S(2)}) collective-permute-start(bf16[2,48,128]{2,1,0:T(8,128)(2,1)S(1)} %pad_maximum_fusion.1), channel_id=1, source_target_pairs={{0,128},{8,136},{16,144},{24,152},{32,160},{40,168},{48,176},{56,1... | collective-permute-start | bytes 73736 | tf_op jit(solution)/shard_map/ppermute | solution.py:27
  43.7 3.0 %collective-permute-start.6 = (f32[73792]{0:T(1024)S(1)}, f32[73792]{0:T(1024)S(1)}, u32[]{:S(2)}, u32[]{:S(2)}) collective-permute-start(f32[73792]{0:T(1024)S(1)} %dynamic_slice.19), channel_id=1, source_target_pairs={{0,8},{8,0},{16,24},{24,16},{32,40},{40,32},{48,56},{56,48},{64,72... | collective-permute-start | bytes 885512 | tf_op jit(solution)/shard_map/ppermute | solution.py:44
  47.0 6.4 %collective-permute-start.7 = (f32[36896]{0:T(1024)S(1)}, f32[36896]{0:T(1024)S(1)}, u32[]{:S(2)}, u32[]{:S(2)}) collective-permute-start(f32[36896]{0:T(1024)S(1)} %dynamic_slice.21), channel_id=1, source_target_pairs={{0,1},{1,0},{2,3},{3,2},{4,5},{5,4},{6,7},{7,6},{8,9},{9,8},{10,11... | collective-permute-start | bytes 442760 | tf_op jit(solution)/shard_map/ppermute | solution.py:44
  53.6 3.3 %collective-permute-start.8 = (f32[18448]{0:T(1024)S(1)}, f32[18448]{0:T(1024)S(1)}, u32[]{:S(2)}, u32[]{:S(2)}) collective-permute-start(f32[18448]{0:T(1024)S(1)} %dynamic_slice.23), channel_id=1, source_target_pairs={{0,32},{8,40},{16,48},{24,56},{32,0},{40,8},{48,16},{56,24},{64,96... | collective-permute-start | bytes 221384 | tf_op jit(solution)/shard_map/ppermute | solution.py:44
  57.0 4.1 %collective-permute-start.9 = (f32[18448]{0:T(1024)S(1)}, f32[18448]{0:T(1024)S(1)}, u32[]{:S(2)}, u32[]{:S(2)}) collective-permute-start(f32[18448]{0:T(1024)S(1)} %dynamic-slice_add_fusion.2), channel_id=1, source_target_pairs={{0,2},{1,3},{2,0},{3,1},{4,6},{5,7},{6,4},{7,5},{8,10},{9,11},{10,... | collective-permute-start | bytes 221384 | tf_op jit(solution)/shard_map/ppermute | solution.py:47
  61.2 4.8 %collective-permute-start.10 = (f32[18448]{0:T(1024)S(1)}, f32[18448]{0:T(1024)S(1)}, u32[]{:S(2)}, u32[]{:S(2)}) collective-permute-start(f32[18448]{0:T(1024)S(1)} %add.123), channel_id=1, source_target_pairs={{0,16},{8,24},{16,0},{24,8},{32,48},{40,56},{48,32},{56,40},{64,80... | collective-permute-start | bytes 221384 | tf_op jit(solution)/shard_map/ppermute | solution.py:47
  66.0 5.1 %collective-permute-start.11 = (f32[18448]{0:T(1024)S(1)}, f32[18448]{0:T(1024)S(1)}, u32[]{:S(2)}, u32[]{:S(2)}) collective-permute-start(f32[18448]{0:T(1024)S(1)} %add.124), channel_id=1, source_target_pairs={{0,64},{8,72},{16,80},{24,88},{32,96},{40,104},{48,112},{56,120},{... | collective-permute-start | bytes 221384 | tf_op jit(solution)/shard_map/ppermute | solution.py:47
  71.1 6.0 %collective-permute-start.12 = (f32[18448]{0:T(1024)S(1)}, f32[18448]{0:T(1024)S(1)}, u32[]{:S(2)}, u32[]{:S(2)}) collective-permute-start(f32[18448]{0:T(1024)S(1)} %add.125), channel_id=1, source_target_pairs={{0,192},{8,200},{16,208},{24,216},{32,224},{40,232},{48,240},{56,2... | collective-permute-start | bytes 221384 | tf_op jit(solution)/shard_map/ppermute | solution.py:47
  77.1 5.1 %collective-permute-start.13 = (f32[18448]{0:T(1024)S(1)}, f32[18448]{0:T(1024)S(1)}, u32[]{:S(2)}, u32[]{:S(2)}) collective-permute-start(f32[18448]{0:T(1024)S(1)} %add.126), channel_id=1, source_target_pairs={{0,6},{1,7},{2,4},{3,5},{4,2},{5,3},{6,0},{7,1},{8,14},{9,15},{10,... | collective-permute-start | bytes 221384 | tf_op jit(solution)/shard_map/ppermute | solution.py:47
  82.2 3.3 %collective-permute-start.14 = (f32[18448]{0:T(1024)S(1)}, f32[18448]{0:T(1024)S(1)}, u32[]{:S(2)}, u32[]{:S(2)}) collective-permute-start(f32[18448]{0:T(1024)S(1)} %add.127), channel_id=1, source_target_pairs={{0,32},{8,40},{16,48},{24,56},{32,0},{40,8},{48,16},{56,24},{64,96... | collective-permute-start | bytes 221384 | tf_op jit(solution)/shard_map/ppermute | solution.py:51
  83.7 2.3 %copy-start.4 = (bf16[3,3,128,128]{3,2,1,0:T(8,128)(2,1)S(1)}, bf16[3,3,128,128]{3,2,1,0:T(8,128)(2,1)}, u32[]{:S(2)}) copy-start(bf16[3,3,128,128]{3,2,1,0:T(8,128)(2,1)} %param.13) | copy-start | bytes 884740
  83.7 2.3 %copy-start.6 = (pred[8,7]{0,1:T(8,128)(4,1)S(1)}, pred[8,7]{0,1:T(8,128)(4,1)}, u32[]{:S(2)}) copy-start(pred[8,7]{0,1:T(8,128)(4,1)} %constant.203) | copy-start | bytes 172
  85.7 4.3 %collective-permute-start.15 = (f32[36896]{0:T(1024)S(1)}, f32[36896]{0:T(1024)S(1)}, u32[]{:S(2)}, u32[]{:S(2)}) collective-permute-start(f32[36896]{0:T(1024)S(1)} %maximum_select_fusion.2), channel_id=1, source_target_pairs={{0,1},{1,0},{2,3},{3,2},{4,5},{5,4},{6,7},{7,6},{8,9},{9,8},{10,11... | collective-permute-start | bytes 442760 | tf_op jit(solution)/shard_map/ppermute | solution.py:51
  90.2 10.3 %collective-permute-start.16 = (f32[73792]{0:T(1024)S(1)}, f32[73792]{0:T(1024)S(1)}, u32[]{:S(2)}, u32[]{:S(2)}) collective-permute-start(f32[73792]{0:T(1024)S(1)} %maximum_select_fusion.1), channel_id=1, source_target_pairs={{0,8},{8,0},{16,24},{24,16},{32,40},{40,32},{48,56},{56,48},{64,72... | collective-permute-start | bytes 885512 | tf_op jit(solution)/shard_map/ppermute | solution.py:51

commit v10 on v4

--- a/solution.py
+++ b/solution.py
@@ -60,7 +60,7 @@
         while step < lax.axis_size(axis):
             near.append((axis, step))
             step *= 2
-    ranked = [("lon", 1), ("lat", 1), ("lon", 4), ("lat", 2)]
+    ranked = [("lon", 1), ("lon", 4), ("lat", 1), ("lat", 2)]
     first = [pair for pair in ranked if pair in near]
     rest = [pair for pair in near if pair not in first]
     return first + rest

time: 96.9 us -> 96.9 us (level)
  transfers between devices with their start and end apart: 17 -> 17, of which waited for: 13 -> 12; matrix products, arithmetic and copies ran while one was open for 12% -> 12% of each run, Pallas kernels for 0% -> 0%
where the time goes in v10:
time: 96.9 us; the launch traced here: 96.3 us
  starting transfers between devices  47.8 us (49%)
  waiting for transfers between devices  18.9 us (20%)
  matrix products  13.5 us (14%)
  other arithmetic  8.35 us (9%)
  local copies, waits for them, and re-layouts  6.75 us (7%)
  between operations  1.07 us (1%)
    ppermute x5, starting transfers between devices, butterfly_sum(): data = data + lax.ppermute(data, axis, pairs)  12.2 us
    ppermute x3, starting transfers between devices, butterfly_sum(): other = lax.ppermute(data, axis, pairs)  12.2 us
    ppermute x2, starting transfers between devices, from_behind(): return lax.ppermute(value, axis, pairs)  10.3 us
    ppermute x5, waiting for transfers between devices, butterfly_sum(): data = data + lax.ppermute(data, axis, pairs)  6.51 us
    ppermute x2, starting transfers between devices, extended(): lax.ppermute(tail, axis, [(i, (i + 1) % count) for i in range(ends)])  6.42 us
    ppermute x3, starting transfers between devices, butterfly_sum(): data = keep + lax.ppermute(send, axis, pairs)  5.38 us
    dot_general x6, matrix products, shards(): jnp.dot(grad_ext[line_at, tap_b:tap_b + cols], weight[tap_a, 2 - tap_b].T...  5.31 us
    ppermute x3, waiting for transfers between devices, butterfly_sum(): data = keep + lax.ppermute(send, axis, pairs)  4.86 us
  transfers between devices with their start and end apart: 17, of which 12 were waited for; matrix products, arithmetic and copies ran while one was open for 12% of the time, Pallas kernels for 0%

profile of v10, /device:TPU:1, one launch (start us, length us, event | category | flops | bytes accessed | tf_op | source)
XLA Modules:
  0.0 96.3 jit_solution(6172277982485480454)
XLA Ops:
  0.6 1.2 %constant_dynamic-update-slice_fusion.1 = bf16[48,48,256]{2,1,0:T(8,128)(2,1)S(1)} fusion(bf16[48,48,128]{2,1,0:T(8,128)(2,1)} %param.12), kind=kLoop, calls=%fused_computation.113 | loop fusion | bytes 1179648
  2.1 4.2 %collective-permute-start = (bf16[48,2,256]{2,1,0:T(2,128)(2,1)S(1)}, bf16[48,2,256]{2,1,0:T(2,128)(2,1)S(1)}, u32[]{:S(2)}, u32[]{:S(2)}) collective-permute-start(bf16[48,2,256]{2,1,0:T(2,128)(2,1)S(1)} %get-tuple-element.57), channel_id=1, source_target_pairs={{0,8},{8,16},{16,24},{24,32},{32,40},{40,48},{48,56},{56,64},{64,7... | collective-permute-start | bytes 147464 | tf_op jit(solution)/shard_map/ppermute | solution.py:15
  6.3 1.2 %collective-permute-done = bf16[48,2,256]{2,1,0:T(2,128)(2,1)S(1)} collective-permute-done((bf16[48,2,256]{2,1,0:T(2,128)(2,1)S(1)}, bf16[48,2,256]{2,1,0:T(2,128)(2,1)S(1)}, u32[]{:S(2)}, u32[]{:S(2)}) %collective-permute-start) | collective-permute-done | bytes 49184 | tf_op jit(solution)/shard_map/ppermute | solution.py:15
  7.5 3.8 %collective-permute-done.1 = bf16[48,2,256]{2,1,0:T(2,128)(2,1)S(1)} collective-permute-done((bf16[48,2,256]{2,1,0:T(2,128)(2,1)S(1)}, bf16[48,2,256]{2,1,0:T(2,128)(2,1)S(1)}, u32[]{:S(2)}, u32[]{:S(2)}) %collective-permute-start.1) | collective-permute-done | bytes 49184 | tf_op jit(solution)/shard_map/ppermute | solution.py:17
  11.4 2.2 %collective-permute-start.2 = (bf16[2,52,256]{2,1,0:T(8,128)(2,1)S(1)}, bf16[2,52,256]{2,1,0:T(8,128)(2,1)S(1)}, u32[]{:S(2)}, u32[]{:S(2)}) collective-permute-start(bf16[2,52,256]{2,1,0:T(8,128)(2,1)S(1)} %get-tuple-element.59), channel_id=1, source_target_pairs={{0,1},{1,2},{2,3},{3,4},{4,5},{5,6},{6,7},{8,9},{9,10},{10,11},{11... | collective-permute-start | bytes 159752 | tf_op jit(solution)/shard_map/ppermute | solution.py:15
  13.6 1.3 %collective-permute-start.3 = (bf16[2,52,256]{2,1,0:T(8,128)(2,1)S(1)}, bf16[2,52,256]{2,1,0:T(8,128)(2,1)S(1)}, u32[]{:S(2)}, u32[]{:S(2)}) collective-permute-start(bf16[2,52,256]{2,1,0:T(8,128)(2,1)S(1)} %get-tuple-element.60), channel_id=1, source_target_pairs={{1,0},{2,1},{3,2},{4,3},{5,4},{6,5},{7,6},{9,8},{10,9},{11,10},{12... | collective-permute-start | bytes 159752 | tf_op jit(solution)/shard_map/ppermute | solution.py:17
  15.0 7.2 %collective-permute-start.4 = (bf16[2,52,256]{2,1,0:T(8,128)(2,1)S(1)}, bf16[2,52,256]{2,1,0:T(8,128)(2,1)S(1)}, u32[]{:S(2)}, u32[]{:S(2)}) collective-permute-start(bf16[2,52,256]{2,1,0:T(8,128)(2,1)S(1)} %get-tuple-element.54), channel_id=1, source_target_pairs={{0,128},{8,136},{16,144},{24,152},{32,160},{40,168},{48,176},{56,1... | collective-permute-start | bytes 159752 | tf_op jit(solution)/shard_map/ppermute | solution.py:27
  22.2 0.8 pad_maximum_fusion
  23.0 0.9 collective-permute-done.4
  24.1 0.9 copy-done
  25.3 0.7 copy-done.3
  26.0 1.9 %convolution_select_fusion.1 = f32[50,8,7,128]{3,1,2,0:T(8,128)S(1)} fusion(bf16[3,3,128,128]{3,2,1,0:T(8,128)(2,1)S(1)} %copy-done.3, bf16[52,1,7,2,128]{4,2,3,0,1:T(8,128)(2,1)S(1)} %slice.267, bf16[52,1,8,7,128]{4,2,3,0,1:T(8,128)(2,1)S(1)} %copy.10, pred[8,7]{0,1:T(8,128)(4,1)S(1)} %copy-done.7), kind=kOutput, calls=%fused_computation.10 | convolution fusion | flops 828987392 | bytes 2660408 | tf_op jit(solution)/shard_map/conv_general_dilated | solution.py:108
  28.3 1.2 %reshape.171 = f32[50,1,56,128]{3,2,0,1:T(8,128)} reshape(f32[50,8,7,128]{3,2,1,0:T(8,128)S(1)} %copy.11) | data formatting | bytes 2867200 | tf_op jit(solution)/shard_map/conv_general_dilated | solution.py:108
  29.5 2.5 %fusion.29 = (bf16[50,50,128]{2,1,0:T(8,128)(2,1)S(1)}, f32[50,50,128]{2,1,0:T(8,128)S(1)}) fusion(bf16[52,52,256]{2,1,0:T(8,128)(2,1)} %copy-done, pred[50]{0:T(512)(128)(4,1)S(1)} %and_or_fusion, f32[128]{0:T(128)S(1)} %copy-done.5, f32[50,1,56,128]{3,2,0,1:T(8,128)} %reshape.171), kind=kLoop, calls=%fused_computation.52 | loop fusion | flops 3840000 | bytes 3840562 | tf_op jit(solution)/shard_map/jit(_where)/select_n | solution.py:121
  32.8 0.5 fusion.11
  33.8 0.5 fusion.9
  34.8 0.5 fusion.7
  35.8 0.5 fusion.5
  37.0 1.8 %collective-permute-start.6 = (f32[73792]{0:T(1024)S(1)}, f32[73792]{0:T(1024)S(1)}, u32[]{:S(2)}, u32[]{:S(2)}) collective-permute-start(f32[73792]{0:T(1024)S(1)} %dynamic_slice.19), channel_id=1, source_target_pairs={{0,8},{8,0},{16,24},{24,16},{32,40},{40,32},{48,56},{56,48},{64,72... | collective-permute-start | bytes 885512 | tf_op jit(solution)/shard_map/ppermute | solution.py:44
  38.8 0.9 fusion.54
  40.3 0.7 collective-permute-start.7
  41.0 0.9 convolution_add_fusion.1
  41.9 3.6 %collective-permute-done.7 = f32[36896]{0:T(1024)S(1)} collective-permute-done((f32[36896]{0:T(1024)S(1)}, f32[36896]{0:T(1024)S(1)}, u32[]{:S(2)}, u32[]{:S(2)}) %collective-permute-start.7) | collective-permute-done | bytes 147616 | tf_op jit(solution)/shard_map/ppermute | solution.py:44
  45.7 2.9 %collective-permute-start.8 = (f32[18448]{0:T(1024)S(1)}, f32[18448]{0:T(1024)S(1)}, u32[]{:S(2)}, u32[]{:S(2)}) collective-permute-start(f32[18448]{0:T(1024)S(1)} %dynamic_slice.23), channel_id=1, source_target_pairs={{0,1},{1,0},{2,3},{3,2},{4,5},{5,4},{6,7},{7,6},{8,9},{9,8},{10,11... | collective-permute-start | bytes 221384 | tf_op jit(solution)/shard_map/ppermute | solution.py:44
  48.6 0.9 fusion.58
  49.5 0.9 collective-permute-done.8
  50.5 3.0 %collective-permute-start.9 = (f32[18448]{0:T(1024)S(1)}, f32[18448]{0:T(1024)S(1)}, u32[]{:S(2)}, u32[]{:S(2)}) collective-permute-start(f32[18448]{0:T(1024)S(1)} %dynamic-slice_add_fusion.2), channel_id=1, source_target_pairs={{0,2},{1,3},{2,0},{3,1},{4,6},{5,7},{6,4},{7,5},{8,10},{9,11},{10,... | collective-permute-start | bytes 221384 | tf_op jit(solution)/shard_map/ppermute | solution.py:47
  53.5 0.9 convolution_add_fusion.3
  54.4 0.9 collective-permute-done.9
  55.3 0.6 collective-permute-start.10
  55.9 0.9 fusion.15
  56.8 3.3 %collective-permute-done.10 = f32[18448]{0:T(1024)S(1)} collective-permute-done((f32[18448]{0:T(1024)S(1)}, f32[18448]{0:T(1024)S(1)}, u32[]{:S(2)}, u32[]{:S(2)}) %collective-permute-start.10) | collective-permute-done | bytes 73824 | tf_op jit(solution)/shard_map/ppermute | solution.py:47
  60.1 2.8 %collective-permute-start.11 = (f32[18448]{0:T(1024)S(1)}, f32[18448]{0:T(1024)S(1)}, u32[]{:S(2)}, u32[]{:S(2)}) collective-permute-start(f32[18448]{0:T(1024)S(1)} %add.124), channel_id=1, source_target_pairs={{0,64},{8,72},{16,80},{24,88},{32,96},{40,104},{48,112},{56,120},{... | collective-permute-start | bytes 221384 | tf_op jit(solution)/shard_map/ppermute | solution.py:47
  63.0 0.9 fusion.16
  63.9 0.9 collective-permute-done.11
  64.8 2.8 %collective-permute-start.12 = (f32[18448]{0:T(1024)S(1)}, f32[18448]{0:T(1024)S(1)}, u32[]{:S(2)}, u32[]{:S(2)}) collective-permute-start(f32[18448]{0:T(1024)S(1)} %add.125), channel_id=1, source_target_pairs={{0,192},{8,200},{16,208},{24,216},{32,224},{40,232},{48,240},{56,2... | collective-permute-start | bytes 221384 | tf_op jit(solution)/shard_map/ppermute | solution.py:47
  67.6 3.1 %collective-permute-start.5 = (bf16[2,48,128]{2,1,0:T(8,128)(2,1)S(1)}, bf16[2,48,128]{2,1,0:T(8,128)(2,1)S(1)}, u32[]{:S(2)}, u32[]{:S(2)}) collective-permute-start(bf16[2,48,128]{2,1,0:T(8,128)(2,1)S(1)} %pad_maximum_fusion.1), channel_id=1, source_target_pairs={{0,128},{8,136},{16,144},{24,152},{32,160},{40,168},{48,176},{56,1... | collective-permute-start | bytes 73736 | tf_op jit(solution)/shard_map/ppermute | solution.py:27
  70.6 3.0 %collective-permute-start.13 = (f32[18448]{0:T(1024)S(1)}, f32[18448]{0:T(1024)S(1)}, u32[]{:S(2)}, u32[]{:S(2)}) collective-permute-start(f32[18448]{0:T(1024)S(1)} %add.126), channel_id=1, source_target_pairs={{0,6},{1,7},{2,4},{3,5},{4,2},{5,3},{6,0},{7,1},{8,14},{9,15},{10,... | collective-permute-start | bytes 221384 | tf_op jit(solution)/shard_map/ppermute | solution.py:47
  74.0 1.4 %collective-permute-done.13 = f32[18448]{0:T(1024)S(1)} collective-permute-done((f32[18448]{0:T(1024)S(1)}, f32[18448]{0:T(1024)S(1)}, u32[]{:S(2)}, u32[]{:S(2)}) %collective-permute-start.13) | collective-permute-done | bytes 73824 | tf_op jit(solution)/shard_map/ppermute | solution.py:47
  75.4 0.7 collective-permute-start.14
  76.1 1.1 %fusion.3 = bf16[48,48,128]{2,1,0:T(8,128)(2,1)} fusion(f32[50,50,128]{2,1,0:T(8,128)S(1)} %add_divide_fusion, f32[50,50,128]{2,1,0:T(8,128)S(1)} %get-tuple-element.53), kind=kLoop, calls=%fused_computation.12 | loop fusion | flops 589824 | bytes 2949120 | tf_op jit(solution)/shard_map/convert.4
  77.7 1.3 %collective-permute-done.14 = f32[18448]{0:T(1024)S(1)} collective-permute-done((f32[18448]{0:T(1024)S(1)}, f32[18448]{0:T(1024)S(1)}, u32[]{:S(2)}, u32[]{:S(2)}) %collective-permute-start.14) | collective-permute-done | bytes 73824 | tf_op jit(solution)/shard_map/ppermute | solution.py:51
  79.1 2.0 %collective-permute-start.15 = (f32[36896]{0:T(1024)S(1)}, f32[36896]{0:T(1024)S(1)}, u32[]{:S(2)}, u32[]{:S(2)}) collective-permute-start(f32[36896]{0:T(1024)S(1)} %maximum_select_fusion.2), channel_id=1, source_target_pairs={{0,32},{8,40},{16,48},{24,56},{32,0},{40,8},{48,16},{56,24},{64,96... | collective-permute-start | bytes 442760 | tf_op jit(solution)/shard_map/ppermute | solution.py:51
  81.2 1.8 %convolution_select_fusion = f32[48,8,7,128]{3,1,2,0:T(8,128)S(1)} fusion(bf16[3,3,128,128]{3,2,1,0:T(8,128)(2,1)S(1)} %copy-done.4, bf16[50,1,7,2,128]{4,2,3,0,1:T(8,128)(2,1)S(1)} %slice.272, bf16[50,1,8,7,128]{4,2,3,0,1:T(8,128)(2,1)S(1)} %copy.13, pred[8,7]{0,1:T(8,128)(4,1)S(1)} %copy-done.6), kind=kOutput, calls=%fused_computation.5 | convolution fusion | flops 795832320 | bytes 2567224 | tf_op jit(solution)/shard_map/conv_general_dilated | solution.py:124
  84.0 9.5 %collective-permute-start.16 = (f32[73792]{0:T(1024)S(1)}, f32[73792]{0:T(1024)S(1)}, u32[]{:S(2)}, u32[]{:S(2)}) collective-permute-start(f32[73792]{0:T(1024)S(1)} %maximum_select_fusion.1), channel_id=1, source_target_pairs={{0,8},{8,0},{16,24},{24,16},{32,40},{40,32},{48,56},{56,48},{64,72... | collective-permute-start | bytes 885512 | tf_op jit(solution)/shard_map/ppermute | solution.py:51
  93.5 0.9 convert_element_type.21
  94.9 0.5 slice_multiply_fusion.2
  95.4 0.9 slice_multiply_fusion.1
  (70 shorter events, 7.5 us)
Async XLA Ops:
  0.6 1.2 %copy-start.2 = (bf16[48,48,128]{2,1,0:T(8,128)(2,1)S(1)}, bf16[48,48,128]{2,1,0:T(8,128)(2,1)}, u32[]{:S(2)}) copy-start(bf16[48,48,128]{2,1,0:T(8,128)(2,1)} %param.15) | copy-start | bytes 1769476
  2.1 5.4 %collective-permute-start = (bf16[48,2,256]{2,1,0:T(2,128)(2,1)S(1)}, bf16[48,2,256]{2,1,0:T(2,128)(2,1)S(1)}, u32[]{:S(2)}, u32[]{:S(2)}) collective-permute-start(bf16[48,2,256]{2,1,0:T(2,128)(2,1)S(1)} %get-tuple-element.57), channel_id=1, source_target_pairs={{0,8},{8,16},{16,24},{24,32},{32,40},{40,48},{48,56},{56,64},{64,7... | collective-permute-start | bytes 147464 | tf_op jit(solution)/shard_map/ppermute | solution.py:15
  6.3 5.0 %collective-permute-start.1 = (bf16[48,2,256]{2,1,0:T(2,128)(2,1)S(1)}, bf16[48,2,256]{2,1,0:T(2,128)(2,1)S(1)}, u32[]{:S(2)}, u32[]{:S(2)}) collective-permute-start(bf16[48,2,256]{2,1,0:T(2,128)(2,1)S(1)} %get-tuple-element.58), channel_id=1, source_target_pairs={{8,0},{16,8},{24,16},{32,24},{40,32},{48,40},{56,48},{64,56},{72,6... | collective-permute-start | bytes 147464 | tf_op jit(solution)/shard_map/ppermute | solution.py:17
  11.4 10.8 %collective-permute-start.2 = (bf16[2,52,256]{2,1,0:T(8,128)(2,1)S(1)}, bf16[2,52,256]{2,1,0:T(8,128)(2,1)S(1)}, u32[]{:S(2)}, u32[]{:S(2)}) collective-permute-start(bf16[2,52,256]{2,1,0:T(8,128)(2,1)S(1)} %get-tuple-element.59), channel_id=1, source_target_pairs={{0,1},{1,2},{2,3},{3,4},{4,5},{5,6},{6,7},{8,9},{9,10},{10,11},{11... | collective-permute-start | bytes 159752 | tf_op jit(solution)/shard_map/ppermute | solution.py:15
  13.6 8.6 %collective-permute-start.3 = (bf16[2,52,256]{2,1,0:T(8,128)(2,1)S(1)}, bf16[2,52,256]{2,1,0:T(8,128)(2,1)S(1)}, u32[]{:S(2)}, u32[]{:S(2)}) collective-permute-start(bf16[2,52,256]{2,1,0:T(8,128)(2,1)S(1)} %get-tuple-element.60), channel_id=1, source_target_pairs={{1,0},{2,1},{3,2},{4,3},{5,4},{6,5},{7,6},{9,8},{10,9},{11,10},{12... | collective-permute-start | bytes 159752 | tf_op jit(solution)/shard_map/ppermute | solution.py:17
  15.0 8.9 %collective-permute-start.4 = (bf16[2,52,256]{2,1,0:T(8,128)(2,1)S(1)}, bf16[2,52,256]{2,1,0:T(8,128)(2,1)S(1)}, u32[]{:S(2)}, u32[]{:S(2)}) collective-permute-start(bf16[2,52,256]{2,1,0:T(8,128)(2,1)S(1)} %get-tuple-element.54), channel_id=1, source_target_pairs={{0,128},{8,136},{16,144},{24,152},{32,160},{40,168},{48,176},{56,1... | collective-permute-start | bytes 159752 | tf_op jit(solution)/shard_map/ppermute | solution.py:27
  23.9 1.1 %copy-start = (bf16[52,52,256]{2,1,0:T(8,128)(2,1)}, bf16[52,52,256]{2,1,0:T(8,128)(2,1)S(1)}, u32[]{:S(2)}) copy-start(bf16[52,52,256]{2,1,0:T(8,128)(2,1)S(1)} %fusion.66) | copy-start | bytes 4153348
  25.0 1.0 copy-start.3
  25.0 1.0 copy-start.7
  28.3 1.3 %copy-start.5 = (f32[128]{0:T(128)S(1)}, f32[128]{0:T(128)}, u32[]{:S(2)}) copy-start(f32[128]{0:T(128)} %param.14) | copy-start | bytes 1540
  29.5 2.8 %copy-start.1 = (bf16[52,52,256]{2,1,0:T(8,128)(2,1)S(1)}, bf16[52,52,256]{2,1,0:T(8,128)(2,1)}, u32[]{:S(2)}) copy-start(bf16[52,52,256]{2,1,0:T(8,128)(2,1)} %copy-done) | copy-start | bytes 4153348
  37.0 3.0 %collective-permute-start.6 = (f32[73792]{0:T(1024)S(1)}, f32[73792]{0:T(1024)S(1)}, u32[]{:S(2)}, u32[]{:S(2)}) collective-permute-start(f32[73792]{0:T(1024)S(1)} %dynamic_slice.19), channel_id=1, source_target_pairs={{0,8},{8,0},{16,24},{24,16},{32,40},{40,32},{48,56},{56,48},{64,72... | collective-permute-start | bytes 885512 | tf_op jit(solution)/shard_map/ppermute | solution.py:44
  40.3 5.2 %collective-permute-start.7 = (f32[36896]{0:T(1024)S(1)}, f32[36896]{0:T(1024)S(1)}, u32[]{:S(2)}, u32[]{:S(2)}) collective-permute-start(f32[36896]{0:T(1024)S(1)} %dynamic_slice.21), channel_id=1, source_target_pairs={{0,32},{8,40},{16,48},{24,56},{32,0},{40,8},{48,16},{56,24},{64,96... | collective-permute-start | bytes 442760 | tf_op jit(solution)/shard_map/ppermute | solution.py:44
  45.7 4.7 %collective-permute-start.8 = (f32[18448]{0:T(1024)S(1)}, f32[18448]{0:T(1024)S(1)}, u32[]{:S(2)}, u32[]{:S(2)}) collective-permute-start(f32[18448]{0:T(1024)S(1)} %dynamic_slice.23), channel_id=1, source_target_pairs={{0,1},{1,0},{2,3},{3,2},{4,5},{5,4},{6,7},{7,6},{8,9},{9,8},{10,11... | collective-permute-start | bytes 221384 | tf_op jit(solution)/shard_map/ppermute | solution.py:44
  50.5 4.8 %collective-permute-start.9 = (f32[18448]{0:T(1024)S(1)}, f32[18448]{0:T(1024)S(1)}, u32[]{:S(2)}, u32[]{:S(2)}) collective-permute-start(f32[18448]{0:T(1024)S(1)} %dynamic-slice_add_fusion.2), channel_id=1, source_target_pairs={{0,2},{1,3},{2,0},{3,1},{4,6},{5,7},{6,4},{7,5},{8,10},{9,11},{10,... | collective-permute-start | bytes 221384 | tf_op jit(solution)/shard_map/ppermute | solution.py:47
  55.3 4.8 %collective-permute-start.10 = (f32[18448]{0:T(1024)S(1)}, f32[18448]{0:T(1024)S(1)}, u32[]{:S(2)}, u32[]{:S(2)}) collective-permute-start(f32[18448]{0:T(1024)S(1)} %add.123), channel_id=1, source_target_pairs={{0,16},{8,24},{16,0},{24,8},{32,48},{40,56},{48,32},{56,40},{64,80... | collective-permute-start | bytes 221384 | tf_op jit(solution)/shard_map/ppermute | solution.py:47
  60.1 4.6 %collective-permute-start.11 = (f32[18448]{0:T(1024)S(1)}, f32[18448]{0:T(1024)S(1)}, u32[]{:S(2)}, u32[]{:S(2)}) collective-permute-start(f32[18448]{0:T(1024)S(1)} %add.124), channel_id=1, source_target_pairs={{0,64},{8,72},{16,80},{24,88},{32,96},{40,104},{48,112},{56,120},{... | collective-permute-start | bytes 221384 | tf_op jit(solution)/shard_map/ppermute | solution.py:47
  64.8 5.8 %collective-permute-start.12 = (f32[18448]{0:T(1024)S(1)}, f32[18448]{0:T(1024)S(1)}, u32[]{:S(2)}, u32[]{:S(2)}) collective-permute-start(f32[18448]{0:T(1024)S(1)} %add.125), channel_id=1, source_target_pairs={{0,192},{8,200},{16,208},{24,216},{32,224},{40,232},{48,240},{56,2... | collective-permute-start | bytes 221384 | tf_op jit(solution)/shard_map/ppermute | solution.py:47
  67.6 16.2 %collective-permute-start.5 = (bf16[2,48,128]{2,1,0:T(8,128)(2,1)S(1)}, bf16[2,48,128]{2,1,0:T(8,128)(2,1)S(1)}, u32[]{:S(2)}, u32[]{:S(2)}) collective-permute-start(bf16[2,48,128]{2,1,0:T(8,128)(2,1)S(1)} %pad_maximum_fusion.1), channel_id=1, source_target_pairs={{0,128},{8,136},{16,144},{24,152},{32,160},{40,168},{48,176},{56,1... | collective-permute-start | bytes 73736 | tf_op jit(solution)/shard_map/ppermute | solution.py:27
  70.6 4.8 %collective-permute-start.13 = (f32[18448]{0:T(1024)S(1)}, f32[18448]{0:T(1024)S(1)}, u32[]{:S(2)}, u32[]{:S(2)}) collective-permute-start(f32[18448]{0:T(1024)S(1)} %add.126), channel_id=1, source_target_pairs={{0,6},{1,7},{2,4},{3,5},{4,2},{5,3},{6,0},{7,1},{8,14},{9,15},{10,... | collective-permute-start | bytes 221384 | tf_op jit(solution)/shard_map/ppermute | solution.py:47
  75.4 3.6 %collective-permute-start.14 = (f32[18448]{0:T(1024)S(1)}, f32[18448]{0:T(1024)S(1)}, u32[]{:S(2)}, u32[]{:S(2)}) collective-permute-start(f32[18448]{0:T(1024)S(1)} %add.127), channel_id=1, source_target_pairs={{0,1},{1,0},{2,3},{3,2},{4,5},{5,4},{6,7},{7,6},{8,9},{9,8},{10,11... | collective-permute-start | bytes 221384 | tf_op jit(solution)/shard_map/ppermute | solution.py:51
  77.5 3.6 %copy-start.4 = (bf16[3,3,128,128]{3,2,1,0:T(8,128)(2,1)S(1)}, bf16[3,3,128,128]{3,2,1,0:T(8,128)(2,1)}, u32[]{:S(2)}) copy-start(bf16[3,3,128,128]{3,2,1,0:T(8,128)(2,1)} %param.13) | copy-start | bytes 884740
  77.5 3.6 %copy-start.6 = (pred[8,7]{0,1:T(8,128)(4,1)S(1)}, pred[8,7]{0,1:T(8,128)(4,1)}, u32[]{:S(2)}) copy-start(pred[8,7]{0,1:T(8,128)(4,1)} %constant.203) | copy-start | bytes 172
  79.1 4.7 %collective-permute-start.15 = (f32[36896]{0:T(1024)S(1)}, f32[36896]{0:T(1024)S(1)}, u32[]{:S(2)}, u32[]{:S(2)}) collective-permute-start(f32[36896]{0:T(1024)S(1)} %maximum_select_fusion.2), channel_id=1, source_target_pairs={{0,32},{8,40},{16,48},{24,56},{32,0},{40,8},{48,16},{56,24},{64,96... | collective-permute-start | bytes 442760 | tf_op jit(solution)/shard_map/ppermute | solution.py:51
  84.0 10.7 %collective-permute-start.16 = (f32[73792]{0:T(1024)S(1)}, f32[73792]{0:T(1024)S(1)}, u32[]{:S(2)}, u32[]{:S(2)}) collective-permute-start(f32[73792]{0:T(1024)S(1)} %maximum_select_fusion.1), channel_id=1, source_target_pairs={{0,8},{8,0},{16,24},{24,16},{32,40},{40,32},{48,56},{56,48},{64,72... | collective-permute-start | bytes 885512 | tf_op jit(solution)/shard_map/ppermute | solution.py:51

commit v11 on v4

--- a/solution.py
+++ b/solution.py
@@ -25,6 +25,16 @@
     count = lax.axis_size(axis)
     pairs = [(source, (source + steps) % count) for source in range(count)]
     return lax.ppermute(value, axis, pairs)
+
+
+def polar_behind(value, steps):
+    count = lax.axis_size("lon")
+    bands = lax.axis_size("lat")
+    pairs = []
+    for band in sorted({0, bands - 1}):
+        for source in range(count):
+            pairs.append((source * bands + band, ((source + steps) % count) * bands + band))
+    return lax.ppermute(value, ("lon", "lat"), pairs)
 
 
 def butterfly_sum(value, scatter, double):
@@ -100,7 +110,7 @@
     both = jnp.concatenate([inputs, cotangent], axis=2)
     wide = extended(both, (("lon", 1),), 2, True)
     tall = extended(wide, (("lat", 0),), 2, False)
-    far = from_behind(jnp.stack([wide[0], wide[-1]]), "lon", half)
+    far = polar_behind(jnp.stack([wide[0], wide[-1]]), half)
     tall = tall.at[1].set(jnp.where(band == 0, far[0], tall[1]))
     tall = tall.at[rows + 2].set(jnp.where(band == bands - 1, far[1], tall[rows + 2]))
     padded = tall[:, :, :chans]
@@ -139,7 +149,7 @@
                 preferred_element_type=jnp.float32,
             )
         polar.append(ring)
-    polar_in = from_behind(jnp.stack(polar).astype(jnp.bfloat16), "lon", half).astype(jnp.float32)
+    polar_in = polar_behind(jnp.stack(polar).astype(jnp.bfloat16), half).astype(jnp.float32)
     cell_grad = cell_grad.at[0].add(jnp.where(band == 0, polar_in[0], 0.0))
     cell_grad = cell_grad.at[-1].add(jnp.where(band == bands - 1, polar_in[1], 0.0))
     input_grad = cell_grad.astype(jnp.bfloat16)

time: 96.9 us -> 99.1 us (1.023); the launches traced: 96.3 us -> 97.2 us
    ppermute x2, starting transfers between devices: 9.94 us -> 14.3 us  [polar_behind(): return lax.ppermute(value, ('lon', 'lat'), pairs)]
    ppermute x3, starting transfers between devices: 5.15 us -> 2.81 us  [butterfly_sum(): data = keep + lax.ppermute(send, axis, pairs)]
    ppermute x5, starting transfers between devices: 12 us -> 10.4 us  [butterfly_sum(): data = data + lax.ppermute(data, axis, pairs)]
where the time goes in v11:
time: 99.1 us; the launch traced here: 97.2 us
  starting transfers between devices  46.9 us (47%)
  waiting for transfers between devices  20.6 us (21%)
  matrix products  13.5 us (14%)
  other arithmetic  8.35 us (8%)
  local copies, waits for them, and re-layouts  6.75 us (7%)
  between operations  1.12 us (1%)
    ppermute x2, starting transfers between devices, polar_behind(): return lax.ppermute(value, ('lon', 'lat'), pairs)  14.3 us
    ppermute x3, starting transfers between devices, butterfly_sum(): other = lax.ppermute(data, axis, pairs)  11.6 us
    ppermute x5, starting transfers between devices, butterfly_sum(): data = data + lax.ppermute(data, axis, pairs)  10.4 us
    ppermute x5, waiting for transfers between devices, butterfly_sum(): data = data + lax.ppermute(data, axis, pairs)  7.48 us
    ppermute x2, starting transfers between devices, extended(): lax.ppermute(tail, axis, [(i, (i + 1) % count) for i in range(ends)])  6.42 us
    ppermute x3, waiting for transfers between devices, butterfly_sum(): data = keep + lax.ppermute(send, axis, pairs)  6.07 us
    dot_general x6, matrix products, shards(): jnp.dot(grad_ext[line_at, tap_b:tap_b + cols], weight[tap_a, 2 - tap_b].T...  5.32 us
    dot_general x9, matrix products, shards(): lax.dot_general(window, pre_grad, (((0,), (0,)), ((), ())), preferred_ele...  4.43 us
  transfers between devices with their start and end apart: 17, of which 13 were waited for; matrix products, arithmetic and copies ran while one was open for 12% of the time, Pallas kernels for 0%

profile of v11, /device:TPU:1, one launch (start us, length us, event | category | flops | bytes accessed | tf_op | source)
XLA Modules:
  0.0 97.2 jit_solution(8573511346376593958)
XLA Ops:
  0.6 1.2 %constant_dynamic-update-slice_fusion.1 = bf16[48,48,256]{2,1,0:T(8,128)(2,1)S(1)} fusion(bf16[48,48,128]{2,1,0:T(8,128)(2,1)} %param.12), kind=kLoop, calls=%fused_computation.113 | loop fusion | bytes 1179648
  2.1 4.2 %collective-permute-start = (bf16[48,2,256]{2,1,0:T(2,128)(2,1)S(1)}, bf16[48,2,256]{2,1,0:T(2,128)(2,1)S(1)}, u32[]{:S(2)}, u32[]{:S(2)}) collective-permute-start(bf16[48,2,256]{2,1,0:T(2,128)(2,1)S(1)} %get-tuple-element.57), channel_id=1, source_target_pairs={{0,8},{8,16},{16,24},{24,32},{32,40},{40,48},{48,56},{56,64},{64,7... | collective-permute-start | bytes 147464 | tf_op jit(solution)/shard_map/ppermute | solution.py:15
  6.3 1.2 %collective-permute-done = bf16[48,2,256]{2,1,0:T(2,128)(2,1)S(1)} collective-permute-done((bf16[48,2,256]{2,1,0:T(2,128)(2,1)S(1)}, bf16[48,2,256]{2,1,0:T(2,128)(2,1)S(1)}, u32[]{:S(2)}, u32[]{:S(2)}) %collective-permute-start) | collective-permute-done | bytes 49184 | tf_op jit(solution)/shard_map/ppermute | solution.py:15
  7.5 3.8 %collective-permute-done.1 = bf16[48,2,256]{2,1,0:T(2,128)(2,1)S(1)} collective-permute-done((bf16[48,2,256]{2,1,0:T(2,128)(2,1)S(1)}, bf16[48,2,256]{2,1,0:T(2,128)(2,1)S(1)}, u32[]{:S(2)}, u32[]{:S(2)}) %collective-permute-start.1) | collective-permute-done | bytes 49184 | tf_op jit(solution)/shard_map/ppermute | solution.py:17
  11.4 2.2 %collective-permute-start.2 = (bf16[2,52,256]{2,1,0:T(8,128)(2,1)S(1)}, bf16[2,52,256]{2,1,0:T(8,128)(2,1)S(1)}, u32[]{:S(2)}, u32[]{:S(2)}) collective-permute-start(bf16[2,52,256]{2,1,0:T(8,128)(2,1)S(1)} %get-tuple-element.59), channel_id=1, source_target_pairs={{0,1},{1,2},{2,3},{3,4},{4,5},{5,6},{6,7},{8,9},{9,10},{10,11},{11... | collective-permute-start | bytes 159752 | tf_op jit(solution)/shard_map/ppermute | solution.py:15
  13.6 1.3 %collective-permute-start.3 = (bf16[2,52,256]{2,1,0:T(8,128)(2,1)S(1)}, bf16[2,52,256]{2,1,0:T(8,128)(2,1)S(1)}, u32[]{:S(2)}, u32[]{:S(2)}) collective-permute-start(bf16[2,52,256]{2,1,0:T(8,128)(2,1)S(1)} %get-tuple-element.60), channel_id=1, source_target_pairs={{1,0},{2,1},{3,2},{4,3},{5,4},{6,5},{7,6},{9,8},{10,9},{11,10},{12... | collective-permute-start | bytes 159752 | tf_op jit(solution)/shard_map/ppermute | solution.py:17
  15.0 9.0 %collective-permute-start.4 = (bf16[2,52,256]{2,1,0:T(8,128)(2,1)S(1)}, bf16[2,52,256]{2,1,0:T(8,128)(2,1)S(1)}, u32[]{:S(2)}, u32[]{:S(2)}) collective-permute-start(bf16[2,52,256]{2,1,0:T(8,128)(2,1)S(1)} %get-tuple-element.54), channel_id=1, source_target_pairs={{0,128},{8,136},{16,144},{24,152},{32,160},{40,168},{48,176},{56,1... | collective-permute-start | bytes 159752 | tf_op jit(solution)/shard_map/ppermute | solution.py:37
  24.0 0.8 pad_maximum_fusion
  24.8 0.8 collective-permute-done.4
  26.0 0.9 copy-done
  27.1 0.7 copy-done.3
  27.8 1.9 %convolution_select_fusion.1 = f32[50,8,7,128]{3,1,2,0:T(8,128)S(1)} fusion(bf16[3,3,128,128]{3,2,1,0:T(8,128)(2,1)S(1)} %copy-done.3, bf16[52,1,7,2,128]{4,2,3,0,1:T(8,128)(2,1)S(1)} %slice.267, bf16[52,1,8,7,128]{4,2,3,0,1:T(8,128)(2,1)S(1)} %copy.10, pred[8,7]{0,1:T(8,128)(4,1)S(1)} %copy-done.7), kind=kOutput, calls=%fused_computation.10 | convolution fusion | flops 828987392 | bytes 2660408 | tf_op jit(solution)/shard_map/conv_general_dilated | solution.py:118
  30.1 1.2 %reshape.171 = f32[50,1,56,128]{3,2,0,1:T(8,128)} reshape(f32[50,8,7,128]{3,2,1,0:T(8,128)S(1)} %copy.11) | data formatting | bytes 2867200 | tf_op jit(solution)/shard_map/conv_general_dilated | solution.py:118
  31.3 2.5 %fusion.29 = (bf16[50,50,128]{2,1,0:T(8,128)(2,1)S(1)}, f32[50,50,128]{2,1,0:T(8,128)S(1)}) fusion(bf16[52,52,256]{2,1,0:T(8,128)(2,1)} %copy-done, pred[50]{0:T(512)(128)(4,1)S(1)} %and_or_fusion, f32[128]{0:T(128)S(1)} %copy-done.5, f32[50,1,56,128]{3,2,0,1:T(8,128)} %reshape.171), kind=kLoop, calls=%fused_computation.52 | loop fusion | flops 3840000 | bytes 3840562 | tf_op jit(solution)/shard_map/jit(_where)/select_n | solution.py:131
  34.6 0.5 fusion.11
  35.6 0.5 fusion.9
  36.6 0.5 fusion.7
  37.1 0.5 fusion.6
  37.6 0.5 fusion.5
  38.1 0.5 fusion.4
  38.8 1.8 %collective-permute-start.6 = (f32[73792]{0:T(1024)S(1)}, f32[73792]{0:T(1024)S(1)}, u32[]{:S(2)}, u32[]{:S(2)}) collective-permute-start(f32[73792]{0:T(1024)S(1)} %dynamic_slice.19), channel_id=1, source_target_pairs={{0,8},{8,0},{16,24},{24,16},{32,40},{40,32},{48,56},{56,48},{64,72... | collective-permute-start | bytes 885512 | tf_op jit(solution)/shard_map/ppermute | solution.py:54
  40.6 0.9 fusion.54
  42.2 0.9 convolution_add_fusion.1
  43.1 4.2 %collective-permute-done.7 = f32[36896]{0:T(1024)S(1)} collective-permute-done((f32[36896]{0:T(1024)S(1)}, f32[36896]{0:T(1024)S(1)}, u32[]{:S(2)}, u32[]{:S(2)}) %collective-permute-start.7) | collective-permute-done | bytes 147616 | tf_op jit(solution)/shard_map/ppermute | solution.py:54
  47.5 0.9 collective-permute-start.8
  48.5 0.9 fusion.58
  49.3 1.5 %collective-permute-done.8 = f32[18448]{0:T(1024)S(1)} collective-permute-done((f32[18448]{0:T(1024)S(1)}, f32[18448]{0:T(1024)S(1)}, u32[]{:S(2)}, u32[]{:S(2)}) %collective-permute-start.8) | collective-permute-done | bytes 73824 | tf_op jit(solution)/shard_map/ppermute | solution.py:54
  51.1 0.9 convolution_add_fusion.3
  52.0 2.3 %collective-permute-done.9 = f32[18448]{0:T(1024)S(1)} collective-permute-done((f32[18448]{0:T(1024)S(1)}, f32[18448]{0:T(1024)S(1)}, u32[]{:S(2)}, u32[]{:S(2)}) %collective-permute-start.9) | collective-permute-done | bytes 73824 | tf_op jit(solution)/shard_map/ppermute | solution.py:57
  54.3 2.1 %collective-permute-start.10 = (f32[18448]{0:T(1024)S(1)}, f32[18448]{0:T(1024)S(1)}, u32[]{:S(2)}, u32[]{:S(2)}) collective-permute-start(f32[18448]{0:T(1024)S(1)} %add.123), channel_id=1, source_target_pairs={{0,16},{8,24},{16,0},{24,8},{32,48},{40,56},{48,32},{56,40},{64,80... | collective-permute-start | bytes 221384 | tf_op jit(solution)/shard_map/ppermute | solution.py:57
  56.4 0.9 fusion.15
  57.3 1.9 %collective-permute-done.10 = f32[18448]{0:T(1024)S(1)} collective-permute-done((f32[18448]{0:T(1024)S(1)}, f32[18448]{0:T(1024)S(1)}, u32[]{:S(2)}, u32[]{:S(2)}) %collective-permute-start.10) | collective-permute-done | bytes 73824 | tf_op jit(solution)/shard_map/ppermute | solution.py:57
  59.2 4.0 %collective-permute-start.11 = (f32[18448]{0:T(1024)S(1)}, f32[18448]{0:T(1024)S(1)}, u32[]{:S(2)}, u32[]{:S(2)}) collective-permute-start(f32[18448]{0:T(1024)S(1)} %add.124), channel_id=1, source_target_pairs={{0,64},{8,72},{16,80},{24,88},{32,96},{40,104},{48,112},{56,120},{... | collective-permute-start | bytes 221384 | tf_op jit(solution)/shard_map/ppermute | solution.py:57
  63.2 0.9 fusion.16
  64.1 0.9 collective-permute-done.11
  65.0 2.4 %collective-permute-start.12 = (f32[18448]{0:T(1024)S(1)}, f32[18448]{0:T(1024)S(1)}, u32[]{:S(2)}, u32[]{:S(2)}) collective-permute-start(f32[18448]{0:T(1024)S(1)} %add.125), channel_id=1, source_target_pairs={{0,192},{8,200},{16,208},{24,216},{32,224},{40,232},{48,240},{56,2... | collective-permute-start | bytes 221384 | tf_op jit(solution)/shard_map/ppermute | solution.py:57
  67.4 5.3 %collective-permute-start.5 = (bf16[2,48,128]{2,1,0:T(8,128)(2,1)S(1)}, bf16[2,48,128]{2,1,0:T(8,128)(2,1)S(1)}, u32[]{:S(2)}, u32[]{:S(2)}) collective-permute-start(bf16[2,48,128]{2,1,0:T(8,128)(2,1)S(1)} %pad_maximum_fusion.1), channel_id=1, source_target_pairs={{0,128},{8,136},{16,144},{24,152},{32,160},{40,168},{48,176},{56,1... | collective-permute-start | bytes 73736 | tf_op jit(solution)/shard_map/ppermute | solution.py:37
  72.7 1.8 %collective-permute-start.13 = (f32[18448]{0:T(1024)S(1)}, f32[18448]{0:T(1024)S(1)}, u32[]{:S(2)}, u32[]{:S(2)}) collective-permute-start(f32[18448]{0:T(1024)S(1)} %add.126), channel_id=1, source_target_pairs={{0,6},{1,7},{2,4},{3,5},{4,2},{5,3},{6,0},{7,1},{8,14},{9,15},{10,... | collective-permute-start | bytes 221384 | tf_op jit(solution)/shard_map/ppermute | solution.py:57
  74.9 2.4 %collective-permute-done.13 = f32[18448]{0:T(1024)S(1)} collective-permute-done((f32[18448]{0:T(1024)S(1)}, f32[18448]{0:T(1024)S(1)}, u32[]{:S(2)}, u32[]{:S(2)}) %collective-permute-start.13) | collective-permute-done | bytes 73824 | tf_op jit(solution)/shard_map/ppermute | solution.py:57
  77.3 2.0 %collective-permute-start.14 = (f32[18448]{0:T(1024)S(1)}, f32[18448]{0:T(1024)S(1)}, u32[]{:S(2)}, u32[]{:S(2)}) collective-permute-start(f32[18448]{0:T(1024)S(1)} %add.127), channel_id=1, source_target_pairs={{0,32},{8,40},{16,48},{24,56},{32,0},{40,8},{48,16},{56,24},{64,96... | collective-permute-start | bytes 221384 | tf_op jit(solution)/shard_map/ppermute | solution.py:61
  79.3 1.1 %fusion.3 = bf16[48,48,128]{2,1,0:T(8,128)(2,1)} fusion(f32[50,50,128]{2,1,0:T(8,128)S(1)} %add_divide_fusion, f32[50,50,128]{2,1,0:T(8,128)S(1)} %get-tuple-element.53), kind=kLoop, calls=%fused_computation.12 | loop fusion | flops 589824 | bytes 2949120 | tf_op jit(solution)/shard_map/convert.4
  81.0 0.8 collective-permute-done.14
  81.8 1.3 %collective-permute-start.15 = (f32[36896]{0:T(1024)S(1)}, f32[36896]{0:T(1024)S(1)}, u32[]{:S(2)}, u32[]{:S(2)}) collective-permute-start(f32[36896]{0:T(1024)S(1)} %maximum_select_fusion.2), channel_id=1, source_target_pairs={{0,1},{1,0},{2,3},{3,2},{4,5},{5,4},{6,7},{7,6},{8,9},{9,8},{10,11... | collective-permute-start | bytes 442760 | tf_op jit(solution)/shard_map/ppermute | solution.py:61
  83.2 1.8 %convolution_select_fusion = f32[48,8,7,128]{3,1,2,0:T(8,128)S(1)} fusion(bf16[3,3,128,128]{3,2,1,0:T(8,128)(2,1)S(1)} %copy-done.4, bf16[50,1,7,2,128]{4,2,3,0,1:T(8,128)(2,1)S(1)} %slice.272, bf16[50,1,8,7,128]{4,2,3,0,1:T(8,128)(2,1)S(1)} %copy.13, pred[8,7]{0,1:T(8,128)(4,1)S(1)} %copy-done.6), kind=kOutput, calls=%fused_computation.5 | convolution fusion | flops 795832320 | bytes 2567224 | tf_op jit(solution)/shard_map/conv_general_dilated | solution.py:134
  86.1 8.3 %collective-permute-start.16 = (f32[73792]{0:T(1024)S(1)}, f32[73792]{0:T(1024)S(1)}, u32[]{:S(2)}, u32[]{:S(2)}) collective-permute-start(f32[73792]{0:T(1024)S(1)} %maximum_select_fusion.1), channel_id=1, source_target_pairs={{0,8},{8,0},{16,24},{24,16},{32,40},{40,32},{48,56},{56,48},{64,72... | collective-permute-start | bytes 885512 | tf_op jit(solution)/shard_map/ppermute | solution.py:61
  94.4 0.9 convert_element_type.21
  95.8 0.5 slice_multiply_fusion.2
  96.3 0.9 slice_multiply_fusion.1
  (70 shorter events, 6.8 us)
Async XLA Ops:
  0.6 1.2 %copy-start.2 = (bf16[48,48,128]{2,1,0:T(8,128)(2,1)S(1)}, bf16[48,48,128]{2,1,0:T(8,128)(2,1)}, u32[]{:S(2)}) copy-start(bf16[48,48,128]{2,1,0:T(8,128)(2,1)} %param.15) | copy-start | bytes 1769476
  2.1 5.4 %collective-permute-start = (bf16[48,2,256]{2,1,0:T(2,128)(2,1)S(1)}, bf16[48,2,256]{2,1,0:T(2,128)(2,1)S(1)}, u32[]{:S(2)}, u32[]{:S(2)}) collective-permute-start(bf16[48,2,256]{2,1,0:T(2,128)(2,1)S(1)} %get-tuple-element.57), channel_id=1, source_target_pairs={{0,8},{8,16},{16,24},{24,32},{32,40},{40,48},{48,56},{56,64},{64,7... | collective-permute-start | bytes 147464 | tf_op jit(solution)/shard_map/ppermute | solution.py:15
  6.3 5.0 %collective-permute-start.1 = (bf16[48,2,256]{2,1,0:T(2,128)(2,1)S(1)}, bf16[48,2,256]{2,1,0:T(2,128)(2,1)S(1)}, u32[]{:S(2)}, u32[]{:S(2)}) collective-permute-start(bf16[48,2,256]{2,1,0:T(2,128)(2,1)S(1)} %get-tuple-element.58), channel_id=1, source_target_pairs={{8,0},{16,8},{24,16},{32,24},{40,32},{48,40},{56,48},{64,56},{72,6... | collective-permute-start | bytes 147464 | tf_op jit(solution)/shard_map/ppermute | solution.py:17
  11.4 12.6 %collective-permute-start.2 = (bf16[2,52,256]{2,1,0:T(8,128)(2,1)S(1)}, bf16[2,52,256]{2,1,0:T(8,128)(2,1)S(1)}, u32[]{:S(2)}, u32[]{:S(2)}) collective-permute-start(bf16[2,52,256]{2,1,0:T(8,128)(2,1)S(1)} %get-tuple-element.59), channel_id=1, source_target_pairs={{0,1},{1,2},{2,3},{3,4},{4,5},{5,6},{6,7},{8,9},{9,10},{10,11},{11... | collective-permute-start | bytes 159752 | tf_op jit(solution)/shard_map/ppermute | solution.py:15
  13.6 10.4 %collective-permute-start.3 = (bf16[2,52,256]{2,1,0:T(8,128)(2,1)S(1)}, bf16[2,52,256]{2,1,0:T(8,128)(2,1)S(1)}, u32[]{:S(2)}, u32[]{:S(2)}) collective-permute-start(bf16[2,52,256]{2,1,0:T(8,128)(2,1)S(1)} %get-tuple-element.60), channel_id=1, source_target_pairs={{1,0},{2,1},{3,2},{4,3},{5,4},{6,5},{7,6},{9,8},{10,9},{11,10},{12... | collective-permute-start | bytes 159752 | tf_op jit(solution)/shard_map/ppermute | solution.py:17
  15.0 10.7 %collective-permute-start.4 = (bf16[2,52,256]{2,1,0:T(8,128)(2,1)S(1)}, bf16[2,52,256]{2,1,0:T(8,128)(2,1)S(1)}, u32[]{:S(2)}, u32[]{:S(2)}) collective-permute-start(bf16[2,52,256]{2,1,0:T(8,128)(2,1)S(1)} %get-tuple-element.54), channel_id=1, source_target_pairs={{0,128},{8,136},{16,144},{24,152},{32,160},{40,168},{48,176},{56,1... | collective-permute-start | bytes 159752 | tf_op jit(solution)/shard_map/ppermute | solution.py:37
  25.7 1.1 %copy-start = (bf16[52,52,256]{2,1,0:T(8,128)(2,1)}, bf16[52,52,256]{2,1,0:T(8,128)(2,1)S(1)}, u32[]{:S(2)}) copy-start(bf16[52,52,256]{2,1,0:T(8,128)(2,1)S(1)} %fusion.66) | copy-start | bytes 4153348
  26.8 1.0 copy-start.3
  26.8 1.0 copy-start.7
  30.1 1.3 %copy-start.5 = (f32[128]{0:T(128)S(1)}, f32[128]{0:T(128)}, u32[]{:S(2)}) copy-start(f32[128]{0:T(128)} %param.14) | copy-start | bytes 1540
  31.3 2.8 %copy-start.1 = (bf16[52,52,256]{2,1,0:T(8,128)(2,1)S(1)}, bf16[52,52,256]{2,1,0:T(8,128)(2,1)}, u32[]{:S(2)}) copy-start(bf16[52,52,256]{2,1,0:T(8,128)(2,1)} %copy-done) | copy-start | bytes 4153348
  38.8 3.0 %collective-permute-start.6 = (f32[73792]{0:T(1024)S(1)}, f32[73792]{0:T(1024)S(1)}, u32[]{:S(2)}, u32[]{:S(2)}) collective-permute-start(f32[73792]{0:T(1024)S(1)} %dynamic_slice.19), channel_id=1, source_target_pairs={{0,8},{8,0},{16,24},{24,16},{32,40},{40,32},{48,56},{56,48},{64,72... | collective-permute-start | bytes 885512 | tf_op jit(solution)/shard_map/ppermute | solution.py:54
  42.1 5.2 %collective-permute-start.7 = (f32[36896]{0:T(1024)S(1)}, f32[36896]{0:T(1024)S(1)}, u32[]{:S(2)}, u32[]{:S(2)}) collective-permute-start(f32[36896]{0:T(1024)S(1)} %dynamic_slice.21), channel_id=1, source_target_pairs={{0,1},{1,0},{2,3},{3,2},{4,5},{5,4},{6,7},{7,6},{8,9},{9,8},{10,11... | collective-permute-start | bytes 442760 | tf_op jit(solution)/shard_map/ppermute | solution.py:54
  47.5 3.3 %collective-permute-start.8 = (f32[18448]{0:T(1024)S(1)}, f32[18448]{0:T(1024)S(1)}, u32[]{:S(2)}, u32[]{:S(2)}) collective-permute-start(f32[18448]{0:T(1024)S(1)} %dynamic_slice.23), channel_id=1, source_target_pairs={{0,32},{8,40},{16,48},{24,56},{32,0},{40,8},{48,16},{56,24},{64,96... | collective-permute-start | bytes 221384 | tf_op jit(solution)/shard_map/ppermute | solution.py:54
  51.0 3.3 %collective-permute-start.9 = (f32[18448]{0:T(1024)S(1)}, f32[18448]{0:T(1024)S(1)}, u32[]{:S(2)}, u32[]{:S(2)}) collective-permute-start(f32[18448]{0:T(1024)S(1)} %dynamic-slice_add_fusion.2), channel_id=1, source_target_pairs={{0,2},{1,3},{2,0},{3,1},{4,6},{5,7},{6,4},{7,5},{8,10},{9,11},{10,... | collective-permute-start | bytes 221384 | tf_op jit(solution)/shard_map/ppermute | solution.py:57
  54.3 4.8 %collective-permute-start.10 = (f32[18448]{0:T(1024)S(1)}, f32[18448]{0:T(1024)S(1)}, u32[]{:S(2)}, u32[]{:S(2)}) collective-permute-start(f32[18448]{0:T(1024)S(1)} %add.123), channel_id=1, source_target_pairs={{0,16},{8,24},{16,0},{24,8},{32,48},{40,56},{48,32},{56,40},{64,80... | collective-permute-start | bytes 221384 | tf_op jit(solution)/shard_map/ppermute | solution.py:57
  59.2 5.8 %collective-permute-start.11 = (f32[18448]{0:T(1024)S(1)}, f32[18448]{0:T(1024)S(1)}, u32[]{:S(2)}, u32[]{:S(2)}) collective-permute-start(f32[18448]{0:T(1024)S(1)} %add.124), channel_id=1, source_target_pairs={{0,64},{8,72},{16,80},{24,88},{32,96},{40,104},{48,112},{56,120},{... | collective-permute-start | bytes 221384 | tf_op jit(solution)/shard_map/ppermute | solution.py:57
  65.0 7.7 %collective-permute-start.12 = (f32[18448]{0:T(1024)S(1)}, f32[18448]{0:T(1024)S(1)}, u32[]{:S(2)}, u32[]{:S(2)}) collective-permute-start(f32[18448]{0:T(1024)S(1)} %add.125), channel_id=1, source_target_pairs={{0,192},{8,200},{16,208},{24,216},{32,224},{40,232},{48,240},{56,2... | collective-permute-start | bytes 221384 | tf_op jit(solution)/shard_map/ppermute | solution.py:57
  67.4 18.4 %collective-permute-start.5 = (bf16[2,48,128]{2,1,0:T(8,128)(2,1)S(1)}, bf16[2,48,128]{2,1,0:T(8,128)(2,1)S(1)}, u32[]{:S(2)}, u32[]{:S(2)}) collective-permute-start(bf16[2,48,128]{2,1,0:T(8,128)(2,1)S(1)} %pad_maximum_fusion.1), channel_id=1, source_target_pairs={{0,128},{8,136},{16,144},{24,152},{32,160},{40,168},{48,176},{56,1... | collective-permute-start | bytes 73736 | tf_op jit(solution)/shard_map/ppermute | solution.py:37
  72.7 4.5 %collective-permute-start.13 = (f32[18448]{0:T(1024)S(1)}, f32[18448]{0:T(1024)S(1)}, u32[]{:S(2)}, u32[]{:S(2)}) collective-permute-start(f32[18448]{0:T(1024)S(1)} %add.126), channel_id=1, source_target_pairs={{0,6},{1,7},{2,4},{3,5},{4,2},{5,3},{6,0},{7,1},{8,14},{9,15},{10,... | collective-permute-start | bytes 221384 | tf_op jit(solution)/shard_map/ppermute | solution.py:57
  77.3 4.4 %collective-permute-start.14 = (f32[18448]{0:T(1024)S(1)}, f32[18448]{0:T(1024)S(1)}, u32[]{:S(2)}, u32[]{:S(2)}) collective-permute-start(f32[18448]{0:T(1024)S(1)} %add.127), channel_id=1, source_target_pairs={{0,32},{8,40},{16,48},{24,56},{32,0},{40,8},{48,16},{56,24},{64,96... | collective-permute-start | bytes 221384 | tf_op jit(solution)/shard_map/ppermute | solution.py:61
  80.7 2.4 %copy-start.4 = (bf16[3,3,128,128]{3,2,1,0:T(8,128)(2,1)S(1)}, bf16[3,3,128,128]{3,2,1,0:T(8,128)(2,1)}, u32[]{:S(2)}) copy-start(bf16[3,3,128,128]{3,2,1,0:T(8,128)(2,1)} %param.13) | copy-start | bytes 884740
  80.8 2.4 %copy-start.6 = (pred[8,7]{0,1:T(8,128)(4,1)S(1)}, pred[8,7]{0,1:T(8,128)(4,1)}, u32[]{:S(2)}) copy-start(pred[8,7]{0,1:T(8,128)(4,1)} %constant.203) | copy-start | bytes 172
  81.8 4.1 %collective-permute-start.15 = (f32[36896]{0:T(1024)S(1)}, f32[36896]{0:T(1024)S(1)}, u32[]{:S(2)}, u32[]{:S(2)}) collective-permute-start(f32[36896]{0:T(1024)S(1)} %maximum_select_fusion.2), channel_id=1, source_target_pairs={{0,1},{1,0},{2,3},{3,2},{4,5},{5,4},{6,7},{7,6},{8,9},{9,8},{10,11... | collective-permute-start | bytes 442760 | tf_op jit(solution)/shard_map/ppermute | solution.py:61
  86.1 9.5 %collective-permute-start.16 = (f32[73792]{0:T(1024)S(1)}, f32[73792]{0:T(1024)S(1)}, u32[]{:S(2)}, u32[]{:S(2)}) collective-permute-start(f32[73792]{0:T(1024)S(1)} %maximum_select_fusion.1), channel_id=1, source_target_pairs={{0,8},{8,0},{16,24},{24,16},{32,40},{40,32},{48,56},{56,48},{64,72... | collective-permute-start | bytes 885512 | tf_op jit(solution)/shard_map/ppermute | solution.py:61

commit v12 on v4

--- a/solution.py
+++ b/solution.py
@@ -49,7 +49,9 @@
         count = lax.axis_size(axis)
         pairs = [(i, i ^ step) for i in range(count)]
         other = lax.ppermute(data, axis, pairs)
-        data = jnp.where(bit == 0, jnp.concatenate([data, other]), jnp.concatenate([other, data]))
+        whole = jnp.zeros((2 * data.shape[0],), data.dtype)
+        whole = lax.dynamic_update_slice_in_dim(whole, data, bit * data.shape[0], 0)
+        data = lax.dynamic_update_slice_in_dim(whole, other, (1 - bit) * data.shape[0], 0)
     return data[: data.shape[0] - pad].reshape(shape)
 
 

time: 96.9 us -> 102 us (1.053)
  local copies, waits for them, and re-layouts: 6.75 us -> 13.9 us
  waiting for transfers between devices: 19.7 us -> 18.4 us
    dynamic_update_slice x0 -> x5, local copies, waits for them, and re-layouts: none -> 7.13 us  [the longest x3 3.86 us: butterfly_sum(): lax.dynamic_update_slice_in_dim(whole, other, (1 - bit) * data.shape[0], 0)]
    ppermute x3, waiting for transfers between devices: 1.9 us -> 0.68 us  [butterfly_sum(): other = lax.ppermute(data, axis, pairs)]
  transfers between devices with their start and end apart: 17 -> 17, of which waited for: 13 -> 11; matrix products, arithmetic and copies ran while one was open for 12% -> 16% of each run, Pallas kernels for 0% -> 0%
where the time goes in v12:
time: 102 us
  starting transfers between devices  46.5 us (46%)
  waiting for transfers between devices  18.4 us (18%)
  local copies, waits for them, and re-layouts  13.9 us (14%)
  matrix products  13.5 us (13%)
  other arithmetic  8.29 us (8%)
  between operations  1.13 us (1%)
    ppermute x5, starting transfers between devices, butterfly_sum(): data = data + lax.ppermute(data, axis, pairs)  12 us
    ppermute x3, starting transfers between devices, butterfly_sum(): other = lax.ppermute(data, axis, pairs)  11.7 us
    ppermute x2, starting transfers between devices, from_behind(): return lax.ppermute(value, axis, pairs)  9.94 us
    ppermute x5, waiting for transfers between devices, butterfly_sum(): data = data + lax.ppermute(data, axis, pairs)  6.5 us
    ppermute x2, starting transfers between devices, extended(): lax.ppermute(tail, axis, [(i, (i + 1) % count) for i in range(ends)])  6.42 us
    ppermute x3, waiting for transfers between devices, butterfly_sum(): data = keep + lax.ppermute(send, axis, pairs)  5.37 us
    dot_general x6, matrix products, shards(): jnp.dot(grad_ext[line_at, tap_b:tap_b + cols], weight[tap_a, 2 - tap_b].T...  5.31 us
    ppermute x3, starting transfers between devices, butterfly_sum(): data = keep + lax.ppermute(send, axis, pairs)  5.14 us
  transfers between devices with their start and end apart: 17, of which 11 were waited for; matrix products, arithmetic and copies ran while one was open for 16% of the time, Pallas kernels for 0%

profile of v12, /device:TPU:1, one launch (start us, length us, event | category | flops | bytes accessed | tf_op | source)
XLA Modules:
  0.0 101.8 jit_solution(16464385507637737501)
XLA Ops:
  0.6 1.2 %constant_dynamic-update-slice_fusion.1 = bf16[48,48,256]{2,1,0:T(8,128)(2,1)S(1)} fusion(bf16[48,48,128]{2,1,0:T(8,128)(2,1)} %param.12), kind=kLoop, calls=%fused_computation.110 | loop fusion | bytes 1179648
  2.1 4.2 %collective-permute-start = (bf16[48,2,256]{2,1,0:T(2,128)(2,1)S(1)}, bf16[48,2,256]{2,1,0:T(2,128)(2,1)S(1)}, u32[]{:S(2)}, u32[]{:S(2)}) collective-permute-start(bf16[48,2,256]{2,1,0:T(2,128)(2,1)S(1)} %get-tuple-element.59), channel_id=1, source_target_pairs={{0,8},{8,16},{16,24},{24,32},{32,40},{40,48},{48,56},{56,64},{64,7... | collective-permute-start | bytes 147464 | tf_op jit(solution)/shard_map/ppermute | solution.py:15
  6.3 1.2 %collective-permute-done = bf16[48,2,256]{2,1,0:T(2,128)(2,1)S(1)} collective-permute-done((bf16[48,2,256]{2,1,0:T(2,128)(2,1)S(1)}, bf16[48,2,256]{2,1,0:T(2,128)(2,1)S(1)}, u32[]{:S(2)}, u32[]{:S(2)}) %collective-permute-start) | collective-permute-done | bytes 49184 | tf_op jit(solution)/shard_map/ppermute | solution.py:15
  7.5 3.8 %collective-permute-done.1 = bf16[48,2,256]{2,1,0:T(2,128)(2,1)S(1)} collective-permute-done((bf16[48,2,256]{2,1,0:T(2,128)(2,1)S(1)}, bf16[48,2,256]{2,1,0:T(2,128)(2,1)S(1)}, u32[]{:S(2)}, u32[]{:S(2)}) %collective-permute-start.1) | collective-permute-done | bytes 49184 | tf_op jit(solution)/shard_map/ppermute | solution.py:17
  11.4 2.2 %collective-permute-start.2 = (bf16[2,52,256]{2,1,0:T(8,128)(2,1)S(1)}, bf16[2,52,256]{2,1,0:T(8,128)(2,1)S(1)}, u32[]{:S(2)}, u32[]{:S(2)}) collective-permute-start(bf16[2,52,256]{2,1,0:T(8,128)(2,1)S(1)} %get-tuple-element.61), channel_id=1, source_target_pairs={{0,1},{1,2},{2,3},{3,4},{4,5},{5,6},{6,7},{8,9},{9,10},{10,11},{11... | collective-permute-start | bytes 159752 | tf_op jit(solution)/shard_map/ppermute | solution.py:15
  13.6 1.3 %collective-permute-start.3 = (bf16[2,52,256]{2,1,0:T(8,128)(2,1)S(1)}, bf16[2,52,256]{2,1,0:T(8,128)(2,1)S(1)}, u32[]{:S(2)}, u32[]{:S(2)}) collective-permute-start(bf16[2,52,256]{2,1,0:T(8,128)(2,1)S(1)} %get-tuple-element.62), channel_id=1, source_target_pairs={{1,0},{2,1},{3,2},{4,3},{5,4},{6,5},{7,6},{9,8},{10,9},{11,10},{12... | collective-permute-start | bytes 159752 | tf_op jit(solution)/shard_map/ppermute | solution.py:17
  15.0 7.2 %collective-permute-start.4 = (bf16[2,52,256]{2,1,0:T(8,128)(2,1)S(1)}, bf16[2,52,256]{2,1,0:T(8,128)(2,1)S(1)}, u32[]{:S(2)}, u32[]{:S(2)}) collective-permute-start(bf16[2,52,256]{2,1,0:T(8,128)(2,1)S(1)} %get-tuple-element.56), channel_id=1, source_target_pairs={{0,128},{8,136},{16,144},{24,152},{32,160},{40,168},{48,176},{56,1... | collective-permute-start | bytes 159752 | tf_op jit(solution)/shard_map/ppermute | solution.py:27
  22.2 0.8 pad_maximum_fusion
  23.0 0.8 collective-permute-done.4
  24.1 0.9 copy-done
  25.3 0.7 copy-done.3
  26.0 1.9 %convolution_select_fusion.1 = f32[50,8,7,128]{3,1,2,0:T(8,128)S(1)} fusion(bf16[3,3,128,128]{3,2,1,0:T(8,128)(2,1)S(1)} %copy-done.3, bf16[52,1,7,2,128]{4,2,3,0,1:T(8,128)(2,1)S(1)} %slice.267, bf16[52,1,8,7,128]{4,2,3,0,1:T(8,128)(2,1)S(1)} %copy.10, pred[8,7]{0,1:T(8,128)(4,1)S(1)} %copy-done.7), kind=kOutput, calls=%fused_computation.10 | convolution fusion | flops 828987392 | bytes 2660408 | tf_op jit(solution)/shard_map/conv_general_dilated | solution.py:110
  28.3 1.2 %reshape.171 = f32[50,1,56,128]{3,2,0,1:T(8,128)} reshape(f32[50,8,7,128]{3,2,1,0:T(8,128)S(1)} %copy.11) | data formatting | bytes 2867200 | tf_op jit(solution)/shard_map/conv_general_dilated | solution.py:110
  29.5 2.5 %fusion.29 = (bf16[50,50,128]{2,1,0:T(8,128)(2,1)S(1)}, f32[50,50,128]{2,1,0:T(8,128)S(1)}) fusion(bf16[52,52,256]{2,1,0:T(8,128)(2,1)} %copy-done, pred[50]{0:T(512)(128)(4,1)S(1)} %and_or_fusion, f32[128]{0:T(128)S(1)} %copy-done.5, f32[50,1,56,128]{3,2,0,1:T(8,128)} %reshape.171), kind=kLoop, calls=%fused_computation.52 | loop fusion | flops 3840000 | bytes 3840562 | tf_op jit(solution)/shard_map/jit(_where)/select_n | solution.py:123
  37.1 1.8 %collective-permute-start.6 = (f32[73792]{0:T(1024)S(1)}, f32[73792]{0:T(1024)S(1)}, u32[]{:S(2)}, u32[]{:S(2)}) collective-permute-start(f32[73792]{0:T(1024)S(1)} %dynamic_slice.19), channel_id=1, source_target_pairs={{0,8},{8,0},{16,24},{24,16},{32,40},{40,32},{48,56},{56,48},{64,72... | collective-permute-start | bytes 885512 | tf_op jit(solution)/shard_map/ppermute | solution.py:44
  38.9 0.9 fusion.58
  40.4 2.9 %collective-permute-start.7 = (f32[36896]{0:T(1024)S(1)}, f32[36896]{0:T(1024)S(1)}, u32[]{:S(2)}, u32[]{:S(2)}) collective-permute-start(f32[36896]{0:T(1024)S(1)} %dynamic_slice.21), channel_id=1, source_target_pairs={{0,1},{1,0},{2,3},{3,2},{4,5},{5,4},{6,7},{7,6},{8,9},{9,8},{10,11... | collective-permute-start | bytes 442760 | tf_op jit(solution)/shard_map/ppermute | solution.py:44
  43.2 0.9 convolution_add_fusion.3
  44.1 3.1 %collective-permute-done.7 = f32[36896]{0:T(1024)S(1)} collective-permute-done((f32[36896]{0:T(1024)S(1)}, f32[36896]{0:T(1024)S(1)}, u32[]{:S(2)}, u32[]{:S(2)}) %collective-permute-start.7) | collective-permute-done | bytes 147616 | tf_op jit(solution)/shard_map/ppermute | solution.py:44
  47.9 0.9 fusion.54
  48.8 2.0 %collective-permute-done.8 = f32[18448]{0:T(1024)S(1)} collective-permute-done((f32[18448]{0:T(1024)S(1)}, f32[18448]{0:T(1024)S(1)}, u32[]{:S(2)}, u32[]{:S(2)}) %collective-permute-start.8) | collective-permute-done | bytes 73824 | tf_op jit(solution)/shard_map/ppermute | solution.py:44
  50.8 2.7 %collective-permute-start.9 = (f32[18448]{0:T(1024)S(1)}, f32[18448]{0:T(1024)S(1)}, u32[]{:S(2)}, u32[]{:S(2)}) collective-permute-start(f32[18448]{0:T(1024)S(1)} %dynamic-slice_add_fusion.2), channel_id=1, source_target_pairs={{0,2},{1,3},{2,0},{3,1},{4,6},{5,7},{6,4},{7,5},{8,10},{9,11},{10,... | collective-permute-start | bytes 221384 | tf_op jit(solution)/shard_map/ppermute | solution.py:47
  53.6 0.9 convolution_add_fusion.1
  54.4 0.9 collective-permute-done.9
  55.4 0.7 collective-permute-start.10
  56.0 0.9 fusion.16
  56.9 3.3 %collective-permute-done.10 = f32[18448]{0:T(1024)S(1)} collective-permute-done((f32[18448]{0:T(1024)S(1)}, f32[18448]{0:T(1024)S(1)}, u32[]{:S(2)}, u32[]{:S(2)}) %collective-permute-start.10) | collective-permute-done | bytes 73824 | tf_op jit(solution)/shard_map/ppermute | solution.py:47
  60.2 2.5 %collective-permute-start.11 = (f32[18448]{0:T(1024)S(1)}, f32[18448]{0:T(1024)S(1)}, u32[]{:S(2)}, u32[]{:S(2)}) collective-permute-start(f32[18448]{0:T(1024)S(1)} %add.130), channel_id=1, source_target_pairs={{0,64},{8,72},{16,80},{24,88},{32,96},{40,104},{48,112},{56,120},{... | collective-permute-start | bytes 221384 | tf_op jit(solution)/shard_map/ppermute | solution.py:47
  62.7 0.9 fusion.15
  63.6 0.9 collective-permute-done.11
  64.5 3.1 %collective-permute-start.12 = (f32[18448]{0:T(1024)S(1)}, f32[18448]{0:T(1024)S(1)}, u32[]{:S(2)}, u32[]{:S(2)}) collective-permute-start(f32[18448]{0:T(1024)S(1)} %add.131), channel_id=1, source_target_pairs={{0,192},{8,200},{16,208},{24,216},{32,224},{40,232},{48,240},{56,2... | collective-permute-start | bytes 221384 | tf_op jit(solution)/shard_map/ppermute | solution.py:47
  67.6 2.7 %collective-permute-start.5 = (bf16[2,48,128]{2,1,0:T(8,128)(2,1)S(1)}, bf16[2,48,128]{2,1,0:T(8,128)(2,1)S(1)}, u32[]{:S(2)}, u32[]{:S(2)}) collective-permute-start(bf16[2,48,128]{2,1,0:T(8,128)(2,1)S(1)} %pad_maximum_fusion.1), channel_id=1, source_target_pairs={{0,128},{8,136},{16,144},{24,152},{32,160},{40,168},{48,176},{56,1... | collective-permute-start | bytes 73736 | tf_op jit(solution)/shard_map/ppermute | solution.py:27
  70.4 3.0 %collective-permute-start.13 = (f32[18448]{0:T(1024)S(1)}, f32[18448]{0:T(1024)S(1)}, u32[]{:S(2)}, u32[]{:S(2)}) collective-permute-start(f32[18448]{0:T(1024)S(1)} %add.132), channel_id=1, source_target_pairs={{0,6},{1,7},{2,4},{3,5},{4,2},{5,3},{6,0},{7,1},{8,14},{9,15},{10,... | collective-permute-start | bytes 221384 | tf_op jit(solution)/shard_map/ppermute | solution.py:47
  73.7 1.4 %collective-permute-done.13 = f32[18448]{0:T(1024)S(1)} collective-permute-done((f32[18448]{0:T(1024)S(1)}, f32[18448]{0:T(1024)S(1)}, u32[]{:S(2)}, u32[]{:S(2)}) %collective-permute-start.13) | collective-permute-done | bytes 73824 | tf_op jit(solution)/shard_map/ppermute | solution.py:47
  75.5 2.1 %collective-permute-start.14 = (f32[18448]{0:T(1024)S(1)}, f32[18448]{0:T(1024)S(1)}, u32[]{:S(2)}, u32[]{:S(2)}) collective-permute-start(f32[18448]{0:T(1024)S(1)} %get-tuple-element.53), channel_id=1, source_target_pairs={{0,32},{8,40},{16,48},{24,56},{32,0},{40,8},{48,16},{56,24},{64,96... | collective-permute-start | bytes 221384 | tf_op jit(solution)/shard_map/ppermute | solution.py:51
  77.6 1.2 %fusion.3 = bf16[48,48,128]{2,1,0:T(8,128)(2,1)} fusion(f32[50,50,128]{2,1,0:T(8,128)S(1)} %add_divide_fusion, f32[50,50,128]{2,1,0:T(8,128)S(1)} %get-tuple-element.55), kind=kLoop, calls=%fused_computation.12 | loop fusion | flops 589824 | bytes 2949120 | tf_op jit(solution)/shard_map/convert.4
  79.3 0.7 collective-permute-done.14
  80.0 0.6 dynamic_update_slice.19
  80.6 0.6 collective-permute-start.15
  81.2 1.8 %convolution_select_fusion = f32[48,8,7,128]{3,1,2,0:T(8,128)S(1)} fusion(bf16[3,3,128,128]{3,2,1,0:T(8,128)(2,1)S(1)} %copy-done.4, bf16[50,1,7,2,128]{4,2,3,0,1:T(8,128)(2,1)S(1)} %slice.272, bf16[50,1,8,7,128]{4,2,3,0,1:T(8,128)(2,1)S(1)} %copy.13, pred[8,7]{0,1:T(8,128)(4,1)S(1)} %copy-done.6), kind=kOutput, calls=%fused_computation.5 | convolution fusion | flops 795832320 | bytes 2567224 | tf_op jit(solution)/shard_map/conv_general_dilated | solution.py:126
  83.9 1.2 %dynamic_update_slice.20 = f32[73792]{0:T(1024)S(1)} dynamic-update-slice(f32[73792]{0:T(1024)S(1)} %broadcast_in_dim.41, f32[36896]{0:T(1024)S(1)} %dynamic_update_slice.19, s32[]{:T(128)S(6)} %select_n.94) | dynamic-update-slice | bytes 295172 | tf_op jit(solution)/shard_map/dynamic_update_slice | solution.py:53
  85.2 1.1 %dynamic_update_slice.21 = f32[73792]{0:T(1024)S(1)} dynamic-update-slice(f32[73792]{0:T(1024)S(1)} %dynamic_update_slice.20, f32[36896]{0:T(1024)S(1)} %collective-permute-done.15, s32[]{:T(128)S(6)} %select_n.95) | dynamic-update-slice | bytes 295172 | tf_op jit(solution)/shard_map/dynamic_update_slice | solution.py:54
  86.3 9.0 %collective-permute-start.16 = (f32[73792]{0:T(1024)S(1)}, f32[73792]{0:T(1024)S(1)}, u32[]{:S(2)}, u32[]{:S(2)}) collective-permute-start(f32[73792]{0:T(1024)S(1)} %dynamic_update_slice.21), channel_id=1, source_target_pairs={{0,8},{8,0},{16,24},{24,16},{32,40},{40,32},{48,56},{56,48},{64,72... | collective-permute-start | bytes 885512 | tf_op jit(solution)/shard_map/ppermute | solution.py:51
  95.3 0.9 convert_element_type.21
  96.3 2.0 %dynamic_update_slice.22 = f32[147584]{0:T(1024)S(1)} dynamic-update-slice(f32[147584]{0:T(1024)S(1)} %broadcast_in_dim.40, f32[73792]{0:T(1024)S(1)} %dynamic_update_slice.21, s32[]{:T(128)S(6)} %select_n.91) | dynamic-update-slice | bytes 590340 | tf_op jit(solution)/shard_map/dynamic_update_slice | solution.py:53
  98.3 2.1 %dynamic_update_slice.23 = f32[147584]{0:T(1024)S(1)} dynamic-update-slice(f32[147584]{0:T(1024)S(1)} %dynamic_update_slice.22, f32[73792]{0:T(1024)S(1)} %collective-permute-done.16, s32[]{:T(128)S(6)} %select_n.92) | dynamic-update-slice | bytes 590340 | tf_op jit(solution)/shard_map/dynamic_update_slice | solution.py:54
  100.4 0.9 slice_multiply_fusion.1
  101.3 0.5 slice_multiply_fusion.2
  (75 shorter events, 9.6 us)
Async XLA Ops:
  0.6 1.2 %copy-start.2 = (bf16[48,48,128]{2,1,0:T(8,128)(2,1)S(1)}, bf16[48,48,128]{2,1,0:T(8,128)(2,1)}, u32[]{:S(2)}) copy-start(bf16[48,48,128]{2,1,0:T(8,128)(2,1)} %param.15) | copy-start | bytes 1769476
  2.1 5.4 %collective-permute-start = (bf16[48,2,256]{2,1,0:T(2,128)(2,1)S(1)}, bf16[48,2,256]{2,1,0:T(2,128)(2,1)S(1)}, u32[]{:S(2)}, u32[]{:S(2)}) collective-permute-start(bf16[48,2,256]{2,1,0:T(2,128)(2,1)S(1)} %get-tuple-element.59), channel_id=1, source_target_pairs={{0,8},{8,16},{16,24},{24,32},{32,40},{40,48},{48,56},{56,64},{64,7... | collective-permute-start | bytes 147464 | tf_op jit(solution)/shard_map/ppermute | solution.py:15
  6.3 5.0 %collective-permute-start.1 = (bf16[48,2,256]{2,1,0:T(2,128)(2,1)S(1)}, bf16[48,2,256]{2,1,0:T(2,128)(2,1)S(1)}, u32[]{:S(2)}, u32[]{:S(2)}) collective-permute-start(bf16[48,2,256]{2,1,0:T(2,128)(2,1)S(1)} %get-tuple-element.60), channel_id=1, source_target_pairs={{8,0},{16,8},{24,16},{32,24},{40,32},{48,40},{56,48},{64,56},{72,6... | collective-permute-start | bytes 147464 | tf_op jit(solution)/shard_map/ppermute | solution.py:17
  11.4 10.8 %collective-permute-start.2 = (bf16[2,52,256]{2,1,0:T(8,128)(2,1)S(1)}, bf16[2,52,256]{2,1,0:T(8,128)(2,1)S(1)}, u32[]{:S(2)}, u32[]{:S(2)}) collective-permute-start(bf16[2,52,256]{2,1,0:T(8,128)(2,1)S(1)} %get-tuple-element.61), channel_id=1, source_target_pairs={{0,1},{1,2},{2,3},{3,4},{4,5},{5,6},{6,7},{8,9},{9,10},{10,11},{11... | collective-permute-start | bytes 159752 | tf_op jit(solution)/shard_map/ppermute | solution.py:15
  13.6 8.6 %collective-permute-start.3 = (bf16[2,52,256]{2,1,0:T(8,128)(2,1)S(1)}, bf16[2,52,256]{2,1,0:T(8,128)(2,1)S(1)}, u32[]{:S(2)}, u32[]{:S(2)}) collective-permute-start(bf16[2,52,256]{2,1,0:T(8,128)(2,1)S(1)} %get-tuple-element.62), channel_id=1, source_target_pairs={{1,0},{2,1},{3,2},{4,3},{5,4},{6,5},{7,6},{9,8},{10,9},{11,10},{12... | collective-permute-start | bytes 159752 | tf_op jit(solution)/shard_map/ppermute | solution.py:17
  15.0 8.9 %collective-permute-start.4 = (bf16[2,52,256]{2,1,0:T(8,128)(2,1)S(1)}, bf16[2,52,256]{2,1,0:T(8,128)(2,1)S(1)}, u32[]{:S(2)}, u32[]{:S(2)}) collective-permute-start(bf16[2,52,256]{2,1,0:T(8,128)(2,1)S(1)} %get-tuple-element.56), channel_id=1, source_target_pairs={{0,128},{8,136},{16,144},{24,152},{32,160},{40,168},{48,176},{56,1... | collective-permute-start | bytes 159752 | tf_op jit(solution)/shard_map/ppermute | solution.py:27
  23.9 1.1 %copy-start = (bf16[52,52,256]{2,1,0:T(8,128)(2,1)}, bf16[52,52,256]{2,1,0:T(8,128)(2,1)S(1)}, u32[]{:S(2)}) copy-start(bf16[52,52,256]{2,1,0:T(8,128)(2,1)S(1)} %fusion.66) | copy-start | bytes 4153348
  25.0 1.0 copy-start.3
  25.0 1.0 copy-start.7
  28.2 1.3 %copy-start.5 = (f32[128]{0:T(128)S(1)}, f32[128]{0:T(128)}, u32[]{:S(2)}) copy-start(f32[128]{0:T(128)} %param.14) | copy-start | bytes 1540
  29.5 2.5 %copy-start.1 = (bf16[52,52,256]{2,1,0:T(8,128)(2,1)S(1)}, bf16[52,52,256]{2,1,0:T(8,128)(2,1)}, u32[]{:S(2)}) copy-start(bf16[52,52,256]{2,1,0:T(8,128)(2,1)} %copy-done) | copy-start | bytes 4153348
  37.1 3.0 %collective-permute-start.6 = (f32[73792]{0:T(1024)S(1)}, f32[73792]{0:T(1024)S(1)}, u32[]{:S(2)}, u32[]{:S(2)}) collective-permute-start(f32[73792]{0:T(1024)S(1)} %dynamic_slice.19), channel_id=1, source_target_pairs={{0,8},{8,0},{16,24},{24,16},{32,40},{40,32},{48,56},{56,48},{64,72... | collective-permute-start | bytes 885512 | tf_op jit(solution)/shard_map/ppermute | solution.py:44
  40.4 6.8 %collective-permute-start.7 = (f32[36896]{0:T(1024)S(1)}, f32[36896]{0:T(1024)S(1)}, u32[]{:S(2)}, u32[]{:S(2)}) collective-permute-start(f32[36896]{0:T(1024)S(1)} %dynamic_slice.21), channel_id=1, source_target_pairs={{0,1},{1,0},{2,3},{3,2},{4,5},{5,4},{6,7},{7,6},{8,9},{9,8},{10,11... | collective-permute-start | bytes 442760 | tf_op jit(solution)/shard_map/ppermute | solution.py:44
  47.4 3.3 %collective-permute-start.8 = (f32[18448]{0:T(1024)S(1)}, f32[18448]{0:T(1024)S(1)}, u32[]{:S(2)}, u32[]{:S(2)}) collective-permute-start(f32[18448]{0:T(1024)S(1)} %dynamic_slice.23), channel_id=1, source_target_pairs={{0,32},{8,40},{16,48},{24,56},{32,0},{40,8},{48,16},{56,24},{64,96... | collective-permute-start | bytes 221384 | tf_op jit(solution)/shard_map/ppermute | solution.py:44
  50.8 4.5 %collective-permute-start.9 = (f32[18448]{0:T(1024)S(1)}, f32[18448]{0:T(1024)S(1)}, u32[]{:S(2)}, u32[]{:S(2)}) collective-permute-start(f32[18448]{0:T(1024)S(1)} %dynamic-slice_add_fusion.2), channel_id=1, source_target_pairs={{0,2},{1,3},{2,0},{3,1},{4,6},{5,7},{6,4},{7,5},{8,10},{9,11},{10,... | collective-permute-start | bytes 221384 | tf_op jit(solution)/shard_map/ppermute | solution.py:47
  55.4 4.8 %collective-permute-start.10 = (f32[18448]{0:T(1024)S(1)}, f32[18448]{0:T(1024)S(1)}, u32[]{:S(2)}, u32[]{:S(2)}) collective-permute-start(f32[18448]{0:T(1024)S(1)} %add.129), channel_id=1, source_target_pairs={{0,16},{8,24},{16,0},{24,8},{32,48},{40,56},{48,32},{56,40},{64,80... | collective-permute-start | bytes 221384 | tf_op jit(solution)/shard_map/ppermute | solution.py:47
  60.2 4.3 %collective-permute-start.11 = (f32[18448]{0:T(1024)S(1)}, f32[18448]{0:T(1024)S(1)}, u32[]{:S(2)}, u32[]{:S(2)}) collective-permute-start(f32[18448]{0:T(1024)S(1)} %add.130), channel_id=1, source_target_pairs={{0,64},{8,72},{16,80},{24,88},{32,96},{40,104},{48,112},{56,120},{... | collective-permute-start | bytes 221384 | tf_op jit(solution)/shard_map/ppermute | solution.py:47
  64.5 5.8 %collective-permute-start.12 = (f32[18448]{0:T(1024)S(1)}, f32[18448]{0:T(1024)S(1)}, u32[]{:S(2)}, u32[]{:S(2)}) collective-permute-start(f32[18448]{0:T(1024)S(1)} %add.131), channel_id=1, source_target_pairs={{0,192},{8,200},{16,208},{24,216},{32,224},{40,232},{48,240},{56,2... | collective-permute-start | bytes 221384 | tf_op jit(solution)/shard_map/ppermute | solution.py:47
  67.6 16.3 %collective-permute-start.5 = (bf16[2,48,128]{2,1,0:T(8,128)(2,1)S(1)}, bf16[2,48,128]{2,1,0:T(8,128)(2,1)S(1)}, u32[]{:S(2)}, u32[]{:S(2)}) collective-permute-start(bf16[2,48,128]{2,1,0:T(8,128)(2,1)S(1)} %pad_maximum_fusion.1), channel_id=1, source_target_pairs={{0,128},{8,136},{16,144},{24,152},{32,160},{40,168},{48,176},{56,1... | collective-permute-start | bytes 73736 | tf_op jit(solution)/shard_map/ppermute | solution.py:27
  70.4 4.8 %collective-permute-start.13 = (f32[18448]{0:T(1024)S(1)}, f32[18448]{0:T(1024)S(1)}, u32[]{:S(2)}, u32[]{:S(2)}) collective-permute-start(f32[18448]{0:T(1024)S(1)} %add.132), channel_id=1, source_target_pairs={{0,6},{1,7},{2,4},{3,5},{4,2},{5,3},{6,0},{7,1},{8,14},{9,15},{10,... | collective-permute-start | bytes 221384 | tf_op jit(solution)/shard_map/ppermute | solution.py:47
  75.5 4.5 %collective-permute-start.14 = (f32[18448]{0:T(1024)S(1)}, f32[18448]{0:T(1024)S(1)}, u32[]{:S(2)}, u32[]{:S(2)}) collective-permute-start(f32[18448]{0:T(1024)S(1)} %get-tuple-element.53), channel_id=1, source_target_pairs={{0,32},{8,40},{16,48},{24,56},{32,0},{40,8},{48,16},{56,24},{64,96... | collective-permute-start | bytes 221384 | tf_op jit(solution)/shard_map/ppermute | solution.py:51
  79.1 2.1 %copy-start.4 = (bf16[3,3,128,128]{3,2,1,0:T(8,128)(2,1)S(1)}, bf16[3,3,128,128]{3,2,1,0:T(8,128)(2,1)}, u32[]{:S(2)}) copy-start(bf16[3,3,128,128]{3,2,1,0:T(8,128)(2,1)} %param.13) | copy-start | bytes 884740
  79.1 2.1 %copy-start.6 = (pred[8,7]{0,1:T(8,128)(4,1)S(1)}, pred[8,7]{0,1:T(8,128)(4,1)}, u32[]{:S(2)}) copy-start(pred[8,7]{0,1:T(8,128)(4,1)} %constant.206) | copy-start | bytes 172
  80.6 4.6 %collective-permute-start.15 = (f32[36896]{0:T(1024)S(1)}, f32[36896]{0:T(1024)S(1)}, u32[]{:S(2)}, u32[]{:S(2)}) collective-permute-start(f32[36896]{0:T(1024)S(1)} %dynamic_update_slice.19), channel_id=1, source_target_pairs={{0,1},{1,0},{2,3},{3,2},{4,5},{5,4},{6,7},{7,6},{8,9},{9,8},{10,11... | collective-permute-start | bytes 442760 | tf_op jit(solution)/shard_map/ppermute | solution.py:51
  86.3 12.0 %collective-permute-start.16 = (f32[73792]{0:T(1024)S(1)}, f32[73792]{0:T(1024)S(1)}, u32[]{:S(2)}, u32[]{:S(2)}) collective-permute-start(f32[73792]{0:T(1024)S(1)} %dynamic_update_slice.21), channel_id=1, source_target_pairs={{0,8},{8,0},{16,24},{24,16},{32,40},{40,32},{48,56},{56,48},{64,72... | collective-permute-start | bytes 885512 | tf_op jit(solution)/shard_map/ppermute | solution.py:51

commit v13 on v9

--- a/solution.py
+++ b/solution.py
@@ -27,7 +27,7 @@
     return lax.ppermute(value, axis, pairs)
 
 
-def butterfly_sum(value, scatter, double):
+def butterfly_sum(value, scatter, double, rider):
     shape = value.shape
     data = value.reshape(-1)
     parts = 2 ** len(scatter)
@@ -45,12 +45,13 @@
         history.append((axis, step, bit))
     for axis, pairs in double:
         data = data + lax.ppermute(data, axis, pairs)
+    data, rider = lax.optimization_barrier((data, rider))
     for axis, step, bit in reversed(history):
         count = lax.axis_size(axis)
         pairs = [(i, i ^ step) for i in range(count)]
         other = lax.ppermute(data, axis, pairs)
         data = jnp.where(bit == 0, jnp.concatenate([data, other]), jnp.concatenate([other, data]))
-    return data[: data.shape[0] - pad].reshape(shape)
+    return data[: data.shape[0] - pad].reshape(shape), rider
 
 
 def pairing_order(mesh_axes):
@@ -139,7 +140,7 @@
                 preferred_element_type=jnp.float32,
             )
         polar.append(ring)
-    polar_in = from_behind(jnp.stack(polar).astype(jnp.bfloat16), "lon", half).astype(jnp.float32)
+    polar_out = jnp.stack(polar).astype(jnp.bfloat16)
     taps = []
     for tap_a in range(3):
         for tap_b in range(3):
@@ -152,13 +153,14 @@
     kernel_terms = jnp.concatenate(taps, axis=0)
     bias_terms = jnp.sum(pre_grad.astype(jnp.float32), axis=0)[None, :]
     order = pairing_order(("lon", "lat"))
-    terms, polar_in = lax.optimization_barrier((jnp.concatenate([kernel_terms, bias_terms], axis=0), polar_in))
-    sums = butterfly_sum(terms, order[:3], doubling_plan(order[3:]))
-    kernel_sum, bias_sum = sums[:-1], sums[-1:]
+    sums, polar_out = butterfly_sum(
+        jnp.concatenate([kernel_terms, bias_terms], axis=0), order[:3], doubling_plan(order[3:]), polar_out
+    )
+    polar_in = from_behind(polar_out, "lon", half).astype(jnp.float32)
     cell_grad = cell_grad.at[0].add(jnp.where(band == 0, polar_in[0], 0.0))
     cell_grad = cell_grad.at[-1].add(jnp.where(band == bands - 1, polar_in[1], 0.0))
     input_grad = cell_grad.astype(jnp.bfloat16)
-
+    kernel_sum, bias_sum = sums[:-1], sums[-1:]
     total_cells = rows * cols * lax.axis_size("lon") * lax.axis_size("lat")
     scale = 1.0 / jnp.sqrt(jnp.float32(total_cells))
     weight_grad = kernel_sum.reshape(3, 3, chans, chans) * scale

time: 102 us -> 100 us (0.980)
  waiting for transfers between devices: 33.6 us -> 26.5 us
  starting transfers between devices: 43.2 us -> 48.5 us
    ppermute x5, waiting for transfers between devices: 16.9 us -> 11.4 us  [butterfly_sum(): data = data + lax.ppermute(data, axis, pairs)]
    ppermute x5, starting transfers between devices: 7.82 us -> 12 us  [butterfly_sum(): data = data + lax.ppermute(data, axis, pairs)]
    ppermute x3, starting transfers between devices: 9.54 us -> 12.3 us  [butterfly_sum(): other = lax.ppermute(data, axis, pairs)]
    ppermute x2, starting transfers between devices: 12.9 us -> 11.4 us  [from_behind(): return lax.ppermute(value, axis, pairs)]
    ppermute x3, waiting for transfers between devices: 3.29 us -> 1.74 us  [butterfly_sum(): other = lax.ppermute(data, axis, pairs)]
    unnamed x19 -> x17, local copies, waits for them, and re-layouts: 3.35 us -> 3.35 us
  transfers between devices with their start and end apart: 17 -> 17, of which waited for: 14 -> 13; matrix products, arithmetic and copies ran while one was open for 10% -> 7% of each run, Pallas kernels for 0% -> 0%
where the time goes in v13:
time: 100 us
  starting transfers between devices  48.5 us (48%)
  waiting for transfers between devices  26.5 us (26%)
  matrix products  8.85 us (9%)
  other arithmetic  8.34 us (8%)
  local copies, waits for them, and re-layouts  6.76 us (7%)
  between operations  1.12 us (1%)
    ppermute x3, starting transfers between devices, butterfly_sum(): other = lax.ppermute(data, axis, pairs)  12.3 us
    ppermute x5, starting transfers between devices, butterfly_sum(): data = data + lax.ppermute(data, axis, pairs)  12 us
    ppermute x5, waiting for transfers between devices, butterfly_sum(): data = data + lax.ppermute(data, axis, pairs)  11.4 us
    ppermute x2, starting transfers between devices, from_behind(): return lax.ppermute(value, axis, pairs)  11.4 us
    ppermute x3, waiting for transfers between devices, butterfly_sum(): data = keep + lax.ppermute(send, axis, pairs)  7.38 us
    ppermute x2, starting transfers between devices, extended(): lax.ppermute(tail, axis, [(i, (i + 1) % count) for i in range(ends)])  6.42 us
    ppermute x3, starting transfers between devices, butterfly_sum(): data = keep + lax.ppermute(send, axis, pairs)  5.15 us
    dot_general x9, matrix products, shards(): lax.dot_general(window, pre_grad, (((0,), (0,)), ((), ())), preferred_ele...  4.46 us
  transfers between devices with their start and end apart: 17, of which 13 were waited for; matrix products, arithmetic and copies ran while one was open for 7% of the time, Pallas kernels for 0%

profile of v13, /device:TPU:1, one launch (start us, length us, event | category | flops | bytes accessed | tf_op | source)
XLA Modules:
  0.0 100.0 jit_solution(12375506778095259003)
XLA Ops:
  0.6 1.2 %constant_dynamic-update-slice_fusion.1 = bf16[48,48,256]{2,1,0:T(8,128)(2,1)S(1)} fusion(bf16[48,48,128]{2,1,0:T(8,128)(2,1)} %param.12), kind=kLoop, calls=%fused_computation.113 | loop fusion | bytes 1179648
  2.1 4.2 %collective-permute-start = (bf16[48,2,256]{2,1,0:T(2,128)(2,1)S(1)}, bf16[48,2,256]{2,1,0:T(2,128)(2,1)S(1)}, u32[]{:S(2)}, u32[]{:S(2)}) collective-permute-start(bf16[48,2,256]{2,1,0:T(2,128)(2,1)S(1)} %get-tuple-element.61), channel_id=1, source_target_pairs={{0,8},{8,16},{16,24},{24,32},{32,40},{40,48},{48,56},{56,64},{64,7... | collective-permute-start | bytes 147464 | tf_op jit(solution)/shard_map/ppermute | solution.py:15
  6.3 1.2 %collective-permute-done = bf16[48,2,256]{2,1,0:T(2,128)(2,1)S(1)} collective-permute-done((bf16[48,2,256]{2,1,0:T(2,128)(2,1)S(1)}, bf16[48,2,256]{2,1,0:T(2,128)(2,1)S(1)}, u32[]{:S(2)}, u32[]{:S(2)}) %collective-permute-start) | collective-permute-done | bytes 49184 | tf_op jit(solution)/shard_map/ppermute | solution.py:15
  7.5 3.8 %collective-permute-done.1 = bf16[48,2,256]{2,1,0:T(2,128)(2,1)S(1)} collective-permute-done((bf16[48,2,256]{2,1,0:T(2,128)(2,1)S(1)}, bf16[48,2,256]{2,1,0:T(2,128)(2,1)S(1)}, u32[]{:S(2)}, u32[]{:S(2)}) %collective-permute-start.1) | collective-permute-done | bytes 49184 | tf_op jit(solution)/shard_map/ppermute | solution.py:17
  11.4 2.2 %collective-permute-start.2 = (bf16[2,52,256]{2,1,0:T(8,128)(2,1)S(1)}, bf16[2,52,256]{2,1,0:T(8,128)(2,1)S(1)}, u32[]{:S(2)}, u32[]{:S(2)}) collective-permute-start(bf16[2,52,256]{2,1,0:T(8,128)(2,1)S(1)} %get-tuple-element.63), channel_id=1, source_target_pairs={{0,1},{1,2},{2,3},{3,4},{4,5},{5,6},{6,7},{8,9},{9,10},{10,11},{11... | collective-permute-start | bytes 159752 | tf_op jit(solution)/shard_map/ppermute | solution.py:15
  13.6 1.3 %collective-permute-start.3 = (bf16[2,52,256]{2,1,0:T(8,128)(2,1)S(1)}, bf16[2,52,256]{2,1,0:T(8,128)(2,1)S(1)}, u32[]{:S(2)}, u32[]{:S(2)}) collective-permute-start(bf16[2,52,256]{2,1,0:T(8,128)(2,1)S(1)} %get-tuple-element.64), channel_id=1, source_target_pairs={{1,0},{2,1},{3,2},{4,3},{5,4},{6,5},{7,6},{9,8},{10,9},{11,10},{12... | collective-permute-start | bytes 159752 | tf_op jit(solution)/shard_map/ppermute | solution.py:17
  15.0 7.2 %collective-permute-start.4 = (bf16[2,52,256]{2,1,0:T(8,128)(2,1)S(1)}, bf16[2,52,256]{2,1,0:T(8,128)(2,1)S(1)}, u32[]{:S(2)}, u32[]{:S(2)}) collective-permute-start(bf16[2,52,256]{2,1,0:T(8,128)(2,1)S(1)} %get-tuple-element.58), channel_id=1, source_target_pairs={{0,128},{8,136},{16,144},{24,152},{32,160},{40,168},{48,176},{56,1... | collective-permute-start | bytes 159752 | tf_op jit(solution)/shard_map/ppermute | solution.py:27
  22.3 0.8 pad_maximum_fusion
  23.0 0.9 collective-permute-done.4
  24.2 0.9 copy-done
  25.3 0.7 copy-done.3
  26.1 1.8 %convolution_select_fusion.1 = f32[50,8,7,128]{3,1,2,0:T(8,128)S(1)} fusion(bf16[3,3,128,128]{3,2,1,0:T(8,128)(2,1)S(1)} %copy-done.3, bf16[52,1,7,2,128]{4,2,3,0,1:T(8,128)(2,1)S(1)} %slice.267, bf16[52,1,8,7,128]{4,2,3,0,1:T(8,128)(2,1)S(1)} %copy.10, pred[8,7]{0,1:T(8,128)(4,1)S(1)} %copy-done.6), kind=kOutput, calls=%fused_computation.10 | convolution fusion | flops 828987392 | bytes 2660408 | tf_op jit(solution)/shard_map/conv_general_dilated | solution.py:109
  28.3 1.3 %reshape.171 = f32[50,1,56,128]{3,2,0,1:T(8,128)} reshape(f32[50,8,7,128]{3,2,1,0:T(8,128)S(1)} %copy.11) | data formatting | bytes 2867200 | tf_op jit(solution)/shard_map/conv_general_dilated | solution.py:109
  29.5 2.5 %fusion.29 = (bf16[50,50,128]{2,1,0:T(8,128)(2,1)S(1)}, f32[50,50,128]{2,1,0:T(8,128)S(1)}) fusion(bf16[52,52,256]{2,1,0:T(8,128)(2,1)} %copy-done, pred[50]{0:T(512)(128)(4,1)S(1)} %and_or_fusion, f32[128]{0:T(128)S(1)} %copy-done.4, f32[50,1,56,128]{3,2,0,1:T(8,128)} %reshape.171), kind=kLoop, calls=%fused_computation.52 | loop fusion | flops 3840000 | bytes 3840562 | tf_op jit(solution)/shard_map/jit(_where)/select_n | solution.py:122
  32.4 0.5 fusion.12
  32.8 0.5 fusion.11
  33.3 0.5 fusion.10
  33.9 0.5 fusion.9
  34.4 0.5 fusion.8
  34.9 0.5 fusion.7
  35.4 0.5 fusion.6
  35.9 0.5 fusion.5
  36.4 0.5 fusion.4
  37.1 1.8 %collective-permute-start.5 = (f32[73792]{0:T(1024)S(1)}, f32[73792]{0:T(1024)S(1)}, u32[]{:S(2)}, u32[]{:S(2)}) collective-permute-start(f32[73792]{0:T(1024)S(1)} %dynamic_slice.19), channel_id=1, source_target_pairs={{0,8},{8,0},{16,24},{24,16},{32,40},{40,32},{48,56},{56,48},{64,72... | collective-permute-start | bytes 885512 | tf_op jit(solution)/shard_map/ppermute | solution.py:44
  39.2 0.8 collective-permute-done.5
  40.3 2.9 %collective-permute-start.6 = (f32[36896]{0:T(1024)S(1)}, f32[36896]{0:T(1024)S(1)}, u32[]{:S(2)}, u32[]{:S(2)}) collective-permute-start(f32[36896]{0:T(1024)S(1)} %dynamic_slice.21), channel_id=1, source_target_pairs={{0,1},{1,0},{2,3},{3,2},{4,5},{5,4},{6,7},{7,6},{8,9},{9,8},{10,11... | collective-permute-start | bytes 442760 | tf_op jit(solution)/shard_map/ppermute | solution.py:44
  43.4 3.8 %collective-permute-done.6 = f32[36896]{0:T(1024)S(1)} collective-permute-done((f32[36896]{0:T(1024)S(1)}, f32[36896]{0:T(1024)S(1)}, u32[]{:S(2)}, u32[]{:S(2)}) %collective-permute-start.6) | collective-permute-done | bytes 147616 | tf_op jit(solution)/shard_map/ppermute | solution.py:44
  47.4 0.5 collective-permute-start.7
  48.0 2.7 %collective-permute-done.7 = f32[18448]{0:T(1024)S(1)} collective-permute-done((f32[18448]{0:T(1024)S(1)}, f32[18448]{0:T(1024)S(1)}, u32[]{:S(2)}, u32[]{:S(2)}) %collective-permute-start.7) | collective-permute-done | bytes 73824 | tf_op jit(solution)/shard_map/ppermute | solution.py:44
  50.8 2.7 %collective-permute-start.8 = (f32[18448]{0:T(1024)S(1)}, f32[18448]{0:T(1024)S(1)}, u32[]{:S(2)}, u32[]{:S(2)}) collective-permute-start(f32[18448]{0:T(1024)S(1)} %dynamic-slice_add_fusion.2), channel_id=1, source_target_pairs={{0,2},{1,3},{2,0},{3,1},{4,6},{5,7},{6,4},{7,5},{8,10},{9,11},{10,... | collective-permute-start | bytes 221384 | tf_op jit(solution)/shard_map/ppermute | solution.py:47
  53.7 1.7 %collective-permute-done.8 = f32[18448]{0:T(1024)S(1)} collective-permute-done((f32[18448]{0:T(1024)S(1)}, f32[18448]{0:T(1024)S(1)}, u32[]{:S(2)}, u32[]{:S(2)}) %collective-permute-start.8) | collective-permute-done | bytes 73824 | tf_op jit(solution)/shard_map/ppermute | solution.py:47
  55.3 0.7 collective-permute-start.9
  56.1 4.1 %collective-permute-done.9 = f32[18448]{0:T(1024)S(1)} collective-permute-done((f32[18448]{0:T(1024)S(1)}, f32[18448]{0:T(1024)S(1)}, u32[]{:S(2)}, u32[]{:S(2)}) %collective-permute-start.9) | collective-permute-done | bytes 73824 | tf_op jit(solution)/shard_map/ppermute | solution.py:47
  60.2 2.5 %collective-permute-start.10 = (f32[18448]{0:T(1024)S(1)}, f32[18448]{0:T(1024)S(1)}, u32[]{:S(2)}, u32[]{:S(2)}) collective-permute-start(f32[18448]{0:T(1024)S(1)} %add.118), channel_id=1, source_target_pairs={{0,64},{8,72},{16,80},{24,88},{32,96},{40,104},{48,112},{56,120},{... | collective-permute-start | bytes 221384 | tf_op jit(solution)/shard_map/ppermute | solution.py:47
  62.9 1.7 %collective-permute-done.10 = f32[18448]{0:T(1024)S(1)} collective-permute-done((f32[18448]{0:T(1024)S(1)}, f32[18448]{0:T(1024)S(1)}, u32[]{:S(2)}, u32[]{:S(2)}) %collective-permute-start.10) | collective-permute-done | bytes 73824 | tf_op jit(solution)/shard_map/ppermute | solution.py:47
  64.5 3.1 %collective-permute-start.11 = (f32[18448]{0:T(1024)S(1)}, f32[18448]{0:T(1024)S(1)}, u32[]{:S(2)}, u32[]{:S(2)}) collective-permute-start(f32[18448]{0:T(1024)S(1)} %add.119), channel_id=1, source_target_pairs={{0,192},{8,200},{16,208},{24,216},{32,224},{40,232},{48,240},{56,2... | collective-permute-start | bytes 221384 | tf_op jit(solution)/shard_map/ppermute | solution.py:47
  67.7 2.3 %collective-permute-done.11 = f32[18448]{0:T(1024)S(1)} collective-permute-done((f32[18448]{0:T(1024)S(1)}, f32[18448]{0:T(1024)S(1)}, u32[]{:S(2)}, u32[]{:S(2)}) %collective-permute-start.11) | collective-permute-done | bytes 73824 | tf_op jit(solution)/shard_map/ppermute | solution.py:47
  70.0 3.0 %collective-permute-start.12 = (f32[18448]{0:T(1024)S(1)}, f32[18448]{0:T(1024)S(1)}, u32[]{:S(2)}, u32[]{:S(2)}) collective-permute-start(f32[18448]{0:T(1024)S(1)} %add.120), channel_id=1, source_target_pairs={{0,6},{1,7},{2,4},{3,5},{4,2},{5,3},{6,0},{7,1},{8,14},{9,15},{10,... | collective-permute-start | bytes 221384 | tf_op jit(solution)/shard_map/ppermute | solution.py:47
  73.0 1.8 %collective-permute-done.12 = f32[18448]{0:T(1024)S(1)} collective-permute-done((f32[18448]{0:T(1024)S(1)}, f32[18448]{0:T(1024)S(1)}, u32[]{:S(2)}, u32[]{:S(2)}) %collective-permute-start.12) | collective-permute-done | bytes 73824 | tf_op jit(solution)/shard_map/ppermute | solution.py:47
  74.8 2.3 %collective-permute-start.14 = (f32[18448]{0:T(1024)S(1)}, f32[18448]{0:T(1024)S(1)}, u32[]{:S(2)}, u32[]{:S(2)}) collective-permute-start(f32[18448]{0:T(1024)S(1)} %add.121), channel_id=1, source_target_pairs={{0,32},{8,40},{16,48},{24,56},{32,0},{40,8},{48,16},{56,24},{64,96... | collective-permute-start | bytes 221384 | tf_op jit(solution)/shard_map/ppermute | solution.py:52
  77.1 1.1 %fusion.3 = bf16[48,48,128]{2,1,0:T(8,128)(2,1)} fusion(f32[50,50,128]{2,1,0:T(8,128)S(1)} %add_divide_fusion, f32[50,50,128]{2,1,0:T(8,128)S(1)} %get-tuple-element.57), kind=kLoop, calls=%fused_computation.12 | loop fusion | flops 589824 | bytes 2949120 | tf_op jit(solution)/shard_map/convert.4
  78.7 4.2 %collective-permute-start.13 = (bf16[2,48,128]{2,1,0:T(8,128)(2,1)S(1)}, bf16[2,48,128]{2,1,0:T(8,128)(2,1)S(1)}, u32[]{:S(2)}, u32[]{:S(2)}) collective-permute-start(bf16[2,48,128]{2,1,0:T(8,128)(2,1)S(1)} %pad_maximum_fusion.1), channel_id=1, source_target_pairs={{0,128},{8,136},{16,144},{24,152},{32,160},{40,168},{48,176},{56,1... | collective-permute-start | bytes 73736 | tf_op jit(solution)/shard_map/ppermute | solution.py:27
  83.4 1.8 %convolution_select_fusion = f32[48,8,7,128]{3,1,2,0:T(8,128)S(1)} fusion(bf16[3,3,128,128]{3,2,1,0:T(8,128)(2,1)S(1)} %copy-done.3, bf16[50,1,7,2,128]{4,2,3,0,1:T(8,128)(2,1)S(1)} %slice.272, bf16[50,1,8,7,128]{4,2,3,0,1:T(8,128)(2,1)S(1)} %copy.13, pred[8,7]{0,1:T(8,128)(4,1)S(1)} %copy-done.5), kind=kOutput, calls=%fused_computation.5 | convolution fusion | flops 795832320 | bytes 2567224 | tf_op jit(solution)/shard_map/conv_general_dilated | solution.py:125
  86.0 1.4 %collective-permute-done.15 = f32[36896]{0:T(1024)S(1)} collective-permute-done((f32[36896]{0:T(1024)S(1)}, f32[36896]{0:T(1024)S(1)}, u32[]{:S(2)}, u32[]{:S(2)}) %collective-permute-start.15) | collective-permute-done | bytes 147616 | tf_op jit(solution)/shard_map/ppermute | solution.py:52
  87.6 9.6 %collective-permute-start.16 = (f32[73792]{0:T(1024)S(1)}, f32[73792]{0:T(1024)S(1)}, u32[]{:S(2)}, u32[]{:S(2)}) collective-permute-start(f32[73792]{0:T(1024)S(1)} %maximum_select_fusion.1), channel_id=1, source_target_pairs={{0,8},{8,0},{16,24},{24,16},{32,40},{40,32},{48,56},{56,48},{64,72... | collective-permute-start | bytes 885512 | tf_op jit(solution)/shard_map/ppermute | solution.py:52
  97.2 0.9 convert_element_type.22
  98.6 0.5 slice_multiply_fusion.2
  99.1 0.9 slice_multiply_fusion.1
  (68 shorter events, 5.8 us)
Async XLA Ops:
  0.6 1.2 %copy-start.2 = (bf16[48,48,128]{2,1,0:T(8,128)(2,1)S(1)}, bf16[48,48,128]{2,1,0:T(8,128)(2,1)}, u32[]{:S(2)}) copy-start(bf16[48,48,128]{2,1,0:T(8,128)(2,1)} %param.15) | copy-start | bytes 1769476
  2.1 5.4 %collective-permute-start = (bf16[48,2,256]{2,1,0:T(2,128)(2,1)S(1)}, bf16[48,2,256]{2,1,0:T(2,128)(2,1)S(1)}, u32[]{:S(2)}, u32[]{:S(2)}) collective-permute-start(bf16[48,2,256]{2,1,0:T(2,128)(2,1)S(1)} %get-tuple-element.61), channel_id=1, source_target_pairs={{0,8},{8,16},{16,24},{24,32},{32,40},{40,48},{48,56},{56,64},{64,7... | collective-permute-start | bytes 147464 | tf_op jit(solution)/shard_map/ppermute | solution.py:15
  6.3 5.0 %collective-permute-start.1 = (bf16[48,2,256]{2,1,0:T(2,128)(2,1)S(1)}, bf16[48,2,256]{2,1,0:T(2,128)(2,1)S(1)}, u32[]{:S(2)}, u32[]{:S(2)}) collective-permute-start(bf16[48,2,256]{2,1,0:T(2,128)(2,1)S(1)} %get-tuple-element.62), channel_id=1, source_target_pairs={{8,0},{16,8},{24,16},{32,24},{40,32},{48,40},{56,48},{64,56},{72,6... | collective-permute-start | bytes 147464 | tf_op jit(solution)/shard_map/ppermute | solution.py:17
  11.4 10.8 %collective-permute-start.2 = (bf16[2,52,256]{2,1,0:T(8,128)(2,1)S(1)}, bf16[2,52,256]{2,1,0:T(8,128)(2,1)S(1)}, u32[]{:S(2)}, u32[]{:S(2)}) collective-permute-start(bf16[2,52,256]{2,1,0:T(8,128)(2,1)S(1)} %get-tuple-element.63), channel_id=1, source_target_pairs={{0,1},{1,2},{2,3},{3,4},{4,5},{5,6},{6,7},{8,9},{9,10},{10,11},{11... | collective-permute-start | bytes 159752 | tf_op jit(solution)/shard_map/ppermute | solution.py:15
  13.6 8.6 %collective-permute-start.3 = (bf16[2,52,256]{2,1,0:T(8,128)(2,1)S(1)}, bf16[2,52,256]{2,1,0:T(8,128)(2,1)S(1)}, u32[]{:S(2)}, u32[]{:S(2)}) collective-permute-start(bf16[2,52,256]{2,1,0:T(8,128)(2,1)S(1)} %get-tuple-element.64), channel_id=1, source_target_pairs={{1,0},{2,1},{3,2},{4,3},{5,4},{6,5},{7,6},{9,8},{10,9},{11,10},{12... | collective-permute-start | bytes 159752 | tf_op jit(solution)/shard_map/ppermute | solution.py:17
  15.0 8.9 %collective-permute-start.4 = (bf16[2,52,256]{2,1,0:T(8,128)(2,1)S(1)}, bf16[2,52,256]{2,1,0:T(8,128)(2,1)S(1)}, u32[]{:S(2)}, u32[]{:S(2)}) collective-permute-start(bf16[2,52,256]{2,1,0:T(8,128)(2,1)S(1)} %get-tuple-element.58), channel_id=1, source_target_pairs={{0,128},{8,136},{16,144},{24,152},{32,160},{40,168},{48,176},{56,1... | collective-permute-start | bytes 159752 | tf_op jit(solution)/shard_map/ppermute | solution.py:27
  23.9 1.1 %copy-start = (bf16[52,52,256]{2,1,0:T(8,128)(2,1)}, bf16[52,52,256]{2,1,0:T(8,128)(2,1)S(1)}, u32[]{:S(2)}) copy-start(bf16[52,52,256]{2,1,0:T(8,128)(2,1)S(1)} %fusion.66) | copy-start | bytes 4153348
  25.1 1.0 copy-start.3
  25.1 1.0 copy-start.6
  28.3 1.3 %copy-start.4 = (f32[128]{0:T(128)S(1)}, f32[128]{0:T(128)}, u32[]{:S(2)}) copy-start(f32[128]{0:T(128)} %param.14) | copy-start | bytes 1540
  29.5 2.8 %copy-start.1 = (bf16[52,52,256]{2,1,0:T(8,128)(2,1)S(1)}, bf16[52,52,256]{2,1,0:T(8,128)(2,1)}, u32[]{:S(2)}) copy-start(bf16[52,52,256]{2,1,0:T(8,128)(2,1)} %copy-done) | copy-start | bytes 4153348
  37.1 3.0 %collective-permute-start.5 = (f32[73792]{0:T(1024)S(1)}, f32[73792]{0:T(1024)S(1)}, u32[]{:S(2)}, u32[]{:S(2)}) collective-permute-start(f32[73792]{0:T(1024)S(1)} %dynamic_slice.19), channel_id=1, source_target_pairs={{0,8},{8,0},{16,24},{24,16},{32,40},{40,32},{48,56},{56,48},{64,72... | collective-permute-start | bytes 885512 | tf_op jit(solution)/shard_map/ppermute | solution.py:44
  40.3 6.8 %collective-permute-start.6 = (f32[36896]{0:T(1024)S(1)}, f32[36896]{0:T(1024)S(1)}, u32[]{:S(2)}, u32[]{:S(2)}) collective-permute-start(f32[36896]{0:T(1024)S(1)} %dynamic_slice.21), channel_id=1, source_target_pairs={{0,1},{1,0},{2,3},{3,2},{4,5},{5,4},{6,7},{7,6},{8,9},{9,8},{10,11... | collective-permute-start | bytes 442760 | tf_op jit(solution)/shard_map/ppermute | solution.py:44
  47.4 3.3 %collective-permute-start.7 = (f32[18448]{0:T(1024)S(1)}, f32[18448]{0:T(1024)S(1)}, u32[]{:S(2)}, u32[]{:S(2)}) collective-permute-start(f32[18448]{0:T(1024)S(1)} %dynamic_slice.23), channel_id=1, source_target_pairs={{0,32},{8,40},{16,48},{24,56},{32,0},{40,8},{48,16},{56,24},{64,96... | collective-permute-start | bytes 221384 | tf_op jit(solution)/shard_map/ppermute | solution.py:44
  50.8 4.5 %collective-permute-start.8 = (f32[18448]{0:T(1024)S(1)}, f32[18448]{0:T(1024)S(1)}, u32[]{:S(2)}, u32[]{:S(2)}) collective-permute-start(f32[18448]{0:T(1024)S(1)} %dynamic-slice_add_fusion.2), channel_id=1, source_target_pairs={{0,2},{1,3},{2,0},{3,1},{4,6},{5,7},{6,4},{7,5},{8,10},{9,11},{10,... | collective-permute-start | bytes 221384 | tf_op jit(solution)/shard_map/ppermute | solution.py:47
  55.3 4.8 %collective-permute-start.9 = (f32[18448]{0:T(1024)S(1)}, f32[18448]{0:T(1024)S(1)}, u32[]{:S(2)}, u32[]{:S(2)}) collective-permute-start(f32[18448]{0:T(1024)S(1)} %add.117), channel_id=1, source_target_pairs={{0,16},{8,24},{16,0},{24,8},{32,48},{40,56},{48,32},{56,40},{64,80... | collective-permute-start | bytes 221384 | tf_op jit(solution)/shard_map/ppermute | solution.py:47
  60.2 4.3 %collective-permute-start.10 = (f32[18448]{0:T(1024)S(1)}, f32[18448]{0:T(1024)S(1)}, u32[]{:S(2)}, u32[]{:S(2)}) collective-permute-start(f32[18448]{0:T(1024)S(1)} %add.118), channel_id=1, source_target_pairs={{0,64},{8,72},{16,80},{24,88},{32,96},{40,104},{48,112},{56,120},{... | collective-permute-start | bytes 221384 | tf_op jit(solution)/shard_map/ppermute | solution.py:47
  64.5 5.5 %collective-permute-start.11 = (f32[18448]{0:T(1024)S(1)}, f32[18448]{0:T(1024)S(1)}, u32[]{:S(2)}, u32[]{:S(2)}) collective-permute-start(f32[18448]{0:T(1024)S(1)} %add.119), channel_id=1, source_target_pairs={{0,192},{8,200},{16,208},{24,216},{32,224},{40,232},{48,240},{56,2... | collective-permute-start | bytes 221384 | tf_op jit(solution)/shard_map/ppermute | solution.py:47
  70.0 4.8 %collective-permute-start.12 = (f32[18448]{0:T(1024)S(1)}, f32[18448]{0:T(1024)S(1)}, u32[]{:S(2)}, u32[]{:S(2)}) collective-permute-start(f32[18448]{0:T(1024)S(1)} %add.120), channel_id=1, source_target_pairs={{0,6},{1,7},{2,4},{3,5},{4,2},{5,3},{6,0},{7,1},{8,14},{9,15},{10,... | collective-permute-start | bytes 221384 | tf_op jit(solution)/shard_map/ppermute | solution.py:47
  74.8 8.1 %collective-permute-start.14 = (f32[18448]{0:T(1024)S(1)}, f32[18448]{0:T(1024)S(1)}, u32[]{:S(2)}, u32[]{:S(2)}) collective-permute-start(f32[18448]{0:T(1024)S(1)} %add.121), channel_id=1, source_target_pairs={{0,32},{8,40},{16,48},{24,56},{32,0},{40,8},{48,16},{56,24},{64,96... | collective-permute-start | bytes 221384 | tf_op jit(solution)/shard_map/ppermute | solution.py:52
  78.5 4.9 %copy-start.5 = (pred[8,7]{0,1:T(8,128)(4,1)S(1)}, pred[8,7]{0,1:T(8,128)(4,1)}, u32[]{:S(2)}) copy-start(pred[8,7]{0,1:T(8,128)(4,1)} %constant.203) | copy-start | bytes 172
  78.7 7.3 %collective-permute-start.13 = (bf16[2,48,128]{2,1,0:T(8,128)(2,1)S(1)}, bf16[2,48,128]{2,1,0:T(8,128)(2,1)S(1)}, u32[]{:S(2)}, u32[]{:S(2)}) collective-permute-start(bf16[2,48,128]{2,1,0:T(8,128)(2,1)S(1)} %pad_maximum_fusion.1), channel_id=1, source_target_pairs={{0,128},{8,136},{16,144},{24,152},{32,160},{40,168},{48,176},{56,1... | collective-permute-start | bytes 73736 | tf_op jit(solution)/shard_map/ppermute | solution.py:27
  83.0 4.4 %collective-permute-start.15 = (f32[36896]{0:T(1024)S(1)}, f32[36896]{0:T(1024)S(1)}, u32[]{:S(2)}, u32[]{:S(2)}) collective-permute-start(f32[36896]{0:T(1024)S(1)} %maximum_select_fusion.2), channel_id=1, source_target_pairs={{0,1},{1,0},{2,3},{3,2},{4,5},{5,4},{6,7},{7,6},{8,9},{9,8},{10,11... | collective-permute-start | bytes 442760 | tf_op jit(solution)/shard_map/ppermute | solution.py:52
  87.6 10.8 %collective-permute-start.16 = (f32[73792]{0:T(1024)S(1)}, f32[73792]{0:T(1024)S(1)}, u32[]{:S(2)}, u32[]{:S(2)}) collective-permute-start(f32[73792]{0:T(1024)S(1)} %maximum_select_fusion.1), channel_id=1, source_target_pairs={{0,8},{8,0},{16,24},{24,16},{32,40},{40,32},{48,56},{56,48},{64,72... | collective-permute-start | bytes 885512 | tf_op jit(solution)/shard_map/ppermute | solution.py:52

commit v14 on v4

--- a/solution.py
+++ b/solution.py
@@ -89,7 +89,7 @@
         if axis == "lon" and step == 16 and count == 32:
             pairs = reflected_ring_pairs(lon, 4, 8)
         plan.append((axis, pairs))
-    return plan
+    return [step for step in plan if step[0] == "lat"] + [step for step in plan if step[0] != "lat"]
 
 
 def shards(inputs, weight, bias, cotangent):

time: 96.9 us -> 97.1 us (level)
  waiting for transfers between devices: 19.7 us -> 20.8 us
    ppermute x5, waiting for transfers between devices: 6.51 us -> 7.82 us  [butterfly_sum(): data = data + lax.ppermute(data, axis, pairs)]
where the time goes in v14:
time: 97.1 us; the launch traced here: 96.5 us
  starting transfers between devices  46.1 us (47%)
  waiting for transfers between devices  20.8 us (21%)
  matrix products  13.5 us (14%)
  other arithmetic  8.35 us (9%)
  local copies, waits for them, and re-layouts  6.75 us (7%)
  between operations  1.07 us (1%)
    ppermute x3, starting transfers between devices, butterfly_sum(): other = lax.ppermute(data, axis, pairs)  12.1 us
    ppermute x5, starting transfers between devices, butterfly_sum(): data = data + lax.ppermute(data, axis, pairs)  11.3 us
    ppermute x2, starting transfers between devices, from_behind(): return lax.ppermute(value, axis, pairs)  9.82 us
    ppermute x5, waiting for transfers between devices, butterfly_sum(): data = data + lax.ppermute(data, axis, pairs)  7.82 us
    ppermute x2, starting transfers between devices, extended(): lax.ppermute(tail, axis, [(i, (i + 1) % count) for i in range(ends)])  6.42 us
    ppermute x3, waiting for transfers between devices, butterfly_sum(): data = keep + lax.ppermute(send, axis, pairs)  5.36 us
    dot_general x6, matrix products, shards(): jnp.dot(grad_ext[line_at, tap_b:tap_b + cols], weight[tap_a, 2 - tap_b].T...  5.31 us
    ppermute x3, starting transfers between devices, butterfly_sum(): data = keep + lax.ppermute(send, axis, pairs)  5.15 us
  transfers between devices with their start and end apart: 17, of which 13 were waited for; matrix products, arithmetic and copies ran while one was open for 12% of the time, Pallas kernels for 0%

profile of v14, /device:TPU:1, one launch (start us, length us, event | category | flops | bytes accessed | tf_op | source)
XLA Modules:
  0.0 96.5 jit_solution(12567566678792675939)
XLA Ops:
  0.6 1.2 %constant_dynamic-update-slice_fusion.1 = bf16[48,48,256]{2,1,0:T(8,128)(2,1)S(1)} fusion(bf16[48,48,128]{2,1,0:T(8,128)(2,1)} %param.12), kind=kLoop, calls=%fused_computation.113 | loop fusion | bytes 1179648
  2.1 4.2 %collective-permute-start = (bf16[48,2,256]{2,1,0:T(2,128)(2,1)S(1)}, bf16[48,2,256]{2,1,0:T(2,128)(2,1)S(1)}, u32[]{:S(2)}, u32[]{:S(2)}) collective-permute-start(bf16[48,2,256]{2,1,0:T(2,128)(2,1)S(1)} %get-tuple-element.57), channel_id=1, source_target_pairs={{0,8},{8,16},{16,24},{24,32},{32,40},{40,48},{48,56},{56,64},{64,7... | collective-permute-start | bytes 147464 | tf_op jit(solution)/shard_map/ppermute | solution.py:15
  6.3 1.2 %collective-permute-done = bf16[48,2,256]{2,1,0:T(2,128)(2,1)S(1)} collective-permute-done((bf16[48,2,256]{2,1,0:T(2,128)(2,1)S(1)}, bf16[48,2,256]{2,1,0:T(2,128)(2,1)S(1)}, u32[]{:S(2)}, u32[]{:S(2)}) %collective-permute-start) | collective-permute-done | bytes 49184 | tf_op jit(solution)/shard_map/ppermute | solution.py:15
  7.5 3.8 %collective-permute-done.1 = bf16[48,2,256]{2,1,0:T(2,128)(2,1)S(1)} collective-permute-done((bf16[48,2,256]{2,1,0:T(2,128)(2,1)S(1)}, bf16[48,2,256]{2,1,0:T(2,128)(2,1)S(1)}, u32[]{:S(2)}, u32[]{:S(2)}) %collective-permute-start.1) | collective-permute-done | bytes 49184 | tf_op jit(solution)/shard_map/ppermute | solution.py:17
  11.4 2.2 %collective-permute-start.2 = (bf16[2,52,256]{2,1,0:T(8,128)(2,1)S(1)}, bf16[2,52,256]{2,1,0:T(8,128)(2,1)S(1)}, u32[]{:S(2)}, u32[]{:S(2)}) collective-permute-start(bf16[2,52,256]{2,1,0:T(8,128)(2,1)S(1)} %get-tuple-element.59), channel_id=1, source_target_pairs={{0,1},{1,2},{2,3},{3,4},{4,5},{5,6},{6,7},{8,9},{9,10},{10,11},{11... | collective-permute-start | bytes 159752 | tf_op jit(solution)/shard_map/ppermute | solution.py:15
  13.6 1.3 %collective-permute-start.3 = (bf16[2,52,256]{2,1,0:T(8,128)(2,1)S(1)}, bf16[2,52,256]{2,1,0:T(8,128)(2,1)S(1)}, u32[]{:S(2)}, u32[]{:S(2)}) collective-permute-start(bf16[2,52,256]{2,1,0:T(8,128)(2,1)S(1)} %get-tuple-element.60), channel_id=1, source_target_pairs={{1,0},{2,1},{3,2},{4,3},{5,4},{6,5},{7,6},{9,8},{10,9},{11,10},{12... | collective-permute-start | bytes 159752 | tf_op jit(solution)/shard_map/ppermute | solution.py:17
  15.0 7.2 %collective-permute-start.4 = (bf16[2,52,256]{2,1,0:T(8,128)(2,1)S(1)}, bf16[2,52,256]{2,1,0:T(8,128)(2,1)S(1)}, u32[]{:S(2)}, u32[]{:S(2)}) collective-permute-start(bf16[2,52,256]{2,1,0:T(8,128)(2,1)S(1)} %get-tuple-element.54), channel_id=1, source_target_pairs={{0,128},{8,136},{16,144},{24,152},{32,160},{40,168},{48,176},{56,1... | collective-permute-start | bytes 159752 | tf_op jit(solution)/shard_map/ppermute | solution.py:27
  22.2 0.8 pad_maximum_fusion
  23.0 0.9 collective-permute-done.4
  24.1 0.9 copy-done
  25.3 0.7 copy-done.3
  26.0 1.9 %convolution_select_fusion.1 = f32[50,8,7,128]{3,1,2,0:T(8,128)S(1)} fusion(bf16[3,3,128,128]{3,2,1,0:T(8,128)(2,1)S(1)} %copy-done.3, bf16[52,1,7,2,128]{4,2,3,0,1:T(8,128)(2,1)S(1)} %slice.267, bf16[52,1,8,7,128]{4,2,3,0,1:T(8,128)(2,1)S(1)} %copy.10, pred[8,7]{0,1:T(8,128)(4,1)S(1)} %copy-done.7), kind=kOutput, calls=%fused_computation.10 | convolution fusion | flops 828987392 | bytes 2660408 | tf_op jit(solution)/shard_map/conv_general_dilated | solution.py:108
  28.3 1.2 %reshape.171 = f32[50,1,56,128]{3,2,0,1:T(8,128)} reshape(f32[50,8,7,128]{3,2,1,0:T(8,128)S(1)} %copy.11) | data formatting | bytes 2867200 | tf_op jit(solution)/shard_map/conv_general_dilated | solution.py:108
  29.5 2.5 %fusion.29 = (bf16[50,50,128]{2,1,0:T(8,128)(2,1)S(1)}, f32[50,50,128]{2,1,0:T(8,128)S(1)}) fusion(bf16[52,52,256]{2,1,0:T(8,128)(2,1)} %copy-done, pred[50]{0:T(512)(128)(4,1)S(1)} %and_or_fusion, f32[128]{0:T(128)S(1)} %copy-done.5, f32[50,1,56,128]{3,2,0,1:T(8,128)} %reshape.171), kind=kLoop, calls=%fused_computation.52 | loop fusion | flops 3840000 | bytes 3840562 | tf_op jit(solution)/shard_map/jit(_where)/select_n | solution.py:121
  32.8 0.5 fusion.11
  33.8 0.5 fusion.9
  34.8 0.5 fusion.7
  35.3 0.5 fusion.6
  35.8 0.5 fusion.5
  37.0 1.8 %collective-permute-start.6 = (f32[73792]{0:T(1024)S(1)}, f32[73792]{0:T(1024)S(1)}, u32[]{:S(2)}, u32[]{:S(2)}) collective-permute-start(f32[73792]{0:T(1024)S(1)} %dynamic_slice.19), channel_id=1, source_target_pairs={{0,8},{8,0},{16,24},{24,16},{32,40},{40,32},{48,56},{56,48},{64,72... | collective-permute-start | bytes 885512 | tf_op jit(solution)/shard_map/ppermute | solution.py:44
  38.8 0.9 fusion.54
  40.3 2.9 %collective-permute-start.7 = (f32[36896]{0:T(1024)S(1)}, f32[36896]{0:T(1024)S(1)}, u32[]{:S(2)}, u32[]{:S(2)}) collective-permute-start(f32[36896]{0:T(1024)S(1)} %dynamic_slice.21), channel_id=1, source_target_pairs={{0,1},{1,0},{2,3},{3,2},{4,5},{5,4},{6,7},{7,6},{8,9},{9,8},{10,11... | collective-permute-start | bytes 442760 | tf_op jit(solution)/shard_map/ppermute | solution.py:44
  43.2 0.9 convolution_add_fusion.1
  44.1 3.1 %collective-permute-done.7 = f32[36896]{0:T(1024)S(1)} collective-permute-done((f32[36896]{0:T(1024)S(1)}, f32[36896]{0:T(1024)S(1)}, u32[]{:S(2)}, u32[]{:S(2)}) %collective-permute-start.7) | collective-permute-done | bytes 147616 | tf_op jit(solution)/shard_map/ppermute | solution.py:44
  47.8 0.9 fusion.58
  48.7 2.0 %collective-permute-done.8 = f32[18448]{0:T(1024)S(1)} collective-permute-done((f32[18448]{0:T(1024)S(1)}, f32[18448]{0:T(1024)S(1)}, u32[]{:S(2)}, u32[]{:S(2)}) %collective-permute-start.8) | collective-permute-done | bytes 73824 | tf_op jit(solution)/shard_map/ppermute | solution.py:44
  50.8 2.7 %collective-permute-start.9 = (f32[18448]{0:T(1024)S(1)}, f32[18448]{0:T(1024)S(1)}, u32[]{:S(2)}, u32[]{:S(2)}) collective-permute-start(f32[18448]{0:T(1024)S(1)} %dynamic-slice_add_fusion.2), channel_id=1, source_target_pairs={{0,2},{1,3},{2,0},{3,1},{4,6},{5,7},{6,4},{7,5},{8,10},{9,11},{10,... | collective-permute-start | bytes 221384 | tf_op jit(solution)/shard_map/ppermute | solution.py:47
  53.5 0.9 convolution_add_fusion.3
  54.4 0.9 collective-permute-done.9
  55.3 3.0 %collective-permute-start.10 = (f32[18448]{0:T(1024)S(1)}, f32[18448]{0:T(1024)S(1)}, u32[]{:S(2)}, u32[]{:S(2)}) collective-permute-start(f32[18448]{0:T(1024)S(1)} %add.123), channel_id=1, source_target_pairs={{0,6},{1,7},{2,4},{3,5},{4,2},{5,3},{6,0},{7,1},{8,14},{9,15},{10,... | collective-permute-start | bytes 221384 | tf_op jit(solution)/shard_map/ppermute | solution.py:47
  58.3 0.9 fusion.15
  59.2 0.9 collective-permute-done.10
  60.1 0.7 collective-permute-start.11
  60.7 0.9 fusion.16
  61.6 3.3 %collective-permute-done.11 = f32[18448]{0:T(1024)S(1)} collective-permute-done((f32[18448]{0:T(1024)S(1)}, f32[18448]{0:T(1024)S(1)}, u32[]{:S(2)}, u32[]{:S(2)}) %collective-permute-start.11) | collective-permute-done | bytes 73824 | tf_op jit(solution)/shard_map/ppermute | solution.py:47
  64.9 2.5 %collective-permute-start.12 = (f32[18448]{0:T(1024)S(1)}, f32[18448]{0:T(1024)S(1)}, u32[]{:S(2)}, u32[]{:S(2)}) collective-permute-start(f32[18448]{0:T(1024)S(1)} %add.125), channel_id=1, source_target_pairs={{0,64},{8,72},{16,80},{24,88},{32,96},{40,104},{48,112},{56,120},{... | collective-permute-start | bytes 221384 | tf_op jit(solution)/shard_map/ppermute | solution.py:47
  67.5 2.6 %collective-permute-start.5 = (bf16[2,48,128]{2,1,0:T(8,128)(2,1)S(1)}, bf16[2,48,128]{2,1,0:T(8,128)(2,1)S(1)}, u32[]{:S(2)}, u32[]{:S(2)}) collective-permute-start(bf16[2,48,128]{2,1,0:T(8,128)(2,1)S(1)} %pad_maximum_fusion.1), channel_id=1, source_target_pairs={{0,128},{8,136},{16,144},{24,152},{32,160},{40,168},{48,176},{56,1... | collective-permute-start | bytes 73736 | tf_op jit(solution)/shard_map/ppermute | solution.py:27
  70.1 2.4 %collective-permute-start.13 = (f32[18448]{0:T(1024)S(1)}, f32[18448]{0:T(1024)S(1)}, u32[]{:S(2)}, u32[]{:S(2)}) collective-permute-start(f32[18448]{0:T(1024)S(1)} %add.126), channel_id=1, source_target_pairs={{0,192},{8,200},{16,208},{24,216},{32,224},{40,232},{48,240},{56,2... | collective-permute-start | bytes 221384 | tf_op jit(solution)/shard_map/ppermute | solution.py:47
  72.9 2.7 %collective-permute-done.13 = f32[18448]{0:T(1024)S(1)} collective-permute-done((f32[18448]{0:T(1024)S(1)}, f32[18448]{0:T(1024)S(1)}, u32[]{:S(2)}, u32[]{:S(2)}) %collective-permute-start.13) | collective-permute-done | bytes 73824 | tf_op jit(solution)/shard_map/ppermute | solution.py:47
  75.7 1.7 %collective-permute-start.14 = (f32[18448]{0:T(1024)S(1)}, f32[18448]{0:T(1024)S(1)}, u32[]{:S(2)}, u32[]{:S(2)}) collective-permute-start(f32[18448]{0:T(1024)S(1)} %add.127), channel_id=1, source_target_pairs={{0,32},{8,40},{16,48},{24,56},{32,0},{40,8},{48,16},{56,24},{64,96... | collective-permute-start | bytes 221384 | tf_op jit(solution)/shard_map/ppermute | solution.py:51
  77.3 1.1 %fusion.3 = bf16[48,48,128]{2,1,0:T(8,128)(2,1)} fusion(f32[50,50,128]{2,1,0:T(8,128)S(1)} %add_divide_fusion, f32[50,50,128]{2,1,0:T(8,128)S(1)} %get-tuple-element.53), kind=kLoop, calls=%fused_computation.12 | loop fusion | flops 589824 | bytes 2949120 | tf_op jit(solution)/shard_map/convert.4
  79.5 0.5 collective-permute-start.15
  80.1 1.8 %convolution_select_fusion = f32[48,8,7,128]{3,1,2,0:T(8,128)S(1)} fusion(bf16[3,3,128,128]{3,2,1,0:T(8,128)(2,1)S(1)} %copy-done.4, bf16[50,1,7,2,128]{4,2,3,0,1:T(8,128)(2,1)S(1)} %slice.272, bf16[50,1,8,7,128]{4,2,3,0,1:T(8,128)(2,1)S(1)} %copy.13, pred[8,7]{0,1:T(8,128)(4,1)S(1)} %copy-done.6), kind=kOutput, calls=%fused_computation.5 | convolution fusion | flops 795832320 | bytes 2567224 | tf_op jit(solution)/shard_map/conv_general_dilated | solution.py:124
  82.7 0.9 collective-permute-done.15
  83.8 9.9 %collective-permute-start.16 = (f32[73792]{0:T(1024)S(1)}, f32[73792]{0:T(1024)S(1)}, u32[]{:S(2)}, u32[]{:S(2)}) collective-permute-start(f32[73792]{0:T(1024)S(1)} %maximum_select_fusion.1), channel_id=1, source_target_pairs={{0,8},{8,0},{16,24},{24,16},{32,40},{40,32},{48,56},{56,48},{64,72... | collective-permute-start | bytes 885512 | tf_op jit(solution)/shard_map/ppermute | solution.py:51
  93.7 0.9 convert_element_type.21
  95.1 0.5 slice_multiply_fusion.2
  95.7 0.9 slice_multiply_fusion.1
  (70 shorter events, 7.9 us)
Async XLA Ops:
  0.6 1.2 %copy-start.2 = (bf16[48,48,128]{2,1,0:T(8,128)(2,1)S(1)}, bf16[48,48,128]{2,1,0:T(8,128)(2,1)}, u32[]{:S(2)}) copy-start(bf16[48,48,128]{2,1,0:T(8,128)(2,1)} %param.15) | copy-start | bytes 1769476
  2.1 5.4 %collective-permute-start = (bf16[48,2,256]{2,1,0:T(2,128)(2,1)S(1)}, bf16[48,2,256]{2,1,0:T(2,128)(2,1)S(1)}, u32[]{:S(2)}, u32[]{:S(2)}) collective-permute-start(bf16[48,2,256]{2,1,0:T(2,128)(2,1)S(1)} %get-tuple-element.57), channel_id=1, source_target_pairs={{0,8},{8,16},{16,24},{24,32},{32,40},{40,48},{48,56},{56,64},{64,7... | collective-permute-start | bytes 147464 | tf_op jit(solution)/shard_map/ppermute | solution.py:15
  6.3 5.0 %collective-permute-start.1 = (bf16[48,2,256]{2,1,0:T(2,128)(2,1)S(1)}, bf16[48,2,256]{2,1,0:T(2,128)(2,1)S(1)}, u32[]{:S(2)}, u32[]{:S(2)}) collective-permute-start(bf16[48,2,256]{2,1,0:T(2,128)(2,1)S(1)} %get-tuple-element.58), channel_id=1, source_target_pairs={{8,0},{16,8},{24,16},{32,24},{40,32},{48,40},{56,48},{64,56},{72,6... | collective-permute-start | bytes 147464 | tf_op jit(solution)/shard_map/ppermute | solution.py:17
  11.4 10.8 %collective-permute-start.2 = (bf16[2,52,256]{2,1,0:T(8,128)(2,1)S(1)}, bf16[2,52,256]{2,1,0:T(8,128)(2,1)S(1)}, u32[]{:S(2)}, u32[]{:S(2)}) collective-permute-start(bf16[2,52,256]{2,1,0:T(8,128)(2,1)S(1)} %get-tuple-element.59), channel_id=1, source_target_pairs={{0,1},{1,2},{2,3},{3,4},{4,5},{5,6},{6,7},{8,9},{9,10},{10,11},{11... | collective-permute-start | bytes 159752 | tf_op jit(solution)/shard_map/ppermute | solution.py:15
  13.6 8.6 %collective-permute-start.3 = (bf16[2,52,256]{2,1,0:T(8,128)(2,1)S(1)}, bf16[2,52,256]{2,1,0:T(8,128)(2,1)S(1)}, u32[]{:S(2)}, u32[]{:S(2)}) collective-permute-start(bf16[2,52,256]{2,1,0:T(8,128)(2,1)S(1)} %get-tuple-element.60), channel_id=1, source_target_pairs={{1,0},{2,1},{3,2},{4,3},{5,4},{6,5},{7,6},{9,8},{10,9},{11,10},{12... | collective-permute-start | bytes 159752 | tf_op jit(solution)/shard_map/ppermute | solution.py:17
  15.0 8.9 %collective-permute-start.4 = (bf16[2,52,256]{2,1,0:T(8,128)(2,1)S(1)}, bf16[2,52,256]{2,1,0:T(8,128)(2,1)S(1)}, u32[]{:S(2)}, u32[]{:S(2)}) collective-permute-start(bf16[2,52,256]{2,1,0:T(8,128)(2,1)S(1)} %get-tuple-element.54), channel_id=1, source_target_pairs={{0,128},{8,136},{16,144},{24,152},{32,160},{40,168},{48,176},{56,1... | collective-permute-start | bytes 159752 | tf_op jit(solution)/shard_map/ppermute | solution.py:27
  23.9 1.1 %copy-start = (bf16[52,52,256]{2,1,0:T(8,128)(2,1)}, bf16[52,52,256]{2,1,0:T(8,128)(2,1)S(1)}, u32[]{:S(2)}) copy-start(bf16[52,52,256]{2,1,0:T(8,128)(2,1)S(1)} %fusion.66) | copy-start | bytes 4153348
  25.0 1.0 copy-start.3
  25.0 1.0 copy-start.7
  28.3 1.3 %copy-start.5 = (f32[128]{0:T(128)S(1)}, f32[128]{0:T(128)}, u32[]{:S(2)}) copy-start(f32[128]{0:T(128)} %param.14) | copy-start | bytes 1540
  29.5 2.8 %copy-start.1 = (bf16[52,52,256]{2,1,0:T(8,128)(2,1)S(1)}, bf16[52,52,256]{2,1,0:T(8,128)(2,1)}, u32[]{:S(2)}) copy-start(bf16[52,52,256]{2,1,0:T(8,128)(2,1)} %copy-done) | copy-start | bytes 4153348
  37.0 3.0 %collective-permute-start.6 = (f32[73792]{0:T(1024)S(1)}, f32[73792]{0:T(1024)S(1)}, u32[]{:S(2)}, u32[]{:S(2)}) collective-permute-start(f32[73792]{0:T(1024)S(1)} %dynamic_slice.19), channel_id=1, source_target_pairs={{0,8},{8,0},{16,24},{24,16},{32,40},{40,32},{48,56},{56,48},{64,72... | collective-permute-start | bytes 885512 | tf_op jit(solution)/shard_map/ppermute | solution.py:44
  40.3 6.8 %collective-permute-start.7 = (f32[36896]{0:T(1024)S(1)}, f32[36896]{0:T(1024)S(1)}, u32[]{:S(2)}, u32[]{:S(2)}) collective-permute-start(f32[36896]{0:T(1024)S(1)} %dynamic_slice.21), channel_id=1, source_target_pairs={{0,1},{1,0},{2,3},{3,2},{4,5},{5,4},{6,7},{7,6},{8,9},{9,8},{10,11... | collective-permute-start | bytes 442760 | tf_op jit(solution)/shard_map/ppermute | solution.py:44
  47.3 3.3 %collective-permute-start.8 = (f32[18448]{0:T(1024)S(1)}, f32[18448]{0:T(1024)S(1)}, u32[]{:S(2)}, u32[]{:S(2)}) collective-permute-start(f32[18448]{0:T(1024)S(1)} %dynamic_slice.23), channel_id=1, source_target_pairs={{0,32},{8,40},{16,48},{24,56},{32,0},{40,8},{48,16},{56,24},{64,96... | collective-permute-start | bytes 221384 | tf_op jit(solution)/shard_map/ppermute | solution.py:44
  50.8 4.5 %collective-permute-start.9 = (f32[18448]{0:T(1024)S(1)}, f32[18448]{0:T(1024)S(1)}, u32[]{:S(2)}, u32[]{:S(2)}) collective-permute-start(f32[18448]{0:T(1024)S(1)} %dynamic-slice_add_fusion.2), channel_id=1, source_target_pairs={{0,2},{1,3},{2,0},{3,1},{4,6},{5,7},{6,4},{7,5},{8,10},{9,11},{10,... | collective-permute-start | bytes 221384 | tf_op jit(solution)/shard_map/ppermute | solution.py:47
  55.3 4.8 %collective-permute-start.10 = (f32[18448]{0:T(1024)S(1)}, f32[18448]{0:T(1024)S(1)}, u32[]{:S(2)}, u32[]{:S(2)}) collective-permute-start(f32[18448]{0:T(1024)S(1)} %add.123), channel_id=1, source_target_pairs={{0,6},{1,7},{2,4},{3,5},{4,2},{5,3},{6,0},{7,1},{8,14},{9,15},{10,... | collective-permute-start | bytes 221384 | tf_op jit(solution)/shard_map/ppermute | solution.py:47
  60.1 4.8 %collective-permute-start.11 = (f32[18448]{0:T(1024)S(1)}, f32[18448]{0:T(1024)S(1)}, u32[]{:S(2)}, u32[]{:S(2)}) collective-permute-start(f32[18448]{0:T(1024)S(1)} %add.124), channel_id=1, source_target_pairs={{0,16},{8,24},{16,0},{24,8},{32,48},{40,56},{48,32},{56,40},{64,80... | collective-permute-start | bytes 221384 | tf_op jit(solution)/shard_map/ppermute | solution.py:47
  64.9 5.2 %collective-permute-start.12 = (f32[18448]{0:T(1024)S(1)}, f32[18448]{0:T(1024)S(1)}, u32[]{:S(2)}, u32[]{:S(2)}) collective-permute-start(f32[18448]{0:T(1024)S(1)} %add.125), channel_id=1, source_target_pairs={{0,64},{8,72},{16,80},{24,88},{32,96},{40,104},{48,112},{56,120},{... | collective-permute-start | bytes 221384 | tf_op jit(solution)/shard_map/ppermute | solution.py:47
  67.5 15.3 %collective-permute-start.5 = (bf16[2,48,128]{2,1,0:T(8,128)(2,1)S(1)}, bf16[2,48,128]{2,1,0:T(8,128)(2,1)S(1)}, u32[]{:S(2)}, u32[]{:S(2)}) collective-permute-start(bf16[2,48,128]{2,1,0:T(8,128)(2,1)S(1)} %pad_maximum_fusion.1), channel_id=1, source_target_pairs={{0,128},{8,136},{16,144},{24,152},{32,160},{40,168},{48,176},{56,1... | collective-permute-start | bytes 73736 | tf_op jit(solution)/shard_map/ppermute | solution.py:27
  70.1 5.5 %collective-permute-start.13 = (f32[18448]{0:T(1024)S(1)}, f32[18448]{0:T(1024)S(1)}, u32[]{:S(2)}, u32[]{:S(2)}) collective-permute-start(f32[18448]{0:T(1024)S(1)} %add.126), channel_id=1, source_target_pairs={{0,192},{8,200},{16,208},{24,216},{32,224},{40,232},{48,240},{56,2... | collective-permute-start | bytes 221384 | tf_op jit(solution)/shard_map/ppermute | solution.py:47
  75.7 3.8 %collective-permute-start.14 = (f32[18448]{0:T(1024)S(1)}, f32[18448]{0:T(1024)S(1)}, u32[]{:S(2)}, u32[]{:S(2)}) collective-permute-start(f32[18448]{0:T(1024)S(1)} %add.127), channel_id=1, source_target_pairs={{0,32},{8,40},{16,48},{24,56},{32,0},{40,8},{48,16},{56,24},{64,96... | collective-permute-start | bytes 221384 | tf_op jit(solution)/shard_map/ppermute | solution.py:51
  78.8 1.3 %copy-start.4 = (bf16[3,3,128,128]{3,2,1,0:T(8,128)(2,1)S(1)}, bf16[3,3,128,128]{3,2,1,0:T(8,128)(2,1)}, u32[]{:S(2)}) copy-start(bf16[3,3,128,128]{3,2,1,0:T(8,128)(2,1)} %param.13) | copy-start | bytes 884740
  78.8 1.3 %copy-start.6 = (pred[8,7]{0,1:T(8,128)(4,1)S(1)}, pred[8,7]{0,1:T(8,128)(4,1)}, u32[]{:S(2)}) copy-start(pred[8,7]{0,1:T(8,128)(4,1)} %constant.203) | copy-start | bytes 172
  79.5 4.1 %collective-permute-start.15 = (f32[36896]{0:T(1024)S(1)}, f32[36896]{0:T(1024)S(1)}, u32[]{:S(2)}, u32[]{:S(2)}) collective-permute-start(f32[36896]{0:T(1024)S(1)} %maximum_select_fusion.2), channel_id=1, source_target_pairs={{0,1},{1,0},{2,3},{3,2},{4,5},{5,4},{6,7},{7,6},{8,9},{9,8},{10,11... | collective-permute-start | bytes 442760 | tf_op jit(solution)/shard_map/ppermute | solution.py:51
  83.8 11.1 %collective-permute-start.16 = (f32[73792]{0:T(1024)S(1)}, f32[73792]{0:T(1024)S(1)}, u32[]{:S(2)}, u32[]{:S(2)}) collective-permute-start(f32[73792]{0:T(1024)S(1)} %maximum_select_fusion.1), channel_id=1, source_target_pairs={{0,8},{8,0},{16,24},{24,16},{32,40},{40,32},{48,56},{56,48},{64,72... | collective-permute-start | bytes 885512 | tf_op jit(solution)/shard_map/ppermute | solution.py:51
